TPU v7x, 32 devices: a whole 2x2x4 slice. The times are simulated.
32 devices in a mesh: ctx: 8 (over z, x), head: 4 (over y, core).
Axes of the slice: x: 2, y: 2, z: 4, core: 2. Of those that a mesh axis runs over, the one named last changes fastest.
Arguments:
- query_raw: bfloat16 [8192, 4096], P('ctx', 'head'), may hold values from -180 to 180
- key_raw: bfloat16 [8192, 2048], P('ctx', 'head'), may hold values from -180 to 180
- value_proj: bfloat16 [8192, 2048], P('ctx', 'head'), may hold values from -6 to 6
- query_gain: float32 [128], replicated, may hold values from 0.1 to 1.9
- key_gain: float32 [128], replicated, may hold values from 0.1 to 1.9
- out_grad: bfloat16 [8192, 4096], P('ctx', 'head'), may hold values from -9 to 9
- doc_lengths: int32 [16], replicated, may hold values from 1 to 2048, 8192 in all
Outputs:
- query_grad: bfloat16 [8192, 4096], P('ctx', 'head')
- key_grad: bfloat16 [8192, 2048], P('ctx', 'head')
- value_grad: bfloat16 [8192, 2048], P('ctx', 'head')
- query_gain_grad: float32 [128], replicated
- key_gain_grad: float32 [128], replicated
All inputs are finite; a program needn't handle non-finite values.
Results may differ from a plain program's by a relative error of at most 0.0083.
Values may be sent and summed in bfloat16 or wider, within the bound.
No kernel may reach another device: no remote copies, remote signals or barrier semaphores. Data moves between devices by JAX's collectives and lax.ppermute only.
A program may use at most 192 MiB of HBM per device.

v0:
```python
import math

import jax
import jax.numpy as jnp
from jax import lax
from jax.sharding import PartitionSpec as P

WINDOW = 1024
QUERY_SCALAR = 168


EPS = 1e-06
FAR = -(2**30)


def shifted(value, axis, steps):
    count = lax.axis_size(axis)
    leading, last = (max(0, -steps), min(count, count - steps))
    return lax.ppermute(value, axis, [(source, source + steps) for source in range(leading, last)])


def norm_rows(raw_rows, head_count):
    values = raw_rows.astype(jnp.float32).reshape(raw_rows.shape[0], head_count, -1)
    inverse = lax.rsqrt(jnp.mean(values * values, axis=-1, keepdims=True) + EPS)
    return (values * inverse, inverse)


def norm_back(raw_rows, gain_vec, head_count, upstream):
    scaled, inverse = norm_rows(raw_rows, head_count)
    incoming = upstream.reshape(scaled.shape)
    weighted = incoming * gain_vec
    inner_sum = jnp.mean(weighted * scaled, axis=-1, keepdims=True)
    result = inverse * (weighted - scaled * inner_sum)
    return (result.reshape(raw_rows.shape), jnp.sum(incoming * scaled, axis=(0, 1)))


def doc_index(positions, doc_ends):
    return jnp.sum((positions[:, None] >= doc_ends[None, :]).astype(jnp.int32), axis=1)


def tile_live(query_pos, query_doc, key_pos, key_doc):
    return (
        (key_pos[None, :] <= query_pos[:, None])
        & (query_pos[:, None] - key_pos[None, :] < WINDOW)
        & (query_doc[:, None] == key_doc[None, :])
    )


def take_rows(array, first, count):
    return lax.dynamic_slice_in_dim(array, first, count, 0)


def stats_pass(query_norm, grad_rows, key_set, own_pos, own_doc):
    keys_all, vals_all, key_pos, key_doc = key_set
    query_rows, key_heads, group_size, head_dim = query_norm.shape
    block_rows = math.gcd(512, WINDOW)
    tile_count = WINDOW // block_rows + 1
    score_scale = QUERY_SCALAR ** (-0.5)

    def stats_block(block_num):
        query_first = block_num * block_rows
        query_tile = take_rows(query_norm, query_first, block_rows)
        query_pos = take_rows(own_pos, query_first, block_rows)
        query_doc = take_rows(own_doc, query_first, block_rows)
        totals = jnp.zeros((key_heads, group_size, block_rows), jnp.float32)
        numerator = jnp.zeros((block_rows, key_heads, group_size, head_dim), jnp.float32)
        for tile_num in range(tile_count):
            key_first = query_first + tile_num * block_rows
            key_tile = take_rows(keys_all, key_first, block_rows)
            value_tile = take_rows(vals_all, key_first, block_rows)
            live_mask = tile_live(
                query_pos,
                query_doc,
                take_rows(key_pos, key_first, block_rows),
                take_rows(key_doc, key_first, block_rows),
            )

            def stats_compute(
                query_tile=query_tile, key_tile=key_tile, value_tile=value_tile, live_mask=live_mask
            ):
                scores = (
                    jnp.einsum(
                        "qhgd,khd->hgqk", query_tile, key_tile, preferred_element_type=jnp.float32
                    )
                    * score_scale
                )
                exp_scores = jnp.where(live_mask, jnp.exp(scores), 0.0)
                return (
                    jnp.sum(exp_scores, axis=-1),
                    jnp.einsum(
                        "hgqk,khd->qhgd",
                        exp_scores.astype(jnp.bfloat16),
                        value_tile,
                        preferred_element_type=jnp.float32,
                    ),
                )

            pieces = stats_compute()
            totals = totals + pieces[0]
            numerator = numerator + pieces[1]
        row_totals = jnp.transpose(totals, (2, 0, 1))
        attn_out = numerator / row_totals[..., None]
        grad_tile = take_rows(grad_rows, query_first, block_rows).astype(jnp.float32)
        return (jnp.log(row_totals), jnp.sum(grad_tile * attn_out, axis=-1))

    log_blocks, delta_blocks = lax.map(
        stats_block, jnp.arange(query_rows // block_rows, dtype=jnp.int32)
    )
    return (
        log_blocks.reshape(query_rows, key_heads, group_size),
        delta_blocks.reshape(query_rows, key_heads, group_size),
    )


def grad_pass(query_set, key_set, tile_count):
    query_norm, grad_rows, log_sums, row_delta, own_pos, own_doc = query_set
    keys_all, vals_all, key_pos, key_doc = key_set
    query_rows, key_heads, group_size, head_dim = query_norm.shape
    block_rows = math.gcd(512, WINDOW)
    score_scale = QUERY_SCALAR ** (-0.5)
    query_shape = (block_rows, key_heads, group_size, head_dim)

    def block_step(carried, block_num):
        key_acc, val_acc = carried
        query_first = block_num * block_rows
        query_tile = take_rows(query_norm, query_first, block_rows)
        grad_tile = take_rows(grad_rows, query_first, block_rows)
        log_here = jnp.transpose(take_rows(log_sums, query_first, block_rows), (1, 2, 0))
        delta_here = jnp.transpose(take_rows(row_delta, query_first, block_rows), (1, 2, 0))
        query_pos = take_rows(own_pos, query_first, block_rows)
        query_doc = take_rows(own_doc, query_first, block_rows)
        query_acc = jnp.zeros(query_shape, jnp.float32)
        for tile_num in range(tile_count):
            key_first = query_first + tile_num * block_rows
            key_tile = take_rows(keys_all, key_first, block_rows)
            value_tile = take_rows(vals_all, key_first, block_rows)
            live_mask = tile_live(
                query_pos,
                query_doc,
                take_rows(key_pos, key_first, block_rows),
                take_rows(key_doc, key_first, block_rows),
            )

            def block_compute(
                query_tile=query_tile,
                grad_tile=grad_tile,
                key_tile=key_tile,
                value_tile=value_tile,
                live_mask=live_mask,
            ):
                scores = (
                    jnp.einsum(
                        "qhgd,khd->hgqk", query_tile, key_tile, preferred_element_type=jnp.float32
                    )
                    * score_scale
                )
                weights = jnp.where(live_mask, jnp.exp(scores - log_here[..., None]), 0.0)
                d_weights = jnp.einsum(
                    "qhgd,khd->hgqk", grad_tile, value_tile, preferred_element_type=jnp.float32
                )
                d_scores = (weights * (d_weights - delta_here[..., None])).astype(jnp.bfloat16)
                outputs = []
                outputs.append(
                    score_scale
                    * jnp.einsum(
                        "hgqk,khd->qhgd", d_scores, key_tile, preferred_element_type=jnp.float32
                    )
                )
                outputs.append(
                    score_scale
                    * jnp.einsum(
                        "hgqk,qhgd->khd", d_scores, query_tile, preferred_element_type=jnp.float32
                    )
                )
                outputs.append(
                    jnp.einsum(
                        "hgqk,qhgd->khd",
                        weights.astype(jnp.bfloat16),
                        grad_tile,
                        preferred_element_type=jnp.float32,
                    )
                )
                return tuple(outputs)

            pieces = block_compute()
            slot_num = 0
            query_acc = query_acc + pieces[0]
            slot_num = 1
            key_acc = lax.dynamic_update_slice_in_dim(
                key_acc, take_rows(key_acc, key_first, block_rows) + pieces[slot_num], key_first, 0
            )
            val_acc = lax.dynamic_update_slice_in_dim(
                val_acc,
                take_rows(val_acc, key_first, block_rows) + pieces[slot_num + 1],
                key_first,
                0,
            )
        return ((key_acc, val_acc), query_acc)

    start_acc = (
        jnp.zeros((keys_all.shape[0], key_heads, head_dim), jnp.float32),
        jnp.zeros((keys_all.shape[0], key_heads, head_dim), jnp.float32),
    )
    (key_acc, val_acc), query_blocks = lax.scan(
        block_step, start_acc, jnp.arange(query_rows // block_rows, dtype=jnp.int32)
    )
    return (query_blocks.reshape(query_rows, key_heads, group_size, head_dim), key_acc, val_acc)


def per_device(query_raw, key_raw, value_proj, query_gain, key_gain, out_grad, doc_lengths):
    tok_rows = query_raw.shape[0]
    head_dim = query_gain.shape[0]
    query_heads = query_raw.shape[1] // head_dim
    key_heads = key_raw.shape[1] // head_dim
    group_size = query_heads // key_heads
    block_rows = math.gcd(512, WINDOW)
    tile_count = WINDOW // block_rows + 1
    first_pos = lax.axis_index("ctx") * tok_rows
    doc_ends = jnp.cumsum(doc_lengths)
    own_pos = first_pos + jnp.arange(tok_rows, dtype=jnp.int32)
    own_doc = doc_index(own_pos, doc_ends)
    halo_raw = first_pos - WINDOW + jnp.arange(WINDOW, dtype=jnp.int32)
    halo_doc = doc_index(halo_raw, doc_ends)
    halo_pos = jnp.where(halo_raw >= 0, halo_raw, FAR)
    query_hat, query_inv = norm_rows(query_raw, query_heads)
    query_norm = (
        (query_hat * query_gain)
        .astype(jnp.bfloat16)
        .reshape(tok_rows, key_heads, group_size, head_dim)
    )
    key_hat, key_inv = norm_rows(key_raw, key_heads)
    key_norm = (key_hat * key_gain).astype(jnp.bfloat16)
    value_rows = value_proj.reshape(tok_rows, key_heads, head_dim)
    grad_rows = out_grad.reshape(tok_rows, key_heads, group_size, head_dim)
    halo_keys, halo_vals = shifted((key_norm, value_rows), "ctx", 1)
    keys_all = jnp.concatenate([halo_keys, key_norm], axis=0)
    vals_all = jnp.concatenate([halo_vals, value_rows], axis=0)
    all_doc = jnp.concatenate([halo_doc, own_doc])
    full_set = (keys_all, vals_all, jnp.concatenate([halo_pos, own_pos]), all_doc)
    log_sums, row_delta = stats_pass(query_norm, grad_rows, full_set, own_pos, own_doc)
    query_set = (query_norm, grad_rows, log_sums, row_delta, own_pos, own_doc)
    query_acc, key_acc, val_acc = grad_pass(query_set, full_set, tile_count)
    back_keys, back_vals = shifted((key_acc[:WINDOW], val_acc[:WINDOW]), "ctx", -1)
    key_own = jnp.concatenate([key_acc[WINDOW:tok_rows], key_acc[tok_rows:] + back_keys], axis=0)
    val_own = jnp.concatenate([val_acc[WINDOW:tok_rows], val_acc[tok_rows:] + back_vals], axis=0)
    query_grad, query_part = norm_back(
        query_raw, query_gain, query_heads, query_acc.reshape(tok_rows, query_heads, head_dim)
    )
    key_grad, key_part = norm_back(key_raw, key_gain, key_heads, key_own)
    query_gain_grad, key_gain_grad = lax.psum((query_part, key_part), ("ctx", "head"))
    value_grad = val_own.reshape(tok_rows, key_heads * head_dim).astype(jnp.bfloat16)
    return (
        query_grad.astype(jnp.bfloat16),
        key_grad.astype(jnp.bfloat16),
        value_grad,
        query_gain_grad,
        key_gain_grad,
    )


def solution(mesh):
    return jax.shard_map(
        per_device,
        mesh=mesh,
        in_specs=(
            P("ctx", "head"),
            P("ctx", "head"),
            P("ctx", "head"),
            P(),
            P(),
            P("ctx", "head"),
            P(),
        ),
        out_specs=(P("ctx", "head"), P("ctx", "head"), P("ctx", "head"), P(), P()),
        check_vma=False,
    )
```

profile of v0, /device:TPU:0, one launch (start us, length us, event | category | flops | bytes accessed | tf_op | source)
XLA Modules:
  0.0 379.6 jit_solution(4857047358779652456)
XLA Ops:
  2.1 5.9 %collective-permute-start.1 = (bf16[1024,4,128]{0,2,1:T(8,128)(2,1)S(1)}, bf16[1024,4,128]{0,2,1:T(8,128)(2,1)}, u32[]{:S(2)}, u32[]{:S(2)}) collective-permute-start(bf16[1024,4,128]{0,2,1:T(8,128)(2,1)S(1)} %bitcast.431), channel_id=1, source_target_pairs={{0,4},{4,8},{8,12},{12,16},{16,20},{20,24},{24,28},{1,5},{5,9},{9,... | collective-permute-start | bytes 3145736 | tf_op jit(solution)/shard_map/ppermute | solution.py:19
  26.2 5.2 %reshape.155 = f32[1024,4,2,128]{3,2,1,0:T(2,128)} reshape(bf16[1024,1024]{1,0:T(8,128)(2,1)S(1)} %copy-done.9) | data formatting | bytes 6291456 | tf_op jit(solution)/shard_map/reshape | solution.py:23
  39.6 12.4 %collective-permute-done = bf16[1024,4,128]{0,2,1:T(8,128)(2,1)} collective-permute-done((bf16[1024,4,128]{0,2,1:T(8,128)(2,1)}, bf16[1024,4,128]{0,2,1:T(8,128)(2,1)}, u32[]{:S(2)}, u32[]{:S(2)}) %collective-permute-start) | collective-permute-done | bytes 1048608 | tf_op jit(solution)/shard_map/ppermute | solution.py:19
  65.7 62.3 %while.30 = (s32[]{:T(128)}, f32[2,512,4,2]{1,0,3,2:T(2,128)S(1)}, f32[2,512,4,2]{1,0,3,2:T(2,128)S(1)}, s32[2]{0:T(128)S(1)}, s32[2048]{0:T(1024)S(1)}, /*index...) while((s32[]{:T(128)}, f32[2,512,4,2]{1,0,3,2:T(2,128)S(1)}, ...), condition=%wide.region_10.11_spmd, body=%wide.region_5.10_spmd.sunk | while | flops 3266830336 | bytes 127484440 | solution.py:106
  75.9 5.2 %fusion.270 = (f32[4,2,512]{2,1,0:T(2,128)S(1)}, f32[4,512,512,2]{2,1,3,0:T(8,128)}) fusion(pred[512,512]{0,1:T(8,128)(4,1)S(1)} %get-tuple-element.794, bf16[1024,4,2,128]{3,0,2,1:T(8,128)(2,1)S(1)} %get-tuple-element.878, s32[]{:T(128)S(6)} %select_n.211, bf16[2048,4,128]{2,0,1:T(8,128)(2,1)S(1)} %copy-done.3, s32[]{:T(128)S(6)} %select_n.214), kind=kOutput, calls=%fused_computation.4.clone.1 | convolution fusion | flops 543158272 | bytes 10240008 | tf_op jit(solution)/shard_map/while/body/eval_jaxpr/qhgd,khd->hgqk/dot_general | solution.py:82
  81.1 5.2 %fusion.271 = (f32[4,2,512]{2,1,0:T(2,128)S(1)}, f32[4,512,512,2]{2,1,3,0:T(8,128)}) fusion(pred[512,512]{0,1:T(8,128)(4,1)S(1)} %get-tuple-element.796, bf16[1024,4,2,128]{3,0,2,1:T(8,128)(2,1)S(1)} %get-tuple-element.878, s32[]{:T(128)S(6)} %select_n.211, bf16[2048,4,128]{2,0,1:T(8,128)(2,1)S(1)} %copy-done.3, s32[]{:T(128)S(6)} %select_n.212), kind=kOutput, calls=%fused_computation.6.clone.1 | convolution fusion | flops 543158272 | bytes 10240008 | tf_op jit(solution)/shard_map/while/body/eval_jaxpr/qhgd,khd->hgqk/dot_general | solution.py:82
  86.5 5.4 %fusion.273 = f32[4,128,2,512]{3,1,2,0:T(8,128)S(1)} fusion(f32[4,512,512,2]{2,1,3,0:T(8,128)} %get-tuple-element.800, pred[512,512]{0,1:T(8,128)(4,1)S(1)} %get-tuple-element.796, bf16[2048,4,128]{0,2,1:T(8,128)(2,1)} %get-tuple-element.880, s32[]{:T(128)S(6)} %select_n.212), kind=kOutput, calls=%fused_computation.10.clone.1 | convolution fusion | flops 543162368 | bytes 11272196 | tf_op jit(solution)/shard_map/while/body/eval_jaxpr/hgqk,khd->qhgd/dot_general | solution.py:90
  106.9 5.2 %fusion.270 = (f32[4,2,512]{2,1,0:T(2,128)S(1)}, f32[4,512,512,2]{2,1,3,0:T(8,128)}) fusion(pred[512,512]{0,1:T(8,128)(4,1)S(1)} %get-tuple-element.794, bf16[1024,4,2,128]{3,0,2,1:T(8,128)(2,1)S(1)} %get-tuple-element.878, s32[]{:T(128)S(6)} %select_n.211, bf16[2048,4,128]{2,0,1:T(8,128)(2,1)S(1)} %copy-done.3, s32[]{:T(128)S(6)} %select_n.214), kind=kOutput, calls=%fused_computation.4.clone.1 | convolution fusion | flops 543158272 | bytes 10240008 | tf_op jit(solution)/shard_map/while/body/eval_jaxpr/qhgd,khd->hgqk/dot_general | solution.py:82
  112.1 5.2 %fusion.271 = (f32[4,2,512]{2,1,0:T(2,128)S(1)}, f32[4,512,512,2]{2,1,3,0:T(8,128)}) fusion(pred[512,512]{0,1:T(8,128)(4,1)S(1)} %get-tuple-element.796, bf16[1024,4,2,128]{3,0,2,1:T(8,128)(2,1)S(1)} %get-tuple-element.878, s32[]{:T(128)S(6)} %select_n.211, bf16[2048,4,128]{2,0,1:T(8,128)(2,1)S(1)} %copy-done.3, s32[]{:T(128)S(6)} %select_n.212), kind=kOutput, calls=%fused_computation.6.clone.1 | convolution fusion | flops 543158272 | bytes 10240008 | tf_op jit(solution)/shard_map/while/body/eval_jaxpr/qhgd,khd->hgqk/dot_general | solution.py:82
  117.5 5.4 %fusion.273 = f32[4,128,2,512]{3,1,2,0:T(8,128)S(1)} fusion(f32[4,512,512,2]{2,1,3,0:T(8,128)} %get-tuple-element.800, pred[512,512]{0,1:T(8,128)(4,1)S(1)} %get-tuple-element.796, bf16[2048,4,128]{0,2,1:T(8,128)(2,1)} %get-tuple-element.880, s32[]{:T(128)S(6)} %select_n.212), kind=kOutput, calls=%fused_computation.10.clone.1 | convolution fusion | flops 543162368 | bytes 11272196 | tf_op jit(solution)/shard_map/while/body/eval_jaxpr/hgqk,khd->qhgd/dot_general | solution.py:90
  133.1 103.0 %while.31 = (s32[]{:T(128)}, f32[2048,4,128]{0,2,1:T(8,128)}, f32[2048,4,128]{0,2,1:T(8,128)}, f32[2,512,4,2,128]{1,4,3,2,0:T(8,128)}, s32[2]{0:T(128)S(1)}, /*i...) while((s32[]{:T(128)}, f32[2048,4,128]{0,2,1:T(8,128)}, ...), condition=%wide.region_12.13_spmd, body=%wide.region_11.12_spmd.sunk | while | flops 8124628992 | bytes 265290480 | solution.py:204
  154.7 4.5 %fusion.316 = f32[2048,4,128]{0,2,1:T(8,128)} fusion(f32[2048,4,128]{0,2,1:T(8,128)} %get-tuple-element.914, s32[]{:T(128)S(6)} %select_n.221, f32[4,512,512,2]{2,1,3,0:T(8,128)S(1)} %fusion.305, f32[4,2,512]{2,1,0:T(2,128)S(1)} %get-tuple-element.819, pred[512,512]{0,1:T(8,128)(4,1)S(1)} %get-tuple-element.826, ...), kind=kOutput, calls=%fused_computation.116.clone.1 | convolution fusion | flops 545521664 | bytes 11812872 | tf_op jit(solution)/shard_map/while/body/eval_jaxpr/hgqk,qhgd->khd/dot_general | solution.py:176
  174.0 4.3 %fusion.318 = f32[2048,4,128]{0,2,1:T(8,128)} fusion(f32[2048,4,128]{0,2,1:T(8,128)} %fusion.317, s32[]{:T(128)S(6)} %select_n.223, f32[4,512,512,2]{2,1,3,0:T(8,128)S(1)} %fusion.313, f32[4,2,512]{2,1,0:T(2,128)S(1)} %get-tuple-element.819, pred[512,512]{0,1:T(8,128)(4,1)S(1)} %get-tuple-element.828, bf16[1024,4,2,128]{0,3,2,1:T(8,128)(2,1)S(1)} %copy-done.18, ...), kind=kOutput, calls=%fused_computation.112.clone.1 | convolution fusion | flops 545521664 | bytes 11812872 | tf_op jit(solution)/shard_map/while/body/eval_jaxpr/hgqk,qhgd->khd/dot_general | solution.py:176
  199.3 4.4 %fusion.316 = f32[2048,4,128]{0,2,1:T(8,128)} fusion(f32[2048,4,128]{0,2,1:T(8,128)} %get-tuple-element.914, s32[]{:T(128)S(6)} %select_n.221, f32[4,512,512,2]{2,1,3,0:T(8,128)S(1)} %fusion.305, f32[4,2,512]{2,1,0:T(2,128)S(1)} %get-tuple-element.819, pred[512,512]{0,1:T(8,128)(4,1)S(1)} %get-tuple-element.826, ...), kind=kOutput, calls=%fused_computation.116.clone.1 | convolution fusion | flops 545521664 | bytes 11812872 | tf_op jit(solution)/shard_map/while/body/eval_jaxpr/hgqk,qhgd->khd/dot_general | solution.py:176
  214.3 4.4 %fusion.317 = f32[2048,4,128]{0,2,1:T(8,128)} fusion(f32[2048,4,128]{0,2,1:T(8,128)} %fusion.316, s32[]{:T(128)S(6)} %select_n.224, f32[4,512,512,2]{2,1,3,0:T(8,128)S(1)} %fusion.310, f32[4,2,512]{2,1,0:T(2,128)S(1)} %get-tuple-element.819, pred[512,512]{0,1:T(8,128)(4,1)S(1)} %get-tuple-element.827, bf16[1024,4,2,128]{0,3,2,1:T(8,128)(2,1)S(1)} %copy-done.18, ...), kind=kOutput, calls=%fused_computation.114.clone.1 | convolution fusion | flops 545521664 | bytes 11812872 | tf_op jit(solution)/shard_map/while/body/eval_jaxpr/hgqk,qhgd->khd/dot_general | solution.py:176
  218.7 4.3 %fusion.318 = f32[2048,4,128]{0,2,1:T(8,128)} fusion(f32[2048,4,128]{0,2,1:T(8,128)} %fusion.317, s32[]{:T(128)S(6)} %select_n.223, f32[4,512,512,2]{2,1,3,0:T(8,128)S(1)} %fusion.313, f32[4,2,512]{2,1,0:T(2,128)S(1)} %get-tuple-element.819, pred[512,512]{0,1:T(8,128)(4,1)S(1)} %get-tuple-element.828, bf16[1024,4,2,128]{0,3,2,1:T(8,128)(2,1)S(1)} %copy-done.18, ...), kind=kOutput, calls=%fused_computation.112.clone.1 | convolution fusion | flops 545521664 | bytes 11812872 | tf_op jit(solution)/shard_map/while/body/eval_jaxpr/hgqk,qhgd->khd/dot_general | solution.py:176
  241.0 5.2 %reshape.164 = f32[2,512,4,2,128]{4,3,2,1,0:T(2,128)} reshape(bf16[1024,1024]{1,0:T(8,128)(2,1)S(1)} %copy-done.10) | data formatting | bytes 6291456 | tf_op jit(solution)/shard_map/reshape | solution.py:23
  246.2 7.2 %copy.245 = f32[2,512,4,2,128]{1,4,3,2,0:T(8,128)} copy(f32[2,512,4,2,128]{4,3,2,1,0:T(2,128)} %reshape.164) | data formatting | bytes 8388608 | tf_op jit(solution)/shard_map/reshape | solution.py:23
  262.0 7.2 %copy.243 = f32[2,512,4,2,128]{4,3,2,1,0:T(2,128)} copy(f32[2,512,4,2,128]{1,4,3,2,0:T(8,128)} %get-tuple-element.346) | data formatting | bytes 8388608 | tf_op jit(solution)/shard_map/while | solution.py:204
  269.2 6.4 %reshape_reshape.3 = f32[1024,1024]{1,0:T(8,128)} reshape(f32[2,512,4,2,128]{4,3,2,1,0:T(2,128)} %copy.243) | data formatting | bytes 8388608 | tf_op jit(solution)/shard_map/reshape;reshape | solution.py:247
  279.7 6.5 %fusion.188 = bf16[1024,1024]{1,0:T(8,128)(2,1)} fusion(f32[128,8,8,128]{3,2,1,0:T(8,128)} %bitcast.428, f32[128,8,8,128]{3,2,1,0:T(8,128)S(1)} %bitcast.427, f32[1024,1024]{1,0:T(8,128)S(1)} %copy-done.12, f32[1024]{0:T(1024)S(1)} %broadcast_bitcast_fusion, bf16[1024,1024]{1,0:T(8,128)(2,1)S(1)} %copy-done.11), kind=kLoop, calls=%fused_computation.187 | loop fusion | flops 7340032 | bytes 16781312 | tf_op jit(solution)/shard_map/convert_element_type | solution.py:253
  286.2 4.4 %collective-permute-done.2 = f32[1024,4,128]{0,2,1:T(8,128)} collective-permute-done((f32[1024,4,128]{0,2,1:T(8,128)}, f32[1024,4,128]{0,2,1:T(8,128)}, u32[]{:S(2)}, u32[]{:S(2)}) %collective-permute-start.2) | collective-permute-done | bytes 2097184 | tf_op jit(solution)/shard_map/ppermute | solution.py:19
  296.8 37.0 %collective-permute-done.3 = f32[1024,4,128]{0,2,1:T(8,128)} collective-permute-done((f32[1024,4,128]{0,2,1:T(8,128)}, f32[1024,4,128]{0,2,1:T(8,128)}, u32[]{:S(2)}, u32[]{:S(2)}) %collective-permute-start.3) | collective-permute-done | bytes 2097184 | tf_op jit(solution)/shard_map/ppermute | solution.py:19
  337.7 41.5 %all-reduce = (f32[128]{0:T(128)}, f32[128]{0:T(128)}) all-reduce(f32[128]{0:T(128)S(1)} %get-tuple-element.511, f32[128]{0:T(128)S(1)} %get-tuple-element.513), channel_id=1, replica_groups=mesh['ctx'=8,'head'=4] {'ctx','head'}, use_global_device_ids=true, to_apply=%region_16.17 | all-reduce | flops 256 | bytes 2048 | tf_op jit(solution)/shard_map/psum | solution.py:250
  (206 shorter events, 168.6 us)
Async XLA Ops:
  0.6 10.0 %copy-start.26 = (f32[128]{0:T(128)S(1)}, f32[128]{0:T(128)}, u32[]{:S(2)}) copy-start(f32[128]{0:T(128)} %param.15) | copy-start | bytes 1540
  2.1 56.9 %collective-permute-start.1 = (bf16[1024,4,128]{0,2,1:T(8,128)(2,1)S(1)}, bf16[1024,4,128]{0,2,1:T(8,128)(2,1)}, u32[]{:S(2)}, u32[]{:S(2)}) collective-permute-start(bf16[1024,4,128]{0,2,1:T(8,128)(2,1)S(1)} %bitcast.431), channel_id=1, source_target_pairs={{0,4},{4,8},{8,12},{12,16},{16,20},{20,24},{24,28},{1,5},{5,9},{9,... | collective-permute-start | bytes 3145736 | tf_op jit(solution)/shard_map/ppermute | solution.py:19
  9.5 8.2 %copy-start.7 = (f32[1024,512]{0,1:T(8,128)}, f32[1024,512]{0,1:T(8,128)S(1)}, u32[]{:S(2)}) copy-start(f32[1024,512]{0,1:T(8,128)S(1)} %copy.234) | copy-start | bytes 6291460
  12.0 40.0 %collective-permute-start = (bf16[1024,4,128]{0,2,1:T(8,128)(2,1)}, bf16[1024,4,128]{0,2,1:T(8,128)(2,1)}, u32[]{:S(2)}, u32[]{:S(2)}) collective-permute-start(bf16[1024,4,128]{0,2,1:T(8,128)(2,1)} %multiply_convert_fusion.1), channel_id=1, source_target_pairs={{0,4},{4,8},{8,12},{12,16},{16,20},{20,24},{24,28},{1,5},{5,9},{9,... | collective-permute-start | bytes 3145736 | tf_op jit(solution)/shard_map/ppermute | solution.py:19
  20.6 5.6 %copy-start.9 = (bf16[1024,1024]{1,0:T(8,128)(2,1)S(1)}, bf16[1024,1024]{1,0:T(8,128)(2,1)}, u32[]{:S(2)}) copy-start(bf16[1024,1024]{1,0:T(8,128)(2,1)} %param.11) | copy-start | bytes 6291460
  24.9 6.5 %copy-start.28 = (s32[16]{0:T(128)S(1)}, s32[16]{0:T(128)}, u32[]{:S(2)}) copy-start(s32[16]{0:T(128)} %param.17) | copy-start | bytes 196
  26.2 9.5 %copy-start.20 = (f32[1024,8]{0,1:T(8,128)}, f32[1024,8]{0,1:T(8,128)S(1)}, u32[]{:S(2)}) copy-start(f32[1024,8]{0,1:T(8,128)S(1)} %add_rsqrt_fusion) | copy-start | bytes 98308
  26.2 9.6 %copy-start.24 = (f32[128]{0:T(128)S(1)}, f32[128]{0:T(128)}, u32[]{:S(2)}) copy-start(f32[128]{0:T(128)} %param.14) | copy-start | bytes 1540
  86.4 5.4 %copy-start.6 = (f32[4,128,2,512]{3,1,2,0:T(8,128)S(1)}, f32[4,128,2,512]{3,1,2,0:T(8,128)}, u32[]{:S(2)}) copy-start(f32[4,128,2,512]{3,1,2,0:T(8,128)} %fusion.272) | copy-start | bytes 6291460 | tf_op jit(solution)/shard_map/while
  86.4 5.4 %copy-start.16 = (bf16[1024,4,2,128]{0,3,2,1:T(8,128)(2,1)S(1)}, bf16[1024,4,2,128]{0,3,2,1:T(8,128)(2,1)}, u32[]{:S(2)}) copy-start(bf16[1024,4,2,128]{0,3,2,1:T(8,128)(2,1)} %get-tuple-element.879) | copy-start | bytes 6291460 | tf_op jit(solution)/shard_map/while
  86.5 7.2 %copy-start.29 = (f32[4,512,512,2]{2,1,3,0:T(8,128)S(1)}, f32[4,512,512,2]{2,1,3,0:T(8,128)}, u32[]{:S(2)}) copy-start(f32[4,512,512,2]{2,1,3,0:T(8,128)} %get-tuple-element.801) | copy-start | bytes 25165828 | tf_op jit(solution)/shard_map/while
  117.5 5.4 %copy-start.6 = (f32[4,128,2,512]{3,1,2,0:T(8,128)S(1)}, f32[4,128,2,512]{3,1,2,0:T(8,128)}, u32[]{:S(2)}) copy-start(f32[4,128,2,512]{3,1,2,0:T(8,128)} %fusion.272) | copy-start | bytes 6291460 | tf_op jit(solution)/shard_map/while
  117.5 5.4 %copy-start.16 = (bf16[1024,4,2,128]{0,3,2,1:T(8,128)(2,1)S(1)}, bf16[1024,4,2,128]{0,3,2,1:T(8,128)(2,1)}, u32[]{:S(2)}) copy-start(bf16[1024,4,2,128]{0,3,2,1:T(8,128)(2,1)} %get-tuple-element.879) | copy-start | bytes 6291460 | tf_op jit(solution)/shard_map/while
  117.5 7.2 %copy-start.29 = (f32[4,512,512,2]{2,1,3,0:T(8,128)S(1)}, f32[4,512,512,2]{2,1,3,0:T(8,128)}, u32[]{:S(2)}) copy-start(f32[4,512,512,2]{2,1,3,0:T(8,128)} %get-tuple-element.801) | copy-start | bytes 25165828 | tf_op jit(solution)/shard_map/while
  236.1 4.6 %copy-start.21 = (f32[1024,8]{0,1:T(8,128)S(1)}, f32[1024,8]{0,1:T(8,128)}, u32[]{:S(2)}) copy-start(f32[1024,8]{0,1:T(8,128)} %copy-done.20) | copy-start | bytes 98308
  236.1 4.9 %copy-start.10 = (bf16[1024,1024]{1,0:T(8,128)(2,1)S(1)}, bf16[1024,1024]{1,0:T(8,128)(2,1)}, u32[]{:S(2)}) copy-start(bf16[1024,1024]{1,0:T(8,128)(2,1)} %param.11) | copy-start | bytes 6291460
  239.4 51.2 %collective-permute-start.2 = (f32[1024,4,128]{0,2,1:T(8,128)}, f32[1024,4,128]{0,2,1:T(8,128)}, u32[]{:S(2)}, u32[]{:S(2)}) collective-permute-start(f32[1024,4,128]{0,2,1:T(8,128)} %slice.13), channel_id=1, source_target_pairs={{4,0},{8,4},{12,8},{16,12},{20,16},{24,20},{28,24},{5,1},{9,5},{13... | collective-permute-start | bytes 6291464 | tf_op jit(solution)/shard_map/ppermute | solution.py:19
  246.2 7.2 %copy-start.25 = (f32[128]{0:T(128)S(1)}, f32[128]{0:T(128)}, u32[]{:S(2)}) copy-start(f32[128]{0:T(128)} %param.14) | copy-start | bytes 1540
  253.4 4.6 %copy-start.15 = (f32[2,512,4,2,128]{1,4,3,2,0:T(8,128)S(1)}, f32[2,512,4,2,128]{1,4,3,2,0:T(8,128)}, u32[]{:S(2)}) copy-start(f32[2,512,4,2,128]{1,4,3,2,0:T(8,128)} %get-tuple-element.346) | copy-start | bytes 12582916
  256.7 77.1 %collective-permute-start.3 = (f32[1024,4,128]{0,2,1:T(8,128)}, f32[1024,4,128]{0,2,1:T(8,128)}, u32[]{:S(2)}, u32[]{:S(2)}) collective-permute-start(f32[1024,4,128]{0,2,1:T(8,128)} %slice.15), channel_id=1, source_target_pairs={{4,0},{8,4},{12,8},{16,12},{20,16},{24,20},{28,24},{5,1},{9,5},{13... | collective-permute-start | bytes 6291464 | tf_op jit(solution)/shard_map/ppermute | solution.py:19
  279.7 10.9 %copy-start.2 = (f32[2048,4,128]{0,2,1:T(8,128)S(1)}, f32[2048,4,128]{0,2,1:T(8,128)}, u32[]{:S(2)}) copy-start(f32[2048,4,128]{0,2,1:T(8,128)} %get-tuple-element.347) | copy-start | bytes 12582916
  279.7 10.9 %copy-start.8 = (f32[1024,512]{0,1:T(8,128)S(1)}, f32[1024,512]{0,1:T(8,128)}, u32[]{:S(2)}) copy-start(f32[1024,512]{0,1:T(8,128)} %copy-done.7) | copy-start | bytes 6291460
  279.7 10.9 %copy-start.23 = (f32[1024,4]{0,1:T(4,128)S(1)}, f32[1024,4]{0,1:T(4,128)}, u32[]{:S(2)}) copy-start(f32[1024,4]{0,1:T(4,128)} %copy-done.22) | copy-start | bytes 49156
  279.7 10.9 %copy-start.27 = (f32[128]{0:T(128)S(1)}, f32[128]{0:T(128)}, u32[]{:S(2)}) copy-start(f32[128]{0:T(128)} %param.15) | copy-start | bytes 1540
  (23 other events, 60.3 us)
where the time goes:
time: 387 us; the launch traced here: 380 us
  matrix products  126 us (33%)
  local copies, waits for them, and re-layouts  87.1 us (23%)
  waiting for transfers between devices  53.7 us (14%)
  blocking collectives  41.5 us (11%)
  other arithmetic  40.4 us (10%)
  loops' own time  17.2 us (4%)
  starting transfers between devices  11.9 us (3%)
    ppermute x4, waiting for transfers between devices, shifted(): lax.ppermute(value, axis, [(source, source + steps) for source in range(l...  53.7 us
    psum x1, blocking collectives, per_device(): lax.psum((query_part, key_part), ('ctx', 'head'))  41.5 us
    dot_general x6, matrix products, stats_compute(): jnp.einsum('qhgd,khd->hgqk', query_tile, key_tile, preferred_element_type...  27.1 us
    dot_general x6, matrix products, block_compute(): jnp.einsum('hgqk,qhgd->khd', weights.astype(jnp.bfloat16), grad_tile, pre...  26.2 us
    dot_general x6, matrix products, stats_compute(): jnp.einsum('hgqk,khd->qhgd', exp_scores.astype(jnp.bfloat16), value_tile,...  25.5 us
    dot_general x6, matrix products, block_compute(): jnp.einsum('qhgd,khd->hgqk', grad_tile, value_tile, preferred_element_typ...  20.3 us
    reshape x4, local copies, waits for them, and re-layouts, norm_rows(): raw_rows.astype(jnp.float32).reshape(raw_rows.shape[0], head_count, -1)  19.1 us
    another operation x1, loops' own time, grad_pass(): lax.scan(block_step, start_acc, jnp.arange(query_rows // block_rows, dtyp...  15.4 us
  transfers between devices with their start and end apart: 4, of which 3 were waited for; matrix products, arithmetic and copies ran while one was open for 22% of the time, Pallas kernels for 0%

commit v1 on v0

v1 whole, which is shorter than its diff:
```python
import functools
import math

import jax
import jax.numpy as jnp
from jax import lax
from jax.experimental import pallas as pl
from jax.experimental.pallas import tpu as pltpu
from jax.sharding import PartitionSpec as P

WINDOW = 1024
QUERY_SCALAR = 168


EPS = 1e-06
BLOCK = 256


def shifted(value, axis, steps):
    count = lax.axis_size(axis)
    leading, last = (max(0, -steps), min(count, count - steps))
    return lax.ppermute(value, axis, [(source, source + steps) for source in range(leading, last)])


def norm_rows(raw_rows, head_count):
    values = raw_rows.astype(jnp.float32).reshape(raw_rows.shape[0], head_count, -1)
    inverse = lax.rsqrt(jnp.mean(values * values, axis=-1, keepdims=True) + EPS)
    return (values * inverse, inverse)


def norm_back(raw_rows, gain_vec, head_count, upstream):
    scaled, inverse = norm_rows(raw_rows, head_count)
    incoming = upstream.reshape(scaled.shape)
    weighted = incoming * gain_vec
    inner_sum = jnp.mean(weighted * scaled, axis=-1, keepdims=True)
    result = inverse * (weighted - scaled * inner_sum)
    return (result.reshape(raw_rows.shape), jnp.sum(incoming * scaled, axis=(0, 1)))


def doc_index(positions, doc_ends):
    return jnp.sum((positions[:, None] >= doc_ends[None, :]).astype(jnp.int32), axis=1)


def attn_kernel(qdoc_ref, kdoc_ref, q_ref, do_ref, k_ref, v_ref, dq_ref, dk_ref, dv_ref, *, group, head_dim):
    blk = BLOCK
    n_tiles = WINDOW // blk + 1
    scale = QUERY_SCALAR ** (-0.5)
    qb = pl.program_id(1)

    @pl.when(qb == 0)
    def _():
        dk_ref[...] = jnp.zeros(dk_ref.shape, jnp.float32)
        dv_ref[...] = jnp.zeros(dv_ref.shape, jnp.float32)

    q_first = pl.multiple_of(qb * blk, blk)
    q_all = q_ref[...]
    do_all = do_ref[...]
    q_g = jnp.concatenate([q_all[:, a * head_dim:(a + 1) * head_dim] for a in range(group)], axis=0)
    do_g = jnp.concatenate([do_all[:, a * head_dim:(a + 1) * head_dim] for a in range(group)], axis=0)
    qdoc = qdoc_ref[...]
    rows = lax.broadcasted_iota(jnp.int32, (blk, blk), 0)
    cols = lax.broadcasted_iota(jnp.int32, (blk, blk), 1)

    def tile_mask(t):
        k_first = pl.multiple_of(q_first + t * blk, blk)
        kdoc = kdoc_ref[:, pl.ds(k_first, blk)]
        live = qdoc == kdoc
        if t == 0:
            live = live & (cols > rows)
        if t == n_tiles - 1:
            live = live & (cols + t * blk <= rows + WINDOW)
        return jnp.concatenate([live] * group, axis=0), k_first

    def scores_of(k_tile):
        return lax.dot_general(q_g, k_tile, (((1,), (1,)), ((), ())), preferred_element_type=jnp.float32) * scale

    totals = jnp.zeros((group * blk, 1), jnp.float32)
    numer = jnp.zeros((group * blk, head_dim), jnp.float32)
    for t in range(n_tiles):
        live, k_first = tile_mask(t)
        k_tile = k_ref[pl.ds(k_first, blk), :]
        v_tile = v_ref[pl.ds(k_first, blk), :]
        exp_s = jnp.where(live, jnp.exp(scores_of(k_tile)), 0.0)
        totals = totals + jnp.sum(exp_s, axis=1, keepdims=True)
        numer = numer + jnp.dot(exp_s.astype(jnp.bfloat16), v_tile, preferred_element_type=jnp.float32)
    log_sums = jnp.log(totals)
    attn_out = numer / totals
    delta = jnp.sum(do_g.astype(jnp.float32) * attn_out, axis=1, keepdims=True)

    dq = jnp.zeros((group * blk, head_dim), jnp.float32)
    for t in range(n_tiles):
        live, k_first = tile_mask(t)
        k_tile = k_ref[pl.ds(k_first, blk), :]
        v_tile = v_ref[pl.ds(k_first, blk), :]
        weights = jnp.where(live, jnp.exp(scores_of(k_tile) - log_sums), 0.0)
        d_weights = lax.dot_general(do_g, v_tile, (((1,), (1,)), ((), ())), preferred_element_type=jnp.float32)
        d_scores = (weights * (d_weights - delta)).astype(jnp.bfloat16)
        dq = dq + jnp.dot(d_scores, k_tile, preferred_element_type=jnp.float32)
        dk_part = lax.dot_general(d_scores, q_g, (((0,), (0,)), ((), ())), preferred_element_type=jnp.float32)
        dv_part = lax.dot_general(
            weights.astype(jnp.bfloat16), do_g, (((0,), (0,)), ((), ())), preferred_element_type=jnp.float32
        )
        dk_ref[pl.ds(k_first, blk), :] += dk_part * scale
        dv_ref[pl.ds(k_first, blk), :] += dv_part
    dq = dq * scale
    dq_ref[...] = jnp.concatenate([dq[a * blk:(a + 1) * blk] for a in range(group)], axis=1)


def attention_grads(query_norm, grad_rows, keys_all, vals_all, own_doc, all_doc, key_heads, head_dim):
    tok_rows, q_cols = query_norm.shape
    key_rows = keys_all.shape[0]
    group = q_cols // (key_heads * head_dim)
    blk = BLOCK
    n_q = tok_rows // blk
    n_tiles = WINDOW // blk + 1
    gw = group * head_dim
    kernel = functools.partial(attn_kernel, group=group, head_dim=head_dim)
    flops = 2 * 7 * key_heads * n_q * n_tiles * (group * blk) * blk * head_dim
    cost = pl.CostEstimate(
        flops=flops,
        transcendentals=2 * key_heads * n_q * n_tiles * group * blk * blk,
        bytes_accessed=2 * 2 * tok_rows * q_cols + 2 * 2 * key_rows * key_heads * head_dim
        + 4 * tok_rows * q_cols + 2 * 4 * key_rows * key_heads * head_dim,
    )
    return pl.pallas_call(
        kernel,
        grid=(key_heads, n_q),
        in_specs=[
            pl.BlockSpec((blk, 1), lambda h, qb: (qb, 0)),
            pl.BlockSpec((1, key_rows), lambda h, qb: (0, 0)),
            pl.BlockSpec((blk, gw), lambda h, qb: (qb, h)),
            pl.BlockSpec((blk, gw), lambda h, qb: (qb, h)),
            pl.BlockSpec((key_rows, head_dim), lambda h, qb: (0, h)),
            pl.BlockSpec((key_rows, head_dim), lambda h, qb: (0, h)),
        ],
        out_specs=[
            pl.BlockSpec((blk, gw), lambda h, qb: (qb, h)),
            pl.BlockSpec((key_rows, head_dim), lambda h, qb: (0, h)),
            pl.BlockSpec((key_rows, head_dim), lambda h, qb: (0, h)),
        ],
        out_shape=[
            jax.ShapeDtypeStruct((tok_rows, q_cols), jnp.float32),
            jax.ShapeDtypeStruct((key_rows, key_heads * head_dim), jnp.float32),
            jax.ShapeDtypeStruct((key_rows, key_heads * head_dim), jnp.float32),
        ],
        compiler_params=pltpu.CompilerParams(dimension_semantics=("arbitrary", "arbitrary")),
        cost_estimate=cost,
    )(own_doc.reshape(tok_rows, 1), all_doc.reshape(1, key_rows), query_norm, grad_rows, keys_all, vals_all)


def per_device(query_raw, key_raw, value_proj, query_gain, key_gain, out_grad, doc_lengths):
    tok_rows = query_raw.shape[0]
    head_dim = query_gain.shape[0]
    query_heads = query_raw.shape[1] // head_dim
    key_heads = key_raw.shape[1] // head_dim
    first_pos = lax.axis_index("ctx") * tok_rows
    doc_ends = jnp.cumsum(doc_lengths)
    own_pos = first_pos + jnp.arange(tok_rows, dtype=jnp.int32)
    own_doc = doc_index(own_pos, doc_ends)
    halo_raw = first_pos - WINDOW + jnp.arange(WINDOW, dtype=jnp.int32)
    halo_doc = jnp.where(halo_raw >= 0, doc_index(halo_raw, doc_ends), -1)
    query_hat, query_inv = norm_rows(query_raw, query_heads)
    query_norm = (query_hat * query_gain).astype(jnp.bfloat16).reshape(tok_rows, query_heads * head_dim)
    key_hat, key_inv = norm_rows(key_raw, key_heads)
    key_norm = (key_hat * key_gain).astype(jnp.bfloat16).reshape(tok_rows, key_heads * head_dim)
    halo_keys, halo_vals = shifted((key_norm[tok_rows - WINDOW:], value_proj[tok_rows - WINDOW:]), "ctx", 1)
    keys_all = jnp.concatenate([halo_keys, key_norm], axis=0)
    vals_all = jnp.concatenate([halo_vals, value_proj], axis=0)
    all_doc = jnp.concatenate([halo_doc, own_doc])
    query_acc, key_acc, val_acc = attention_grads(
        query_norm, out_grad, keys_all, vals_all, own_doc, all_doc, key_heads, head_dim
    )
    back_keys, back_vals = shifted((key_acc[:WINDOW], val_acc[:WINDOW]), "ctx", -1)
    key_own = jnp.concatenate(
        [key_acc[WINDOW:tok_rows], key_acc[tok_rows:] + back_keys], axis=0
    ).reshape(tok_rows, key_heads, head_dim)
    val_own = jnp.concatenate([val_acc[WINDOW:tok_rows], val_acc[tok_rows:] + back_vals], axis=0)
    query_grad, query_part = norm_back(
        query_raw, query_gain, query_heads, query_acc.reshape(tok_rows, query_heads, head_dim)
    )
    key_grad, key_part = norm_back(key_raw, key_gain, key_heads, key_own)
    query_gain_grad, key_gain_grad = lax.psum((query_part, key_part), ("ctx", "head"))
    value_grad = val_own.astype(jnp.bfloat16)
    return (
        query_grad.astype(jnp.bfloat16),
        key_grad.astype(jnp.bfloat16),
        value_grad,
        query_gain_grad,
        key_gain_grad,
    )


def solution(mesh):
    return jax.shard_map(
        per_device,
        mesh=mesh,
        in_specs=(
            P("ctx", "head"),
            P("ctx", "head"),
            P("ctx", "head"),
            P(),
            P(),
            P("ctx", "head"),
            P(),
        ),
        out_specs=(P("ctx", "head"), P("ctx", "head"), P("ctx", "head"), P(), P()),
        check_vma=False,
    )
```

time: 387 us -> 257 us (0.66); the launches traced: 380 us -> 256 us
  matrix products: 126 us -> 0 us
  local copies, waits for them, and re-layouts: 87.1 us -> 23.1 us
  Pallas kernels: 0 us -> 59.3 us
  blocking collectives: 41.5 us -> 73.9 us
  loops' own time: 17.2 us -> 0 us
  waiting for transfers between devices: 53.7 us -> 41.4 us
  other arithmetic: 40.4 us -> 45.5 us
    dot_general x42 -> x0, matrix products: 126 us -> none  [the longest x6 27.1 us: stats_compute(): jnp.einsum('qhgd,khd->hgqk', query_tile, key_tile, preferred_element_type...]
    pallas_call x0 -> x1, Pallas kernels: none -> 59.3 us  [attention_grads(): pl.pallas_call(kernel, grid=(key_heads, n_q), in_specs=[pl.BlockSpec((blk...]
    psum x1, blocking collectives: 41.5 us -> 73.9 us  [per_device(): lax.psum((query_part, key_part), ('ctx', 'head'))]
    while x55 -> x0, local copies, waits for them, and re-layouts: 28.7 us -> none  [the longest x3 15.1 us: grad_pass(): lax.scan(block_step, start_acc, jnp.arange(query_rows // block_rows, dtyp...]
    reduce_sum x0 -> x2, other arithmetic: none -> 19 us  [norm_back(): inner_sum = jnp.mean(weighted * scaled, axis=-1, keepdims=True)]
    reshape x4 -> x1, local copies, waits for them, and re-layouts: 19.1 us -> 1.72 us  [norm_rows(): raw_rows.astype(jnp.float32).reshape(raw_rows.shape[0], head_count, -1)]
    another operation x2 -> x0, loops' own time: 17.2 us -> none  [the longest x1 15.4 us: grad_pass(): lax.scan(block_step, start_acc, jnp.arange(query_rows // block_rows, dtyp...]
    ppermute x4, waiting for transfers between devices: 53.7 us -> 41.4 us  [shifted(): lax.ppermute(value, axis, [(source, source + steps) for source in range(l...]
  transfers between devices with their start and end apart: 4 -> 4, of which waited for: 3 -> 3; matrix products, arithmetic and copies ran while one was open for 22% -> 21% of each run, Pallas kernels for 0% -> 0%
where the time goes in v1:
time: 257 us; the launch traced here: 256 us
  blocking collectives  73.9 us (29%)
  Pallas kernels  59.3 us (23%)
  other arithmetic  45.5 us (18%)
  waiting for transfers between devices  41.4 us (16%)
  local copies, waits for them, and re-layouts  23.1 us (9%)
  starting transfers between devices  12.3 us (5%)
    psum x1, blocking collectives, per_device(): lax.psum((query_part, key_part), ('ctx', 'head'))  73.9 us
    pallas_call x1, Pallas kernels, attention_grads(): pl.pallas_call(kernel, grid=(key_heads, n_q), in_specs=[pl.BlockSpec((blk...  59.3 us
    ppermute x4, waiting for transfers between devices, shifted(): lax.ppermute(value, axis, [(source, source + steps) for source in range(l...  41.4 us
    reduce_sum x2, other arithmetic, norm_back(): inner_sum = jnp.mean(weighted * scaled, axis=-1, keepdims=True)  19 us
    ppermute x4, starting transfers between devices, shifted(): lax.ppermute(value, axis, [(source, source + steps) for source in range(l...  12.3 us
    unnamed x42, local copies, waits for them, and re-layouts  8.51 us
    reduce_sum x4, other arithmetic, norm_back(): jnp.sum(incoming * scaled, axis=(0, 1))  6.16 us
  transfers between devices with their start and end apart: 4, of which 3 were waited for; matrix products, arithmetic and copies ran while one was open for 21% of the time, Pallas kernels for 0%

profile of v1, /device:TPU:0, one launch (start us, length us, event | category | flops | bytes accessed | tf_op | source)
XLA Modules:
  0.0 256.4 jit_solution(1079754801178688886)
XLA Ops:
  0.6 5.9 %collective-permute-start.1 = (bf16[1024,512]{1,0:T(8,128)(2,1)}, bf16[1024,512]{1,0:T(8,128)(2,1)}, u32[]{:S(2)}, u32[]{:S(2)}) collective-permute-start(bf16[1024,512]{1,0:T(8,128)(2,1)} %param.9), channel_id=1, source_target_pairs={{0,4},{4,8},{8,12},{12,16},{16,20},{20,24},{24,28},{1,5},{5,9},{9,... | collective-permute-start | bytes 3145736 | tf_op jit(solution)/shard_map/ppermute | solution.py:22
  7.2 1.7 reshape.113
  12.4 1.4 multiply_convert_fusion.1
  13.8 3.5 %collective-permute-start = (bf16[1024,512]{1,0:T(8,128)(2,1)}, bf16[1024,512]{1,0:T(8,128)(2,1)}, u32[]{:S(2)}, u32[]{:S(2)}) collective-permute-start(bf16[1024,512]{1,0:T(8,128)(2,1)} %multiply_convert_fusion.1), channel_id=1, source_target_pairs={{0,4},{4,8},{8,12},{12,16},{16,20},{20,24},{24,28},{1,5},{5,9},{9,... | collective-permute-start | bytes 3145736 | tf_op jit(solution)/shard_map/ppermute | solution.py:22
  18.7 2.0 convert_bitcast_fusion
  26.2 2.7 %multiply_convert_fusion.q_ref = bf16[1024,1024]{1,0:T(8,128)(2,1)} fusion(f32[128,8,8,128]{3,2,1,0:T(8,128)S(1)} %bitcast.57, bf16[1024,1024]{1,0:T(8,128)(2,1)S(1)} %copy-done.6, f32[1024]{0:T(1024)S(1)} %broadcast_bitcast_fusion), kind=kLoop, calls=%fused_computation.9 | loop fusion | flops 4194304 | bytes 8392704 | tf_op jit(solution)/shard_map/convert_element_type | solution.py:163
  29.4 2.7 %pad_maximum_fusion.1.v_ref = bf16[2048,512]{1,0:T(8,128)(2,1)} fusion(bf16[1024,512]{1,0:T(8,128)(2,1)S(1)} %copy-done.16, bf16[1024,512]{1,0:T(8,128)(2,1)} %collective-permute-done.1), kind=kLoop, calls=%fused_computation.17 | loop fusion | flops 4194304 | bytes 4194304 | tf_op jit(solution)/shard_map/concatenate | solution.py:168
  32.1 18.6 %collective-permute-done = bf16[1024,512]{1,0:T(8,128)(2,1)} collective-permute-done((bf16[1024,512]{1,0:T(8,128)(2,1)}, bf16[1024,512]{1,0:T(8,128)(2,1)}, u32[]{:S(2)}, u32[]{:S(2)}) %collective-permute-start) | collective-permute-done | bytes 1048608 | tf_op jit(solution)/shard_map/ppermute | solution.py:22
  50.7 3.1 %pad_maximum_fusion.k_ref = bf16[2048,512]{1,0:T(8,128)(2,1)} fusion(bf16[1024,512]{1,0:T(8,128)(2,1)} %multiply_convert_fusion.1, bf16[1024,512]{1,0:T(8,128)(2,1)} %collective-permute-done), kind=kLoop, calls=%fused_computation.16 | loop fusion | flops 4194304 | bytes 4194304 | tf_op jit(solution)/shard_map/concatenate | solution.py:167
  53.8 59.3 %shard_map.110 = (f32[1024,1024]{1,0:T(8,128)}, f32[2048,512]{1,0:T(8,128)}, f32[2048,512]{1,0:T(8,128)}) custom-call(s32[1024,1]{1,0:T(8,128)} %copy.16.qdoc_ref, s32[1,2048]{1,0:T(1,128)} %bitcast.66, bf16[1024,1024]{1,0:T(8,128)(2,1)} %multiply_convert_fusion.q_ref, bf16[1024,1024]{1,0:T(8,128)(2,1)} %do_ref.1, bf16[2048,512]{1,0:T(8,128)(2,1)} %pad_maximum_fusion.k_ref, ...), custom_call_target="tpu_custom_call" | custom-call | flops 18790481920 | bytes 20971520 | tf_op jit(solution)/shard_map/pallas_call | solution.py:125
  113.0 1.9 slice.13
  114.9 1.5 collective-permute-start.2
  116.5 1.6 slice.15
  118.0 1.4 collective-permute-start.3
  120.8 1.9 copy-done.1
  122.8 14.4 %multiply_reduce_fusion.1 = f32[1024,8]{1,0:T(8,128)S(1)} fusion(f32[1024,8,128]{2,1,0:T(8,128)S(1)} %bitcast_multiply_fusion.1, f32[1024,8,128]{2,1,0:T(8,128)S(1)} %bitcast.56, f32[1024,8]{1,0:T(8,128)S(1)} %copy-done.11), kind=kLoop, calls=%fused_computation.8 | loop fusion | flops 3137536 | bytes 8454144 | tf_op jit(solution)/shard_map/reduce_sum | solution.py:35
  139.4 4.0 %multiply_reduce_fusion = (f32[1024]{0:T(1024)S(1)}, bf16[1024,1024]{1,0:T(8,128)(2,1)}) fusion(f32[1024,1024]{1,0:T(8,128)S(1)} %copy-done.9, f32[128,8,8,128]{3,2,1,0:T(8,128)S(1)} %bitcast.58, bf16[1024,1024]{1,0:T(8,128)(2,1)S(1)} %copy-done.7, f32[128,8,8,128]{3,2,1,0:T(8,128)S(1)} %bitcast.63, f32[1024]{0:T(1024)S(1)} %broadcast_bitcast_fusion), kind=kLoop, calls=%fused_computation.7 | loop fusion | flops 9436160 | bytes 16785408 | tf_op jit(solution)/shard_map/reduce_sum | solution.py:37
  143.5 22.3 %collective-permute-done.2 = f32[1024,512]{1,0:T(8,128)S(1)} collective-permute-done((f32[1024,512]{1,0:T(8,128)S(1)}, f32[1024,512]{1,0:T(8,128)S(1)}, u32[]{:S(2)}, u32[]{:S(2)}) %collective-permute-start.2) | collective-permute-done | bytes 2097184 | tf_op jit(solution)/shard_map/ppermute | solution.py:22
  165.8 2.1 multiply_reduce_fusion.3
  167.9 2.9 %reshape.115 = f32[1024,4,128]{2,1,0:T(4,128)} reshape(f32[1024,512]{1,0:T(8,128)} %get-tuple-element.16) | data formatting | bytes 4194304 | tf_op jit(solution)/shard_map/reshape | solution.py:176
  170.9 73.9 %all-reduce = (f32[128]{0:T(128)}, f32[128]{0:T(128)}) all-reduce(f32[128]{0:T(128)S(1)} %bitcast_reduce_fusion, f32[128]{0:T(128)S(1)} %bitcast_reduce_fusion.1), channel_id=1, replica_groups=mesh['ctx'=8,'head'=4] {'ctx','head'}, use_global_device_ids=true, to_apply=%region_9.10 | all-reduce | flops 256 | bytes 2048 | tf_op jit(solution)/shard_map/psum | solution.py:182
  244.8 4.5 %multiply_reduce_fusion.4 = f32[1024,4]{1,0:T(8,128)S(1)} fusion(f32[1024,4,128]{2,1,0:T(4,128)} %copy-done.5, f32[1024,4,128]{2,1,0:T(4,128)} %reshape.115, f32[128]{0:T(128)S(1)} %copy-done.18, f32[1024,4]{1,0:T(8,128)} %copy-done.12), kind=kLoop, calls=%fused_computation.20 | loop fusion | flops 2093056 | bytes 4227584 | tf_op jit(solution)/shard_map/reduce_sum | solution.py:35
  250.9 1.9 fusion.5
  253.5 2.9 %add_convert_fusion = bf16[1024,512]{1,0:T(8,128)(2,1)} fusion(f32[1024,512]{1,0:T(8,128)} %collective-permute-done.3, f32[2048,512]{1,0:T(8,128)S(1)} %copy-done.15), kind=kLoop, calls=%fused_computation.19 | loop fusion | flops 1048576 | bytes 5242880 | tf_op jit(solution)/shard_map/convert_element_type | solution.py:183
  (66 shorter events, 17.3 us)
Async XLA Ops:
  0.6 28.7 %collective-permute-start.1 = (bf16[1024,512]{1,0:T(8,128)(2,1)}, bf16[1024,512]{1,0:T(8,128)(2,1)}, u32[]{:S(2)}, u32[]{:S(2)}) collective-permute-start(bf16[1024,512]{1,0:T(8,128)(2,1)} %param.9), channel_id=1, source_target_pairs={{0,4},{4,8},{8,12},{12,16},{16,20},{20,24},{24,28},{1,5},{5,9},{9,... | collective-permute-start | bytes 3145736 | tf_op jit(solution)/shard_map/ppermute | solution.py:22
  8.9 1.3 copy-start.5
  10.2 2.1 copy-start.8
  10.3 0.8 copy-start.12
  12.4 4.9 %copy-start.17 = (f32[128]{0:T(128)S(1)}, f32[128]{0:T(128)}, u32[]{:S(2)}) copy-start(f32[128]{0:T(128)} %param.10) | copy-start | bytes 1540
  12.4 4.9 %copy-start.19 = (s32[16]{0:T(128)S(1)}, s32[16]{0:T(128)}, u32[]{:S(2)}) copy-start(s32[16]{0:T(128)} %param.13) | copy-start | bytes 196
  13.8 36.9 %collective-permute-start = (bf16[1024,512]{1,0:T(8,128)(2,1)}, bf16[1024,512]{1,0:T(8,128)(2,1)}, u32[]{:S(2)}, u32[]{:S(2)}) collective-permute-start(bf16[1024,512]{1,0:T(8,128)(2,1)} %multiply_convert_fusion.1), channel_id=1, source_target_pairs={{0,4},{4,8},{8,12},{12,16},{16,20},{20,24},{24,28},{1,5},{5,9},{9,... | collective-permute-start | bytes 3145736 | tf_op jit(solution)/shard_map/ppermute | solution.py:22
  21.8 2.0 copy-start
  24.4 1.2 copy-start.10
  24.4 1.8 copy-start.6
  25.6 3.3 %copy-start.2 = (f32[1024,8,128]{2,1,0:T(8,128)}, f32[1024,8,128]{2,1,0:T(8,128)S(1)}, u32[]{:S(2)}) copy-start(f32[1024,8,128]{2,1,0:T(8,128)S(1)} %mul.148) | copy-start | bytes 12582916
  26.2 3.2 %copy-start.16 = (bf16[1024,512]{1,0:T(8,128)(2,1)S(1)}, bf16[1024,512]{1,0:T(8,128)(2,1)}, u32[]{:S(2)}) copy-start(bf16[1024,512]{1,0:T(8,128)(2,1)} %param.9) | copy-start | bytes 3145732
  113.0 3.4 %copy-start.14 = (f32[2048,512]{1,0:T(8,128)S(1)}, f32[2048,512]{1,0:T(8,128)}, u32[]{:S(2)}) copy-start(f32[2048,512]{1,0:T(8,128)} %get-tuple-element.10) | copy-start | bytes 12582916
  114.9 50.9 %collective-permute-start.2 = (f32[1024,512]{1,0:T(8,128)S(1)}, f32[1024,512]{1,0:T(8,128)S(1)}, u32[]{:S(2)}, u32[]{:S(2)}) collective-permute-start(f32[1024,512]{1,0:T(8,128)S(1)} %slice.13), channel_id=1, source_target_pairs={{4,0},{8,4},{12,8},{16,12},{20,16},{24,20},{28,24},{5,1},{9,5},{13... | collective-permute-start | bytes 6291464 | tf_op jit(solution)/shard_map/ppermute | solution.py:22
  116.4 3.0 %copy-start.9 = (f32[1024,1024]{1,0:T(8,128)S(1)}, f32[1024,1024]{1,0:T(8,128)}, u32[]{:S(2)}) copy-start(f32[1024,1024]{1,0:T(8,128)} %get-tuple-element.8) | copy-start | bytes 12582916
  118.0 134.8 %collective-permute-start.3 = (f32[1024,512]{1,0:T(8,128)}, f32[1024,512]{1,0:T(8,128)}, u32[]{:S(2)}, u32[]{:S(2)}) collective-permute-start(f32[1024,512]{1,0:T(8,128)} %slice.15), channel_id=1, source_target_pairs={{4,0},{8,4},{12,8},{16,12},{20,16},{24,20},{28,24},{5,1},{9,5},{13... | collective-permute-start | bytes 6291464 | tf_op jit(solution)/shard_map/ppermute | solution.py:22
  120.5 2.2 copy-start.1
  120.5 2.3 copy-start.11
  122.8 15.6 %copy-start.7 = (bf16[1024,1024]{1,0:T(8,128)(2,1)S(1)}, bf16[1024,1024]{1,0:T(8,128)(2,1)}, u32[]{:S(2)}) copy-start(bf16[1024,1024]{1,0:T(8,128)(2,1)} %param.7) | copy-start | bytes 6291460
  137.3 2.2 copy-start.3
  139.4 26.4 %copy-start.13 = (f32[2048,512]{1,0:T(8,128)S(1)}, f32[2048,512]{1,0:T(8,128)}, u32[]{:S(2)}) copy-start(f32[2048,512]{1,0:T(8,128)} %get-tuple-element.9) | copy-start | bytes 12582916
  167.9 76.8 %copy-start.18 = (f32[128]{0:T(128)S(1)}, f32[128]{0:T(128)}, u32[]{:S(2)}) copy-start(f32[128]{0:T(128)} %param.11) | copy-start | bytes 1540
  249.3 1.6 copy-start.4
  250.9 2.6 %copy-start.15 = (f32[2048,512]{1,0:T(8,128)S(1)}, f32[2048,512]{1,0:T(8,128)}, u32[]{:S(2)}) copy-start(f32[2048,512]{1,0:T(8,128)} %get-tuple-element.10) | copy-start | bytes 12582916

commit v2 on v1

--- a/solution.py
+++ b/solution.py
@@ -20,6 +20,20 @@
     count = lax.axis_size(axis)
     leading, last = (max(0, -steps), min(count, count - steps))
     return lax.ppermute(value, axis, [(source, source + steps) for source in range(leading, last)])
+
+
+def butterfly_sum(value, axes):
+    for axis in axes:
+        count = lax.axis_size(axis)
+        if count & (count - 1):
+            value = lax.psum(value, axis)
+            continue
+        step = 1
+        while step < count:
+            pairs = [(source, source ^ step) for source in range(count)]
+            value = value + lax.ppermute(value, axis, pairs)
+            step *= 2
+    return value
 
 
 def norm_rows(raw_rows, head_count):
@@ -179,7 +193,8 @@
         query_raw, query_gain, query_heads, query_acc.reshape(tok_rows, query_heads, head_dim)
     )
     key_grad, key_part = norm_back(key_raw, key_gain, key_heads, key_own)
-    query_gain_grad, key_gain_grad = lax.psum((query_part, key_part), ("ctx", "head"))
+    query_gain_grad = butterfly_sum(query_part, ("ctx", "head"))
+    key_gain_grad = butterfly_sum(key_part, ("ctx", "head"))
     value_grad = val_own.astype(jnp.bfloat16)
     return (
         query_grad.astype(jnp.bfloat16),

time: 257 us -> 246 us (0.957)
  blocking collectives: 73.9 us -> 0 us
  waiting for transfers between devices: 41.4 us -> 87.3 us
  starting transfers between devices: 12.3 us -> 29.3 us
    psum x1 -> x0, blocking collectives: 73.9 us -> none  [per_device(): lax.psum((query_part, key_part), ('ctx', 'head'))]
    ppermute x0 -> x10, waiting for transfers between devices: none -> 68.1 us  [butterfly_sum(): value = value + lax.ppermute(value, axis, pairs)]
    ppermute x4, waiting for transfers between devices: 41.4 us -> 19.1 us  [shifted(): lax.ppermute(value, axis, [(source, source + steps) for source in range(l...]
    ppermute x0 -> x10, starting transfers between devices: none -> 17 us  [butterfly_sum(): value = value + lax.ppermute(value, axis, pairs)]
  transfers between devices with their start and end apart: 4 -> 14, of which waited for: 3 -> 8; matrix products, arithmetic and copies ran while one was open for 21% -> 24% of each run, Pallas kernels for 0% -> 0%
where the time goes in v2:
time: 246 us; the launch traced here: 245 us
  waiting for transfers between devices  87.3 us (35%)
  Pallas kernels  59.2 us (24%)
  other arithmetic  46.5 us (19%)
  starting transfers between devices  29.3 us (12%)
  local copies, waits for them, and re-layouts  22 us (9%)
    ppermute x10, waiting for transfers between devices, butterfly_sum(): value = value + lax.ppermute(value, axis, pairs)  68.1 us
    pallas_call x1, Pallas kernels, attention_grads(): pl.pallas_call(kernel, grid=(key_heads, n_q), in_specs=[pl.BlockSpec((blk...  59.2 us
    ppermute x4, waiting for transfers between devices, shifted(): lax.ppermute(value, axis, [(source, source + steps) for source in range(l...  19.1 us
    reduce_sum x2, other arithmetic, norm_back(): inner_sum = jnp.mean(weighted * scaled, axis=-1, keepdims=True)  19 us
    ppermute x10, starting transfers between devices, butterfly_sum(): value = value + lax.ppermute(value, axis, pairs)  17 us
    ppermute x4, starting transfers between devices, shifted(): lax.ppermute(value, axis, [(source, source + steps) for source in range(l...  12.2 us
    unnamed x42, local copies, waits for them, and re-layouts  7.47 us
    reduce_sum x4, other arithmetic, norm_back(): jnp.sum(incoming * scaled, axis=(0, 1))  6.15 us
  transfers between devices with their start and end apart: 14, of which 8 were waited for; matrix products, arithmetic and copies ran while one was open for 24% of the time, Pallas kernels for 0%

profile of v2, /device:TPU:0, one launch (start us, length us, event | category | flops | bytes accessed | tf_op | source)
XLA Modules:
  0.0 245.3 jit_solution(4917657452193058426)
XLA Ops:
  0.6 5.8 %collective-permute-start.1 = (bf16[1024,512]{1,0:T(8,128)(2,1)}, bf16[1024,512]{1,0:T(8,128)(2,1)}, u32[]{:S(2)}, u32[]{:S(2)}) collective-permute-start(bf16[1024,512]{1,0:T(8,128)(2,1)} %param.9), channel_id=1, source_target_pairs={{0,4},{4,8},{8,12},{12,16},{16,20},{20,24},{24,28},{1,5},{5,9},{9,... | collective-permute-start | bytes 3145736 | tf_op jit(solution)/shard_map/ppermute | solution.py:22
  13.7 3.5 %collective-permute-start = (bf16[1024,512]{1,0:T(8,128)(2,1)}, bf16[1024,512]{1,0:T(8,128)(2,1)}, u32[]{:S(2)}, u32[]{:S(2)}) collective-permute-start(bf16[1024,512]{1,0:T(8,128)(2,1)} %multiply_convert_fusion.1), channel_id=1, source_target_pairs={{0,4},{4,8},{8,12},{12,16},{16,20},{20,24},{24,28},{1,5},{5,9},{9,... | collective-permute-start | bytes 3145736 | tf_op jit(solution)/shard_map/ppermute | solution.py:22
  18.6 2.0 convert_bitcast_fusion
  26.1 2.7 %multiply_convert_fusion.q_ref = bf16[1024,1024]{1,0:T(8,128)(2,1)} fusion(f32[128,8,8,128]{3,2,1,0:T(8,128)S(1)} %bitcast.57, bf16[1024,1024]{1,0:T(8,128)(2,1)S(1)} %copy-done.6, f32[1024]{0:T(1024)S(1)} %broadcast_bitcast_fusion), kind=kLoop, calls=%fused_computation.9 | loop fusion | flops 4194304 | bytes 8392704 | tf_op jit(solution)/shard_map/convert_element_type | solution.py:177
  29.4 2.7 %pad_maximum_fusion.1.v_ref = bf16[2048,512]{1,0:T(8,128)(2,1)} fusion(bf16[1024,512]{1,0:T(8,128)(2,1)S(1)} %copy-done.16, bf16[1024,512]{1,0:T(8,128)(2,1)} %collective-permute-done.1), kind=kLoop, calls=%fused_computation.17 | loop fusion | flops 4194304 | bytes 4194304 | tf_op jit(solution)/shard_map/concatenate | solution.py:182
  32.1 18.6 %collective-permute-done = bf16[1024,512]{1,0:T(8,128)(2,1)} collective-permute-done((bf16[1024,512]{1,0:T(8,128)(2,1)}, bf16[1024,512]{1,0:T(8,128)(2,1)}, u32[]{:S(2)}, u32[]{:S(2)}) %collective-permute-start) | collective-permute-done | bytes 1048608 | tf_op jit(solution)/shard_map/ppermute | solution.py:22
  50.7 3.0 %pad_maximum_fusion.k_ref = bf16[2048,512]{1,0:T(8,128)(2,1)} fusion(bf16[1024,512]{1,0:T(8,128)(2,1)} %multiply_convert_fusion.1, bf16[1024,512]{1,0:T(8,128)(2,1)} %collective-permute-done), kind=kLoop, calls=%fused_computation.16 | loop fusion | flops 4194304 | bytes 4194304 | tf_op jit(solution)/shard_map/concatenate | solution.py:181
  53.7 59.2 %shard_map.110 = (f32[1024,1024]{1,0:T(8,128)}, f32[2048,512]{1,0:T(8,128)}, f32[2048,512]{1,0:T(8,128)}) custom-call(s32[1024,1]{1,0:T(8,128)} %copy.16.qdoc_ref, s32[1,2048]{1,0:T(1,128)} %bitcast.66, bf16[1024,1024]{1,0:T(8,128)(2,1)} %multiply_convert_fusion.q_ref, bf16[1024,1024]{1,0:T(8,128)(2,1)} %do_ref.1, bf16[2048,512]{1,0:T(8,128)(2,1)} %pad_maximum_fusion.k_ref, ...), custom_call_target="tpu_custom_call" | custom-call | flops 18790481920 | bytes 20971520 | tf_op jit(solution)/shard_map/pallas_call | solution.py:139
  113.0 1.9 slice.13
  120.7 1.9 copy-done.1
  122.7 14.4 %multiply_reduce_fusion.1 = f32[1024,8]{1,0:T(8,128)S(1)} fusion(f32[1024,8,128]{2,1,0:T(8,128)S(1)} %bitcast_multiply_fusion.1, f32[1024,8,128]{2,1,0:T(8,128)S(1)} %bitcast.56, f32[1024,8]{1,0:T(8,128)S(1)} %copy-done.11), kind=kLoop, calls=%fused_computation.8 | loop fusion | flops 3137536 | bytes 8454144 | tf_op jit(solution)/shard_map/reduce_sum | solution.py:49
  139.3 4.0 %multiply_reduce_fusion = (f32[1024]{0:T(1024)S(1)}, bf16[1024,1024]{1,0:T(8,128)(2,1)}) fusion(f32[1024,1024]{1,0:T(8,128)S(1)} %copy-done.9, f32[128,8,8,128]{3,2,1,0:T(8,128)S(1)} %bitcast.58, bf16[1024,1024]{1,0:T(8,128)(2,1)S(1)} %copy-done.7, f32[128,8,8,128]{3,2,1,0:T(8,128)S(1)} %bitcast.63, f32[1024]{0:T(1024)S(1)} %broadcast_bitcast_fusion), kind=kLoop, calls=%fused_computation.7 | loop fusion | flops 9436160 | bytes 16785408 | tf_op jit(solution)/shard_map/reduce_sum | solution.py:51
  143.4 3.8 %collective-permute-start.4 = (f32[128]{0:T(128)S(1)}, f32[128]{0:T(128)S(1)}, u32[]{:S(2)}, u32[]{:S(2)}) collective-permute-start(f32[128]{0:T(128)S(1)} %bitcast_reduce_fusion), channel_id=1, source_target_pairs={{0,4},{4,0},{8,12},{12,8},{16,20},{20,16},{24,28},{28,24},{1,5},{5... | collective-permute-start | bytes 1544 | tf_op jit(solution)/shard_map/ppermute | solution.py:34
  147.2 61.9 %collective-permute-done.4 = f32[128]{0:T(128)S(1)} collective-permute-done((f32[128]{0:T(128)S(1)}, f32[128]{0:T(128)S(1)}, u32[]{:S(2)}, u32[]{:S(2)}) %collective-permute-start.4) | collective-permute-done | bytes 544 | tf_op jit(solution)/shard_map/ppermute | solution.py:34
  209.1 2.7 %collective-permute-start.5 = (f32[128]{0:T(128)S(1)}, f32[128]{0:T(128)S(1)}, u32[]{:S(2)}, u32[]{:S(2)}) collective-permute-start(f32[128]{0:T(128)S(1)} %add.83), channel_id=1, source_target_pairs={{0,8},{4,12},{8,0},{12,4},{16,24},{20,28},{24,16},{28,20},{1,9},{5... | collective-permute-start | bytes 1544 | tf_op jit(solution)/shard_map/ppermute | solution.py:34
  213.4 3.0 %collective-permute-start.6 = (f32[128]{0:T(128)S(1)}, f32[128]{0:T(128)S(1)}, u32[]{:S(2)}, u32[]{:S(2)}) collective-permute-start(f32[128]{0:T(128)S(1)} %add.84), channel_id=1, source_target_pairs={{0,16},{4,20},{8,24},{12,28},{16,0},{20,4},{24,8},{28,12},{1,17},{... | collective-permute-start | bytes 1544 | tf_op jit(solution)/shard_map/ppermute | solution.py:34
  220.6 2.1 multiply_reduce_fusion.3
  223.4 2.9 %reshape.115 = f32[1024,4,128]{2,1,0:T(4,128)} reshape(f32[1024,512]{1,0:T(8,128)} %get-tuple-element.14) | data formatting | bytes 4194304 | tf_op jit(solution)/shard_map/reshape | solution.py:190
  226.4 1.9 collective-permute-start.10
  228.3 4.5 %multiply_reduce_fusion.4 = f32[1024,4]{1,0:T(8,128)S(1)} fusion(f32[1024,4,128]{2,1,0:T(4,128)} %copy-done.5, f32[1024,4,128]{2,1,0:T(4,128)} %reshape.115, f32[128]{0:T(128)S(1)} %copy-done.18, f32[1024,4]{1,0:T(8,128)} %copy-done.12), kind=kLoop, calls=%fused_computation.20 | loop fusion | flops 2093056 | bytes 4227584 | tf_op jit(solution)/shard_map/reduce_sum | solution.py:49
  232.9 2.7 %collective-permute-start.11 = (f32[128]{0:T(128)S(1)}, f32[128]{0:T(128)S(1)}, u32[]{:S(2)}, u32[]{:S(2)}) collective-permute-start(f32[128]{0:T(128)S(1)} %add.89), channel_id=1, source_target_pairs={{0,16},{4,20},{8,24},{12,28},{16,0},{20,4},{24,8},{28,12},{1,17},{... | collective-permute-start | bytes 1544 | tf_op jit(solution)/shard_map/ppermute | solution.py:34
  235.6 1.8 collective-permute-done.11
  238.7 1.9 fusion.5
  241.9 2.9 %add_convert_fusion = bf16[1024,512]{1,0:T(8,128)(2,1)} fusion(f32[1024,512]{1,0:T(8,128)} %collective-permute-done.3, f32[2048,512]{1,0:T(8,128)S(1)} %copy-done.15), kind=kLoop, calls=%fused_computation.19 | loop fusion | flops 1048576 | bytes 5242880 | tf_op jit(solution)/shard_map/convert_element_type | solution.py:198
  (95 shorter events, 32.1 us)
Async XLA Ops:
  0.6 28.7 %collective-permute-start.1 = (bf16[1024,512]{1,0:T(8,128)(2,1)}, bf16[1024,512]{1,0:T(8,128)(2,1)}, u32[]{:S(2)}, u32[]{:S(2)}) collective-permute-start(bf16[1024,512]{1,0:T(8,128)(2,1)} %param.9), channel_id=1, source_target_pairs={{0,4},{4,8},{8,12},{12,16},{16,20},{20,24},{24,28},{1,5},{5,9},{9,... | collective-permute-start | bytes 3145736 | tf_op jit(solution)/shard_map/ppermute | solution.py:22
  12.3 4.9 %copy-start.17 = (f32[128]{0:T(128)S(1)}, f32[128]{0:T(128)}, u32[]{:S(2)}) copy-start(f32[128]{0:T(128)} %param.10) | copy-start | bytes 1540
  12.3 4.9 %copy-start.19 = (s32[16]{0:T(128)S(1)}, s32[16]{0:T(128)}, u32[]{:S(2)}) copy-start(s32[16]{0:T(128)} %param.13) | copy-start | bytes 196
  13.7 37.0 %collective-permute-start = (bf16[1024,512]{1,0:T(8,128)(2,1)}, bf16[1024,512]{1,0:T(8,128)(2,1)}, u32[]{:S(2)}, u32[]{:S(2)}) collective-permute-start(bf16[1024,512]{1,0:T(8,128)(2,1)} %multiply_convert_fusion.1), channel_id=1, source_target_pairs={{0,4},{4,8},{8,12},{12,16},{16,20},{20,24},{24,28},{1,5},{5,9},{9,... | collective-permute-start | bytes 3145736 | tf_op jit(solution)/shard_map/ppermute | solution.py:22
  25.5 3.4 %copy-start.2 = (f32[1024,8,128]{2,1,0:T(8,128)}, f32[1024,8,128]{2,1,0:T(8,128)S(1)}, u32[]{:S(2)}) copy-start(f32[1024,8,128]{2,1,0:T(8,128)S(1)} %mul.148) | copy-start | bytes 12582916
  26.1 3.2 %copy-start.16 = (bf16[1024,512]{1,0:T(8,128)(2,1)S(1)}, bf16[1024,512]{1,0:T(8,128)(2,1)}, u32[]{:S(2)}) copy-start(bf16[1024,512]{1,0:T(8,128)(2,1)} %param.9) | copy-start | bytes 3145732
  113.0 3.4 %copy-start.14 = (f32[2048,512]{1,0:T(8,128)S(1)}, f32[2048,512]{1,0:T(8,128)}, u32[]{:S(2)}) copy-start(f32[2048,512]{1,0:T(8,128)} %get-tuple-element.10) | copy-start | bytes 12582916
  114.9 105.8 %collective-permute-start.2 = (f32[1024,512]{1,0:T(8,128)S(1)}, f32[1024,512]{1,0:T(8,128)S(1)}, u32[]{:S(2)}, u32[]{:S(2)}) collective-permute-start(f32[1024,512]{1,0:T(8,128)S(1)} %slice.13), channel_id=1, source_target_pairs={{4,0},{8,4},{12,8},{16,12},{20,16},{24,20},{28,24},{5,1},{9,5},{13... | collective-permute-start | bytes 6291464 | tf_op jit(solution)/shard_map/ppermute | solution.py:22
  117.9 124.0 %collective-permute-start.3 = (f32[1024,512]{1,0:T(8,128)}, f32[1024,512]{1,0:T(8,128)}, u32[]{:S(2)}, u32[]{:S(2)}) collective-permute-start(f32[1024,512]{1,0:T(8,128)} %slice.15), channel_id=1, source_target_pairs={{4,0},{8,4},{12,8},{16,12},{20,16},{24,20},{28,24},{5,1},{9,5},{13... | collective-permute-start | bytes 6291464 | tf_op jit(solution)/shard_map/ppermute | solution.py:22
  122.7 15.6 %copy-start.7 = (bf16[1024,1024]{1,0:T(8,128)(2,1)S(1)}, bf16[1024,1024]{1,0:T(8,128)(2,1)}, u32[]{:S(2)}) copy-start(bf16[1024,1024]{1,0:T(8,128)(2,1)} %param.7) | copy-start | bytes 6291460
  139.3 81.3 %copy-start.13 = (f32[2048,512]{1,0:T(8,128)S(1)}, f32[2048,512]{1,0:T(8,128)}, u32[]{:S(2)}) copy-start(f32[2048,512]{1,0:T(8,128)} %get-tuple-element.9) | copy-start | bytes 12582916
  143.4 65.7 %collective-permute-start.4 = (f32[128]{0:T(128)S(1)}, f32[128]{0:T(128)S(1)}, u32[]{:S(2)}, u32[]{:S(2)}) collective-permute-start(f32[128]{0:T(128)S(1)} %bitcast_reduce_fusion), channel_id=1, source_target_pairs={{0,4},{4,0},{8,12},{12,8},{16,20},{20,16},{24,28},{28,24},{1,5},{5... | collective-permute-start | bytes 1544 | tf_op jit(solution)/shard_map/ppermute | solution.py:34
  209.1 4.3 %collective-permute-start.5 = (f32[128]{0:T(128)S(1)}, f32[128]{0:T(128)S(1)}, u32[]{:S(2)}, u32[]{:S(2)}) collective-permute-start(f32[128]{0:T(128)S(1)} %add.83), channel_id=1, source_target_pairs={{0,8},{4,12},{8,0},{12,4},{16,24},{20,28},{24,16},{28,20},{1,9},{5... | collective-permute-start | bytes 1544 | tf_op jit(solution)/shard_map/ppermute | solution.py:34
  213.4 4.6 %collective-permute-start.6 = (f32[128]{0:T(128)S(1)}, f32[128]{0:T(128)S(1)}, u32[]{:S(2)}, u32[]{:S(2)}) collective-permute-start(f32[128]{0:T(128)S(1)} %add.84), channel_id=1, source_target_pairs={{0,16},{4,20},{8,24},{12,28},{16,0},{20,4},{24,8},{28,12},{1,17},{... | collective-permute-start | bytes 1544 | tf_op jit(solution)/shard_map/ppermute | solution.py:34
  218.0 1.2 collective-permute-start.7
  219.1 3.7 %collective-permute-start.8 = (f32[128]{0:T(128)S(1)}, f32[128]{0:T(128)S(1)}, u32[]{:S(2)}, u32[]{:S(2)}) collective-permute-start(f32[128]{0:T(128)S(1)} %add.86), channel_id=1, source_target_pairs={{0,2},{1,3},{2,0},{3,1},{4,6},{5,7},{6,4},{7,5},{8,10},{9,11},{10,... | collective-permute-start | bytes 1544 | tf_op jit(solution)/shard_map/ppermute | solution.py:34
  222.8 3.6 %collective-permute-start.9 = (f32[128]{0:T(128)S(1)}, f32[128]{0:T(128)S(1)}, u32[]{:S(2)}, u32[]{:S(2)}) collective-permute-start(f32[128]{0:T(128)S(1)} %bitcast_reduce_fusion.1), channel_id=1, source_target_pairs={{0,4},{4,0},{8,12},{12,8},{16,20},{20,16},{24,28},{28,24},{1,5},{5... | collective-permute-start | bytes 1544 | tf_op jit(solution)/shard_map/ppermute | solution.py:34
  223.4 4.9 %copy-start.18 = (f32[128]{0:T(128)S(1)}, f32[128]{0:T(128)}, u32[]{:S(2)}) copy-start(f32[128]{0:T(128)} %param.11) | copy-start | bytes 1540
  226.4 6.5 %collective-permute-start.10 = (f32[128]{0:T(128)S(1)}, f32[128]{0:T(128)S(1)}, u32[]{:S(2)}, u32[]{:S(2)}) collective-permute-start(f32[128]{0:T(128)S(1)} %add.88), channel_id=1, source_target_pairs={{0,8},{4,12},{8,0},{12,4},{16,24},{20,28},{24,16},{28,20},{1,9},{5... | collective-permute-start | bytes 1544 | tf_op jit(solution)/shard_map/ppermute | solution.py:34
  232.9 5.8 %copy-start.4 = (f32[1024,512]{1,0:T(8,128)S(1)}, f32[1024,512]{1,0:T(8,128)}, u32[]{:S(2)}) copy-start(f32[1024,512]{1,0:T(8,128)} %get-tuple-element.14) | copy-start | bytes 6291460
  232.9 4.5 %collective-permute-start.11 = (f32[128]{0:T(128)S(1)}, f32[128]{0:T(128)S(1)}, u32[]{:S(2)}, u32[]{:S(2)}) collective-permute-start(f32[128]{0:T(128)S(1)} %add.89), channel_id=1, source_target_pairs={{0,16},{4,20},{8,24},{12,28},{16,0},{20,4},{24,8},{28,12},{1,17},{... | collective-permute-start | bytes 1544 | tf_op jit(solution)/shard_map/ppermute | solution.py:34
  237.4 3.1 %collective-permute-start.12 = (f32[128]{0:T(128)S(1)}, f32[128]{0:T(128)S(1)}, u32[]{:S(2)}, u32[]{:S(2)}) collective-permute-start(f32[128]{0:T(128)S(1)} %add.90), channel_id=1, source_target_pairs={{0,1},{1,0},{2,3},{3,2},{4,5},{5,4},{6,7},{7,6},{8,9},{9,8},{10,11... | collective-permute-start | bytes 1544 | tf_op jit(solution)/shard_map/ppermute | solution.py:34
  238.7 3.2 %copy-start.15 = (f32[2048,512]{1,0:T(8,128)S(1)}, f32[2048,512]{1,0:T(8,128)}, u32[]{:S(2)}) copy-start(f32[2048,512]{1,0:T(8,128)} %get-tuple-element.10) | copy-start | bytes 12582916
  240.6 4.2 %collective-permute-start.13 = (f32[128]{0:T(128)S(1)}, f32[128]{0:T(128)S(1)}, u32[]{:S(2)}, u32[]{:S(2)}) collective-permute-start(f32[128]{0:T(128)S(1)} %add.91), channel_id=1, source_target_pairs={{0,2},{1,3},{2,0},{3,1},{4,6},{5,7},{6,4},{7,5},{8,10},{9,11},{10,... | collective-permute-start | bytes 1544 | tf_op jit(solution)/shard_map/ppermute | solution.py:34
  (10 other events, 18.8 us)

commit v3 on v2

v3 whole, which is shorter than its diff:
```python
import functools
import math

import jax
import jax.numpy as jnp
from jax import lax
from jax.experimental import pallas as pl
from jax.experimental.pallas import tpu as pltpu
from jax.sharding import PartitionSpec as P

WINDOW = 1024
QUERY_SCALAR = 168


EPS = 1e-06
BLOCK = 256


def shifted(value, axis, steps):
    count = lax.axis_size(axis)
    leading, last = (max(0, -steps), min(count, count - steps))
    return lax.ppermute(value, axis, [(source, source + steps) for source in range(leading, last)])


def butterfly_sum(value, axes):
    for axis in axes:
        count = lax.axis_size(axis)
        if count & (count - 1):
            value = lax.psum(value, axis)
            continue
        step = 1
        while step < count:
            pairs = [(source, source ^ step) for source in range(count)]
            value = value + lax.ppermute(value, axis, pairs)
            step *= 2
    return value


def norm_rows(raw_rows, head_count):
    values = raw_rows.astype(jnp.float32).reshape(raw_rows.shape[0], head_count, -1)
    inverse = lax.rsqrt(jnp.mean(values * values, axis=-1, keepdims=True) + EPS)
    return (values * inverse, inverse)


def norm_back(raw_rows, gain_vec, head_count, upstream):
    scaled, inverse = norm_rows(raw_rows, head_count)
    incoming = upstream.reshape(scaled.shape)
    weighted = incoming * gain_vec
    inner_sum = jnp.mean(weighted * scaled, axis=-1, keepdims=True)
    result = inverse * (weighted - scaled * inner_sum)
    return (result.reshape(raw_rows.shape), jnp.sum(incoming * scaled, axis=(0, 1)))


def doc_index(positions, doc_ends):
    return jnp.sum((positions[:, None] >= doc_ends[None, :]).astype(jnp.int32), axis=1)


def tile_mask(qdoc_ref, kdoc_ref, q_first, t, group):
    blk = BLOCK
    n_tiles = WINDOW // blk + 1
    rows = lax.broadcasted_iota(jnp.int32, (blk, blk), 0)
    cols = lax.broadcasted_iota(jnp.int32, (blk, blk), 1)
    k_first = pl.multiple_of(q_first + t * blk, blk)
    live = qdoc_ref[...] == kdoc_ref[:, pl.ds(k_first, blk)]
    if t == 0:
        live = live & (cols > rows)
    if t == n_tiles - 1:
        live = live & (cols + t * blk <= rows + WINDOW)
    return jnp.concatenate([live] * group, axis=0), k_first


def stacked(ref, group, head_dim):
    block = ref[...]
    return jnp.concatenate([block[:, a * head_dim:(a + 1) * head_dim] for a in range(group)], axis=0)


def grad_tile(q_g, do_g, k_tile, v_tile, live, log_sums, delta):
    scale = QUERY_SCALAR ** (-0.5)
    scores = lax.dot_general(q_g, k_tile, (((1,), (1,)), ((), ())), preferred_element_type=jnp.float32) * scale
    weights = jnp.where(live, jnp.exp(scores - log_sums), 0.0)
    d_weights = lax.dot_general(do_g, v_tile, (((1,), (1,)), ((), ())), preferred_element_type=jnp.float32)
    d_scores = (weights * (d_weights - delta)).astype(jnp.bfloat16)
    dq_part = jnp.dot(d_scores, k_tile, preferred_element_type=jnp.float32)
    dk_part = lax.dot_general(d_scores, q_g, (((0,), (0,)), ((), ())), preferred_element_type=jnp.float32)
    dv_part = lax.dot_general(
        weights.astype(jnp.bfloat16), do_g, (((0,), (0,)), ((), ())), preferred_element_type=jnp.float32
    )
    return dq_part, dk_part * scale, dv_part


def halo_kernel(qdoc_ref, kdoc_ref, q_ref, do_ref, k_ref, v_ref,
                dq_ref, dkv_ref, lse_ref, delta_ref, dq_scr, dk_ref, dv_ref, *, group, head_dim):
    blk = BLOCK
    n_tiles = WINDOW // blk + 1
    n_halo = WINDOW // blk
    scale = QUERY_SCALAR ** (-0.5)
    qb = pl.program_id(1)

    @pl.when(qb == 0)
    def _():
        dk_ref[...] = jnp.zeros(dk_ref.shape, jnp.float32)
        dv_ref[...] = jnp.zeros(dv_ref.shape, jnp.float32)

    q_first = pl.multiple_of(qb * blk, blk)
    q_g = stacked(q_ref, group, head_dim)
    do_g = stacked(do_ref, group, head_dim)
    totals = jnp.zeros((group * blk, 1), jnp.float32)
    numer = jnp.zeros((group * blk, head_dim), jnp.float32)
    for t in range(n_tiles):
        live, k_first = tile_mask(qdoc_ref, kdoc_ref, q_first, t, group)
        k_tile = k_ref[pl.ds(k_first, blk), :]
        v_tile = v_ref[pl.ds(k_first, blk), :]
        scores = lax.dot_general(q_g, k_tile, (((1,), (1,)), ((), ())), preferred_element_type=jnp.float32) * scale
        exp_s = jnp.where(live, jnp.exp(scores), 0.0)
        totals = totals + jnp.sum(exp_s, axis=1, keepdims=True)
        numer = numer + jnp.dot(exp_s.astype(jnp.bfloat16), v_tile, preferred_element_type=jnp.float32)
    log_sums = jnp.log(totals)
    attn_out = numer / totals
    delta = jnp.sum(do_g.astype(jnp.float32) * attn_out, axis=1, keepdims=True)
    lse_ref[...] = log_sums
    delta_ref[...] = delta

    dq_scr[...] = jnp.zeros(dq_scr.shape, jnp.float32)
    for t in range(n_halo):
        @pl.when(qb + t < n_halo)
        def _():
            live, k_first = tile_mask(qdoc_ref, kdoc_ref, q_first, t, group)
            k_tile = k_ref[pl.ds(k_first, blk), :]
            v_tile = v_ref[pl.ds(k_first, blk), :]
            dq_part, dk_part, dv_part = grad_tile(q_g, do_g, k_tile, v_tile, live, log_sums, delta)
            dq_scr[...] += dq_part
            dk_ref[pl.ds(k_first, blk), :] += dk_part
            dv_ref[pl.ds(k_first, blk), :] += dv_part
    dq = dq_scr[...]
    dq_ref[...] = jnp.concatenate([dq[a * blk:(a + 1) * blk] for a in range(group)], axis=1) * scale

    @pl.when(qb == pl.num_programs(1) - 1)
    def _():
        dkv_ref[:, :head_dim] = dk_ref[...].astype(jnp.bfloat16)
        dkv_ref[:, head_dim:] = dv_ref[...].astype(jnp.bfloat16)


def own_kernel(qdoc_ref, kdoc_ref, q_ref, do_ref, k_ref, v_ref, lse_ref, delta_ref, dq_in_ref,
               dq_ref, dk_ref, dv_ref, dq_scr, *, group, head_dim):
    blk = BLOCK
    n_tiles = WINDOW // blk + 1
    n_halo = WINDOW // blk
    scale = QUERY_SCALAR ** (-0.5)
    qb = pl.program_id(1)

    @pl.when(qb == 0)
    def _():
        dk_ref[...] = jnp.zeros(dk_ref.shape, jnp.float32)
        dv_ref[...] = jnp.zeros(dv_ref.shape, jnp.float32)

    q_first = pl.multiple_of(qb * blk, blk)
    q_g = stacked(q_ref, group, head_dim)
    do_g = stacked(do_ref, group, head_dim)
    log_sums = lse_ref[...]
    delta = delta_ref[...]
    dq_scr[...] = jnp.zeros(dq_scr.shape, jnp.float32)
    for t in range(n_tiles):
        @pl.when(qb + t >= n_halo)
        def _():
            live, k_first = tile_mask(qdoc_ref, kdoc_ref, q_first, t, group)
            k_tile = k_ref[pl.ds(k_first, blk), :]
            v_tile = v_ref[pl.ds(k_first, blk), :]
            dq_part, dk_part, dv_part = grad_tile(q_g, do_g, k_tile, v_tile, live, log_sums, delta)
            dq_scr[...] += dq_part
            own_first = pl.multiple_of(k_first - WINDOW, blk)
            dk_ref[pl.ds(own_first, blk), :] += dk_part
            dv_ref[pl.ds(own_first, blk), :] += dv_part
    dq = dq_scr[...]
    dq_ref[...] = dq_in_ref[...] + jnp.concatenate([dq[a * blk:(a + 1) * blk] for a in range(group)], axis=1) * scale


def attention_grads(query_norm, grad_rows, keys_all, vals_all, own_doc, all_doc, key_heads, head_dim):
    tok_rows, q_cols = query_norm.shape
    key_rows = keys_all.shape[0]
    group = q_cols // (key_heads * head_dim)
    blk = BLOCK
    n_q = tok_rows // blk
    n_tiles = WINDOW // blk + 1
    gw = group * head_dim
    kv_cols = key_heads * head_dim
    stat_rows = key_heads * n_q * group * blk
    tile_flops = 2 * (group * blk) * blk * head_dim
    halo_tiles = sum(max(0, WINDOW // blk - qb) for qb in range(n_q))
    own_tiles = n_q * n_tiles - halo_tiles
    common_specs = [
        pl.BlockSpec((blk, 1), lambda h, qb: (qb, 0)),
        pl.BlockSpec((1, key_rows), lambda h, qb: (0, 0)),
        pl.BlockSpec((blk, gw), lambda h, qb: (qb, h)),
        pl.BlockSpec((blk, gw), lambda h, qb: (qb, h)),
        pl.BlockSpec((key_rows, head_dim), lambda h, qb: (0, h)),
        pl.BlockSpec((key_rows, head_dim), lambda h, qb: (0, h)),
    ]
    stat_spec = pl.BlockSpec((group * blk, 1), lambda h, qb: (h * n_q + qb, 0))
    dq_spec = pl.BlockSpec((blk, gw), lambda h, qb: (qb, h))
    params = pltpu.CompilerParams(dimension_semantics=("arbitrary", "arbitrary"))
    in_bytes = 2 * 2 * tok_rows * q_cols + 2 * 2 * key_rows * kv_cols
    operands = (own_doc.reshape(tok_rows, 1), all_doc.reshape(1, key_rows), query_norm, grad_rows, keys_all, vals_all)
    dq_half, dkv_halo, log_sums, delta = pl.pallas_call(
        functools.partial(halo_kernel, group=group, head_dim=head_dim),
        grid=(key_heads, n_q),
        in_specs=common_specs,
        out_specs=[
            dq_spec,
            pl.BlockSpec((WINDOW, 2 * head_dim), lambda h, qb: (0, h)),
            stat_spec,
            stat_spec,
        ],
        out_shape=[
            jax.ShapeDtypeStruct((tok_rows, q_cols), jnp.float32),
            jax.ShapeDtypeStruct((WINDOW, 2 * kv_cols), jnp.bfloat16),
            jax.ShapeDtypeStruct((stat_rows, 1), jnp.float32),
            jax.ShapeDtypeStruct((stat_rows, 1), jnp.float32),
        ],
        scratch_shapes=[
            pltpu.VMEM((group * blk, head_dim), jnp.float32),
            pltpu.VMEM((WINDOW, head_dim), jnp.float32),
            pltpu.VMEM((WINDOW, head_dim), jnp.float32),
        ],
        compiler_params=params,
        cost_estimate=pl.CostEstimate(
            flops=key_heads * (2 * n_q * n_tiles + 5 * halo_tiles) * tile_flops,
            transcendentals=key_heads * (n_q * n_tiles + halo_tiles) * group * blk * blk,
            bytes_accessed=in_bytes + 4 * tok_rows * q_cols + 2 * 2 * WINDOW * kv_cols,
        ),
    )(*operands)
    dq, dk_own, dv_own = pl.pallas_call(
        functools.partial(own_kernel, group=group, head_dim=head_dim),
        grid=(key_heads, n_q),
        in_specs=common_specs + [stat_spec, stat_spec, dq_spec],
        out_specs=[
            dq_spec,
            pl.BlockSpec((tok_rows, head_dim), lambda h, qb: (0, h)),
            pl.BlockSpec((tok_rows, head_dim), lambda h, qb: (0, h)),
        ],
        out_shape=[
            jax.ShapeDtypeStruct((tok_rows, q_cols), jnp.float32),
            jax.ShapeDtypeStruct((tok_rows, kv_cols), jnp.float32),
            jax.ShapeDtypeStruct((tok_rows, kv_cols), jnp.float32),
        ],
        scratch_shapes=[pltpu.VMEM((group * blk, head_dim), jnp.float32)],
        input_output_aliases={8: 0},
        compiler_params=params,
        cost_estimate=pl.CostEstimate(
            flops=key_heads * own_tiles * 5 * tile_flops,
            transcendentals=key_heads * own_tiles * group * blk * blk,
            bytes_accessed=in_bytes + 2 * 4 * tok_rows * q_cols + 2 * 4 * tok_rows * kv_cols,
        ),
    )(*operands, log_sums, delta, dq_half)
    return dq, dkv_halo, dk_own, dv_own


def per_device(query_raw, key_raw, value_proj, query_gain, key_gain, out_grad, doc_lengths):
    tok_rows = query_raw.shape[0]
    head_dim = query_gain.shape[0]
    query_heads = query_raw.shape[1] // head_dim
    key_heads = key_raw.shape[1] // head_dim
    first_pos = lax.axis_index("ctx") * tok_rows
    doc_ends = jnp.cumsum(doc_lengths)
    own_pos = first_pos + jnp.arange(tok_rows, dtype=jnp.int32)
    own_doc = doc_index(own_pos, doc_ends)
    halo_raw = first_pos - WINDOW + jnp.arange(WINDOW, dtype=jnp.int32)
    halo_doc = jnp.where(halo_raw >= 0, doc_index(halo_raw, doc_ends), -1)
    query_hat, query_inv = norm_rows(query_raw, query_heads)
    query_norm = (query_hat * query_gain).astype(jnp.bfloat16).reshape(tok_rows, query_heads * head_dim)
    key_hat, key_inv = norm_rows(key_raw, key_heads)
    key_norm = (key_hat * key_gain).astype(jnp.bfloat16).reshape(tok_rows, key_heads * head_dim)
    halo_keys, halo_vals = shifted((key_norm[tok_rows - WINDOW:], value_proj[tok_rows - WINDOW:]), "ctx", 1)
    keys_all = jnp.concatenate([halo_keys, key_norm], axis=0)
    vals_all = jnp.concatenate([halo_vals, value_proj], axis=0)
    all_doc = jnp.concatenate([halo_doc, own_doc])
    query_acc, dkv_halo, dk_own, dv_own = attention_grads(
        query_norm, out_grad, keys_all, vals_all, own_doc, all_doc, key_heads, head_dim
    )
    back = shifted(dkv_halo, "ctx", -1).reshape(WINDOW, key_heads, 2, head_dim)
    back_keys = back[:, :, 0].reshape(WINDOW, key_heads * head_dim)
    back_vals = back[:, :, 1].reshape(WINDOW, key_heads * head_dim)
    key_own = jnp.concatenate(
        [dk_own[: tok_rows - WINDOW], dk_own[tok_rows - WINDOW:] + back_keys.astype(jnp.float32)], axis=0
    ).reshape(tok_rows, key_heads, head_dim)
    val_own = jnp.concatenate(
        [dv_own[: tok_rows - WINDOW], dv_own[tok_rows - WINDOW:] + back_vals.astype(jnp.float32)], axis=0
    )
    query_grad, query_part = norm_back(
        query_raw, query_gain, query_heads, query_acc.reshape(tok_rows, query_heads, head_dim)
    )
    key_grad, key_part = norm_back(key_raw, key_gain, key_heads, key_own)
    gain_grads = butterfly_sum(jnp.stack([query_part, key_part]), ("head", "ctx"))
    query_gain_grad, key_gain_grad = gain_grads[0], gain_grads[1]
    value_grad = val_own.astype(jnp.bfloat16)
    return (
        query_grad.astype(jnp.bfloat16),
        key_grad.astype(jnp.bfloat16),
        value_grad,
        query_gain_grad,
        key_gain_grad,
    )


def solution(mesh):
    return jax.shard_map(
        per_device,
        mesh=mesh,
        in_specs=(
            P("ctx", "head"),
            P("ctx", "head"),
            P("ctx", "head"),
            P(),
            P(),
            P("ctx", "head"),
            P(),
        ),
        out_specs=(P("ctx", "head"), P("ctx", "head"), P("ctx", "head"), P(), P()),
        check_vma=False,
    )
```

time: 246 us -> 209 us (0.85)
  waiting for transfers between devices: 87.3 us -> 22.7 us
  Pallas kernels: 59.2 us -> 83.9 us
  local copies, waits for them, and re-layouts: 22 us -> 36.1 us
  starting transfers between devices: 29.3 us -> 22.3 us
  other arithmetic: 46.5 us -> 41.7 us
    ppermute x10 -> x5, waiting for transfers between devices: 68.1 us -> 3.57 us  [butterfly_sum(): value = value + lax.ppermute(value, axis, pairs)]
    pallas_call x1 -> x2, Pallas kernels: 59.2 us -> 83.9 us  [the longest x1 49.7 us: attention_grads(): pl.pallas_call(functools.partial(halo_kernel, group=group, head_dim=head_...]
    unnamed x42 -> x45, local copies, waits for them, and re-layouts: 7.47 us -> 13.6 us
    ppermute x10 -> x5, starting transfers between devices: 17 us -> 11.5 us  [butterfly_sum(): value = value + lax.ppermute(value, axis, pairs)]
    reshape x1 -> x2, local copies, waits for them, and re-layouts: 2.93 us -> 7.36 us  [the longest x1 4.43 us: per_device(): back = shifted(dkv_halo, 'ctx', -1).reshape(WINDOW, key_heads, 2, head_dim)]
    slice x2 -> x1, local copies, waits for them, and re-layouts: 3.44 us -> 6.32 us  [per_device(): back_vals = back[:, :, 1].reshape(WINDOW, key_heads * head_dim)]
    concatenate x1 -> x0, other arithmetic: 2.7 us -> none  [per_device(): vals_all = jnp.concatenate([halo_vals, value_proj], axis=0)]
    ppermute x4 -> x3, starting transfers between devices: 12.2 us -> 10.8 us  [shifted(): lax.ppermute(value, axis, [(source, source + steps) for source in range(l...]
  transfers between devices with their start and end apart: 14 -> 8, of which waited for: 8 -> 5; matrix products, arithmetic and copies ran while one was open for 24% -> 24% of each run, Pallas kernels for 0% -> 16%
where the time goes in v3:
time: 209 us; the launch traced here: 208 us
  Pallas kernels  83.9 us (40%)
  other arithmetic  41.7 us (20%)
  local copies, waits for them, and re-layouts  36.1 us (17%)
  waiting for transfers between devices  22.7 us (11%)
  starting transfers between devices  22.3 us (11%)
    pallas_call x1, Pallas kernels, attention_grads(): pl.pallas_call(functools.partial(halo_kernel, group=group, head_dim=head_...  49.7 us
    pallas_call x1, Pallas kernels, attention_grads(): pl.pallas_call(functools.partial(own_kernel, group=group, head_dim=head_d...  34.2 us
    ppermute x3, waiting for transfers between devices, shifted(): lax.ppermute(value, axis, [(source, source + steps) for source in range(l...  19.2 us
    reduce_sum x2, other arithmetic, norm_back(): inner_sum = jnp.mean(weighted * scaled, axis=-1, keepdims=True)  19 us
    unnamed x45, local copies, waits for them, and re-layouts  13.6 us
    ppermute x5, starting transfers between devices, butterfly_sum(): value = value + lax.ppermute(value, axis, pairs)  11.5 us
    ppermute x3, starting transfers between devices, shifted(): lax.ppermute(value, axis, [(source, source + steps) for source in range(l...  10.8 us
    slice x1, local copies, waits for them, and re-layouts, per_device(): back_vals = back[:, :, 1].reshape(WINDOW, key_heads * head_dim)  6.32 us
  transfers between devices with their start and end apart: 8, of which 5 were waited for; matrix products, arithmetic and copies ran while one was open for 24% of the time, Pallas kernels for 16%

profile of v3, /device:TPU:0, one launch (start us, length us, event | category | flops | bytes accessed | tf_op | source)
XLA Modules:
  0.0 207.7 jit_solution(12609308406754224120)
XLA Ops:
  0.6 5.9 %collective-permute-start.1 = (bf16[1024,512]{1,0:T(8,128)(2,1)}, bf16[1024,512]{1,0:T(8,128)(2,1)}, u32[]{:S(2)}, u32[]{:S(2)}) collective-permute-start(bf16[1024,512]{1,0:T(8,128)(2,1)} %param.9), channel_id=1, source_target_pairs={{0,4},{4,8},{8,12},{12,16},{16,20},{20,24},{24,28},{1,5},{5,9},{9,... | collective-permute-start | bytes 3145736 | tf_op jit(solution)/shard_map/ppermute | solution.py:22
  7.2 1.7 reshape.120
  13.8 3.4 %collective-permute-start = (bf16[1024,512]{1,0:T(8,128)(2,1)}, bf16[1024,512]{1,0:T(8,128)(2,1)}, u32[]{:S(2)}, u32[]{:S(2)}) collective-permute-start(bf16[1024,512]{1,0:T(8,128)(2,1)} %multiply_convert_fusion.1), channel_id=1, source_target_pairs={{0,4},{4,8},{8,12},{12,16},{16,20},{20,24},{24,28},{1,5},{5,9},{9,... | collective-permute-start | bytes 3145736 | tf_op jit(solution)/shard_map/ppermute | solution.py:22
  18.6 2.0 convert_bitcast_fusion
  26.1 2.7 %multiply_convert_fusion.q_ref = bf16[1024,1024]{1,0:T(8,128)(2,1)} fusion(f32[128,8,8,128]{3,2,1,0:T(8,128)S(1)} %bitcast.76, bf16[1024,1024]{1,0:T(8,128)(2,1)S(1)} %copy-done.6, f32[1024]{0:T(1024)S(1)} %broadcast_bitcast_fusion), kind=kLoop, calls=%fused_computation.9 | loop fusion | flops 4194304 | bytes 8392704 | tf_op jit(solution)/shard_map/convert_element_type | solution.py:269
  32.1 18.6 %collective-permute-done = bf16[1024,512]{1,0:T(8,128)(2,1)} collective-permute-done((bf16[1024,512]{1,0:T(8,128)(2,1)}, bf16[1024,512]{1,0:T(8,128)(2,1)}, u32[]{:S(2)}, u32[]{:S(2)}) %collective-permute-start) | collective-permute-done | bytes 1048608 | tf_op jit(solution)/shard_map/ppermute | solution.py:22
  50.7 3.0 %pad_maximum_fusion.k_ref = bf16[2048,512]{1,0:T(8,128)(2,1)} fusion(bf16[1024,512]{1,0:T(8,128)(2,1)} %multiply_convert_fusion.1, bf16[1024,512]{1,0:T(8,128)(2,1)} %collective-permute-done), kind=kLoop, calls=%fused_computation.19 | loop fusion | flops 4194304 | bytes 4194304 | tf_op jit(solution)/shard_map/concatenate | solution.py:273
  53.7 49.7 %shard_map.110 = (f32[1024,1024]{1,0:T(8,128)}, bf16[1024,1024]{1,0:T(8,128)(2,1)}, f32[8192,1]{1,0:T(8,128)}, f32[8192,1]{1,0:T(8,128)}) custom-call(s32[1024,1]{1,0:T(8,128)} %copy.23.qdoc_ref, s32[1,2048]{1,0:T(1,128)} %bitcast.87, bf16[1024,1024]{1,0:T(8,128)(2,1)} %multiply_convert_fusion.q_ref, bf16[1024,1024]{1,0:T(8,128)(2,1)} %do_ref.3, ...), custom_call_target="tpu_custom_call" | custom-call | flops 12079595520 | bytes 14680064 | tf_op jit(solution)/shard_map/pallas_call | solution.py:203
  104.8 34.2 %shard_map.111 = (f32[1024,1024]{1,0:T(8,128)}, f32[1024,512]{1,0:T(8,128)}, f32[1024,512]{1,0:T(8,128)}) custom-call(s32[1024,1]{1,0:T(8,128)} %copy.23.qdoc_ref, s32[1,2048]{1,0:T(1,128)} %bitcast.88, bf16[1024,1024]{1,0:T(8,128)(2,1)} %multiply_convert_fusion.q_ref, bf16[1024,1024]{1,0:T(8,128)(2,1)} %do_ref.3, ...), custom_call_target="tpu_custom_call", output_to_operand_aliasing={{0}: (8, {})} | custom-call | flops 6710886400 | bytes 20971520 | tf_op jit(solution)/shard_map/pallas_call | solution.py:231
  139.1 3.2 %copy.31 = f32[128,8,8,128]{3,2,1,0:T(8,128)S(1)} copy(f32[128,8,8,128]{3,1,2,0:T(8,128)} %bitcast.81) | data formatting | bytes 8388608
  142.6 1.9 copy-done.1
  144.6 14.4 %multiply_reduce_fusion.1 = f32[1024,8]{1,0:T(8,128)S(1)} fusion(f32[1024,8,128]{2,1,0:T(8,128)S(1)} %bitcast_multiply_fusion.1, f32[1024,8,128]{2,1,0:T(8,128)S(1)} %bitcast.75, f32[1024,8]{1,0:T(8,128)S(1)} %copy-done.12), kind=kLoop, calls=%fused_computation.8 | loop fusion | flops 3137536 | bytes 8454144 | tf_op jit(solution)/shard_map/reduce_sum | solution.py:49
  161.3 4.0 %multiply_reduce_fusion = (f32[1024]{0:T(1024)S(1)}, bf16[1024,1024]{1,0:T(8,128)(2,1)}) fusion(f32[1024,1024]{1,0:T(8,128)S(1)} %copy-done.9, f32[128,8,8,128]{3,2,1,0:T(8,128)S(1)} %bitcast.77, bf16[1024,1024]{1,0:T(8,128)(2,1)S(1)} %copy-done.7, f32[128,8,8,128]{3,2,1,0:T(8,128)S(1)} %bitcast.82, f32[1024]{0:T(1024)S(1)} %broadcast_bitcast_fusion), kind=kLoop, calls=%fused_computation.7 | loop fusion | flops 9436160 | bytes 16785408 | tf_op jit(solution)/shard_map/reduce_sum | solution.py:51
  165.3 4.4 %reshape.122 = bf16[1024,4,2,128]{3,2,1,0:T(2,128)(2,1)} reshape(bf16[1024,1024]{1,0:T(8,128)(2,1)} %collective-permute-done.2) | data formatting | bytes 4194304 | tf_op jit(solution)/shard_map/reshape | solution.py:279
  169.7 6.3 %fusion.8 = (bf16[1024,4,1,128]{3,2,1,0:T(2,128)(2,1)}, bf16[1024,4,1,128]{3,2,1,0:T(2,128)(2,1)S(1)}) fusion(bf16[1024,4,2,128]{3,2,1,0:T(2,128)(2,1)} %reshape.122), kind=kLoop, calls=%fused_computation.46 | loop fusion | bytes 4194304 | tf_op jit(solution)/shard_map/slice | solution.py:281
  177.6 2.1 %multiply_reduce_fusion.3 = (f32[512]{0:T(512)S(1)}, f32[1024,512]{1,0:T(8,128)}) fusion(f32[128,8,4,128]{3,2,1,0:T(4,128)S(1)} %bitcast.79, bf16[1024,512]{1,0:T(8,128)(2,1)S(1)} %copy-done.8, f32[1024,512]{1,0:T(8,128)S(1)} %copy-done.14, f32[128,8,4,128]{3,2,1,0:T(4,128)S(1)} %bitcast.84), kind=kLoop, calls=%fused_computation.20 | loop fusion | flops 2620928 | bytes 9439232 | tf_op jit(solution)/shard_map/reduce_sum | solution.py:51
  179.8 2.9 %reshape.123 = f32[1024,4,128]{2,1,0:T(4,128)} reshape(f32[1024,512]{1,0:T(8,128)} %get-tuple-element.22) | data formatting | bytes 4194304 | tf_op jit(solution)/shard_map/reshape | solution.py:284
  182.8 4.5 %multiply_reduce_fusion.4 = f32[1024,4]{1,0:T(8,128)S(1)} fusion(f32[1024,4,128]{2,1,0:T(4,128)} %copy-done.5, f32[1024,4,128]{2,1,0:T(4,128)} %reshape.123, f32[128]{0:T(128)S(1)} %copy-done.19, f32[1024,4]{1,0:T(8,128)} %copy-done.13), kind=kLoop, calls=%fused_computation.21 | loop fusion | flops 2093056 | bytes 4227584 | tf_op jit(solution)/shard_map/reduce_sum | solution.py:49
  187.4 1.6 collective-permute-start.4
  189.0 2.0 collective-permute-done.4
  191.0 3.2 %collective-permute-start.5 = (f32[2,128]{1,0:T(2,128)S(1)}, f32[2,128]{1,0:T(2,128)S(1)}, u32[]{:S(2)}, u32[]{:S(2)}) collective-permute-start(f32[2,128]{1,0:T(2,128)S(1)} %fusion.9), channel_id=1, source_target_pairs={{0,4},{4,0},{8,12},{12,8},{16,20},{20,16},{24,28},{28,24},{1,5},{5... | collective-permute-start | bytes 3080 | tf_op jit(solution)/shard_map/ppermute | solution.py:34
  195.5 1.9 fusion.6
  197.4 3.0 %collective-permute-start.6 = (f32[2,128]{1,0:T(2,128)S(1)}, f32[2,128]{1,0:T(2,128)S(1)}, u32[]{:S(2)}, u32[]{:S(2)}) collective-permute-start(f32[2,128]{1,0:T(2,128)S(1)} %add.70), channel_id=1, source_target_pairs={{0,8},{4,12},{8,0},{12,4},{16,24},{20,28},{24,16},{28,20},{1,9},{5... | collective-permute-start | bytes 3080 | tf_op jit(solution)/shard_map/ppermute | solution.py:34
  201.9 3.7 %collective-permute-start.7 = (f32[2,128]{1,0:T(2,128)S(1)}, f32[2,128]{1,0:T(2,128)S(1)}, u32[]{:S(2)}, u32[]{:S(2)}) collective-permute-start(f32[2,128]{1,0:T(2,128)S(1)} %add.71), channel_id=1, source_target_pairs={{0,16},{4,20},{8,24},{12,28},{16,0},{20,4},{24,8},{28,12},{1,17},{... | collective-permute-start | bytes 3080 | tf_op jit(solution)/shard_map/ppermute | solution.py:34
  (86 shorter events, 26.1 us)
Async XLA Ops:
  0.6 28.7 %collective-permute-start.1 = (bf16[1024,512]{1,0:T(8,128)(2,1)}, bf16[1024,512]{1,0:T(8,128)(2,1)}, u32[]{:S(2)}, u32[]{:S(2)}) collective-permute-start(bf16[1024,512]{1,0:T(8,128)(2,1)} %param.9), channel_id=1, source_target_pairs={{0,4},{4,8},{8,12},{12,16},{16,20},{20,24},{24,28},{1,5},{5,9},{9,... | collective-permute-start | bytes 3145736 | tf_op jit(solution)/shard_map/ppermute | solution.py:22
  10.3 2.1 %copy-start.8 = (bf16[1024,512]{1,0:T(8,128)(2,1)S(1)}, bf16[1024,512]{1,0:T(8,128)(2,1)}, u32[]{:S(2)}) copy-start(bf16[1024,512]{1,0:T(8,128)(2,1)} %param.8) | copy-start | bytes 3145732
  12.4 4.8 %copy-start.18 = (f32[128]{0:T(128)S(1)}, f32[128]{0:T(128)}, u32[]{:S(2)}) copy-start(f32[128]{0:T(128)} %param.10) | copy-start | bytes 1540
  12.4 4.8 %copy-start.20 = (s32[16]{0:T(128)S(1)}, s32[16]{0:T(128)}, u32[]{:S(2)}) copy-start(s32[16]{0:T(128)} %param.13) | copy-start | bytes 196
  13.8 36.9 %collective-permute-start = (bf16[1024,512]{1,0:T(8,128)(2,1)}, bf16[1024,512]{1,0:T(8,128)(2,1)}, u32[]{:S(2)}, u32[]{:S(2)}) collective-permute-start(bf16[1024,512]{1,0:T(8,128)(2,1)} %multiply_convert_fusion.1), channel_id=1, source_target_pairs={{0,4},{4,8},{8,12},{12,16},{16,20},{20,24},{24,28},{1,5},{5,9},{9,... | collective-permute-start | bytes 3145736 | tf_op jit(solution)/shard_map/ppermute | solution.py:22
  21.7 2.0 copy-start
  24.3 1.8 copy-start.6
  25.5 3.3 %copy-start.2 = (f32[1024,8,128]{2,1,0:T(8,128)}, f32[1024,8,128]{2,1,0:T(8,128)S(1)}, u32[]{:S(2)}) copy-start(f32[1024,8,128]{2,1,0:T(8,128)S(1)} %mul.148) | copy-start | bytes 12582916
  28.8 1.8 copy-start.16
  103.4 61.9 %collective-permute-start.2 = (bf16[1024,1024]{1,0:T(8,128)(2,1)}, bf16[1024,1024]{1,0:T(8,128)(2,1)}, u32[]{:S(2)}, u32[]{:S(2)}) collective-permute-start(bf16[1024,1024]{1,0:T(8,128)(2,1)} %get-tuple-element.17), channel_id=1, source_target_pairs={{4,0},{8,4},{12,8},{16,12},{20,16},{24,20},{28,24},{5,1},{9,5},{13... | collective-permute-start | bytes 6291464 | tf_op jit(solution)/shard_map/ppermute | solution.py:22
  142.3 2.2 %copy-start.1 = (f32[128,8,8,128]{3,2,1,0:T(8,128)S(1)}, f32[128,8,8,128]{3,2,1,0:T(8,128)}, u32[]{:S(2)}) copy-start(f32[128,8,8,128]{3,2,1,0:T(8,128)} %copy-done) | copy-start | bytes 12582916
  142.3 2.3 %copy-start.12 = (f32[1024,8]{1,0:T(8,128)S(1)}, f32[1024,8]{1,0:T(8,128)}, u32[]{:S(2)}) copy-start(f32[1024,8]{1,0:T(8,128)} %copy-done.11) | copy-start | bytes 98308
  144.6 15.6 %copy-start.7 = (bf16[1024,1024]{1,0:T(8,128)(2,1)S(1)}, bf16[1024,1024]{1,0:T(8,128)(2,1)}, u32[]{:S(2)}) copy-start(bf16[1024,1024]{1,0:T(8,128)(2,1)} %param.7) | copy-start | bytes 6291460
  144.6 15.7 %copy-start.9 = (f32[1024,1024]{1,0:T(8,128)S(1)}, f32[1024,1024]{1,0:T(8,128)}, u32[]{:S(2)}) copy-start(f32[1024,1024]{1,0:T(8,128)} %get-tuple-element.15) | copy-start | bytes 12582916
  159.1 2.2 %copy-start.3 = (f32[1024,8,128]{2,1,0:T(8,128)S(1)}, f32[1024,8,128]{2,1,0:T(8,128)}, u32[]{:S(2)}) copy-start(f32[1024,8,128]{2,1,0:T(8,128)} %copy-done.2) | copy-start | bytes 12582916
  179.8 3.0 %copy-start.19 = (f32[128]{0:T(128)S(1)}, f32[128]{0:T(128)}, u32[]{:S(2)}) copy-start(f32[128]{0:T(128)} %param.11) | copy-start | bytes 1540
  182.7 4.7 %collective-permute-start.3 = (f32[2,128]{1,0:T(2,128)S(1)}, f32[2,128]{1,0:T(2,128)S(1)}, u32[]{:S(2)}, u32[]{:S(2)}) collective-permute-start(f32[2,128]{1,0:T(2,128)S(1)} %pad_maximum_fusion.1), channel_id=1, source_target_pairs={{0,1},{1,0},{2,3},{3,2},{4,5},{5,4},{6,7},{7,6},{8,9},{9,8},{10,11... | collective-permute-start | bytes 3080 | tf_op jit(solution)/shard_map/ppermute | solution.py:34
  187.4 8.1 %copy-start.4 = (f32[1024,512]{1,0:T(8,128)S(1)}, f32[1024,512]{1,0:T(8,128)}, u32[]{:S(2)}) copy-start(f32[1024,512]{1,0:T(8,128)} %get-tuple-element.22) | copy-start | bytes 6291460
  187.4 3.6 %collective-permute-start.4 = (f32[2,128]{1,0:T(2,128)S(1)}, f32[2,128]{1,0:T(2,128)S(1)}, u32[]{:S(2)}, u32[]{:S(2)}) collective-permute-start(f32[2,128]{1,0:T(2,128)S(1)} %fusion.7), channel_id=1, source_target_pairs={{0,2},{1,3},{2,0},{3,1},{4,6},{5,7},{6,4},{7,5},{8,10},{9,11},{10,... | collective-permute-start | bytes 3080 | tf_op jit(solution)/shard_map/ppermute | solution.py:34
  191.0 6.3 %collective-permute-start.5 = (f32[2,128]{1,0:T(2,128)S(1)}, f32[2,128]{1,0:T(2,128)S(1)}, u32[]{:S(2)}, u32[]{:S(2)}) collective-permute-start(f32[2,128]{1,0:T(2,128)S(1)} %fusion.9), channel_id=1, source_target_pairs={{0,4},{4,0},{8,12},{12,8},{16,20},{20,16},{24,28},{28,24},{1,5},{5... | collective-permute-start | bytes 3080 | tf_op jit(solution)/shard_map/ppermute | solution.py:34
  195.5 4.9 %copy-start.10 = (bf16[1024,4,1,128]{3,2,1,0:T(2,128)(2,1)S(1)}, bf16[1024,4,1,128]{3,2,1,0:T(2,128)(2,1)}, u32[]{:S(2)}) copy-start(bf16[1024,4,1,128]{3,2,1,0:T(2,128)(2,1)} %get-tuple-element.25) | copy-start | bytes 3145732
  197.4 4.5 %collective-permute-start.6 = (f32[2,128]{1,0:T(2,128)S(1)}, f32[2,128]{1,0:T(2,128)S(1)}, u32[]{:S(2)}, u32[]{:S(2)}) collective-permute-start(f32[2,128]{1,0:T(2,128)S(1)} %add.70), channel_id=1, source_target_pairs={{0,8},{4,12},{8,0},{12,4},{16,24},{20,28},{24,16},{28,20},{1,9},{5... | collective-permute-start | bytes 3080 | tf_op jit(solution)/shard_map/ppermute | solution.py:34
  200.4 5.2 %copy-start.15 = (f32[1024,512]{1,0:T(8,128)S(1)}, f32[1024,512]{1,0:T(8,128)}, u32[]{:S(2)}) copy-start(f32[1024,512]{1,0:T(8,128)} %get-tuple-element.18) | copy-start | bytes 6291460
  201.9 5.2 %collective-permute-start.7 = (f32[2,128]{1,0:T(2,128)S(1)}, f32[2,128]{1,0:T(2,128)S(1)}, u32[]{:S(2)}, u32[]{:S(2)}) collective-permute-start(f32[2,128]{1,0:T(2,128)S(1)} %add.71), channel_id=1, source_target_pairs={{0,16},{4,20},{8,24},{12,28},{16,0},{20,4},{24,8},{28,12},{1,17},{... | collective-permute-start | bytes 3080 | tf_op jit(solution)/shard_map/ppermute | solution.py:34
  (5 other events, 6.2 us)

commit v4 on v3

--- a/solution.py
+++ b/solution.py
@@ -140,8 +140,17 @@
         dkv_ref[:, head_dim:] = dv_ref[...].astype(jnp.bfloat16)
 
 
-def own_kernel(qdoc_ref, kdoc_ref, q_ref, do_ref, k_ref, v_ref, lse_ref, delta_ref, dq_in_ref,
-               dq_ref, dk_ref, dv_ref, dq_scr, *, group, head_dim):
+def norm_grad(raw, gain, upstream):
+    inverse = lax.rsqrt(jnp.mean(raw * raw, axis=1, keepdims=True) + EPS)
+    scaled = raw * inverse
+    weighted = upstream * gain
+    inner_sum = jnp.mean(weighted * scaled, axis=1, keepdims=True)
+    result = inverse * (weighted - scaled * inner_sum)
+    return result, jnp.sum(upstream * scaled, axis=0, keepdims=True)
+
+
+def own_kernel(qdoc_ref, kdoc_ref, q_ref, do_ref, k_ref, v_ref, lse_ref, delta_ref, dq_in_ref, raw_ref, gain_ref,
+               qgrad_ref, qgain_ref, dk_ref, dv_ref, dq_scr, *, group, head_dim):
     blk = BLOCK
     n_tiles = WINDOW // blk + 1
     n_halo = WINDOW // blk
@@ -171,10 +180,63 @@
             dk_ref[pl.ds(own_first, blk), :] += dk_part
             dv_ref[pl.ds(own_first, blk), :] += dv_part
     dq = dq_scr[...]
-    dq_ref[...] = dq_in_ref[...] + jnp.concatenate([dq[a * blk:(a + 1) * blk] for a in range(group)], axis=1) * scale
-
-
-def attention_grads(query_norm, grad_rows, keys_all, vals_all, own_doc, all_doc, key_heads, head_dim):
+    dq_in = dq_in_ref[...]
+    raw = raw_ref[...].astype(jnp.float32)
+    gain = gain_ref[...]
+    gain_sum = jnp.zeros((1, head_dim), jnp.float32)
+    for a in range(group):
+        cols = slice(a * head_dim, (a + 1) * head_dim)
+        upstream = dq_in[:, cols] + dq[a * blk:(a + 1) * blk] * scale
+        result, part = norm_grad(raw[:, cols], gain, upstream)
+        qgrad_ref[:, cols] = result.astype(qgrad_ref.dtype)
+        gain_sum = gain_sum + part
+    qgain_ref[...] = gain_sum.reshape(qgain_ref.shape)
+
+
+def kv_final_kernel(dk_ref, dv_ref, back_ref, raw_ref, gain_ref, kgrad_ref, vgrad_ref, kgain_ref, *, head_dim):
+    tok_rows = dk_ref.shape[0]
+    lead = tok_rows - WINDOW
+    back = back_ref[...].astype(jnp.float32)
+    dk = dk_ref[...]
+    dv = dv_ref[...]
+    if lead:
+        dk = jnp.concatenate([dk[:lead], dk[lead:] + back[:, :head_dim]], axis=0)
+        dv = jnp.concatenate([dv[:lead], dv[lead:] + back[:, head_dim:]], axis=0)
+    else:
+        dk = dk + back[:, :head_dim]
+        dv = dv + back[:, head_dim:]
+    vgrad_ref[...] = dv.astype(vgrad_ref.dtype)
+    result, part = norm_grad(raw_ref[...].astype(jnp.float32), gain_ref[...], dk)
+    kgrad_ref[...] = result.astype(kgrad_ref.dtype)
+    kgain_ref[...] = part.reshape(kgain_ref.shape)
+
+
+def kv_final(dk_own, dv_own, back, key_raw, key_gain, key_heads, head_dim):
+    tok_rows = dk_own.shape[0]
+    kv_cols = key_heads * head_dim
+    col_spec = pl.BlockSpec((tok_rows, head_dim), lambda h: (0, h))
+    return pl.pallas_call(
+        functools.partial(kv_final_kernel, head_dim=head_dim),
+        grid=(key_heads,),
+        in_specs=[
+            col_spec,
+            col_spec,
+            pl.BlockSpec((WINDOW, 2 * head_dim), lambda h: (0, h)),
+            col_spec,
+            pl.BlockSpec((1, head_dim), lambda h: (0, 0)),
+        ],
+        out_specs=[col_spec, col_spec, pl.BlockSpec((1, 1, head_dim), lambda h: (h, 0, 0))],
+        out_shape=[
+            jax.ShapeDtypeStruct((tok_rows, kv_cols), jnp.bfloat16),
+            jax.ShapeDtypeStruct((tok_rows, kv_cols), jnp.bfloat16),
+            jax.ShapeDtypeStruct((key_heads, 1, head_dim), jnp.float32),
+        ],
+        compiler_params=pltpu.CompilerParams(dimension_semantics=("arbitrary",)),
+    )(dk_own, dv_own, back, key_raw, key_gain.reshape(1, head_dim))
+
+
+def attention_grads(query_norm, grad_rows, keys_all, vals_all, own_doc, all_doc, key_heads, head_dim,
+                    query_raw, query_gain):
     tok_rows, q_cols = query_norm.shape
     key_rows = keys_all.shape[0]
     group = q_cols // (key_heads * head_dim)
@@ -228,30 +290,33 @@
             bytes_accessed=in_bytes + 4 * tok_rows * q_cols + 2 * 2 * WINDOW * kv_cols,
         ),
     )(*operands)
-    dq, dk_own, dv_own = pl.pallas_call(
+    raw_spec = pl.BlockSpec((blk, gw), lambda h, qb: (qb, h))
+    gain_spec = pl.BlockSpec((1, head_dim), lambda h, qb: (0, 0))
+    query_grad, qgain_parts, dk_own, dv_own = pl.pallas_call(
         functools.partial(own_kernel, group=group, head_dim=head_dim),
         grid=(key_heads, n_q),
-        in_specs=common_specs + [stat_spec, stat_spec, dq_spec],
+        in_specs=common_specs + [stat_spec, stat_spec, dq_spec, raw_spec, gain_spec],
         out_specs=[
-            dq_spec,
+            raw_spec,
+            pl.BlockSpec((1, 1, head_dim), lambda h, qb: (h * n_q + qb, 0, 0)),
             pl.BlockSpec((tok_rows, head_dim), lambda h, qb: (0, h)),
             pl.BlockSpec((tok_rows, head_dim), lambda h, qb: (0, h)),
         ],
         out_shape=[
-            jax.ShapeDtypeStruct((tok_rows, q_cols), jnp.float32),
+            jax.ShapeDtypeStruct((tok_rows, q_cols), jnp.bfloat16),
+            jax.ShapeDtypeStruct((key_heads * n_q, 1, head_dim), jnp.float32),
             jax.ShapeDtypeStruct((tok_rows, kv_cols), jnp.float32),
             jax.ShapeDtypeStruct((tok_rows, kv_cols), jnp.float32),
         ],
         scratch_shapes=[pltpu.VMEM((group * blk, head_dim), jnp.float32)],
-        input_output_aliases={8: 0},
         compiler_params=params,
         cost_estimate=pl.CostEstimate(
             flops=key_heads * own_tiles * 5 * tile_flops,
             transcendentals=key_heads * own_tiles * group * blk * blk,
             bytes_accessed=in_bytes + 2 * 4 * tok_rows * q_cols + 2 * 4 * tok_rows * kv_cols,
         ),
-    )(*operands, log_sums, delta, dq_half)
-    return dq, dkv_halo, dk_own, dv_own
+    )(*operands, log_sums, delta, dq_half, query_raw, query_gain.reshape(1, head_dim))
+    return query_grad, jnp.sum(qgain_parts, axis=(0, 1)), dkv_halo, dk_own, dv_own
 
 
 def per_device(query_raw, key_raw, value_proj, query_gain, key_gain, out_grad, doc_lengths):
@@ -273,32 +338,14 @@
     keys_all = jnp.concatenate([halo_keys, key_norm], axis=0)
     vals_all = jnp.concatenate([halo_vals, value_proj], axis=0)
     all_doc = jnp.concatenate([halo_doc, own_doc])
-    query_acc, dkv_halo, dk_own, dv_own = attention_grads(
-        query_norm, out_grad, keys_all, vals_all, own_doc, all_doc, key_heads, head_dim
+    query_grad, query_part, dkv_halo, dk_own, dv_own = attention_grads(
+        query_norm, out_grad, keys_all, vals_all, own_doc, all_doc, key_heads, head_dim, query_raw, query_gain
     )
-    back = shifted(dkv_halo, "ctx", -1).reshape(WINDOW, key_heads, 2, head_dim)
-    back_keys = back[:, :, 0].reshape(WINDOW, key_heads * head_dim)
-    back_vals = back[:, :, 1].reshape(WINDOW, key_heads * head_dim)
-    key_own = jnp.concatenate(
-        [dk_own[: tok_rows - WINDOW], dk_own[tok_rows - WINDOW:] + back_keys.astype(jnp.float32)], axis=0
-    ).reshape(tok_rows, key_heads, head_dim)
-    val_own = jnp.concatenate(
-        [dv_own[: tok_rows - WINDOW], dv_own[tok_rows - WINDOW:] + back_vals.astype(jnp.float32)], axis=0
-    )
-    query_grad, query_part = norm_back(
-        query_raw, query_gain, query_heads, query_acc.reshape(tok_rows, query_heads, head_dim)
-    )
-    key_grad, key_part = norm_back(key_raw, key_gain, key_heads, key_own)
+    back = shifted(dkv_halo, "ctx", -1)
+    key_grad, value_grad, key_parts = kv_final(dk_own, dv_own, back, key_raw, key_gain, key_heads, head_dim)
+    key_part = jnp.sum(key_parts, axis=(0, 1))
     gain_grads = butterfly_sum(jnp.stack([query_part, key_part]), ("head", "ctx"))
-    query_gain_grad, key_gain_grad = gain_grads[0], gain_grads[1]
-    value_grad = val_own.astype(jnp.bfloat16)
-    return (
-        query_grad.astype(jnp.bfloat16),
-        key_grad.astype(jnp.bfloat16),
-        value_grad,
-        query_gain_grad,
-        key_gain_grad,
-    )
+    return (query_grad, key_grad, value_grad, gain_grads[0], gain_grads[1])
 
 
 def solution(mesh):

time: 209 us -> 179 us (0.86)
  other arithmetic: 41.7 us -> 16.9 us
  local copies, waits for them, and re-layouts: 36.1 us -> 15.7 us
  waiting for transfers between devices: 22.7 us -> 32.1 us
  Pallas kernels: 83.9 us -> 91.9 us
    reduce_sum x6 -> x2, other arithmetic: 25.1 us -> 1.44 us  [the longest x1 0.73 us: attention_grads(): jnp.sum(qgain_parts, axis=(0, 1))]
    reshape x3 -> x0, local copies, waits for them, and re-layouts: 9.09 us -> none  [the longest x1 4.43 us: per_device(): back = shifted(dkv_halo, 'ctx', -1).reshape(WINDOW, key_heads, 2, head_dim)]
    unnamed x45 -> x16, local copies, waits for them, and re-layouts: 13.6 us -> 5.84 us
    slice x1 -> x0, local copies, waits for them, and re-layouts: 6.32 us -> none  [per_device(): back_vals = back[:, :, 1].reshape(WINDOW, key_heads * head_dim)]
    pallas_call x0 -> x1, Pallas kernels: none -> 5.53 us  [kv_final(): pl.pallas_call(functools.partial(kv_final_kernel, head_dim=head_dim), gri...]
    ppermute x3, waiting for transfers between devices: 19.2 us -> 24.2 us  [shifted(): lax.ppermute(value, axis, [(source, source + steps) for source in range(l...]
    ppermute x5, waiting for transfers between devices: 3.57 us -> 7.86 us  [butterfly_sum(): value = value + lax.ppermute(value, axis, pairs)]
    convert_element_type x4 -> x0, other arithmetic: 3.67 us -> none  [the longest x1 1.89 us: per_device(): key_grad.astype(jnp.bfloat16)]
  transfers between devices with their start and end apart: 8 -> 8, of which waited for: 5 -> 7; matrix products, arithmetic and copies ran while one was open for 24% -> 15% of each run, Pallas kernels for 16% -> 21%
where the time goes in v4:
time: 179 us; the launch traced here: 178 us
  Pallas kernels  91.9 us (51%)
  waiting for transfers between devices  32.1 us (18%)
  starting transfers between devices  20.4 us (11%)
  other arithmetic  16.9 us (9%)
  local copies, waits for them, and re-layouts  15.7 us (9%)
    pallas_call x1, Pallas kernels, attention_grads(): pl.pallas_call(functools.partial(halo_kernel, group=group, head_dim=head_...  49.6 us
    pallas_call x1, Pallas kernels, attention_grads(): pl.pallas_call(functools.partial(own_kernel, group=group, head_dim=head_d...  36.7 us
    ppermute x3, waiting for transfers between devices, shifted(): lax.ppermute(value, axis, [(source, source + steps) for source in range(l...  24.2 us
    ppermute x3, starting transfers between devices, shifted(): lax.ppermute(value, axis, [(source, source + steps) for source in range(l...  10.9 us
    ppermute x5, starting transfers between devices, butterfly_sum(): value = value + lax.ppermute(value, axis, pairs)  9.5 us
    ppermute x5, waiting for transfers between devices, butterfly_sum(): value = value + lax.ppermute(value, axis, pairs)  7.86 us
    unnamed x16, local copies, waits for them, and re-layouts  5.84 us
    pallas_call x1, Pallas kernels, kv_final(): pl.pallas_call(functools.partial(kv_final_kernel, head_dim=head_dim), gri...  5.53 us
  transfers between devices with their start and end apart: 8, of which 7 were waited for; matrix products, arithmetic and copies ran while one was open for 15% of the time, Pallas kernels for 21%

profile of v4, /device:TPU:0, one launch (start us, length us, event | category | flops | bytes accessed | tf_op | source)
XLA Modules:
  0.0 177.9 jit_solution(16603992822537270247)
XLA Ops:
  0.6 5.9 %collective-permute-start.1 = (bf16[1024,512]{1,0:T(8,128)(2,1)}, bf16[1024,512]{1,0:T(8,128)(2,1)}, u32[]{:S(2)}, u32[]{:S(2)}) collective-permute-start(bf16[1024,512]{1,0:T(8,128)(2,1)} %param.9), channel_id=1, source_target_pairs={{0,4},{4,8},{8,12},{12,16},{16,20},{20,24},{24,28},{1,5},{5,9},{9,... | collective-permute-start | bytes 3145736 | tf_op jit(solution)/shard_map/ppermute | solution.py:22
  7.1 2.8 %convert_multiply_fusion.3 = f32[1024,512]{1,0:T(8,128)} fusion(bf16[1024,512]{1,0:T(8,128)(2,1)} %raw_ref.3), kind=kLoop, calls=%fused_computation.6 | loop fusion | flops 1048576 | bytes 3145728 | tf_op jit(solution)/shard_map/mul | solution.py:41
  10.0 1.9 %mul.74 = f32[1024,4,128]{2,1,0:T(4,128)S(1)} reshape(f32[1024,512]{1,0:T(8,128)} %convert_multiply_fusion.3) | data formatting | bytes 4194304 | tf_op jit(solution)/shard_map/mul | solution.py:41
  14.9 3.6 %collective-permute-start = (bf16[1024,512]{1,0:T(8,128)(2,1)S(1)}, bf16[1024,512]{1,0:T(8,128)(2,1)}, u32[]{:S(2)}, u32[]{:S(2)}) collective-permute-start(bf16[1024,512]{1,0:T(8,128)(2,1)S(1)} %fusion.4), channel_id=1, source_target_pairs={{0,4},{4,8},{8,12},{12,16},{16,20},{20,24},{24,28},{1,5},{5,9},{9,... | collective-permute-start | bytes 3145736 | tf_op jit(solution)/shard_map/ppermute | solution.py:22
  19.3 2.9 %copy.31 = f32[128,8,8,128]{3,2,1,0:T(8,128)} copy(f32[128,8,8,128]{3,1,2,0:T(8,128)S(1)} %fusion) | data formatting | bytes 8388608
  22.3 4.2 %reduce_sum.56 = f32[1024,8]{1,0:T(8,128)} reduce(f32[1024,8,128]{2,1,0:T(8,128)} %bitcast.25, f32[]{:T(128)} %constant.25.clone.1), dimensions={2}, to_apply=%region_3.4 | reduce | flops 1040384 | bytes 4227076 | tf_op jit(solution)/shard_map/reduce_sum | solution.py:41
  30.4 2.2 %mul.66 = f32[1024,8,128]{2,1,0:T(8,128)S(1)} broadcast(f32[1024,8]{1,0:T(8,128)} %copy.26), dimensions={0,1} | broadcast | bytes 4227072 | tf_op jit(solution)/shard_map/mul | solution.py:42
  32.6 2.7 %fusion.2.q_ref = bf16[1024,1024]{1,0:T(8,128)(2,1)} fusion(bf16[1024,1024]{1,0:T(8,128)(2,1)S(1)} %copy-done.1, f32[128,8,8,128]{3,2,1,0:T(8,128)S(1)} %bitcast.24, f32[1024]{0:T(1024)S(1)} %broadcast_bitcast_fusion), kind=kLoop, calls=%fused_computation.4 | loop fusion | flops 4194304 | bytes 8392704 | tf_op jit(solution)/shard_map/convert_element_type | solution.py:334
  35.3 1.4 constant_dynamic-update-slice_fusion.1
  36.9 13.7 %collective-permute-done = bf16[1024,512]{1,0:T(8,128)(2,1)} collective-permute-done((bf16[1024,512]{1,0:T(8,128)(2,1)S(1)}, bf16[1024,512]{1,0:T(8,128)(2,1)}, u32[]{:S(2)}, u32[]{:S(2)}) %collective-permute-start) | collective-permute-done | bytes 1048608 | tf_op jit(solution)/shard_map/ppermute | solution.py:22
  50.6 2.7 %pad_maximum_fusion.k_ref = bf16[2048,512]{1,0:T(8,128)(2,1)} fusion(bf16[1024,512]{1,0:T(8,128)(2,1)S(1)} %fusion.4, bf16[1024,512]{1,0:T(8,128)(2,1)} %collective-permute-done), kind=kLoop, calls=%fused_computation.9 | loop fusion | flops 4194304 | bytes 4194304 | tf_op jit(solution)/shard_map/concatenate | solution.py:338
  53.3 49.6 %shard_map.110 = (f32[1024,1024]{1,0:T(8,128)}, bf16[1024,1024]{1,0:T(8,128)(2,1)}, f32[8192,1]{1,0:T(8,128)}, f32[8192,1]{1,0:T(8,128)}) custom-call(s32[1024,1]{1,0:T(8,128)} %copy.30.qdoc_ref, s32[1,2048]{1,0:T(1,128)} %bitcast.28, bf16[1024,1024]{1,0:T(8,128)(2,1)} %fusion.2.q_ref, bf16[1024,1024]{1,0:T(8,128)(2,1)} %do_ref.3, ...), custom_call_target="tpu_custom_call" | custom-call | flops 12079595520 | bytes 14680064 | tf_op jit(solution)/shard_map/pallas_call | solution.py:265
  102.9 1.5 collective-permute-start.2
  104.4 36.7 %shard_map.111 = (bf16[1024,1024]{1,0:T(8,128)(2,1)}, f32[16,1,128]{2,1,0:T(1,128)}, f32[1024,512]{1,0:T(8,128)}, f32[1024,512]{1,0:T(8,128)}) custom-call(s32[1024,1]{1,0:T(8,128)} %copy.30.qdoc_ref, s32[1,2048]{1,0:T(1,128)} %bitcast.29, bf16[1024,1024]{1,0:T(8,128)(2,1)} %fusion.2.q_ref, bf16[1024,1024]{1,0:T(8,128)(2,1)} %do_ref.3, ...), custom_call_target="tpu_custom_call" | custom-call | flops 6710886400 | bytes 20971520 | tf_op jit(solution)/shard_map/pallas_call | solution.py:295
  141.8 10.5 %collective-permute-done.2.back_ref = bf16[1024,1024]{1,0:T(8,128)(2,1)S(1)} collective-permute-done((bf16[1024,1024]{1,0:T(8,128)(2,1)}, bf16[1024,1024]{1,0:T(8,128)(2,1)S(1)}, u32[]{:S(2)}, u32[]{:S(2)}) %collective-permute-start.2) | collective-permute-done | bytes 2097184 | tf_op jit(solution)/shard_map/ppermute | solution.py:22
  153.7 5.5 %shard_map.112 = (bf16[1024,512]{1,0:T(8,128)(2,1)}, bf16[1024,512]{1,0:T(8,128)(2,1)}, f32[4,1,128]{2,1,0:T(1,128)}) custom-call(f32[1024,512]{1,0:T(8,128)} %get-tuple-element.20.dk_ref, f32[1024,512]{1,0:T(8,128)} %get-tuple-element.21.dv_ref, bf16[1024,1024]{1,0:T(8,128)(2,1)} %copy-done.2, bf16[1024,512]{1,0:T(8,128)(2,1)} %raw_ref.3, f32[1,128]{1,0:T(1,128)} %bitcast.36), custom_call_target="tpu_custom_call" | custom-call | tf_op jit(solution)/shard_map/pallas_call | solution.py:218
  161.2 1.6 collective-permute-start.4
  162.8 2.1 %collective-permute-done.4 = f32[2,128]{1,0:T(2,128)S(1)} collective-permute-done((f32[2,128]{1,0:T(2,128)S(1)}, f32[2,128]{1,0:T(2,128)S(1)}, u32[]{:S(2)}, u32[]{:S(2)}) %collective-permute-start.4) | collective-permute-done | bytes 1056 | tf_op jit(solution)/shard_map/ppermute | solution.py:34
  164.8 2.7 %collective-permute-start.5 = (f32[2,128]{1,0:T(2,128)S(1)}, f32[2,128]{1,0:T(2,128)S(1)}, u32[]{:S(2)}, u32[]{:S(2)}) collective-permute-start(f32[2,128]{1,0:T(2,128)S(1)} %fusion.6), channel_id=1, source_target_pairs={{0,4},{4,0},{8,12},{12,8},{16,20},{20,16},{24,28},{28,24},{1,5},{5... | collective-permute-start | bytes 3080 | tf_op jit(solution)/shard_map/ppermute | solution.py:34
  167.5 1.6 collective-permute-done.5
  169.1 2.1 %collective-permute-start.6 = (f32[2,128]{1,0:T(2,128)S(1)}, f32[2,128]{1,0:T(2,128)S(1)}, u32[]{:S(2)}, u32[]{:S(2)}) collective-permute-start(f32[2,128]{1,0:T(2,128)S(1)} %add.68), channel_id=1, source_target_pairs={{0,8},{4,12},{8,0},{12,4},{16,24},{20,28},{24,16},{28,20},{1,9},{5... | collective-permute-start | bytes 3080 | tf_op jit(solution)/shard_map/ppermute | solution.py:34
  171.2 1.6 collective-permute-done.6
  172.8 3.0 %collective-permute-start.7 = (f32[2,128]{1,0:T(2,128)S(1)}, f32[2,128]{1,0:T(2,128)S(1)}, u32[]{:S(2)}, u32[]{:S(2)}) collective-permute-start(f32[2,128]{1,0:T(2,128)S(1)} %add.69), channel_id=1, source_target_pairs={{0,16},{4,20},{8,24},{12,28},{16,0},{20,4},{24,8},{28,12},{1,17},{... | collective-permute-start | bytes 3080 | tf_op jit(solution)/shard_map/ppermute | solution.py:34
  175.8 1.6 collective-permute-done.7
  (45 shorter events, 13.1 us)
Async XLA Ops:
  0.6 34.6 %collective-permute-start.1 = (bf16[1024,512]{1,0:T(8,128)(2,1)}, bf16[1024,512]{1,0:T(8,128)(2,1)}, u32[]{:S(2)}, u32[]{:S(2)}) collective-permute-start(bf16[1024,512]{1,0:T(8,128)(2,1)} %param.9), channel_id=1, source_target_pairs={{0,4},{4,8},{8,12},{12,16},{16,20},{20,24},{24,28},{1,5},{5,9},{9,... | collective-permute-start | bytes 3145736 | tf_op jit(solution)/shard_map/ppermute | solution.py:22
  13.1 1.3 copy-start
  14.4 4.1 %copy-start.5 = (s32[16]{0:T(128)S(1)}, s32[16]{0:T(128)}, u32[]{:S(2)}) copy-start(s32[16]{0:T(128)} %param.13) | copy-start | bytes 196
  14.4 4.3 %copy-start.1 = (bf16[1024,1024]{1,0:T(8,128)(2,1)S(1)}, bf16[1024,1024]{1,0:T(8,128)(2,1)}, u32[]{:S(2)}) copy-start(bf16[1024,1024]{1,0:T(8,128)(2,1)} %raw_ref.2) | copy-start | bytes 6291460
  14.9 35.7 %collective-permute-start = (bf16[1024,512]{1,0:T(8,128)(2,1)S(1)}, bf16[1024,512]{1,0:T(8,128)(2,1)}, u32[]{:S(2)}, u32[]{:S(2)}) collective-permute-start(bf16[1024,512]{1,0:T(8,128)(2,1)S(1)} %fusion.4), channel_id=1, source_target_pairs={{0,4},{4,8},{8,12},{12,16},{16,20},{20,24},{24,28},{1,5},{5,9},{9,... | collective-permute-start | bytes 3145736 | tf_op jit(solution)/shard_map/ppermute | solution.py:22
  22.3 8.1 %copy-start.6 = (f32[128]{0:T(128)S(1)}, f32[128]{0:T(128)}, u32[]{:S(2)}) copy-start(f32[128]{0:T(128)} %param.10) | copy-start | bytes 1540
  35.3 1.5 copy-start.3
  36.9 16.4 %copy-start.4 = (bf16[2048,512]{1,0:T(8,128)(2,1)}, bf16[2048,512]{1,0:T(8,128)(2,1)S(1)}, u32[]{:S(2)}) copy-start(bf16[2048,512]{1,0:T(8,128)(2,1)S(1)} %constant_dynamic-update-slice_fusion.v_ref) | copy-start | bytes 6291460
  102.9 49.5 %collective-permute-start.2 = (bf16[1024,1024]{1,0:T(8,128)(2,1)}, bf16[1024,1024]{1,0:T(8,128)(2,1)S(1)}, u32[]{:S(2)}, u32[]{:S(2)}) collective-permute-start(bf16[1024,1024]{1,0:T(8,128)(2,1)} %get-tuple-element.22), channel_id=1, source_target_pairs={{4,0},{8,4},{12,8},{16,12},{20,16},{24,20},{28,24},{5,1},{9,5},{13... | collective-permute-start | bytes 6291464 | tf_op jit(solution)/shard_map/ppermute | solution.py:22
  152.3 1.4 copy-start.2
  159.9 1.2 collective-permute-start.3
  161.2 3.6 %collective-permute-start.4 = (f32[2,128]{1,0:T(2,128)S(1)}, f32[2,128]{1,0:T(2,128)S(1)}, u32[]{:S(2)}, u32[]{:S(2)}) collective-permute-start(f32[2,128]{1,0:T(2,128)S(1)} %fusion.5), channel_id=1, source_target_pairs={{0,2},{1,3},{2,0},{3,1},{4,6},{5,7},{6,4},{7,5},{8,10},{9,11},{10,... | collective-permute-start | bytes 3080 | tf_op jit(solution)/shard_map/ppermute | solution.py:34
  164.8 4.3 %collective-permute-start.5 = (f32[2,128]{1,0:T(2,128)S(1)}, f32[2,128]{1,0:T(2,128)S(1)}, u32[]{:S(2)}, u32[]{:S(2)}) collective-permute-start(f32[2,128]{1,0:T(2,128)S(1)} %fusion.6), channel_id=1, source_target_pairs={{0,4},{4,0},{8,12},{12,8},{16,20},{20,16},{24,28},{28,24},{1,5},{5... | collective-permute-start | bytes 3080 | tf_op jit(solution)/shard_map/ppermute | solution.py:34
  169.1 3.7 %collective-permute-start.6 = (f32[2,128]{1,0:T(2,128)S(1)}, f32[2,128]{1,0:T(2,128)S(1)}, u32[]{:S(2)}, u32[]{:S(2)}) collective-permute-start(f32[2,128]{1,0:T(2,128)S(1)} %add.68), channel_id=1, source_target_pairs={{0,8},{4,12},{8,0},{12,4},{16,24},{20,28},{24,16},{28,20},{1,9},{5... | collective-permute-start | bytes 3080 | tf_op jit(solution)/shard_map/ppermute | solution.py:34
  172.8 4.6 %collective-permute-start.7 = (f32[2,128]{1,0:T(2,128)S(1)}, f32[2,128]{1,0:T(2,128)S(1)}, u32[]{:S(2)}, u32[]{:S(2)}) collective-permute-start(f32[2,128]{1,0:T(2,128)S(1)} %add.69), channel_id=1, source_target_pairs={{0,16},{4,20},{8,24},{12,28},{16,0},{20,4},{24,8},{28,12},{1,17},{... | collective-permute-start | bytes 3080 | tf_op jit(solution)/shard_map/ppermute | solution.py:34

commit v5 on v4

--- a/solution.py
+++ b/solution.py
@@ -22,17 +22,28 @@
     return lax.ppermute(value, axis, [(source, source + steps) for source in range(leading, last)])
 
 
+def xor_tree(values):
+    while len(values) > 1:
+        values = [values[i] + values[i + 1] for i in range(0, len(values), 2)]
+    return values[0]
+
+
 def butterfly_sum(value, axes):
     for axis in axes:
         count = lax.axis_size(axis)
         if count & (count - 1):
             value = lax.psum(value, axis)
             continue
-        step = 1
-        while step < count:
-            pairs = [(source, source ^ step) for source in range(count)]
-            value = value + lax.ppermute(value, axis, pairs)
-            step *= 2
+        bits = count.bit_length() - 1
+        low = 0
+        while low < bits:
+            width = min(3, bits - low)
+            shifted_parts = [value]
+            for mask in range(1, 1 << width):
+                pairs = [(source, source ^ (mask << low)) for source in range(count)]
+                shifted_parts.append(lax.ppermute(value, axis, pairs))
+            value = xor_tree(shifted_parts)
+            low += width
     return value
 
 
@@ -60,8 +71,8 @@
     n_tiles = WINDOW // blk + 1
     rows = lax.broadcasted_iota(jnp.int32, (blk, blk), 0)
     cols = lax.broadcasted_iota(jnp.int32, (blk, blk), 1)
-    k_first = pl.multiple_of(q_first + t * blk, blk)
-    live = qdoc_ref[...] == kdoc_ref[:, pl.ds(k_first, blk)]
+    k_first = q_first + t * blk
+    live = qdoc_ref[q_first:q_first + blk, :] == kdoc_ref[:, k_first:k_first + blk]
     if t == 0:
         live = live & (cols > rows)
     if t == n_tiles - 1:
@@ -69,9 +80,11 @@
     return jnp.concatenate([live] * group, axis=0), k_first
 
 
-def stacked(ref, group, head_dim):
-    block = ref[...]
-    return jnp.concatenate([block[:, a * head_dim:(a + 1) * head_dim] for a in range(group)], axis=0)
+def stacked(ref, group, head_dim, first):
+    blk = BLOCK
+    return jnp.concatenate(
+        [ref[first:first + blk, a * head_dim:(a + 1) * head_dim] for a in range(group)], axis=0
+    )
 
 
 def grad_tile(q_g, do_g, k_tile, v_tile, live, log_sums, delta):
@@ -89,55 +102,51 @@
 
 
 def halo_kernel(qdoc_ref, kdoc_ref, q_ref, do_ref, k_ref, v_ref,
-                dq_ref, dkv_ref, lse_ref, delta_ref, dq_scr, dk_ref, dv_ref, *, group, head_dim):
+                dq_ref, dkv_ref, lse_ref, delta_ref, dk_ref, dv_ref, *, group, head_dim):
     blk = BLOCK
     n_tiles = WINDOW // blk + 1
     n_halo = WINDOW // blk
+    n_q = q_ref.shape[0] // blk
+    gb = group * blk
     scale = QUERY_SCALAR ** (-0.5)
-    qb = pl.program_id(1)
-
-    @pl.when(qb == 0)
-    def _():
-        dk_ref[...] = jnp.zeros(dk_ref.shape, jnp.float32)
-        dv_ref[...] = jnp.zeros(dv_ref.shape, jnp.float32)
-
-    q_first = pl.multiple_of(qb * blk, blk)
-    q_g = stacked(q_ref, group, head_dim)
-    do_g = stacked(do_ref, group, head_dim)
-    totals = jnp.zeros((group * blk, 1), jnp.float32)
-    numer = jnp.zeros((group * blk, head_dim), jnp.float32)
-    for t in range(n_tiles):
-        live, k_first = tile_mask(qdoc_ref, kdoc_ref, q_first, t, group)
-        k_tile = k_ref[pl.ds(k_first, blk), :]
-        v_tile = v_ref[pl.ds(k_first, blk), :]
-        scores = lax.dot_general(q_g, k_tile, (((1,), (1,)), ((), ())), preferred_element_type=jnp.float32) * scale
-        exp_s = jnp.where(live, jnp.exp(scores), 0.0)
-        totals = totals + jnp.sum(exp_s, axis=1, keepdims=True)
-        numer = numer + jnp.dot(exp_s.astype(jnp.bfloat16), v_tile, preferred_element_type=jnp.float32)
-    log_sums = jnp.log(totals)
-    attn_out = numer / totals
-    delta = jnp.sum(do_g.astype(jnp.float32) * attn_out, axis=1, keepdims=True)
-    lse_ref[...] = log_sums
-    delta_ref[...] = delta
-
-    dq_scr[...] = jnp.zeros(dq_scr.shape, jnp.float32)
-    for t in range(n_halo):
-        @pl.when(qb + t < n_halo)
-        def _():
-            live, k_first = tile_mask(qdoc_ref, kdoc_ref, q_first, t, group)
-            k_tile = k_ref[pl.ds(k_first, blk), :]
-            v_tile = v_ref[pl.ds(k_first, blk), :]
-            dq_part, dk_part, dv_part = grad_tile(q_g, do_g, k_tile, v_tile, live, log_sums, delta)
-            dq_scr[...] += dq_part
-            dk_ref[pl.ds(k_first, blk), :] += dk_part
-            dv_ref[pl.ds(k_first, blk), :] += dv_part
-    dq = dq_scr[...]
-    dq_ref[...] = jnp.concatenate([dq[a * blk:(a + 1) * blk] for a in range(group)], axis=1) * scale
-
-    @pl.when(qb == pl.num_programs(1) - 1)
-    def _():
-        dkv_ref[:, :head_dim] = dk_ref[...].astype(jnp.bfloat16)
-        dkv_ref[:, head_dim:] = dv_ref[...].astype(jnp.bfloat16)
+    dk_ref[...] = jnp.zeros(dk_ref.shape, jnp.float32)
+    dv_ref[...] = jnp.zeros(dv_ref.shape, jnp.float32)
+    for qb in range(n_q):
+        q_first = qb * blk
+        q_g = stacked(q_ref, group, head_dim, q_first)
+        do_g = stacked(do_ref, group, head_dim, q_first)
+        masks = [tile_mask(qdoc_ref, kdoc_ref, q_first, t, group)[0] for t in range(n_tiles)]
+        totals = jnp.zeros((gb, 1), jnp.float32)
+        numer = jnp.zeros((gb, head_dim), jnp.float32)
+        for t in range(n_tiles):
+            k_first = q_first + t * blk
+            k_tile = k_ref[k_first:k_first + blk, :]
+            v_tile = v_ref[k_first:k_first + blk, :]
+            scores = lax.dot_general(
+                q_g, k_tile, (((1,), (1,)), ((), ())), preferred_element_type=jnp.float32
+            ) * scale
+            exp_s = jnp.where(masks[t], jnp.exp(scores), 0.0)
+            totals = totals + jnp.sum(exp_s, axis=1, keepdims=True)
+            numer = numer + jnp.dot(exp_s.astype(jnp.bfloat16), v_tile, preferred_element_type=jnp.float32)
+        log_sums = jnp.log(totals)
+        attn_out = numer / totals
+        delta = jnp.sum(do_g.astype(jnp.float32) * attn_out, axis=1, keepdims=True)
+        lse_ref[qb * gb:(qb + 1) * gb, :] = log_sums
+        delta_ref[qb * gb:(qb + 1) * gb, :] = delta
+        dq = jnp.zeros((gb, head_dim), jnp.float32)
+        for t in range(n_halo - qb):
+            k_first = q_first + t * blk
+            k_tile = k_ref[k_first:k_first + blk, :]
+            v_tile = v_ref[k_first:k_first + blk, :]
+            dq_part, dk_part, dv_part = grad_tile(q_g, do_g, k_tile, v_tile, masks[t], log_sums, delta)
+            dq = dq + dq_part
+            dk_ref[k_first:k_first + blk, :] += dk_part
+            dv_ref[k_first:k_first + blk, :] += dv_part
+        dq_ref[q_first:q_first + blk, :] = jnp.concatenate(
+            [dq[a * blk:(a + 1) * blk] for a in range(group)], axis=1
+        ) * scale
+    dkv_ref[:, :head_dim] = dk_ref[...].astype(jnp.bfloat16)
+    dkv_ref[:, head_dim:] = dv_ref[...].astype(jnp.bfloat16)
 
 
 def norm_grad(raw, gain, upstream):
@@ -150,46 +159,42 @@
 
 
 def own_kernel(qdoc_ref, kdoc_ref, q_ref, do_ref, k_ref, v_ref, lse_ref, delta_ref, dq_in_ref, raw_ref, gain_ref,
-               qgrad_ref, qgain_ref, dk_ref, dv_ref, dq_scr, *, group, head_dim):
+               qgrad_ref, qgain_ref, dk_ref, dv_ref, *, group, head_dim):
     blk = BLOCK
     n_tiles = WINDOW // blk + 1
     n_halo = WINDOW // blk
+    n_q = q_ref.shape[0] // blk
+    gb = group * blk
     scale = QUERY_SCALAR ** (-0.5)
-    qb = pl.program_id(1)
-
-    @pl.when(qb == 0)
-    def _():
-        dk_ref[...] = jnp.zeros(dk_ref.shape, jnp.float32)
-        dv_ref[...] = jnp.zeros(dv_ref.shape, jnp.float32)
-
-    q_first = pl.multiple_of(qb * blk, blk)
-    q_g = stacked(q_ref, group, head_dim)
-    do_g = stacked(do_ref, group, head_dim)
-    log_sums = lse_ref[...]
-    delta = delta_ref[...]
-    dq_scr[...] = jnp.zeros(dq_scr.shape, jnp.float32)
-    for t in range(n_tiles):
-        @pl.when(qb + t >= n_halo)
-        def _():
-            live, k_first = tile_mask(qdoc_ref, kdoc_ref, q_first, t, group)
-            k_tile = k_ref[pl.ds(k_first, blk), :]
-            v_tile = v_ref[pl.ds(k_first, blk), :]
-            dq_part, dk_part, dv_part = grad_tile(q_g, do_g, k_tile, v_tile, live, log_sums, delta)
-            dq_scr[...] += dq_part
-            own_first = pl.multiple_of(k_first - WINDOW, blk)
-            dk_ref[pl.ds(own_first, blk), :] += dk_part
-            dv_ref[pl.ds(own_first, blk), :] += dv_part
-    dq = dq_scr[...]
-    dq_in = dq_in_ref[...]
-    raw = raw_ref[...].astype(jnp.float32)
+    dk_ref[...] = jnp.zeros(dk_ref.shape, jnp.float32)
+    dv_ref[...] = jnp.zeros(dv_ref.shape, jnp.float32)
     gain = gain_ref[...]
     gain_sum = jnp.zeros((1, head_dim), jnp.float32)
-    for a in range(group):
-        cols = slice(a * head_dim, (a + 1) * head_dim)
-        upstream = dq_in[:, cols] + dq[a * blk:(a + 1) * blk] * scale
-        result, part = norm_grad(raw[:, cols], gain, upstream)
-        qgrad_ref[:, cols] = result.astype(qgrad_ref.dtype)
-        gain_sum = gain_sum + part
+    for qb in range(n_q):
+        q_first = qb * blk
+        q_g = stacked(q_ref, group, head_dim, q_first)
+        do_g = stacked(do_ref, group, head_dim, q_first)
+        log_sums = lse_ref[qb * gb:(qb + 1) * gb, :]
+        delta = delta_ref[qb * gb:(qb + 1) * gb, :]
+        dq = jnp.zeros((gb, head_dim), jnp.float32)
+        for t in range(max(0, n_halo - qb), n_tiles):
+            live, _ = tile_mask(qdoc_ref, kdoc_ref, q_first, t, group)
+            k_first = q_first + t * blk
+            k_tile = k_ref[k_first:k_first + blk, :]
+            v_tile = v_ref[k_first:k_first + blk, :]
+            dq_part, dk_part, dv_part = grad_tile(q_g, do_g, k_tile, v_tile, live, log_sums, delta)
+            dq = dq + dq_part
+            own_first = k_first - WINDOW
+            dk_ref[own_first:own_first + blk, :] += dk_part
+            dv_ref[own_first:own_first + blk, :] += dv_part
+        dq_in = dq_in_ref[q_first:q_first + blk, :]
+        raw = raw_ref[q_first:q_first + blk, :].astype(jnp.float32)
+        for a in range(group):
+            cols = slice(a * head_dim, (a + 1) * head_dim)
+            upstream = dq_in[:, cols] + dq[a * blk:(a + 1) * blk] * scale
+            result, part = norm_grad(raw[:, cols], gain, upstream)
+            qgrad_ref[q_first:q_first + blk, cols] = result.astype(qgrad_ref.dtype)
+            gain_sum = gain_sum + part
     qgain_ref[...] = gain_sum.reshape(qgain_ref.shape)
 
 
@@ -250,25 +255,25 @@
     halo_tiles = sum(max(0, WINDOW // blk - qb) for qb in range(n_q))
     own_tiles = n_q * n_tiles - halo_tiles
     common_specs = [
-        pl.BlockSpec((blk, 1), lambda h, qb: (qb, 0)),
-        pl.BlockSpec((1, key_rows), lambda h, qb: (0, 0)),
-        pl.BlockSpec((blk, gw), lambda h, qb: (qb, h)),
-        pl.BlockSpec((blk, gw), lambda h, qb: (qb, h)),
-        pl.BlockSpec((key_rows, head_dim), lambda h, qb: (0, h)),
-        pl.BlockSpec((key_rows, head_dim), lambda h, qb: (0, h)),
+        pl.BlockSpec((tok_rows, 1), lambda h: (0, 0)),
+        pl.BlockSpec((1, key_rows), lambda h: (0, 0)),
+        pl.BlockSpec((tok_rows, gw), lambda h: (0, h)),
+        pl.BlockSpec((tok_rows, gw), lambda h: (0, h)),
+        pl.BlockSpec((key_rows, head_dim), lambda h: (0, h)),
+        pl.BlockSpec((key_rows, head_dim), lambda h: (0, h)),
     ]
-    stat_spec = pl.BlockSpec((group * blk, 1), lambda h, qb: (h * n_q + qb, 0))
-    dq_spec = pl.BlockSpec((blk, gw), lambda h, qb: (qb, h))
-    params = pltpu.CompilerParams(dimension_semantics=("arbitrary", "arbitrary"))
+    stat_spec = pl.BlockSpec((n_q * group * blk, 1), lambda h: (h, 0))
+    dq_spec = pl.BlockSpec((tok_rows, gw), lambda h: (0, h))
+    params = pltpu.CompilerParams(dimension_semantics=("arbitrary",))
     in_bytes = 2 * 2 * tok_rows * q_cols + 2 * 2 * key_rows * kv_cols
     operands = (own_doc.reshape(tok_rows, 1), all_doc.reshape(1, key_rows), query_norm, grad_rows, keys_all, vals_all)
     dq_half, dkv_halo, log_sums, delta = pl.pallas_call(
         functools.partial(halo_kernel, group=group, head_dim=head_dim),
-        grid=(key_heads, n_q),
+        grid=(key_heads,),
         in_specs=common_specs,
         out_specs=[
             dq_spec,
-            pl.BlockSpec((WINDOW, 2 * head_dim), lambda h, qb: (0, h)),
+            pl.BlockSpec((WINDOW, 2 * head_dim), lambda h: (0, h)),
             stat_spec,
             stat_spec,
         ],
@@ -279,7 +284,6 @@
             jax.ShapeDtypeStruct((stat_rows, 1), jnp.float32),
         ],
         scratch_shapes=[
-            pltpu.VMEM((group * blk, head_dim), jnp.float32),
             pltpu.VMEM((WINDOW, head_dim), jnp.float32),
             pltpu.VMEM((WINDOW, head_dim), jnp.float32),
         ],
@@ -290,25 +294,24 @@
             bytes_accessed=in_bytes + 4 * tok_rows * q_cols + 2 * 2 * WINDOW * kv_cols,
         ),
     )(*operands)
-    raw_spec = pl.BlockSpec((blk, gw), lambda h, qb: (qb, h))
-    gain_spec = pl.BlockSpec((1, head_dim), lambda h, qb: (0, 0))
+    raw_spec = pl.BlockSpec((tok_rows, gw), lambda h: (0, h))
+    gain_spec = pl.BlockSpec((1, head_dim), lambda h: (0, 0))
     query_grad, qgain_parts, dk_own, dv_own = pl.pallas_call(
         functools.partial(own_kernel, group=group, head_dim=head_dim),
-        grid=(key_heads, n_q),
+        grid=(key_heads,),
         in_specs=common_specs + [stat_spec, stat_spec, dq_spec, raw_spec, gain_spec],
         out_specs=[
             raw_spec,
-            pl.BlockSpec((1, 1, head_dim), lambda h, qb: (h * n_q + qb, 0, 0)),
-            pl.BlockSpec((tok_rows, head_dim), lambda h, qb: (0, h)),
-            pl.BlockSpec((tok_rows, head_dim), lambda h, qb: (0, h)),
+            pl.BlockSpec((1, 1, head_dim), lambda h: (h, 0, 0)),
+            pl.BlockSpec((tok_rows, head_dim), lambda h: (0, h)),
+            pl.BlockSpec((tok_rows, head_dim), lambda h: (0, h)),
         ],
         out_shape=[
             jax.ShapeDtypeStruct((tok_rows, q_cols), jnp.bfloat16),
-            jax.ShapeDtypeStruct((key_heads * n_q, 1, head_dim), jnp.float32),
+            jax.ShapeDtypeStruct((key_heads, 1, head_dim), jnp.float32),
             jax.ShapeDtypeStruct((tok_rows, kv_cols), jnp.float32),
             jax.ShapeDtypeStruct((tok_rows, kv_cols), jnp.float32),
         ],
-        scratch_shapes=[pltpu.VMEM((group * blk, head_dim), jnp.float32)],
         compiler_params=params,
         cost_estimate=pl.CostEstimate(
             flops=key_heads * own_tiles * 5 * tile_flops,

time: 179 us -> 168 us (0.939)
  Pallas kernels: 91.9 us -> 68.3 us
  waiting for transfers between devices: 32.1 us -> 41 us
  starting transfers between devices: 20.4 us -> 25.1 us
    pallas_call x1, Pallas kernels: 49.6 us -> 37 us  [attention_grads(): pl.pallas_call(functools.partial(halo_kernel, group=group, head_dim=head_...]
    ppermute x3, waiting for transfers between devices: 24.2 us -> 35.4 us  [shifted(): lax.ppermute(value, axis, [(source, source + steps) for source in range(l...]
    pallas_call x1, Pallas kernels: 36.7 us -> 25.8 us  [attention_grads(): pl.pallas_call(functools.partial(own_kernel, group=group, head_dim=head_d...]
    ppermute x5 -> x10, starting transfers between devices: 9.5 us -> 14.3 us  [butterfly_sum(): shifted_parts.append(lax.ppermute(value, axis, pairs))]
    ppermute x5 -> x10, waiting for transfers between devices: 7.86 us -> 5.64 us  [butterfly_sum(): shifted_parts.append(lax.ppermute(value, axis, pairs))]
  transfers between devices with their start and end apart: 8 -> 13, of which waited for: 7 -> 7; matrix products, arithmetic and copies ran while one was open for 15% -> 16% of each run, Pallas kernels for 21% -> 15%
where the time goes in v5:
time: 168 us
  Pallas kernels  68.3 us (41%)
  waiting for transfers between devices  41 us (24%)
  starting transfers between devices  25.1 us (15%)
  other arithmetic  16.9 us (10%)
  local copies, waits for them, and re-layouts  15.7 us (9%)
    pallas_call x1, Pallas kernels, attention_grads(): pl.pallas_call(functools.partial(halo_kernel, group=group, head_dim=head_...  37 us
    ppermute x3, waiting for transfers between devices, shifted(): lax.ppermute(value, axis, [(source, source + steps) for source in range(l...  35.4 us
    pallas_call x1, Pallas kernels, attention_grads(): pl.pallas_call(functools.partial(own_kernel, group=group, head_dim=head_d...  25.8 us
    ppermute x10, starting transfers between devices, butterfly_sum(): shifted_parts.append(lax.ppermute(value, axis, pairs))  14.3 us
    ppermute x3, starting transfers between devices, shifted(): lax.ppermute(value, axis, [(source, source + steps) for source in range(l...  10.8 us
    unnamed x16, local copies, waits for them, and re-layouts  5.83 us
    ppermute x10, waiting for transfers between devices, butterfly_sum(): shifted_parts.append(lax.ppermute(value, axis, pairs))  5.64 us
    pallas_call x1, Pallas kernels, kv_final(): pl.pallas_call(functools.partial(kv_final_kernel, head_dim=head_dim), gri...  5.53 us
  transfers between devices with their start and end apart: 13, of which 7 were waited for; matrix products, arithmetic and copies ran while one was open for 16% of the time, Pallas kernels for 15%

profile of v5, /device:TPU:0, one launch (start us, length us, event | category | flops | bytes accessed | tf_op | source)
XLA Modules:
  0.0 167.8 jit_solution(16116345234232548039)
XLA Ops:
  0.6 5.9 %collective-permute-start.1 = (bf16[1024,512]{1,0:T(8,128)(2,1)}, bf16[1024,512]{1,0:T(8,128)(2,1)}, u32[]{:S(2)}, u32[]{:S(2)}) collective-permute-start(bf16[1024,512]{1,0:T(8,128)(2,1)} %param.9), channel_id=1, source_target_pairs={{0,4},{4,8},{8,12},{12,16},{16,20},{20,24},{24,28},{1,5},{5,9},{9,... | collective-permute-start | bytes 3145736 | tf_op jit(solution)/shard_map/ppermute | solution.py:22
  7.1 2.8 %convert_multiply_fusion.3 = f32[1024,512]{1,0:T(8,128)} fusion(bf16[1024,512]{1,0:T(8,128)(2,1)} %raw_ref.3), kind=kLoop, calls=%fused_computation.6 | loop fusion | flops 1048576 | bytes 3145728 | tf_op jit(solution)/shard_map/mul | solution.py:52
  10.0 1.9 %mul.74 = f32[1024,4,128]{2,1,0:T(4,128)S(1)} reshape(f32[1024,512]{1,0:T(8,128)} %convert_multiply_fusion.3) | data formatting | bytes 4194304 | tf_op jit(solution)/shard_map/mul | solution.py:52
  14.9 3.6 %collective-permute-start = (bf16[1024,512]{1,0:T(8,128)(2,1)S(1)}, bf16[1024,512]{1,0:T(8,128)(2,1)}, u32[]{:S(2)}, u32[]{:S(2)}) collective-permute-start(bf16[1024,512]{1,0:T(8,128)(2,1)S(1)} %fusion.4), channel_id=1, source_target_pairs={{0,4},{4,8},{8,12},{12,16},{16,20},{20,24},{24,28},{1,5},{5,9},{9,... | collective-permute-start | bytes 3145736 | tf_op jit(solution)/shard_map/ppermute | solution.py:22
  19.3 2.9 %copy.31 = f32[128,8,8,128]{3,2,1,0:T(8,128)} copy(f32[128,8,8,128]{3,1,2,0:T(8,128)S(1)} %fusion) | data formatting | bytes 8388608
  22.3 4.2 %reduce_sum.56 = f32[1024,8]{1,0:T(8,128)} reduce(f32[1024,8,128]{2,1,0:T(8,128)} %bitcast.25, f32[]{:T(128)} %constant.25.clone.1), dimensions={2}, to_apply=%region_3.4 | reduce | flops 1040384 | bytes 4227076 | tf_op jit(solution)/shard_map/reduce_sum | solution.py:52
  30.4 2.2 %mul.66 = f32[1024,8,128]{2,1,0:T(8,128)S(1)} broadcast(f32[1024,8]{1,0:T(8,128)} %copy.26), dimensions={0,1} | broadcast | bytes 4227072 | tf_op jit(solution)/shard_map/mul | solution.py:53
  32.6 2.7 %fusion.2.q_ref = bf16[1024,1024]{1,0:T(8,128)(2,1)} fusion(bf16[1024,1024]{1,0:T(8,128)(2,1)S(1)} %copy-done.1, f32[128,8,8,128]{3,2,1,0:T(8,128)S(1)} %bitcast.24, f32[1024]{0:T(1024)S(1)} %broadcast_bitcast_fusion), kind=kLoop, calls=%fused_computation.4 | loop fusion | flops 4194304 | bytes 8392704 | tf_op jit(solution)/shard_map/convert_element_type | solution.py:337
  35.3 1.4 constant_dynamic-update-slice_fusion.1
  36.9 13.7 %collective-permute-done = bf16[1024,512]{1,0:T(8,128)(2,1)} collective-permute-done((bf16[1024,512]{1,0:T(8,128)(2,1)S(1)}, bf16[1024,512]{1,0:T(8,128)(2,1)}, u32[]{:S(2)}, u32[]{:S(2)}) %collective-permute-start) | collective-permute-done | bytes 1048608 | tf_op jit(solution)/shard_map/ppermute | solution.py:22
  50.6 2.7 %pad_maximum_fusion.k_ref = bf16[2048,512]{1,0:T(8,128)(2,1)} fusion(bf16[1024,512]{1,0:T(8,128)(2,1)S(1)} %fusion.4, bf16[1024,512]{1,0:T(8,128)(2,1)} %collective-permute-done), kind=kLoop, calls=%fused_computation.9 | loop fusion | flops 4194304 | bytes 4194304 | tf_op jit(solution)/shard_map/concatenate | solution.py:341
  53.3 37.0 %shard_map.110 = (f32[1024,1024]{1,0:T(8,128)}, bf16[1024,1024]{1,0:T(8,128)(2,1)}, f32[8192,1]{1,0:T(8,128)}, f32[8192,1]{1,0:T(8,128)}) custom-call(s32[1024,1]{1,0:T(8,128)} %copy.30.qdoc_ref, s32[1,2048]{1,0:T(1,128)} %bitcast.28, bf16[1024,1024]{1,0:T(8,128)(2,1)} %fusion.2.q_ref, bf16[1024,1024]{1,0:T(8,128)(2,1)} %do_ref.3, ...), custom_call_target="tpu_custom_call" | custom-call | flops 12079595520 | bytes 14680064 | tf_op jit(solution)/shard_map/pallas_call | solution.py:270
  91.6 25.8 %shard_map.111 = (bf16[1024,1024]{1,0:T(8,128)(2,1)}, f32[4,1,128]{2,1,0:T(1,128)}, f32[1024,512]{1,0:T(8,128)}, f32[1024,512]{1,0:T(8,128)}) custom-call(s32[1024,1]{1,0:T(8,128)} %copy.30.qdoc_ref, s32[1,2048]{1,0:T(1,128)} %bitcast.29, bf16[1024,1024]{1,0:T(8,128)(2,1)} %fusion.2.q_ref, bf16[1024,1024]{1,0:T(8,128)(2,1)} %do_ref.3, ...), custom_call_target="tpu_custom_call" | custom-call | flops 6710886400 | bytes 20971520 | tf_op jit(solution)/shard_map/pallas_call | solution.py:299
  118.1 21.7 %collective-permute-done.2.back_ref = bf16[1024,1024]{1,0:T(8,128)(2,1)S(1)} collective-permute-done((bf16[1024,1024]{1,0:T(8,128)(2,1)}, bf16[1024,1024]{1,0:T(8,128)(2,1)S(1)}, u32[]{:S(2)}, u32[]{:S(2)}) %collective-permute-start.2) | collective-permute-done | bytes 2097184 | tf_op jit(solution)/shard_map/ppermute | solution.py:22
  139.8 1.3 copy-done.2
  141.1 5.5 %shard_map.112 = (bf16[1024,512]{1,0:T(8,128)(2,1)}, bf16[1024,512]{1,0:T(8,128)(2,1)}, f32[4,1,128]{2,1,0:T(1,128)}) custom-call(f32[1024,512]{1,0:T(8,128)} %get-tuple-element.20.dk_ref, f32[1024,512]{1,0:T(8,128)} %get-tuple-element.21.dv_ref, bf16[1024,1024]{1,0:T(8,128)(2,1)} %copy-done.2, bf16[1024,512]{1,0:T(8,128)(2,1)} %raw_ref.3, f32[1,128]{1,0:T(1,128)} %bitcast.34), custom_call_target="tpu_custom_call" | custom-call | tf_op jit(solution)/shard_map/pallas_call | solution.py:223
  147.3 1.6 collective-permute-start.4
  149.5 1.4 collective-permute-done.4
  151.9 3.9 %collective-permute-start.12 = (f32[2,128]{1,0:T(2,128)S(1)}, f32[2,128]{1,0:T(2,128)S(1)}, u32[]{:S(2)}, u32[]{:S(2)}) collective-permute-start(f32[2,128]{1,0:T(2,128)S(1)} %add_add_fusion.1), channel_id=1, source_target_pairs={{0,28},{4,24},{8,20},{12,16},{16,12},{20,8},{24,4},{28,0},{1,29},{... | collective-permute-start | bytes 3080 | tf_op jit(solution)/shard_map/ppermute | solution.py:44
  155.8 2.1 %collective-permute-start.11 = (f32[2,128]{1,0:T(2,128)S(1)}, f32[2,128]{1,0:T(2,128)S(1)}, u32[]{:S(2)}, u32[]{:S(2)}) collective-permute-start(f32[2,128]{1,0:T(2,128)S(1)} %add_add_fusion.1), channel_id=1, source_target_pairs={{0,24},{4,28},{8,16},{12,20},{16,8},{20,12},{24,0},{28,4},{1,25},{... | collective-permute-start | bytes 3080 | tf_op jit(solution)/shard_map/ppermute | solution.py:44
  158.6 1.9 %collective-permute-start.9 = (f32[2,128]{1,0:T(2,128)S(1)}, f32[2,128]{1,0:T(2,128)S(1)}, u32[]{:S(2)}, u32[]{:S(2)}) collective-permute-start(f32[2,128]{1,0:T(2,128)S(1)} %add_add_fusion.1), channel_id=1, source_target_pairs={{0,16},{4,20},{8,24},{12,28},{16,0},{20,4},{24,8},{28,12},{1,17},{... | collective-permute-start | bytes 3080 | tf_op jit(solution)/shard_map/ppermute | solution.py:44
  160.5 1.5 collective-permute-start.8
  162.0 1.7 %collective-permute-start.7 = (f32[2,128]{1,0:T(2,128)S(1)}, f32[2,128]{1,0:T(2,128)S(1)}, u32[]{:S(2)}, u32[]{:S(2)}) collective-permute-start(f32[2,128]{1,0:T(2,128)S(1)} %add_add_fusion.1), channel_id=1, source_target_pairs={{0,8},{4,12},{8,0},{12,4},{16,24},{20,28},{24,16},{28,20},{1,9},{5... | collective-permute-start | bytes 3080 | tf_op jit(solution)/shard_map/ppermute | solution.py:44
  165.6 1.7 %collective-permute-done.6 = f32[2,128]{1,0:T(2,128)S(1)} collective-permute-done((f32[2,128]{1,0:T(2,128)S(1)}, f32[2,128]{1,0:T(2,128)S(1)}, u32[]{:S(2)}, u32[]{:S(2)}) %collective-permute-start.6) | collective-permute-done | bytes 1056 | tf_op jit(solution)/shard_map/ppermute | solution.py:44
  (52 shorter events, 16.0 us)
Async XLA Ops:
  0.6 34.6 %collective-permute-start.1 = (bf16[1024,512]{1,0:T(8,128)(2,1)}, bf16[1024,512]{1,0:T(8,128)(2,1)}, u32[]{:S(2)}, u32[]{:S(2)}) collective-permute-start(bf16[1024,512]{1,0:T(8,128)(2,1)} %param.9), channel_id=1, source_target_pairs={{0,4},{4,8},{8,12},{12,16},{16,20},{20,24},{24,28},{1,5},{5,9},{9,... | collective-permute-start | bytes 3145736 | tf_op jit(solution)/shard_map/ppermute | solution.py:22
  13.1 1.3 copy-start
  14.4 4.1 %copy-start.5 = (s32[16]{0:T(128)S(1)}, s32[16]{0:T(128)}, u32[]{:S(2)}) copy-start(s32[16]{0:T(128)} %param.13) | copy-start | bytes 196
  14.4 4.3 %copy-start.1 = (bf16[1024,1024]{1,0:T(8,128)(2,1)S(1)}, bf16[1024,1024]{1,0:T(8,128)(2,1)}, u32[]{:S(2)}) copy-start(bf16[1024,1024]{1,0:T(8,128)(2,1)} %raw_ref.2) | copy-start | bytes 6291460
  14.9 35.7 %collective-permute-start = (bf16[1024,512]{1,0:T(8,128)(2,1)S(1)}, bf16[1024,512]{1,0:T(8,128)(2,1)}, u32[]{:S(2)}, u32[]{:S(2)}) collective-permute-start(bf16[1024,512]{1,0:T(8,128)(2,1)S(1)} %fusion.4), channel_id=1, source_target_pairs={{0,4},{4,8},{8,12},{12,16},{16,20},{20,24},{24,28},{1,5},{5,9},{9,... | collective-permute-start | bytes 3145736 | tf_op jit(solution)/shard_map/ppermute | solution.py:22
  22.3 8.1 %copy-start.6 = (f32[128]{0:T(128)S(1)}, f32[128]{0:T(128)}, u32[]{:S(2)}) copy-start(f32[128]{0:T(128)} %param.10) | copy-start | bytes 1540
  35.3 1.5 copy-start.3
  36.9 16.4 %copy-start.4 = (bf16[2048,512]{1,0:T(8,128)(2,1)}, bf16[2048,512]{1,0:T(8,128)(2,1)S(1)}, u32[]{:S(2)}) copy-start(bf16[2048,512]{1,0:T(8,128)(2,1)S(1)} %constant_dynamic-update-slice_fusion.v_ref) | copy-start | bytes 6291460
  90.3 49.5 %collective-permute-start.2 = (bf16[1024,1024]{1,0:T(8,128)(2,1)}, bf16[1024,1024]{1,0:T(8,128)(2,1)S(1)}, u32[]{:S(2)}, u32[]{:S(2)}) collective-permute-start(bf16[1024,1024]{1,0:T(8,128)(2,1)} %get-tuple-element.22), channel_id=1, source_target_pairs={{4,0},{8,4},{12,8},{16,12},{20,16},{24,20},{28,24},{5,1},{9,5},{13... | collective-permute-start | bytes 6291464 | tf_op jit(solution)/shard_map/ppermute | solution.py:22
  139.8 1.3 copy-start.2
  147.3 3.6 %collective-permute-start.4 = (f32[2,128]{1,0:T(2,128)S(1)}, f32[2,128]{1,0:T(2,128)S(1)}, u32[]{:S(2)}, u32[]{:S(2)}) collective-permute-start(f32[2,128]{1,0:T(2,128)S(1)} %pad_maximum_fusion.1), channel_id=1, source_target_pairs={{0,2},{1,3},{2,0},{3,1},{4,6},{5,7},{6,4},{7,5},{8,10},{9,11},{10,... | collective-permute-start | bytes 3080 | tf_op jit(solution)/shard_map/ppermute | solution.py:44
  148.9 3.0 %collective-permute-start.5 = (f32[2,128]{1,0:T(2,128)S(1)}, f32[2,128]{1,0:T(2,128)S(1)}, u32[]{:S(2)}, u32[]{:S(2)}) collective-permute-start(f32[2,128]{1,0:T(2,128)S(1)} %pad_maximum_fusion.1), channel_id=1, source_target_pairs={{0,3},{1,2},{2,1},{3,0},{4,7},{5,6},{6,5},{7,4},{8,11},{9,10},{10,... | collective-permute-start | bytes 3080 | tf_op jit(solution)/shard_map/ppermute | solution.py:44
  148.9 3.0 %collective-permute-start.3 = (f32[2,128]{1,0:T(2,128)S(1)}, f32[2,128]{1,0:T(2,128)S(1)}, u32[]{:S(2)}, u32[]{:S(2)}) collective-permute-start(f32[2,128]{1,0:T(2,128)S(1)} %pad_maximum_fusion.1), channel_id=1, source_target_pairs={{0,1},{1,0},{2,3},{3,2},{4,5},{5,4},{6,7},{7,6},{8,9},{9,8},{10,11... | collective-permute-start | bytes 3080 | tf_op jit(solution)/shard_map/ppermute | solution.py:44
  151.9 10.1 %collective-permute-start.12 = (f32[2,128]{1,0:T(2,128)S(1)}, f32[2,128]{1,0:T(2,128)S(1)}, u32[]{:S(2)}, u32[]{:S(2)}) collective-permute-start(f32[2,128]{1,0:T(2,128)S(1)} %add_add_fusion.1), channel_id=1, source_target_pairs={{0,28},{4,24},{8,20},{12,16},{16,12},{20,8},{24,4},{28,0},{1,29},{... | collective-permute-start | bytes 3080 | tf_op jit(solution)/shard_map/ppermute | solution.py:44
  155.8 7.9 %collective-permute-start.11 = (f32[2,128]{1,0:T(2,128)S(1)}, f32[2,128]{1,0:T(2,128)S(1)}, u32[]{:S(2)}, u32[]{:S(2)}) collective-permute-start(f32[2,128]{1,0:T(2,128)S(1)} %add_add_fusion.1), channel_id=1, source_target_pairs={{0,24},{4,28},{8,16},{12,20},{16,8},{20,12},{24,0},{28,4},{1,25},{... | collective-permute-start | bytes 3080 | tf_op jit(solution)/shard_map/ppermute | solution.py:44
  157.9 6.2 %collective-permute-start.10 = (f32[2,128]{1,0:T(2,128)S(1)}, f32[2,128]{1,0:T(2,128)S(1)}, u32[]{:S(2)}, u32[]{:S(2)}) collective-permute-start(f32[2,128]{1,0:T(2,128)S(1)} %add_add_fusion.1), channel_id=1, source_target_pairs={{0,20},{4,16},{8,28},{12,24},{16,4},{20,0},{24,12},{28,8},{1,21},{... | collective-permute-start | bytes 3080 | tf_op jit(solution)/shard_map/ppermute | solution.py:44
  158.6 5.4 %collective-permute-start.9 = (f32[2,128]{1,0:T(2,128)S(1)}, f32[2,128]{1,0:T(2,128)S(1)}, u32[]{:S(2)}, u32[]{:S(2)}) collective-permute-start(f32[2,128]{1,0:T(2,128)S(1)} %add_add_fusion.1), channel_id=1, source_target_pairs={{0,16},{4,20},{8,24},{12,28},{16,0},{20,4},{24,8},{28,12},{1,17},{... | collective-permute-start | bytes 3080 | tf_op jit(solution)/shard_map/ppermute | solution.py:44
  160.5 4.5 %collective-permute-start.8 = (f32[2,128]{1,0:T(2,128)S(1)}, f32[2,128]{1,0:T(2,128)S(1)}, u32[]{:S(2)}, u32[]{:S(2)}) collective-permute-start(f32[2,128]{1,0:T(2,128)S(1)} %add_add_fusion.1), channel_id=1, source_target_pairs={{0,12},{4,8},{8,4},{12,0},{16,28},{20,24},{24,20},{28,16},{1,13},{... | collective-permute-start | bytes 3080 | tf_op jit(solution)/shard_map/ppermute | solution.py:44
  162.0 3.6 %collective-permute-start.7 = (f32[2,128]{1,0:T(2,128)S(1)}, f32[2,128]{1,0:T(2,128)S(1)}, u32[]{:S(2)}, u32[]{:S(2)}) collective-permute-start(f32[2,128]{1,0:T(2,128)S(1)} %add_add_fusion.1), channel_id=1, source_target_pairs={{0,8},{4,12},{8,0},{12,4},{16,24},{20,28},{24,16},{28,20},{1,9},{5... | collective-permute-start | bytes 3080 | tf_op jit(solution)/shard_map/ppermute | solution.py:44
  163.7 3.6 %collective-permute-start.6 = (f32[2,128]{1,0:T(2,128)S(1)}, f32[2,128]{1,0:T(2,128)S(1)}, u32[]{:S(2)}, u32[]{:S(2)}) collective-permute-start(f32[2,128]{1,0:T(2,128)S(1)} %add_add_fusion.1), channel_id=1, source_target_pairs={{0,4},{4,0},{8,12},{12,8},{16,20},{20,16},{24,28},{28,24},{1,5},{5... | collective-permute-start | bytes 3080 | tf_op jit(solution)/shard_map/ppermute | solution.py:44

commit v6 on v5

--- a/solution.py
+++ b/solution.py
@@ -37,7 +37,7 @@
         bits = count.bit_length() - 1
         low = 0
         while low < bits:
-            width = min(3, bits - low)
+            width = 1
             shifted_parts = [value]
             for mask in range(1, 1 << width):
                 pairs = [(source, source ^ (mask << low)) for source in range(count)]

time: 168 us -> 166 us (0.988)
  starting transfers between devices: 25.1 us -> 20.3 us
  waiting for transfers between devices: 41 us -> 43.2 us
    ppermute x10 -> x5, starting transfers between devices: 14.3 us -> 9.5 us  [butterfly_sum(): shifted_parts.append(lax.ppermute(value, axis, pairs))]
    ppermute x10 -> x5, waiting for transfers between devices: 5.64 us -> 7.86 us  [butterfly_sum(): shifted_parts.append(lax.ppermute(value, axis, pairs))]
  transfers between devices with their start and end apart: 13 -> 8, of which waited for: 7 -> 7; matrix products, arithmetic and copies ran while one was open for 16% -> 16% of each run, Pallas kernels for 15% -> 16%
where the time goes in v6:
time: 166 us; the launch traced here: 165 us
  Pallas kernels  68.4 us (41%)
  waiting for transfers between devices  43.2 us (26%)
  starting transfers between devices  20.3 us (12%)
  other arithmetic  16.9 us (10%)
  local copies, waits for them, and re-layouts  15.7 us (9%)
    pallas_call x1, Pallas kernels, attention_grads(): pl.pallas_call(functools.partial(halo_kernel, group=group, head_dim=head_...  37 us
    ppermute x3, waiting for transfers between devices, shifted(): lax.ppermute(value, axis, [(source, source + steps) for source in range(l...  35.3 us
    pallas_call x1, Pallas kernels, attention_grads(): pl.pallas_call(functools.partial(own_kernel, group=group, head_dim=head_d...  25.8 us
    ppermute x3, starting transfers between devices, shifted(): lax.ppermute(value, axis, [(source, source + steps) for source in range(l...  10.8 us
    ppermute x5, starting transfers between devices, butterfly_sum(): shifted_parts.append(lax.ppermute(value, axis, pairs))  9.5 us
    ppermute x5, waiting for transfers between devices, butterfly_sum(): shifted_parts.append(lax.ppermute(value, axis, pairs))  7.86 us
    unnamed x16, local copies, waits for them, and re-layouts  5.84 us
    pallas_call x1, Pallas kernels, kv_final(): pl.pallas_call(functools.partial(kv_final_kernel, head_dim=head_dim), gri...  5.53 us
  transfers between devices with their start and end apart: 8, of which 7 were waited for; matrix products, arithmetic and copies ran while one was open for 16% of the time, Pallas kernels for 16%

profile of v6, /device:TPU:0, one launch (start us, length us, event | category | flops | bytes accessed | tf_op | source)
XLA Modules:
  0.0 165.3 jit_solution(13183498340610977907)
XLA Ops:
  0.6 5.9 %collective-permute-start.1 = (bf16[1024,512]{1,0:T(8,128)(2,1)}, bf16[1024,512]{1,0:T(8,128)(2,1)}, u32[]{:S(2)}, u32[]{:S(2)}) collective-permute-start(bf16[1024,512]{1,0:T(8,128)(2,1)} %param.9), channel_id=1, source_target_pairs={{0,4},{4,8},{8,12},{12,16},{16,20},{20,24},{24,28},{1,5},{5,9},{9,... | collective-permute-start | bytes 3145736 | tf_op jit(solution)/shard_map/ppermute | solution.py:22
  7.1 2.8 %convert_multiply_fusion.3 = f32[1024,512]{1,0:T(8,128)} fusion(bf16[1024,512]{1,0:T(8,128)(2,1)} %raw_ref.3), kind=kLoop, calls=%fused_computation.6 | loop fusion | flops 1048576 | bytes 3145728 | tf_op jit(solution)/shard_map/mul | solution.py:52
  10.0 1.9 %mul.74 = f32[1024,4,128]{2,1,0:T(4,128)S(1)} reshape(f32[1024,512]{1,0:T(8,128)} %convert_multiply_fusion.3) | data formatting | bytes 4194304 | tf_op jit(solution)/shard_map/mul | solution.py:52
  14.9 3.6 %collective-permute-start = (bf16[1024,512]{1,0:T(8,128)(2,1)S(1)}, bf16[1024,512]{1,0:T(8,128)(2,1)}, u32[]{:S(2)}, u32[]{:S(2)}) collective-permute-start(bf16[1024,512]{1,0:T(8,128)(2,1)S(1)} %fusion.4), channel_id=1, source_target_pairs={{0,4},{4,8},{8,12},{12,16},{16,20},{20,24},{24,28},{1,5},{5,9},{9,... | collective-permute-start | bytes 3145736 | tf_op jit(solution)/shard_map/ppermute | solution.py:22
  19.3 2.9 %copy.31 = f32[128,8,8,128]{3,2,1,0:T(8,128)} copy(f32[128,8,8,128]{3,1,2,0:T(8,128)S(1)} %fusion) | data formatting | bytes 8388608
  22.3 4.2 %reduce_sum.56 = f32[1024,8]{1,0:T(8,128)} reduce(f32[1024,8,128]{2,1,0:T(8,128)} %bitcast.25, f32[]{:T(128)} %constant.25.clone.1), dimensions={2}, to_apply=%region_3.4 | reduce | flops 1040384 | bytes 4227076 | tf_op jit(solution)/shard_map/reduce_sum | solution.py:52
  30.4 2.2 %mul.66 = f32[1024,8,128]{2,1,0:T(8,128)S(1)} broadcast(f32[1024,8]{1,0:T(8,128)} %copy.26), dimensions={0,1} | broadcast | bytes 4227072 | tf_op jit(solution)/shard_map/mul | solution.py:53
  32.6 2.7 %fusion.2.q_ref = bf16[1024,1024]{1,0:T(8,128)(2,1)} fusion(bf16[1024,1024]{1,0:T(8,128)(2,1)S(1)} %copy-done.1, f32[128,8,8,128]{3,2,1,0:T(8,128)S(1)} %bitcast.24, f32[1024]{0:T(1024)S(1)} %broadcast_bitcast_fusion), kind=kLoop, calls=%fused_computation.4 | loop fusion | flops 4194304 | bytes 8392704 | tf_op jit(solution)/shard_map/convert_element_type | solution.py:337
  35.3 1.4 constant_dynamic-update-slice_fusion.1
  36.9 13.7 %collective-permute-done = bf16[1024,512]{1,0:T(8,128)(2,1)} collective-permute-done((bf16[1024,512]{1,0:T(8,128)(2,1)S(1)}, bf16[1024,512]{1,0:T(8,128)(2,1)}, u32[]{:S(2)}, u32[]{:S(2)}) %collective-permute-start) | collective-permute-done | bytes 1048608 | tf_op jit(solution)/shard_map/ppermute | solution.py:22
  50.6 2.7 %pad_maximum_fusion.k_ref = bf16[2048,512]{1,0:T(8,128)(2,1)} fusion(bf16[1024,512]{1,0:T(8,128)(2,1)S(1)} %fusion.4, bf16[1024,512]{1,0:T(8,128)(2,1)} %collective-permute-done), kind=kLoop, calls=%fused_computation.9 | loop fusion | flops 4194304 | bytes 4194304 | tf_op jit(solution)/shard_map/concatenate | solution.py:341
  53.3 37.0 %shard_map.110 = (f32[1024,1024]{1,0:T(8,128)}, bf16[1024,1024]{1,0:T(8,128)(2,1)}, f32[8192,1]{1,0:T(8,128)}, f32[8192,1]{1,0:T(8,128)}) custom-call(s32[1024,1]{1,0:T(8,128)} %copy.30.qdoc_ref, s32[1,2048]{1,0:T(1,128)} %bitcast.28, bf16[1024,1024]{1,0:T(8,128)(2,1)} %fusion.2.q_ref, bf16[1024,1024]{1,0:T(8,128)(2,1)} %do_ref.3, ...), custom_call_target="tpu_custom_call" | custom-call | flops 12079595520 | bytes 14680064 | tf_op jit(solution)/shard_map/pallas_call | solution.py:270
  91.6 25.8 %shard_map.111 = (bf16[1024,1024]{1,0:T(8,128)(2,1)}, f32[4,1,128]{2,1,0:T(1,128)}, f32[1024,512]{1,0:T(8,128)}, f32[1024,512]{1,0:T(8,128)}) custom-call(s32[1024,1]{1,0:T(8,128)} %copy.30.qdoc_ref, s32[1,2048]{1,0:T(1,128)} %bitcast.29, bf16[1024,1024]{1,0:T(8,128)(2,1)} %fusion.2.q_ref, bf16[1024,1024]{1,0:T(8,128)(2,1)} %do_ref.3, ...), custom_call_target="tpu_custom_call" | custom-call | flops 6710886400 | bytes 20971520 | tf_op jit(solution)/shard_map/pallas_call | solution.py:299
  118.1 21.6 %collective-permute-done.2.back_ref = bf16[1024,1024]{1,0:T(8,128)(2,1)S(1)} collective-permute-done((bf16[1024,1024]{1,0:T(8,128)(2,1)}, bf16[1024,1024]{1,0:T(8,128)(2,1)S(1)}, u32[]{:S(2)}, u32[]{:S(2)}) %collective-permute-start.2) | collective-permute-done | bytes 2097184 | tf_op jit(solution)/shard_map/ppermute | solution.py:22
  139.8 1.3 copy-done.2
  141.1 5.5 %shard_map.112 = (bf16[1024,512]{1,0:T(8,128)(2,1)}, bf16[1024,512]{1,0:T(8,128)(2,1)}, f32[4,1,128]{2,1,0:T(1,128)}) custom-call(f32[1024,512]{1,0:T(8,128)} %get-tuple-element.20.dk_ref, f32[1024,512]{1,0:T(8,128)} %get-tuple-element.21.dv_ref, bf16[1024,1024]{1,0:T(8,128)(2,1)} %copy-done.2, bf16[1024,512]{1,0:T(8,128)(2,1)} %raw_ref.3, f32[1,128]{1,0:T(1,128)} %bitcast.36), custom_call_target="tpu_custom_call" | custom-call | tf_op jit(solution)/shard_map/pallas_call | solution.py:223
  148.6 1.6 collective-permute-start.4
  150.2 2.1 %collective-permute-done.4 = f32[2,128]{1,0:T(2,128)S(1)} collective-permute-done((f32[2,128]{1,0:T(2,128)S(1)}, f32[2,128]{1,0:T(2,128)S(1)}, u32[]{:S(2)}, u32[]{:S(2)}) %collective-permute-start.4) | collective-permute-done | bytes 1056 | tf_op jit(solution)/shard_map/ppermute | solution.py:44
  152.2 2.7 %collective-permute-start.5 = (f32[2,128]{1,0:T(2,128)S(1)}, f32[2,128]{1,0:T(2,128)S(1)}, u32[]{:S(2)}, u32[]{:S(2)}) collective-permute-start(f32[2,128]{1,0:T(2,128)S(1)} %fusion.6), channel_id=1, source_target_pairs={{0,4},{4,0},{8,12},{12,8},{16,20},{20,16},{24,28},{28,24},{1,5},{5... | collective-permute-start | bytes 3080 | tf_op jit(solution)/shard_map/ppermute | solution.py:44
  154.9 1.6 collective-permute-done.5
  156.5 2.1 %collective-permute-start.6 = (f32[2,128]{1,0:T(2,128)S(1)}, f32[2,128]{1,0:T(2,128)S(1)}, u32[]{:S(2)}, u32[]{:S(2)}) collective-permute-start(f32[2,128]{1,0:T(2,128)S(1)} %add.68), channel_id=1, source_target_pairs={{0,8},{4,12},{8,0},{12,4},{16,24},{20,28},{24,16},{28,20},{1,9},{5... | collective-permute-start | bytes 3080 | tf_op jit(solution)/shard_map/ppermute | solution.py:44
  158.6 1.6 collective-permute-done.6
  160.2 3.0 %collective-permute-start.7 = (f32[2,128]{1,0:T(2,128)S(1)}, f32[2,128]{1,0:T(2,128)S(1)}, u32[]{:S(2)}, u32[]{:S(2)}) collective-permute-start(f32[2,128]{1,0:T(2,128)S(1)} %add.69), channel_id=1, source_target_pairs={{0,16},{4,20},{8,24},{12,28},{16,0},{20,4},{24,8},{28,12},{1,17},{... | collective-permute-start | bytes 3080 | tf_op jit(solution)/shard_map/ppermute | solution.py:44
  163.2 1.6 collective-permute-done.7
  (45 shorter events, 13.0 us)
Async XLA Ops:
  0.6 34.6 %collective-permute-start.1 = (bf16[1024,512]{1,0:T(8,128)(2,1)}, bf16[1024,512]{1,0:T(8,128)(2,1)}, u32[]{:S(2)}, u32[]{:S(2)}) collective-permute-start(bf16[1024,512]{1,0:T(8,128)(2,1)} %param.9), channel_id=1, source_target_pairs={{0,4},{4,8},{8,12},{12,16},{16,20},{20,24},{24,28},{1,5},{5,9},{9,... | collective-permute-start | bytes 3145736 | tf_op jit(solution)/shard_map/ppermute | solution.py:22
  13.1 1.3 copy-start
  14.4 4.1 %copy-start.5 = (s32[16]{0:T(128)S(1)}, s32[16]{0:T(128)}, u32[]{:S(2)}) copy-start(s32[16]{0:T(128)} %param.13) | copy-start | bytes 196
  14.4 4.3 %copy-start.1 = (bf16[1024,1024]{1,0:T(8,128)(2,1)S(1)}, bf16[1024,1024]{1,0:T(8,128)(2,1)}, u32[]{:S(2)}) copy-start(bf16[1024,1024]{1,0:T(8,128)(2,1)} %raw_ref.2) | copy-start | bytes 6291460
  14.9 35.7 %collective-permute-start = (bf16[1024,512]{1,0:T(8,128)(2,1)S(1)}, bf16[1024,512]{1,0:T(8,128)(2,1)}, u32[]{:S(2)}, u32[]{:S(2)}) collective-permute-start(bf16[1024,512]{1,0:T(8,128)(2,1)S(1)} %fusion.4), channel_id=1, source_target_pairs={{0,4},{4,8},{8,12},{12,16},{16,20},{20,24},{24,28},{1,5},{5,9},{9,... | collective-permute-start | bytes 3145736 | tf_op jit(solution)/shard_map/ppermute | solution.py:22
  22.3 8.1 %copy-start.6 = (f32[128]{0:T(128)S(1)}, f32[128]{0:T(128)}, u32[]{:S(2)}) copy-start(f32[128]{0:T(128)} %param.10) | copy-start | bytes 1540
  35.3 1.5 copy-start.3
  36.9 16.4 %copy-start.4 = (bf16[2048,512]{1,0:T(8,128)(2,1)}, bf16[2048,512]{1,0:T(8,128)(2,1)S(1)}, u32[]{:S(2)}) copy-start(bf16[2048,512]{1,0:T(8,128)(2,1)S(1)} %constant_dynamic-update-slice_fusion.v_ref) | copy-start | bytes 6291460
  90.3 49.5 %collective-permute-start.2 = (bf16[1024,1024]{1,0:T(8,128)(2,1)}, bf16[1024,1024]{1,0:T(8,128)(2,1)S(1)}, u32[]{:S(2)}, u32[]{:S(2)}) collective-permute-start(bf16[1024,1024]{1,0:T(8,128)(2,1)} %get-tuple-element.22), channel_id=1, source_target_pairs={{4,0},{8,4},{12,8},{16,12},{20,16},{24,20},{28,24},{5,1},{9,5},{13... | collective-permute-start | bytes 6291464 | tf_op jit(solution)/shard_map/ppermute | solution.py:22
  139.8 1.4 copy-start.2
  147.4 1.2 collective-permute-start.3
  148.6 3.6 %collective-permute-start.4 = (f32[2,128]{1,0:T(2,128)S(1)}, f32[2,128]{1,0:T(2,128)S(1)}, u32[]{:S(2)}, u32[]{:S(2)}) collective-permute-start(f32[2,128]{1,0:T(2,128)S(1)} %fusion.5), channel_id=1, source_target_pairs={{0,2},{1,3},{2,0},{3,1},{4,6},{5,7},{6,4},{7,5},{8,10},{9,11},{10,... | collective-permute-start | bytes 3080 | tf_op jit(solution)/shard_map/ppermute | solution.py:44
  152.2 4.3 %collective-permute-start.5 = (f32[2,128]{1,0:T(2,128)S(1)}, f32[2,128]{1,0:T(2,128)S(1)}, u32[]{:S(2)}, u32[]{:S(2)}) collective-permute-start(f32[2,128]{1,0:T(2,128)S(1)} %fusion.6), channel_id=1, source_target_pairs={{0,4},{4,0},{8,12},{12,8},{16,20},{20,16},{24,28},{28,24},{1,5},{5... | collective-permute-start | bytes 3080 | tf_op jit(solution)/shard_map/ppermute | solution.py:44
  156.5 3.7 %collective-permute-start.6 = (f32[2,128]{1,0:T(2,128)S(1)}, f32[2,128]{1,0:T(2,128)S(1)}, u32[]{:S(2)}, u32[]{:S(2)}) collective-permute-start(f32[2,128]{1,0:T(2,128)S(1)} %add.68), channel_id=1, source_target_pairs={{0,8},{4,12},{8,0},{12,4},{16,24},{20,28},{24,16},{28,20},{1,9},{5... | collective-permute-start | bytes 3080 | tf_op jit(solution)/shard_map/ppermute | solution.py:44
  160.2 4.6 %collective-permute-start.7 = (f32[2,128]{1,0:T(2,128)S(1)}, f32[2,128]{1,0:T(2,128)S(1)}, u32[]{:S(2)}, u32[]{:S(2)}) collective-permute-start(f32[2,128]{1,0:T(2,128)S(1)} %add.69), channel_id=1, source_target_pairs={{0,16},{4,20},{8,24},{12,28},{16,0},{20,4},{24,8},{28,12},{1,17},{... | collective-permute-start | bytes 3080 | tf_op jit(solution)/shard_map/ppermute | solution.py:44

commit v7 on v6

--- a/solution.py
+++ b/solution.py
@@ -101,8 +101,8 @@
     return dq_part, dk_part * scale, dv_part
 
 
-def halo_kernel(qdoc_ref, kdoc_ref, q_ref, do_ref, k_ref, v_ref,
-                dq_ref, dkv_ref, lse_ref, delta_ref, dk_ref, dv_ref, *, group, head_dim):
+def halo_kernel(qdoc_ref, kdoc_ref, q_ref, do_ref, k_ref, v_ref, kgain_ref,
+                dq_ref, dkv_ref, lse_ref, delta_ref, kpart_ref, dk_ref, dv_ref, kn_ref, *, group, head_dim):
     blk = BLOCK
     n_tiles = WINDOW // blk + 1
     n_halo = WINDOW // blk
@@ -111,6 +111,13 @@
     scale = QUERY_SCALAR ** (-0.5)
     dk_ref[...] = jnp.zeros(dk_ref.shape, jnp.float32)
     dv_ref[...] = jnp.zeros(dv_ref.shape, jnp.float32)
+    halo_raw = k_ref[0:WINDOW, :].astype(jnp.float32)
+    halo_inv = lax.rsqrt(jnp.mean(halo_raw * halo_raw, axis=1, keepdims=True) + EPS)
+    kn_ref[...] = (halo_raw * halo_inv * kgain_ref[...]).astype(jnp.bfloat16)
+
+    def key_tile(k_first):
+        src = kn_ref if k_first < WINDOW else k_ref
+        return src[k_first:k_first + blk, :], v_ref[k_first:k_first + blk, :]
     for qb in range(n_q):
         q_first = qb * blk
         q_g = stacked(q_ref, group, head_dim, q_first)
@@ -120,8 +127,7 @@
         numer = jnp.zeros((gb, head_dim), jnp.float32)
         for t in range(n_tiles):
             k_first = q_first + t * blk
-            k_tile = k_ref[k_first:k_first + blk, :]
-            v_tile = v_ref[k_first:k_first + blk, :]
+            k_tile, v_tile = key_tile(k_first)
             scores = lax.dot_general(
                 q_g, k_tile, (((1,), (1,)), ((), ())), preferred_element_type=jnp.float32
             ) * scale
@@ -136,8 +142,7 @@
         dq = jnp.zeros((gb, head_dim), jnp.float32)
         for t in range(n_halo - qb):
             k_first = q_first + t * blk
-            k_tile = k_ref[k_first:k_first + blk, :]
-            v_tile = v_ref[k_first:k_first + blk, :]
+            k_tile, v_tile = key_tile(k_first)
             dq_part, dk_part, dv_part = grad_tile(q_g, do_g, k_tile, v_tile, masks[t], log_sums, delta)
             dq = dq + dq_part
             dk_ref[k_first:k_first + blk, :] += dk_part
@@ -147,6 +152,9 @@
         ) * scale
     dkv_ref[:, :head_dim] = dk_ref[...].astype(jnp.bfloat16)
     dkv_ref[:, head_dim:] = dv_ref[...].astype(jnp.bfloat16)
+    halo_raw = k_ref[0:WINDOW, :].astype(jnp.float32)
+    halo_hat = halo_raw * lax.rsqrt(jnp.mean(halo_raw * halo_raw, axis=1, keepdims=True) + EPS)
+    kpart_ref[...] = jnp.sum(dk_ref[...] * halo_hat, axis=0, keepdims=True).reshape(kpart_ref.shape)
 
 
 def norm_grad(raw, gain, upstream):
@@ -159,7 +167,7 @@
 
 
 def own_kernel(qdoc_ref, kdoc_ref, q_ref, do_ref, k_ref, v_ref, lse_ref, delta_ref, dq_in_ref, raw_ref, gain_ref,
-               qgrad_ref, qgain_ref, dk_ref, dv_ref, *, group, head_dim):
+               kraw_ref, qgrad_ref, qgain_ref, kpart_ref, dk_ref, dv_ref, *, group, head_dim):
     blk = BLOCK
     n_tiles = WINDOW // blk + 1
     n_halo = WINDOW // blk
@@ -196,6 +204,9 @@
             qgrad_ref[q_first:q_first + blk, cols] = result.astype(qgrad_ref.dtype)
             gain_sum = gain_sum + part
     qgain_ref[...] = gain_sum.reshape(qgain_ref.shape)
+    key_raw = kraw_ref[...].astype(jnp.float32)
+    key_hat = key_raw * lax.rsqrt(jnp.mean(key_raw * key_raw, axis=1, keepdims=True) + EPS)
+    kpart_ref[...] = jnp.sum(dk_ref[...] * key_hat, axis=0, keepdims=True).reshape(kpart_ref.shape)
 
 
 def kv_final_kernel(dk_ref, dv_ref, back_ref, raw_ref, gain_ref, kgrad_ref, vgrad_ref, kgain_ref, *, head_dim):
@@ -241,7 +252,7 @@
 
 
 def attention_grads(query_norm, grad_rows, keys_all, vals_all, own_doc, all_doc, key_heads, head_dim,
-                    query_raw, query_gain):
+                    query_raw, query_gain, key_raw, key_gain):
     tok_rows, q_cols = query_norm.shape
     key_rows = keys_all.shape[0]
     group = q_cols // (key_heads * head_dim)
@@ -267,25 +278,31 @@
     params = pltpu.CompilerParams(dimension_semantics=("arbitrary",))
     in_bytes = 2 * 2 * tok_rows * q_cols + 2 * 2 * key_rows * kv_cols
     operands = (own_doc.reshape(tok_rows, 1), all_doc.reshape(1, key_rows), query_norm, grad_rows, keys_all, vals_all)
-    dq_half, dkv_halo, log_sums, delta = pl.pallas_call(
+    part_spec = pl.BlockSpec((1, 1, head_dim), lambda h: (h, 0, 0))
+    part_shape = jax.ShapeDtypeStruct((key_heads, 1, head_dim), jnp.float32)
+    gain_spec = pl.BlockSpec((1, head_dim), lambda h: (0, 0))
+    dq_half, dkv_halo, log_sums, delta, khalo_parts = pl.pallas_call(
         functools.partial(halo_kernel, group=group, head_dim=head_dim),
         grid=(key_heads,),
-        in_specs=common_specs,
+        in_specs=common_specs + [gain_spec],
         out_specs=[
             dq_spec,
             pl.BlockSpec((WINDOW, 2 * head_dim), lambda h: (0, h)),
             stat_spec,
             stat_spec,
+            part_spec,
         ],
         out_shape=[
             jax.ShapeDtypeStruct((tok_rows, q_cols), jnp.float32),
             jax.ShapeDtypeStruct((WINDOW, 2 * kv_cols), jnp.bfloat16),
             jax.ShapeDtypeStruct((stat_rows, 1), jnp.float32),
             jax.ShapeDtypeStruct((stat_rows, 1), jnp.float32),
+            part_shape,
         ],
         scratch_shapes=[
             pltpu.VMEM((WINDOW, head_dim), jnp.float32),
             pltpu.VMEM((WINDOW, head_dim), jnp.float32),
+            pltpu.VMEM((WINDOW, head_dim), jnp.bfloat16),
         ],
         compiler_params=params,
         cost_estimate=pl.CostEstimate(
@@ -293,22 +310,24 @@
             transcendentals=key_heads * (n_q * n_tiles + halo_tiles) * group * blk * blk,
             bytes_accessed=in_bytes + 4 * tok_rows * q_cols + 2 * 2 * WINDOW * kv_cols,
         ),
-    )(*operands)
+    )(*operands, key_gain.reshape(1, head_dim))
     raw_spec = pl.BlockSpec((tok_rows, gw), lambda h: (0, h))
-    gain_spec = pl.BlockSpec((1, head_dim), lambda h: (0, 0))
-    query_grad, qgain_parts, dk_own, dv_own = pl.pallas_call(
+    kraw_spec = pl.BlockSpec((tok_rows, head_dim), lambda h: (0, h))
+    query_grad, qgain_parts, kown_parts, dk_own, dv_own = pl.pallas_call(
         functools.partial(own_kernel, group=group, head_dim=head_dim),
         grid=(key_heads,),
-        in_specs=common_specs + [stat_spec, stat_spec, dq_spec, raw_spec, gain_spec],
+        in_specs=common_specs + [stat_spec, stat_spec, dq_spec, raw_spec, gain_spec, kraw_spec],
         out_specs=[
             raw_spec,
-            pl.BlockSpec((1, 1, head_dim), lambda h: (h, 0, 0)),
+            part_spec,
+            part_spec,
             pl.BlockSpec((tok_rows, head_dim), lambda h: (0, h)),
             pl.BlockSpec((tok_rows, head_dim), lambda h: (0, h)),
         ],
         out_shape=[
             jax.ShapeDtypeStruct((tok_rows, q_cols), jnp.bfloat16),
-            jax.ShapeDtypeStruct((key_heads, 1, head_dim), jnp.float32),
+            part_shape,
+            part_shape,
             jax.ShapeDtypeStruct((tok_rows, kv_cols), jnp.float32),
             jax.ShapeDtypeStruct((tok_rows, kv_cols), jnp.float32),
         ],
@@ -318,8 +337,9 @@
             transcendentals=key_heads * own_tiles * group * blk * blk,
             bytes_accessed=in_bytes + 2 * 4 * tok_rows * q_cols + 2 * 4 * tok_rows * kv_cols,
         ),
-    )(*operands, log_sums, delta, dq_half, query_raw, query_gain.reshape(1, head_dim))
-    return query_grad, jnp.sum(qgain_parts, axis=(0, 1)), dkv_halo, dk_own, dv_own
+    )(*operands, log_sums, delta, dq_half, query_raw, query_gain.reshape(1, head_dim), key_raw)
+    key_part = jnp.sum(khalo_parts, axis=(0, 1)) + jnp.sum(kown_parts, axis=(0, 1))
+    return query_grad, jnp.sum(qgain_parts, axis=(0, 1)), key_part, dkv_halo, dk_own, dv_own
 
 
 def per_device(query_raw, key_raw, value_proj, query_gain, key_gain, out_grad, doc_lengths):
@@ -337,17 +357,17 @@
     query_norm = (query_hat * query_gain).astype(jnp.bfloat16).reshape(tok_rows, query_heads * head_dim)
     key_hat, key_inv = norm_rows(key_raw, key_heads)
     key_norm = (key_hat * key_gain).astype(jnp.bfloat16).reshape(tok_rows, key_heads * head_dim)
-    halo_keys, halo_vals = shifted((key_norm[tok_rows - WINDOW:], value_proj[tok_rows - WINDOW:]), "ctx", 1)
+    halo_keys, halo_vals = shifted((key_raw[tok_rows - WINDOW:], value_proj[tok_rows - WINDOW:]), "ctx", 1)
     keys_all = jnp.concatenate([halo_keys, key_norm], axis=0)
     vals_all = jnp.concatenate([halo_vals, value_proj], axis=0)
     all_doc = jnp.concatenate([halo_doc, own_doc])
-    query_grad, query_part, dkv_halo, dk_own, dv_own = attention_grads(
-        query_norm, out_grad, keys_all, vals_all, own_doc, all_doc, key_heads, head_dim, query_raw, query_gain
+    query_grad, query_part, key_part, dkv_halo, dk_own, dv_own = attention_grads(
+        query_norm, out_grad, keys_all, vals_all, own_doc, all_doc, key_heads, head_dim, query_raw, query_gain,
+        key_raw, key_gain,
     )
+    gain_grads = butterfly_sum(jnp.stack([query_part, key_part]), ("head", "ctx"))
     back = shifted(dkv_halo, "ctx", -1)
-    key_grad, value_grad, key_parts = kv_final(dk_own, dv_own, back, key_raw, key_gain, key_heads, head_dim)
-    key_part = jnp.sum(key_parts, axis=(0, 1))
-    gain_grads = butterfly_sum(jnp.stack([query_part, key_part]), ("head", "ctx"))
+    key_grad, value_grad, _ = kv_final(dk_own, dv_own, back, key_raw, key_gain, key_heads, head_dim)
     return (query_grad, key_grad, value_grad, gain_grads[0], gain_grads[1])
 
 

time: 166 us -> 158 us (0.952)
  waiting for transfers between devices: 43.2 us -> 31.7 us
    ppermute x3, waiting for transfers between devices: 35.3 us -> 13 us  [shifted(): lax.ppermute(value, axis, [(source, source + steps) for source in range(l...]
    ppermute x5, waiting for transfers between devices: 7.86 us -> 18.7 us  [butterfly_sum(): shifted_parts.append(lax.ppermute(value, axis, pairs))]
    reduce_sum x2, other arithmetic: 5.31 us -> 7.08 us  [norm_rows(): inverse = lax.rsqrt(jnp.mean(values * values, axis=-1, keepdims=True) + EPS)]
    unnamed x16 -> x22, local copies, waits for them, and re-layouts: 5.84 us -> 6.45 us
  transfers between devices with their start and end apart: 8 -> 8, of which waited for: 7 -> 6; matrix products, arithmetic and copies ran while one was open for 16% -> 18% of each run, Pallas kernels for 16% -> 17%
where the time goes in v7:
time: 158 us; the launch traced here: 157 us
  Pallas kernels  69.6 us (44%)
  waiting for transfers between devices  31.7 us (20%)
  starting transfers between devices  21.3 us (13%)
  other arithmetic  18.2 us (12%)
  local copies, waits for them, and re-layouts  15.5 us (10%)
    pallas_call x1, Pallas kernels, attention_grads(): pl.pallas_call(functools.partial(halo_kernel, group=group, head_dim=head_...  37.9 us
    pallas_call x1, Pallas kernels, attention_grads(): pl.pallas_call(functools.partial(own_kernel, group=group, head_dim=head_d...  26.2 us
    ppermute x5, waiting for transfers between devices, butterfly_sum(): shifted_parts.append(lax.ppermute(value, axis, pairs))  18.7 us
    ppermute x3, waiting for transfers between devices, shifted(): lax.ppermute(value, axis, [(source, source + steps) for source in range(l...  13 us
    ppermute x3, starting transfers between devices, shifted(): lax.ppermute(value, axis, [(source, source + steps) for source in range(l...  10.8 us
    ppermute x5, starting transfers between devices, butterfly_sum(): shifted_parts.append(lax.ppermute(value, axis, pairs))  10.6 us
    reduce_sum x2, other arithmetic, norm_rows(): inverse = lax.rsqrt(jnp.mean(values * values, axis=-1, keepdims=True) + EPS)  7.08 us
    unnamed x22, local copies, waits for them, and re-layouts  6.45 us
  transfers between devices with their start and end apart: 8, of which 6 were waited for; matrix products, arithmetic and copies ran while one was open for 18% of the time, Pallas kernels for 17%

profile of v7, /device:TPU:0, one launch (start us, length us, event | category | flops | bytes accessed | tf_op | source)
XLA Modules:
  0.0 157.1 jit_solution(8650599686231361063)
XLA Ops:
  0.7 6.0 %collective-permute-start.1 = (bf16[1024,512]{1,0:T(8,128)(2,1)}, bf16[1024,512]{1,0:T(8,128)(2,1)}, u32[]{:S(2)}, u32[]{:S(2)}) collective-permute-start(bf16[1024,512]{1,0:T(8,128)(2,1)} %param.9), channel_id=1, source_target_pairs={{0,4},{4,8},{8,12},{12,16},{16,20},{20,24},{24,28},{1,5},{5,9},{9,... | collective-permute-start | bytes 3145736 | tf_op jit(solution)/shard_map/ppermute | solution.py:22
  6.6 3.5 %collective-permute-start = (bf16[1024,512]{1,0:T(8,128)(2,1)}, bf16[1024,512]{1,0:T(8,128)(2,1)}, u32[]{:S(2)}, u32[]{:S(2)}) collective-permute-start(bf16[1024,512]{1,0:T(8,128)(2,1)} %raw_ref.3), channel_id=1, source_target_pairs={{0,4},{4,8},{8,12},{12,16},{16,20},{20,24},{24,28},{1,5},{5,9},{9,... | collective-permute-start | bytes 3145736 | tf_op jit(solution)/shard_map/ppermute | solution.py:22
  10.1 1.5 convert_multiply_fusion.3
  12.0 1.7 %mul.74 = f32[1024,4,128]{2,1,0:T(4,128)} reshape(f32[1024,512]{1,0:T(8,128)S(1)} %convert_multiply_fusion.3) | data formatting | bytes 4194304 | tf_op jit(solution)/shard_map/mul | solution.py:52
  13.8 2.9 %reduce_sum.66 = f32[1024,4]{1,0:T(8,128)S(1)} reduce(f32[1024,4,128]{2,1,0:T(4,128)} %mul.74, f32[]{:T(128)} %constant.25.clone.1), dimensions={2}, to_apply=%region_4.5 | reduce | flops 520192 | bytes 2113540 | tf_op jit(solution)/shard_map/reduce_sum | solution.py:52
  18.2 2.9 %copy.31 = f32[128,8,8,128]{3,2,1,0:T(8,128)} copy(f32[128,8,8,128]{3,1,2,0:T(8,128)S(1)} %fusion) | data formatting | bytes 8388608
  21.1 4.2 %reduce_sum.65 = f32[1024,8]{1,0:T(8,128)} reduce(f32[1024,8,128]{2,1,0:T(8,128)} %bitcast.26, f32[]{:T(128)} %constant.25.clone.1), dimensions={2}, to_apply=%region_3.4 | reduce | flops 1040384 | bytes 4227076 | tf_op jit(solution)/shard_map/reduce_sum | solution.py:52
  29.2 2.2 %mul.75 = f32[1024,4,128]{2,1,0:T(4,128)S(1)} broadcast(f32[1024,4]{1,0:T(8,128)} %add_rsqrt_fusion), dimensions={0,1} | broadcast | bytes 2113536 | tf_op jit(solution)/shard_map/mul | solution.py:53
  33.6 2.7 %fusion.2.q_ref = bf16[1024,1024]{1,0:T(8,128)(2,1)} fusion(bf16[1024,1024]{1,0:T(8,128)(2,1)S(1)} %copy-done.1, f32[128,8,8,128]{3,2,1,0:T(8,128)S(1)} %bitcast.25, f32[1024]{0:T(1024)S(1)} %broadcast_bitcast_fusion), kind=kLoop, calls=%fused_computation.4 | loop fusion | flops 4194304 | bytes 8392704 | tf_op jit(solution)/shard_map/convert_element_type | solution.py:357
  36.3 1.4 constant_dynamic-update-slice_fusion.1
  37.9 12.9 %collective-permute-done = bf16[1024,512]{1,0:T(8,128)(2,1)} collective-permute-done((bf16[1024,512]{1,0:T(8,128)(2,1)}, bf16[1024,512]{1,0:T(8,128)(2,1)}, u32[]{:S(2)}, u32[]{:S(2)}) %collective-permute-start) | collective-permute-done | bytes 1048608 | tf_op jit(solution)/shard_map/ppermute | solution.py:22
  50.9 2.7 %pad_maximum_fusion.k_ref = bf16[2048,512]{1,0:T(8,128)(2,1)} fusion(bf16[1024,512]{1,0:T(8,128)(2,1)S(1)} %fusion.4, bf16[1024,512]{1,0:T(8,128)(2,1)} %collective-permute-done), kind=kLoop, calls=%fused_computation.9 | loop fusion | flops 4194304 | bytes 4194304 | tf_op jit(solution)/shard_map/concatenate | solution.py:361
  53.5 37.9 %shard_map.110 = (f32[1024,1024]{1,0:T(8,128)}, bf16[1024,1024]{1,0:T(8,128)(2,1)}, f32[8192,1]{1,0:T(8,128)}, f32[8192,1]{1,0:T(8,128)}, f32[4,1,128]{2,1,0:T(1,128)}) custom-call(s32[1024,1]{1,0:T(8,128)} %copy.30.qdoc_ref, s32[1,2048]{1,0:T(1,128)} %bitcast.29, bf16[1024,1024]{1,0:T(8,128)(2,1)} %fusion.2.q_ref, bf16[1024,1024]{1,0:T(8,128)(2,1)} %do_ref.3, ...), custom_call_target="tpu_custom_call" | custom-call | flops 12079595520 | bytes 14680064 | tf_op jit(solution)/shard_map/pallas_call | solution.py:284
  92.7 26.2 %shard_map.111 = (bf16[1024,1024]{1,0:T(8,128)(2,1)}, f32[4,1,128]{2,1,0:T(1,128)}, f32[4,1,128]{2,1,0:T(1,128)}, f32[1024,512]{1,0:T(8,128)}, f32[1024,512]{1,0:T(8,128)}) custom-call(s32[1024,1]{1,0:T(8,128)} %copy.30.qdoc_ref, s32[1,2048]{1,0:T(1,128)} %bitcast.30, bf16[1024,1024]{1,0:T(8,128)(2,1)} %fusion.2.q_ref, bf16[1024,1024]{1,0:T(8,128)(2,1)} %do_ref.3, ...), custom_call_target="tpu_custom_call" | custom-call | flops 6710886400 | bytes 20971520 | tf_op jit(solution)/shard_map/pallas_call | solution.py:316
  121.6 1.6 %collective-permute-start.4 = (f32[2,128]{1,0:T(2,128)S(1)}, f32[2,128]{1,0:T(2,128)S(1)}, u32[]{:S(2)}, u32[]{:S(2)}) collective-permute-start(f32[2,128]{1,0:T(2,128)S(1)} %fusion.5), channel_id=1, source_target_pairs={{0,2},{1,3},{2,0},{3,1},{4,6},{5,7},{6,4},{7,5},{8,10},{9,11},{10,... | collective-permute-start | bytes 3080 | tf_op jit(solution)/shard_map/ppermute | solution.py:44
  123.2 2.1 %collective-permute-done.4 = f32[2,128]{1,0:T(2,128)S(1)} collective-permute-done((f32[2,128]{1,0:T(2,128)S(1)}, f32[2,128]{1,0:T(2,128)S(1)}, u32[]{:S(2)}, u32[]{:S(2)}) %collective-permute-start.4) | collective-permute-done | bytes 1056 | tf_op jit(solution)/shard_map/ppermute | solution.py:44
  125.2 3.2 %collective-permute-start.5 = (f32[2,128]{1,0:T(2,128)S(1)}, f32[2,128]{1,0:T(2,128)S(1)}, u32[]{:S(2)}, u32[]{:S(2)}) collective-permute-start(f32[2,128]{1,0:T(2,128)S(1)} %fusion.6), channel_id=1, source_target_pairs={{0,4},{4,0},{8,12},{12,8},{16,20},{20,16},{24,28},{28,24},{1,5},{5... | collective-permute-start | bytes 3080 | tf_op jit(solution)/shard_map/ppermute | solution.py:44
  128.4 12.4 %collective-permute-done.5 = f32[2,128]{1,0:T(2,128)S(1)} collective-permute-done((f32[2,128]{1,0:T(2,128)S(1)}, f32[2,128]{1,0:T(2,128)S(1)}, u32[]{:S(2)}, u32[]{:S(2)}) %collective-permute-start.5) | collective-permute-done | bytes 1056 | tf_op jit(solution)/shard_map/ppermute | solution.py:44
  140.8 2.7 %collective-permute-start.6 = (f32[2,128]{1,0:T(2,128)S(1)}, f32[2,128]{1,0:T(2,128)S(1)}, u32[]{:S(2)}, u32[]{:S(2)}) collective-permute-start(f32[2,128]{1,0:T(2,128)S(1)} %add.83), channel_id=1, source_target_pairs={{0,8},{4,12},{8,0},{12,4},{16,24},{20,28},{24,16},{28,20},{1,9},{5... | collective-permute-start | bytes 3080 | tf_op jit(solution)/shard_map/ppermute | solution.py:44
  143.6 1.6 collective-permute-done.6
  145.1 3.0 %collective-permute-start.7 = (f32[2,128]{1,0:T(2,128)S(1)}, f32[2,128]{1,0:T(2,128)S(1)}, u32[]{:S(2)}, u32[]{:S(2)}) collective-permute-start(f32[2,128]{1,0:T(2,128)S(1)} %add.84), channel_id=1, source_target_pairs={{0,16},{4,20},{8,24},{12,28},{16,0},{20,4},{24,8},{28,12},{1,17},{... | collective-permute-start | bytes 3080 | tf_op jit(solution)/shard_map/ppermute | solution.py:44
  148.2 1.6 collective-permute-done.7
  150.2 1.4 copy-done.3
  151.6 5.5 %shard_map.112 = (bf16[1024,512]{1,0:T(8,128)(2,1)}, bf16[1024,512]{1,0:T(8,128)(2,1)}, f32[4,1,128]{2,1,0:T(1,128)}) custom-call(f32[1024,512]{1,0:T(8,128)} %get-tuple-element.21.dk_ref, f32[1024,512]{1,0:T(8,128)} %get-tuple-element.22.dv_ref, bf16[1024,1024]{1,0:T(8,128)(2,1)} %copy-done.3, bf16[1024,512]{1,0:T(8,128)(2,1)} %raw_ref.3, f32[1,128]{1,0:T(1,128)} %bitcast.35), custom_call_target="tpu_custom_call" | custom-call | tf_op jit(solution)/shard_map/pallas_call | solution.py:234
  (53 shorter events, 12.6 us)
Async XLA Ops:
  0.6 11.0 %copy-start.9 = (f32[128]{0:T(128)S(1)}, f32[128]{0:T(128)}, u32[]{:S(2)}) copy-start(f32[128]{0:T(128)} %param.10) | copy-start | bytes 1540
  0.6 11.0 %copy-start.8 = (s32[16]{0:T(128)S(1)}, s32[16]{0:T(128)}, u32[]{:S(2)}) copy-start(s32[16]{0:T(128)} %param.13) | copy-start | bytes 196
  0.7 35.6 %collective-permute-start.1 = (bf16[1024,512]{1,0:T(8,128)(2,1)}, bf16[1024,512]{1,0:T(8,128)(2,1)}, u32[]{:S(2)}, u32[]{:S(2)}) collective-permute-start(bf16[1024,512]{1,0:T(8,128)(2,1)} %param.9), channel_id=1, source_target_pairs={{0,4},{4,8},{8,12},{12,16},{16,20},{20,24},{24,28},{1,5},{5,9},{9,... | collective-permute-start | bytes 3145736 | tf_op jit(solution)/shard_map/ppermute | solution.py:22
  6.6 44.2 %collective-permute-start = (bf16[1024,512]{1,0:T(8,128)(2,1)}, bf16[1024,512]{1,0:T(8,128)(2,1)}, u32[]{:S(2)}, u32[]{:S(2)}) collective-permute-start(bf16[1024,512]{1,0:T(8,128)(2,1)} %raw_ref.3), channel_id=1, source_target_pairs={{0,4},{4,8},{8,12},{12,16},{16,20},{20,24},{24,28},{1,5},{5,9},{9,... | collective-permute-start | bytes 3145736 | tf_op jit(solution)/shard_map/ppermute | solution.py:22
  13.8 3.8 %copy-start.1 = (bf16[1024,1024]{1,0:T(8,128)(2,1)S(1)}, bf16[1024,1024]{1,0:T(8,128)(2,1)}, u32[]{:S(2)}) copy-start(bf16[1024,1024]{1,0:T(8,128)(2,1)} %raw_ref.2) | copy-start | bytes 6291460
  21.1 5.5 %copy-start.7 = (f32[128]{0:T(128)S(1)}, f32[128]{0:T(128)}, u32[]{:S(2)}) copy-start(f32[128]{0:T(128)} %param.11) | copy-start | bytes 1540
  25.2 6.2 %copy-start = (bf16[1024,512]{1,0:T(8,128)(2,1)S(1)}, bf16[1024,512]{1,0:T(8,128)(2,1)}, u32[]{:S(2)}) copy-start(bf16[1024,512]{1,0:T(8,128)(2,1)} %raw_ref.3) | copy-start | bytes 3145732
  31.4 1.0 copy-start.2
  36.3 1.5 copy-start.4
  37.9 15.6 %copy-start.5 = (bf16[2048,512]{1,0:T(8,128)(2,1)}, bf16[2048,512]{1,0:T(8,128)(2,1)S(1)}, u32[]{:S(2)}) copy-start(bf16[2048,512]{1,0:T(8,128)(2,1)S(1)} %constant_dynamic-update-slice_fusion.v_ref) | copy-start | bytes 6291460
  91.4 58.8 %collective-permute-start.2 = (bf16[1024,1024]{1,0:T(8,128)(2,1)}, bf16[1024,1024]{1,0:T(8,128)(2,1)S(1)}, u32[]{:S(2)}, u32[]{:S(2)}) collective-permute-start(bf16[1024,1024]{1,0:T(8,128)(2,1)} %get-tuple-element.23), channel_id=1, source_target_pairs={{4,0},{8,4},{12,8},{16,12},{20,16},{24,20},{28,24},{5,1},{9,5},{13... | collective-permute-start | bytes 6291464 | tf_op jit(solution)/shard_map/ppermute | solution.py:22
  92.7 27.6 %copy-start.6 = (f32[4,1,128]{2,1,0:T(1,128)S(1)}, f32[4,1,128]{2,1,0:T(1,128)}, u32[]{:S(2)}) copy-start(f32[4,1,128]{2,1,0:T(1,128)} %get-tuple-element.27) | copy-start | bytes 6148
  120.4 1.2 collective-permute-start.3
  121.6 3.6 %collective-permute-start.4 = (f32[2,128]{1,0:T(2,128)S(1)}, f32[2,128]{1,0:T(2,128)S(1)}, u32[]{:S(2)}, u32[]{:S(2)}) collective-permute-start(f32[2,128]{1,0:T(2,128)S(1)} %fusion.5), channel_id=1, source_target_pairs={{0,2},{1,3},{2,0},{3,1},{4,6},{5,7},{6,4},{7,5},{8,10},{9,11},{10,... | collective-permute-start | bytes 3080 | tf_op jit(solution)/shard_map/ppermute | solution.py:44
  125.2 15.6 %collective-permute-start.5 = (f32[2,128]{1,0:T(2,128)S(1)}, f32[2,128]{1,0:T(2,128)S(1)}, u32[]{:S(2)}, u32[]{:S(2)}) collective-permute-start(f32[2,128]{1,0:T(2,128)S(1)} %fusion.6), channel_id=1, source_target_pairs={{0,4},{4,0},{8,12},{12,8},{16,20},{20,16},{24,28},{28,24},{1,5},{5... | collective-permute-start | bytes 3080 | tf_op jit(solution)/shard_map/ppermute | solution.py:44
  140.8 4.3 %collective-permute-start.6 = (f32[2,128]{1,0:T(2,128)S(1)}, f32[2,128]{1,0:T(2,128)S(1)}, u32[]{:S(2)}, u32[]{:S(2)}) collective-permute-start(f32[2,128]{1,0:T(2,128)S(1)} %add.83), channel_id=1, source_target_pairs={{0,8},{4,12},{8,0},{12,4},{16,24},{20,28},{24,16},{28,20},{1,9},{5... | collective-permute-start | bytes 3080 | tf_op jit(solution)/shard_map/ppermute | solution.py:44
  145.1 4.6 %collective-permute-start.7 = (f32[2,128]{1,0:T(2,128)S(1)}, f32[2,128]{1,0:T(2,128)S(1)}, u32[]{:S(2)}, u32[]{:S(2)}) collective-permute-start(f32[2,128]{1,0:T(2,128)S(1)} %add.84), channel_id=1, source_target_pairs={{0,16},{4,20},{8,24},{12,28},{16,0},{20,4},{24,8},{28,12},{1,17},{... | collective-permute-start | bytes 3080 | tf_op jit(solution)/shard_map/ppermute | solution.py:44
  150.2 1.4 copy-start.3

commit v8 on v7

--- a/solution.py
+++ b/solution.py
@@ -101,8 +101,9 @@
     return dq_part, dk_part * scale, dv_part
 
 
-def halo_kernel(qdoc_ref, kdoc_ref, q_ref, do_ref, k_ref, v_ref, kgain_ref,
-                dq_ref, dkv_ref, lse_ref, delta_ref, kpart_ref, dk_ref, dv_ref, kn_ref, *, group, head_dim):
+def halo_kernel(qdoc_ref, kdoc_ref, q_ref, do_ref, hk_ref, hv_ref, k_ref, v_ref, kgain_ref, *refs,
+                group, head_dim, n_alias):
+    dq_ref, dkv_ref, lse_ref, delta_ref, kpart_ref, dk_ref, dv_ref, kn_ref = refs[n_alias:]
     blk = BLOCK
     n_tiles = WINDOW // blk + 1
     n_halo = WINDOW // blk
@@ -111,13 +112,16 @@
     scale = QUERY_SCALAR ** (-0.5)
     dk_ref[...] = jnp.zeros(dk_ref.shape, jnp.float32)
     dv_ref[...] = jnp.zeros(dv_ref.shape, jnp.float32)
-    halo_raw = k_ref[0:WINDOW, :].astype(jnp.float32)
+    halo_raw = hk_ref[...].astype(jnp.float32)
     halo_inv = lax.rsqrt(jnp.mean(halo_raw * halo_raw, axis=1, keepdims=True) + EPS)
     kn_ref[...] = (halo_raw * halo_inv * kgain_ref[...]).astype(jnp.bfloat16)
 
     def key_tile(k_first):
-        src = kn_ref if k_first < WINDOW else k_ref
-        return src[k_first:k_first + blk, :], v_ref[k_first:k_first + blk, :]
+        if k_first < WINDOW:
+            return kn_ref[k_first:k_first + blk, :], hv_ref[k_first:k_first + blk, :]
+        own_first = k_first - WINDOW
+        return k_ref[own_first:own_first + blk, :], v_ref[own_first:own_first + blk, :]
+
     for qb in range(n_q):
         q_first = qb * blk
         q_g = stacked(q_ref, group, head_dim, q_first)
@@ -152,8 +156,7 @@
         ) * scale
     dkv_ref[:, :head_dim] = dk_ref[...].astype(jnp.bfloat16)
     dkv_ref[:, head_dim:] = dv_ref[...].astype(jnp.bfloat16)
-    halo_raw = k_ref[0:WINDOW, :].astype(jnp.float32)
-    halo_hat = halo_raw * lax.rsqrt(jnp.mean(halo_raw * halo_raw, axis=1, keepdims=True) + EPS)
+    halo_hat = halo_raw * halo_inv
     kpart_ref[...] = jnp.sum(dk_ref[...] * halo_hat, axis=0, keepdims=True).reshape(kpart_ref.shape)
 
 
@@ -188,11 +191,11 @@
         for t in range(max(0, n_halo - qb), n_tiles):
             live, _ = tile_mask(qdoc_ref, kdoc_ref, q_first, t, group)
             k_first = q_first + t * blk
-            k_tile = k_ref[k_first:k_first + blk, :]
-            v_tile = v_ref[k_first:k_first + blk, :]
+            own_first = k_first - WINDOW
+            k_tile = k_ref[own_first:own_first + blk, :]
+            v_tile = v_ref[own_first:own_first + blk, :]
             dq_part, dk_part, dv_part = grad_tile(q_g, do_g, k_tile, v_tile, live, log_sums, delta)
             dq = dq + dq_part
-            own_first = k_first - WINDOW
             dk_ref[own_first:own_first + blk, :] += dk_part
             dv_ref[own_first:own_first + blk, :] += dv_part
         dq_in = dq_in_ref[q_first:q_first + blk, :]
@@ -251,10 +254,10 @@
     )(dk_own, dv_own, back, key_raw, key_gain.reshape(1, head_dim))
 
 
-def attention_grads(query_norm, grad_rows, keys_all, vals_all, own_doc, all_doc, key_heads, head_dim,
-                    query_raw, query_gain, key_raw, key_gain):
+def attention_grads(query_norm, grad_rows, halo_pieces, key_norm, value_proj, own_doc, all_doc, key_heads,
+                    head_dim, query_raw, query_gain, key_raw, key_gain):
     tok_rows, q_cols = query_norm.shape
-    key_rows = keys_all.shape[0]
+    key_rows = WINDOW + tok_rows
     group = q_cols // (key_heads * head_dim)
     blk = BLOCK
     n_q = tok_rows // blk
@@ -265,65 +268,65 @@
     tile_flops = 2 * (group * blk) * blk * head_dim
     halo_tiles = sum(max(0, WINDOW // blk - qb) for qb in range(n_q))
     own_tiles = n_q * n_tiles - halo_tiles
-    common_specs = [
-        pl.BlockSpec((tok_rows, 1), lambda h: (0, 0)),
-        pl.BlockSpec((1, key_rows), lambda h: (0, 0)),
-        pl.BlockSpec((tok_rows, gw), lambda h: (0, h)),
-        pl.BlockSpec((tok_rows, gw), lambda h: (0, h)),
-        pl.BlockSpec((key_rows, head_dim), lambda h: (0, h)),
-        pl.BlockSpec((key_rows, head_dim), lambda h: (0, h)),
-    ]
-    stat_spec = pl.BlockSpec((n_q * group * blk, 1), lambda h: (h, 0))
-    dq_spec = pl.BlockSpec((tok_rows, gw), lambda h: (0, h))
+    n_piece = key_heads // len(halo_pieces)
     params = pltpu.CompilerParams(dimension_semantics=("arbitrary",))
-    in_bytes = 2 * 2 * tok_rows * q_cols + 2 * 2 * key_rows * kv_cols
-    operands = (own_doc.reshape(tok_rows, 1), all_doc.reshape(1, key_rows), query_norm, grad_rows, keys_all, vals_all)
+    gain_spec = pl.BlockSpec((1, head_dim), lambda h: (0, 0))
+    doc_specs = [pl.BlockSpec((tok_rows, 1), lambda h: (0, 0)), pl.BlockSpec((1, key_rows), lambda h: (0, 0))]
+    qdoc, kdoc = own_doc.reshape(tok_rows, 1), all_doc.reshape(1, key_rows)
+    buffers = ()
+    kparts = []
+    for piece, (hk, hv) in enumerate(halo_pieces):
+        h0 = piece * n_piece
+        qcol = pl.BlockSpec((tok_rows, gw), lambda h, h0=h0: (0, h + h0))
+        kcol = pl.BlockSpec((tok_rows, head_dim), lambda h, h0=h0: (0, h + h0))
+        hcol = pl.BlockSpec((WINDOW, head_dim), lambda h: (0, h))
+        stat = pl.BlockSpec((n_q * group * blk, 1), lambda h, h0=h0: (h + h0, 0))
+        outs = pl.pallas_call(
+            functools.partial(halo_kernel, group=group, head_dim=head_dim, n_alias=len(buffers)),
+            grid=(n_piece,),
+            in_specs=doc_specs + [qcol, qcol, hcol, hcol, kcol, kcol, gain_spec]
+            + [pl.BlockSpec(memory_space=pl.ANY)] * len(buffers),
+            out_specs=[
+                qcol,
+                pl.BlockSpec((WINDOW, 2 * head_dim), lambda h, h0=h0: (0, h + h0)),
+                stat,
+                stat,
+                pl.BlockSpec((1, 1, head_dim), lambda h: (h, 0, 0)),
+            ],
+            out_shape=[
+                jax.ShapeDtypeStruct((tok_rows, q_cols), jnp.float32),
+                jax.ShapeDtypeStruct((WINDOW, 2 * kv_cols), jnp.bfloat16),
+                jax.ShapeDtypeStruct((stat_rows, 1), jnp.float32),
+                jax.ShapeDtypeStruct((stat_rows, 1), jnp.float32),
+                jax.ShapeDtypeStruct((n_piece, 1, head_dim), jnp.float32),
+            ],
+            scratch_shapes=[
+                pltpu.VMEM((WINDOW, head_dim), jnp.float32),
+                pltpu.VMEM((WINDOW, head_dim), jnp.float32),
+                pltpu.VMEM((WINDOW, head_dim), jnp.bfloat16),
+            ],
+            input_output_aliases={9 + i: i for i in range(len(buffers))},
+            compiler_params=params,
+            cost_estimate=pl.CostEstimate(
+                flops=n_piece * (2 * n_q * n_tiles + 5 * halo_tiles) * tile_flops,
+                transcendentals=n_piece * (n_q * n_tiles + halo_tiles) * group * blk * blk,
+                bytes_accessed=n_piece * (2 * 2 * tok_rows * gw + 2 * 2 * key_rows * head_dim
+                                          + 4 * tok_rows * gw + 2 * 2 * WINDOW * head_dim),
+            ),
+        )(qdoc, kdoc, query_norm, grad_rows, hk, hv, key_norm, value_proj, key_gain.reshape(1, head_dim), *buffers)
+        buffers = tuple(outs[:4])
+        kparts.append(outs[4])
+    dq_half, dkv_halo, log_sums, delta = buffers
+    qcol = pl.BlockSpec((tok_rows, gw), lambda h: (0, h))
+    kcol = pl.BlockSpec((tok_rows, head_dim), lambda h: (0, h))
+    stat = pl.BlockSpec((n_q * group * blk, 1), lambda h: (h, 0))
     part_spec = pl.BlockSpec((1, 1, head_dim), lambda h: (h, 0, 0))
     part_shape = jax.ShapeDtypeStruct((key_heads, 1, head_dim), jnp.float32)
-    gain_spec = pl.BlockSpec((1, head_dim), lambda h: (0, 0))
-    dq_half, dkv_halo, log_sums, delta, khalo_parts = pl.pallas_call(
-        functools.partial(halo_kernel, group=group, head_dim=head_dim),
-        grid=(key_heads,),
-        in_specs=common_specs + [gain_spec],
-        out_specs=[
-            dq_spec,
-            pl.BlockSpec((WINDOW, 2 * head_dim), lambda h: (0, h)),
-            stat_spec,
-            stat_spec,
-            part_spec,
-        ],
-        out_shape=[
-            jax.ShapeDtypeStruct((tok_rows, q_cols), jnp.float32),
-            jax.ShapeDtypeStruct((WINDOW, 2 * kv_cols), jnp.bfloat16),
-            jax.ShapeDtypeStruct((stat_rows, 1), jnp.float32),
-            jax.ShapeDtypeStruct((stat_rows, 1), jnp.float32),
-            part_shape,
-        ],
-        scratch_shapes=[
-            pltpu.VMEM((WINDOW, head_dim), jnp.float32),
-            pltpu.VMEM((WINDOW, head_dim), jnp.float32),
-            pltpu.VMEM((WINDOW, head_dim), jnp.bfloat16),
-        ],
-        compiler_params=params,
-        cost_estimate=pl.CostEstimate(
-            flops=key_heads * (2 * n_q * n_tiles + 5 * halo_tiles) * tile_flops,
-            transcendentals=key_heads * (n_q * n_tiles + halo_tiles) * group * blk * blk,
-            bytes_accessed=in_bytes + 4 * tok_rows * q_cols + 2 * 2 * WINDOW * kv_cols,
-        ),
-    )(*operands, key_gain.reshape(1, head_dim))
-    raw_spec = pl.BlockSpec((tok_rows, gw), lambda h: (0, h))
-    kraw_spec = pl.BlockSpec((tok_rows, head_dim), lambda h: (0, h))
     query_grad, qgain_parts, kown_parts, dk_own, dv_own = pl.pallas_call(
         functools.partial(own_kernel, group=group, head_dim=head_dim),
         grid=(key_heads,),
-        in_specs=common_specs + [stat_spec, stat_spec, dq_spec, raw_spec, gain_spec, kraw_spec],
-        out_specs=[
-            raw_spec,
-            part_spec,
-            part_spec,
-            pl.BlockSpec((tok_rows, head_dim), lambda h: (0, h)),
-            pl.BlockSpec((tok_rows, head_dim), lambda h: (0, h)),
-        ],
+        in_specs=doc_specs + [qcol, qcol, kcol, kcol, stat, stat, qcol, qcol, gain_spec, kcol],
+        out_specs=[qcol, part_spec, part_spec, kcol, kcol],
         out_shape=[
             jax.ShapeDtypeStruct((tok_rows, q_cols), jnp.bfloat16),
             part_shape,
@@ -335,10 +338,14 @@
         cost_estimate=pl.CostEstimate(
             flops=key_heads * own_tiles * 5 * tile_flops,
             transcendentals=key_heads * own_tiles * group * blk * blk,
-            bytes_accessed=in_bytes + 2 * 4 * tok_rows * q_cols + 2 * 4 * tok_rows * kv_cols,
+            bytes_accessed=2 * 2 * tok_rows * q_cols + 2 * 2 * tok_rows * kv_cols + 2 * 4 * tok_rows * q_cols
+            + 2 * 4 * tok_rows * kv_cols,
         ),
-    )(*operands, log_sums, delta, dq_half, query_raw, query_gain.reshape(1, head_dim), key_raw)
-    key_part = jnp.sum(khalo_parts, axis=(0, 1)) + jnp.sum(kown_parts, axis=(0, 1))
+    )(qdoc, kdoc, query_norm, grad_rows, key_norm, value_proj, log_sums, delta, dq_half, query_raw,
+      query_gain.reshape(1, head_dim), key_raw)
+    key_part = jnp.sum(kown_parts, axis=(0, 1))
+    for part in kparts:
+        key_part = key_part + jnp.sum(part, axis=(0, 1))
     return query_grad, jnp.sum(qgain_parts, axis=(0, 1)), key_part, dkv_halo, dk_own, dv_own
 
 
@@ -357,13 +364,19 @@
     query_norm = (query_hat * query_gain).astype(jnp.bfloat16).reshape(tok_rows, query_heads * head_dim)
     key_hat, key_inv = norm_rows(key_raw, key_heads)
     key_norm = (key_hat * key_gain).astype(jnp.bfloat16).reshape(tok_rows, key_heads * head_dim)
-    halo_keys, halo_vals = shifted((key_raw[tok_rows - WINDOW:], value_proj[tok_rows - WINDOW:]), "ctx", 1)
-    keys_all = jnp.concatenate([halo_keys, key_norm], axis=0)
-    vals_all = jnp.concatenate([halo_vals, value_proj], axis=0)
+    n_pieces = 2 if key_heads % 2 == 0 else 1
+    width = key_heads * head_dim // n_pieces
+    halo_pieces = []
+    for piece in range(n_pieces):
+        cols = slice(piece * width, (piece + 1) * width)
+        send = (key_raw[tok_rows - WINDOW:, cols], value_proj[tok_rows - WINDOW:, cols])
+        if halo_pieces:
+            send = lax.optimization_barrier((send, halo_pieces[-1][0]))[0]
+        halo_pieces.append(shifted(send, "ctx", 1))
     all_doc = jnp.concatenate([halo_doc, own_doc])
     query_grad, query_part, key_part, dkv_halo, dk_own, dv_own = attention_grads(
-        query_norm, out_grad, keys_all, vals_all, own_doc, all_doc, key_heads, head_dim, query_raw, query_gain,
-        key_raw, key_gain,
+        query_norm, out_grad, halo_pieces, key_norm, value_proj, own_doc, all_doc, key_heads, head_dim,
+        query_raw, query_gain, key_raw, key_gain,
     )
     gain_grads = butterfly_sum(jnp.stack([query_part, key_part]), ("head", "ctx"))
     back = shifted(dkv_halo, "ctx", -1)

time: 158 us -> 154 us (0.975)
  waiting for transfers between devices: 31.7 us -> 20.1 us
  Pallas kernels: 69.6 us -> 73.2 us
  starting transfers between devices: 21.3 us -> 24.3 us
  local copies, waits for them, and re-layouts: 15.5 us -> 17.6 us
    ppermute x3 -> x5, waiting for transfers between devices: 13 us -> 0.01 us  [shifted(): lax.ppermute(value, axis, [(source, source + steps) for source in range(l...]
    ppermute x3 -> x5, starting transfers between devices: 10.8 us -> 16.8 us  [shifted(): lax.ppermute(value, axis, [(source, source + steps) for source in range(l...]
    pallas_call x1 -> x2, Pallas kernels: 37.9 us -> 41.6 us  [attention_grads(): pl.pallas_call(functools.partial(halo_kernel, group=group, head_dim=head_...]
    slice x0 -> x2, local copies, waits for them, and re-layouts: none -> 3.45 us  [the longest x1 2.37 us: per_device(): value_proj[tok_rows - WINDOW:, cols]]
    ppermute x5, starting transfers between devices: 10.6 us -> 7.53 us  [butterfly_sum(): shifted_parts.append(lax.ppermute(value, axis, pairs))]
    concatenate x1 -> x0, other arithmetic: 2.69 us -> none  [per_device(): keys_all = jnp.concatenate([halo_keys, key_norm], axis=0)]
    unnamed x22 -> x23, local copies, waits for them, and re-layouts: 6.45 us -> 5.26 us
  transfers between devices with their start and end apart: 8 -> 10, of which waited for: 6 -> 5; matrix products, arithmetic and copies ran while one was open for 18% -> 20% of each run, Pallas kernels for 17% -> 31%
where the time goes in v8:
time: 154 us; the launch traced here: 153 us
  Pallas kernels  73.2 us (48%)
  starting transfers between devices  24.3 us (16%)
  waiting for transfers between devices  20.1 us (13%)
  local copies, waits for them, and re-layouts  17.6 us (11%)
  other arithmetic  17.1 us (11%)
    pallas_call x2, Pallas kernels, attention_grads(): pl.pallas_call(functools.partial(halo_kernel, group=group, head_dim=head_...  41.6 us
    pallas_call x1, Pallas kernels, attention_grads(): pl.pallas_call(functools.partial(own_kernel, group=group, head_dim=head_d...  26 us
    ppermute x5, waiting for transfers between devices, butterfly_sum(): shifted_parts.append(lax.ppermute(value, axis, pairs))  20.1 us
    ppermute x5, starting transfers between devices, shifted(): lax.ppermute(value, axis, [(source, source + steps) for source in range(l...  16.8 us
    reduce_sum x2, other arithmetic, norm_rows(): inverse = lax.rsqrt(jnp.mean(values * values, axis=-1, keepdims=True) + EPS)  7.88 us
    ppermute x5, starting transfers between devices, butterfly_sum(): shifted_parts.append(lax.ppermute(value, axis, pairs))  7.53 us
    pallas_call x1, Pallas kernels, kv_final(): pl.pallas_call(functools.partial(kv_final_kernel, head_dim=head_dim), gri...  5.53 us
    unnamed x23, local copies, waits for them, and re-layouts  5.26 us
  transfers between devices with their start and end apart: 10, of which 5 were waited for; matrix products, arithmetic and copies ran while one was open for 20% of the time, Pallas kernels for 31%

profile of v8, /device:TPU:0, one launch (start us, length us, event | category | flops | bytes accessed | tf_op | source)
XLA Modules:
  0.0 153.1 jit_solution(6928980669134093497)
XLA Ops:
  0.6 2.4 %fusion.6 = (bf16[1024,256]{1,0:T(8,128)(2,1)}, bf16[1024,256]{1,0:T(8,128)(2,1)}) fusion(bf16[1024,512]{1,0:T(8,128)(2,1)} %v_ref.5), kind=kLoop, calls=%fused_computation.24 | loop fusion | bytes 2097152 | tf_op jit(solution)/shard_map/slice | solution.py:372
  3.0 5.7 %collective-permute-start.3 = (bf16[1024,256]{1,0:T(8,128)(2,1)}, bf16[1024,256]{1,0:T(8,128)(2,1)}, u32[]{:S(2)}, u32[]{:S(2)}) collective-permute-start(bf16[1024,256]{1,0:T(8,128)(2,1)} %get-tuple-element.45), channel_id=1, source_target_pairs={{0,4},{4,8},{8,12},{12,16},{16,20},{20,24},{24,28},{1,5},{5,9},{9,... | collective-permute-start | bytes 1572872 | tf_op jit(solution)/shard_map/ppermute | solution.py:22
  9.8 3.6 %collective-permute-start = (bf16[1024,256]{1,0:T(8,128)(2,1)}, bf16[1024,256]{1,0:T(8,128)(2,1)}, u32[]{:S(2)}, u32[]{:S(2)}) collective-permute-start(bf16[1024,256]{1,0:T(8,128)(2,1)} %get-tuple-element.47), channel_id=1, source_target_pairs={{0,4},{4,8},{8,12},{12,16},{16,20},{20,24},{24,28},{1,5},{5,9},{9,... | collective-permute-start | bytes 1572872 | tf_op jit(solution)/shard_map/ppermute | solution.py:22
  15.1 1.7 %mul.74 = f32[1024,4,128]{2,1,0:T(4,128)} reshape(f32[1024,512]{1,0:T(8,128)S(1)} %convert_multiply_fusion.3) | data formatting | bytes 4194304 | tf_op jit(solution)/shard_map/mul | solution.py:52
  16.8 3.7 %reduce_sum.75 = f32[1024,4]{1,0:T(8,128)} reduce(f32[1024,4,128]{2,1,0:T(4,128)} %mul.74, f32[]{:T(128)} %constant.25.clone.1), dimensions={2}, to_apply=%region_4.5 | reduce | flops 520192 | bytes 2113540 | tf_op jit(solution)/shard_map/reduce_sum | solution.py:52
  20.5 1.9 %add_rsqrt_fusion = f32[1024,4]{1,0:T(8,128)} fusion(f32[1024,4]{1,0:T(8,128)} %reduce_sum.75), kind=kLoop, calls=%fused_computation.9 | loop fusion | flops 8192 | bytes 32768 | tf_op jit(solution)/shard_map/rsqrt | solution.py:52
  23.1 2.9 %copy.39 = f32[128,8,8,128]{3,2,1,0:T(8,128)} copy(f32[128,8,8,128]{3,1,2,0:T(8,128)S(1)} %fusion) | data formatting | bytes 8388608
  26.0 4.2 %reduce_sum.74 = f32[1024,8]{1,0:T(8,128)} reduce(f32[1024,8,128]{2,1,0:T(8,128)} %bitcast.26, f32[]{:T(128)} %constant.25.clone.1), dimensions={2}, to_apply=%region_3.4 | reduce | flops 1040384 | bytes 4227076 | tf_op jit(solution)/shard_map/reduce_sum | solution.py:52
  32.4 2.2 %mul.75 = f32[1024,4,128]{2,1,0:T(4,128)S(1)} broadcast(f32[1024,4]{1,0:T(8,128)} %add_rsqrt_fusion), dimensions={0,1} | broadcast | bytes 2113536 | tf_op jit(solution)/shard_map/mul | solution.py:53
  37.7 2.7 %fusion.2.q_ref = bf16[1024,1024]{1,0:T(8,128)(2,1)} fusion(bf16[1024,1024]{1,0:T(8,128)(2,1)S(1)} %copy-done.1, f32[128,8,8,128]{3,2,1,0:T(8,128)S(1)} %bitcast.25, f32[1024]{0:T(1024)S(1)} %broadcast_bitcast_fusion), kind=kLoop, calls=%fused_computation.4 | loop fusion | flops 4194304 | bytes 8392704 | tf_op jit(solution)/shard_map/convert_element_type | solution.py:364
  40.4 2.6 %collective-permute-start.1 = (bf16[1024,256]{1,0:T(8,128)(2,1)}, bf16[1024,256]{1,0:T(8,128)(2,1)S(1)}, u32[]{:S(2)}, u32[]{:S(2)}) collective-permute-start(bf16[1024,256]{1,0:T(8,128)(2,1)} %get-tuple-element.24), channel_id=1, source_target_pairs={{0,4},{4,8},{8,12},{12,16},{16,20},{20,24},{24,28},{1,5},{5,9},{9,... | collective-permute-start | bytes 1572872 | tf_op jit(solution)/shard_map/ppermute | solution.py:22
  43.0 3.6 %collective-permute-start.2 = (bf16[1024,256]{1,0:T(8,128)(2,1)}, bf16[1024,256]{1,0:T(8,128)(2,1)S(1)}, u32[]{:S(2)}, u32[]{:S(2)}) collective-permute-start(bf16[1024,256]{1,0:T(8,128)(2,1)} %get-tuple-element.25), channel_id=1, source_target_pairs={{0,4},{4,8},{8,12},{12,16},{16,20},{20,24},{24,28},{1,5},{5,9},{9,... | collective-permute-start | bytes 1572872 | tf_op jit(solution)/shard_map/ppermute | solution.py:22
  46.7 20.7 %shard_map.110 = (f32[1024,1024]{1,0:T(8,128)}, bf16[1024,1024]{1,0:T(8,128)(2,1)}, f32[8192,1]{1,0:T(8,128)}, f32[8192,1]{1,0:T(8,128)}, f32[2,1,128]{2,1,0:T(1,128)}) custom-call(s32[1024,1]{1,0:T(8,128)} %copy.38.qdoc_ref, s32[1,2048]{1,0:T(1,128)} %bitcast.29, bf16[1024,1024]{1,0:T(8,128)(2,1)} %fusion.2.q_ref, bf16[1024,1024]{1,0:T(8,128)(2,1)} %do_ref.5, ...), custom_call_target="tpu_custom_call" | custom-call | flops 6039797760 | bytes 7340032 | tf_op jit(solution)/shard_map/pallas_call | solution.py:284
  68.4 20.9 %shard_map.111 = (f32[1024,1024]{1,0:T(8,128)}, bf16[1024,1024]{1,0:T(8,128)(2,1)}, f32[8192,1]{1,0:T(8,128)}, f32[8192,1]{1,0:T(8,128)}, f32[2,1,128]{2,1,0:T(1,128)}) custom-call(s32[1024,1]{1,0:T(8,128)} %copy.38.qdoc_ref, s32[1,2048]{1,0:T(1,128)} %bitcast.30, ...), custom_call_target="tpu_custom_call", output_to_operand_aliasing={{0}: (9, {}), {1}: (10, {}), {2}: (11, {}), {3}: (12, {})} | custom-call | flops 6039797760 | bytes 7340032 | tf_op jit(solution)/shard_map/pallas_call | solution.py:284
  90.6 26.0 %shard_map.112 = (bf16[1024,1024]{1,0:T(8,128)(2,1)}, f32[4,1,128]{2,1,0:T(1,128)}, f32[4,1,128]{2,1,0:T(1,128)}, f32[1024,512]{1,0:T(8,128)}, f32[1024,512]{1,0:T(8,128)}) custom-call(s32[1024,1]{1,0:T(8,128)} %copy.38.qdoc_ref, s32[1,2048]{1,0:T(1,128)} %bitcast.31, bf16[1024,1024]{1,0:T(8,128)(2,1)} %fusion.2.q_ref, bf16[1024,1024]{1,0:T(8,128)(2,1)} %do_ref.5, ...), custom_call_target="tpu_custom_call" | custom-call | flops 6710886400 | bytes 18874368 | tf_op jit(solution)/shard_map/pallas_call | solution.py:325
  119.3 1.6 %collective-permute-start.6 = (f32[2,128]{1,0:T(2,128)S(1)}, f32[2,128]{1,0:T(2,128)S(1)}, u32[]{:S(2)}, u32[]{:S(2)}) collective-permute-start(f32[2,128]{1,0:T(2,128)S(1)} %fusion.5), channel_id=1, source_target_pairs={{0,2},{1,3},{2,0},{3,1},{4,6},{5,7},{6,4},{7,5},{8,10},{9,11},{10,... | collective-permute-start | bytes 3080 | tf_op jit(solution)/shard_map/ppermute | solution.py:44
  120.9 2.1 %collective-permute-done.6 = f32[2,128]{1,0:T(2,128)S(1)} collective-permute-done((f32[2,128]{1,0:T(2,128)S(1)}, f32[2,128]{1,0:T(2,128)S(1)}, u32[]{:S(2)}, u32[]{:S(2)}) %collective-permute-start.6) | collective-permute-done | bytes 1056 | tf_op jit(solution)/shard_map/ppermute | solution.py:44
  123.0 2.7 %collective-permute-start.7 = (f32[2,128]{1,0:T(2,128)S(1)}, f32[2,128]{1,0:T(2,128)S(1)}, u32[]{:S(2)}, u32[]{:S(2)}) collective-permute-start(f32[2,128]{1,0:T(2,128)S(1)} %fusion.8), channel_id=1, source_target_pairs={{0,4},{4,0},{8,12},{12,8},{16,20},{20,16},{24,28},{28,24},{1,5},{5... | collective-permute-start | bytes 3080 | tf_op jit(solution)/shard_map/ppermute | solution.py:44
  125.7 12.0 %collective-permute-done.7 = f32[2,128]{1,0:T(2,128)S(1)} collective-permute-done((f32[2,128]{1,0:T(2,128)S(1)}, f32[2,128]{1,0:T(2,128)S(1)}, u32[]{:S(2)}, u32[]{:S(2)}) %collective-permute-start.7) | collective-permute-done | bytes 1056 | tf_op jit(solution)/shard_map/ppermute | solution.py:44
  137.7 1.5 %collective-permute-start.8 = (f32[2,128]{1,0:T(2,128)S(1)}, f32[2,128]{1,0:T(2,128)S(1)}, u32[]{:S(2)}, u32[]{:S(2)}) collective-permute-start(f32[2,128]{1,0:T(2,128)S(1)} %add.95), channel_id=1, source_target_pairs={{0,8},{4,12},{8,0},{12,4},{16,24},{20,28},{24,16},{28,20},{1,9},{5... | collective-permute-start | bytes 3080 | tf_op jit(solution)/shard_map/ppermute | solution.py:44
  139.2 2.0 %collective-permute-done.8 = f32[2,128]{1,0:T(2,128)S(1)} collective-permute-done((f32[2,128]{1,0:T(2,128)S(1)}, f32[2,128]{1,0:T(2,128)S(1)}, u32[]{:S(2)}, u32[]{:S(2)}) %collective-permute-start.8) | collective-permute-done | bytes 1056 | tf_op jit(solution)/shard_map/ppermute | solution.py:44
  141.3 1.6 %collective-permute-start.9 = (f32[2,128]{1,0:T(2,128)S(1)}, f32[2,128]{1,0:T(2,128)S(1)}, u32[]{:S(2)}, u32[]{:S(2)}) collective-permute-start(f32[2,128]{1,0:T(2,128)S(1)} %add.96), channel_id=1, source_target_pairs={{0,16},{4,20},{8,24},{12,28},{16,0},{20,4},{24,8},{28,12},{1,17},{... | collective-permute-start | bytes 3080 | tf_op jit(solution)/shard_map/ppermute | solution.py:44
  142.9 2.8 %collective-permute-done.9 = f32[2,128]{1,0:T(2,128)S(1)} collective-permute-done((f32[2,128]{1,0:T(2,128)S(1)}, f32[2,128]{1,0:T(2,128)S(1)}, u32[]{:S(2)}, u32[]{:S(2)}) %collective-permute-start.9) | collective-permute-done | bytes 1056 | tf_op jit(solution)/shard_map/ppermute | solution.py:44
  147.6 5.5 %shard_map.113 = (bf16[1024,512]{1,0:T(8,128)(2,1)}, bf16[1024,512]{1,0:T(8,128)(2,1)}, f32[4,1,128]{2,1,0:T(1,128)}) custom-call(f32[1024,512]{1,0:T(8,128)} %get-tuple-element.34.dk_ref, f32[1024,512]{1,0:T(8,128)} %get-tuple-element.35.dv_ref, bf16[1024,1024]{1,0:T(8,128)(2,1)} %copy-done.3, bf16[1024,512]{1,0:T(8,128)(2,1)} %raw_ref.3, f32[1,128]{1,0:T(1,128)} %bitcast.37), custom_call_target="tpu_custom_call" | custom-call | tf_op jit(solution)/shard_map/pallas_call | solution.py:237
  (60 shorter events, 15.5 us)
Async XLA Ops:
  0.6 8.1 %copy-start = (bf16[1024,512]{1,0:T(8,128)(2,1)S(1)}, bf16[1024,512]{1,0:T(8,128)(2,1)}, u32[]{:S(2)}) copy-start(bf16[1024,512]{1,0:T(8,128)(2,1)} %raw_ref.3) | copy-start | bytes 3145732
  3.0 43.6 %collective-permute-start.3 = (bf16[1024,256]{1,0:T(8,128)(2,1)}, bf16[1024,256]{1,0:T(8,128)(2,1)}, u32[]{:S(2)}, u32[]{:S(2)}) collective-permute-start(bf16[1024,256]{1,0:T(8,128)(2,1)} %get-tuple-element.45), channel_id=1, source_target_pairs={{0,4},{4,8},{8,12},{12,16},{16,20},{20,24},{24,28},{1,5},{5,9},{9,... | collective-permute-start | bytes 1572872 | tf_op jit(solution)/shard_map/ppermute | solution.py:22
  9.8 3.9 %copy-start.6 = (f32[128]{0:T(128)S(1)}, f32[128]{0:T(128)}, u32[]{:S(2)}) copy-start(f32[128]{0:T(128)} %param.11) | copy-start | bytes 1540
  9.8 3.9 %copy-start.10 = (f32[128]{0:T(128)S(1)}, f32[128]{0:T(128)}, u32[]{:S(2)}) copy-start(f32[128]{0:T(128)} %param.10) | copy-start | bytes 1540
  9.8 4.0 %copy-start.9 = (s32[16]{0:T(128)S(1)}, s32[16]{0:T(128)}, u32[]{:S(2)}) copy-start(s32[16]{0:T(128)} %param.13) | copy-start | bytes 196
  9.8 30.6 %collective-permute-start = (bf16[1024,256]{1,0:T(8,128)(2,1)}, bf16[1024,256]{1,0:T(8,128)(2,1)}, u32[]{:S(2)}, u32[]{:S(2)}) collective-permute-start(bf16[1024,256]{1,0:T(8,128)(2,1)} %get-tuple-element.47), channel_id=1, source_target_pairs={{0,4},{4,8},{8,12},{12,16},{16,20},{20,24},{24,28},{1,5},{5,9},{9,... | collective-permute-start | bytes 1572872 | tf_op jit(solution)/shard_map/ppermute | solution.py:22
  16.8 5.6 %copy-start.1 = (bf16[1024,1024]{1,0:T(8,128)(2,1)S(1)}, bf16[1024,1024]{1,0:T(8,128)(2,1)}, u32[]{:S(2)}) copy-start(bf16[1024,1024]{1,0:T(8,128)(2,1)} %raw_ref.2) | copy-start | bytes 6291460
  34.6 2.0 %copy-start.2 = (f32[1024,8]{1,0:T(8,128)S(1)}, f32[1024,8]{1,0:T(8,128)}, u32[]{:S(2)}) copy-start(f32[1024,8]{1,0:T(8,128)} %copy.33) | copy-start | bytes 98308
  40.4 27.0 %collective-permute-start.1 = (bf16[1024,256]{1,0:T(8,128)(2,1)}, bf16[1024,256]{1,0:T(8,128)(2,1)S(1)}, u32[]{:S(2)}, u32[]{:S(2)}) collective-permute-start(bf16[1024,256]{1,0:T(8,128)(2,1)} %get-tuple-element.24), channel_id=1, source_target_pairs={{0,4},{4,8},{8,12},{12,16},{16,20},{20,24},{24,28},{1,5},{5,9},{9,... | collective-permute-start | bytes 1572872 | tf_op jit(solution)/shard_map/ppermute | solution.py:22
  43.0 24.4 %collective-permute-start.2 = (bf16[1024,256]{1,0:T(8,128)(2,1)}, bf16[1024,256]{1,0:T(8,128)(2,1)S(1)}, u32[]{:S(2)}, u32[]{:S(2)}) collective-permute-start(bf16[1024,256]{1,0:T(8,128)(2,1)} %get-tuple-element.25), channel_id=1, source_target_pairs={{0,4},{4,8},{8,12},{12,16},{16,20},{20,24},{24,28},{1,5},{5,9},{9,... | collective-permute-start | bytes 1572872 | tf_op jit(solution)/shard_map/ppermute | solution.py:22
  67.4 0.8 copy-start.4
  67.4 0.9 copy-start.5
  68.4 22.2 %copy-start.8 = (f32[2,1,128]{2,1,0:T(1,128)S(1)}, f32[2,1,128]{2,1,0:T(1,128)}, u32[]{:S(2)}) copy-start(f32[2,1,128]{2,1,0:T(1,128)} %get-tuple-element.41) | copy-start | bytes 3076
  89.3 57.0 %collective-permute-start.4 = (bf16[1024,1024]{1,0:T(8,128)(2,1)}, bf16[1024,1024]{1,0:T(8,128)(2,1)S(1)}, u32[]{:S(2)}, u32[]{:S(2)}) collective-permute-start(bf16[1024,1024]{1,0:T(8,128)(2,1)} %get-tuple-element.36), channel_id=1, source_target_pairs={{4,0},{8,4},{12,8},{16,12},{20,16},{24,20},{28,24},{5,1},{9,5},{13... | collective-permute-start | bytes 6291464 | tf_op jit(solution)/shard_map/ppermute | solution.py:22
  90.6 27.4 %copy-start.7 = (f32[2,1,128]{2,1,0:T(1,128)S(1)}, f32[2,1,128]{2,1,0:T(1,128)}, u32[]{:S(2)}) copy-start(f32[2,1,128]{2,1,0:T(1,128)} %get-tuple-element.42) | copy-start | bytes 3076
  118.1 1.2 collective-permute-start.5
  119.3 3.6 %collective-permute-start.6 = (f32[2,128]{1,0:T(2,128)S(1)}, f32[2,128]{1,0:T(2,128)S(1)}, u32[]{:S(2)}, u32[]{:S(2)}) collective-permute-start(f32[2,128]{1,0:T(2,128)S(1)} %fusion.5), channel_id=1, source_target_pairs={{0,2},{1,3},{2,0},{3,1},{4,6},{5,7},{6,4},{7,5},{8,10},{9,11},{10,... | collective-permute-start | bytes 3080 | tf_op jit(solution)/shard_map/ppermute | solution.py:44
  123.0 14.7 %collective-permute-start.7 = (f32[2,128]{1,0:T(2,128)S(1)}, f32[2,128]{1,0:T(2,128)S(1)}, u32[]{:S(2)}, u32[]{:S(2)}) collective-permute-start(f32[2,128]{1,0:T(2,128)S(1)} %fusion.8), channel_id=1, source_target_pairs={{0,4},{4,0},{8,12},{12,8},{16,20},{20,16},{24,28},{28,24},{1,5},{5... | collective-permute-start | bytes 3080 | tf_op jit(solution)/shard_map/ppermute | solution.py:44
  137.7 3.6 %collective-permute-start.8 = (f32[2,128]{1,0:T(2,128)S(1)}, f32[2,128]{1,0:T(2,128)S(1)}, u32[]{:S(2)}, u32[]{:S(2)}) collective-permute-start(f32[2,128]{1,0:T(2,128)S(1)} %add.95), channel_id=1, source_target_pairs={{0,8},{4,12},{8,0},{12,4},{16,24},{20,28},{24,16},{28,20},{1,9},{5... | collective-permute-start | bytes 3080 | tf_op jit(solution)/shard_map/ppermute | solution.py:44
  141.3 4.5 %collective-permute-start.9 = (f32[2,128]{1,0:T(2,128)S(1)}, f32[2,128]{1,0:T(2,128)S(1)}, u32[]{:S(2)}, u32[]{:S(2)}) collective-permute-start(f32[2,128]{1,0:T(2,128)S(1)} %add.96), channel_id=1, source_target_pairs={{0,16},{4,20},{8,24},{12,28},{16,0},{20,4},{24,8},{28,12},{1,17},{... | collective-permute-start | bytes 3080 | tf_op jit(solution)/shard_map/ppermute | solution.py:44
  146.3 1.3 copy-start.3

commit v9 on v8

--- a/solution.py
+++ b/solution.py
@@ -80,6 +80,20 @@
     return jnp.concatenate([live] * group, axis=0), k_first
 
 
+def normed_rows(raw, gain):
+    inverse = lax.rsqrt(jnp.mean(raw * raw, axis=1, keepdims=True) + EPS)
+    return (raw * inverse * gain).astype(jnp.bfloat16)
+
+
+def normed_stack(ref, gain, group, head_dim, first):
+    blk = BLOCK
+    return jnp.concatenate(
+        [normed_rows(ref[first:first + blk, a * head_dim:(a + 1) * head_dim].astype(jnp.float32), gain)
+         for a in range(group)],
+        axis=0,
+    )
+
+
 def stacked(ref, group, head_dim, first):
     blk = BLOCK
     return jnp.concatenate(
@@ -101,9 +115,9 @@
     return dq_part, dk_part * scale, dv_part
 
 
-def halo_kernel(qdoc_ref, kdoc_ref, q_ref, do_ref, hk_ref, hv_ref, k_ref, v_ref, kgain_ref, *refs,
+def halo_kernel(qdoc_ref, kdoc_ref, q_ref, do_ref, hk_ref, hv_ref, kraw_ref, v_ref, kgain_ref, qgain_ref, *refs,
                 group, head_dim, n_alias):
-    dq_ref, dkv_ref, lse_ref, delta_ref, kpart_ref, dk_ref, dv_ref, kn_ref = refs[n_alias:]
+    dq_ref, dkv_ref, lse_ref, delta_ref, kpart_ref, dk_ref, dv_ref, kn_ref, k_ref = refs[n_alias:]
     blk = BLOCK
     n_tiles = WINDOW // blk + 1
     n_halo = WINDOW // blk
@@ -115,6 +129,8 @@
     halo_raw = hk_ref[...].astype(jnp.float32)
     halo_inv = lax.rsqrt(jnp.mean(halo_raw * halo_raw, axis=1, keepdims=True) + EPS)
     kn_ref[...] = (halo_raw * halo_inv * kgain_ref[...]).astype(jnp.bfloat16)
+    k_ref[...] = normed_rows(kraw_ref[...].astype(jnp.float32), kgain_ref[...])
+    qgain = qgain_ref[...]
 
     def key_tile(k_first):
         if k_first < WINDOW:
@@ -124,7 +140,7 @@
 
     for qb in range(n_q):
         q_first = qb * blk
-        q_g = stacked(q_ref, group, head_dim, q_first)
+        q_g = normed_stack(q_ref, qgain, group, head_dim, q_first)
         do_g = stacked(do_ref, group, head_dim, q_first)
         masks = [tile_mask(qdoc_ref, kdoc_ref, q_first, t, group)[0] for t in range(n_tiles)]
         totals = jnp.zeros((gb, 1), jnp.float32)
@@ -169,8 +185,9 @@
     return result, jnp.sum(upstream * scaled, axis=0, keepdims=True)
 
 
-def own_kernel(qdoc_ref, kdoc_ref, q_ref, do_ref, k_ref, v_ref, lse_ref, delta_ref, dq_in_ref, raw_ref, gain_ref,
-               kraw_ref, qgrad_ref, qgain_ref, kpart_ref, dk_ref, dv_ref, *, group, head_dim):
+def own_kernel(qdoc_ref, kdoc_ref, do_ref, v_ref, lse_ref, delta_ref, dq_in_ref, raw_ref, gain_ref,
+               kraw_ref, kgain_ref, qgrad_ref, qgain_ref, kpart_ref, dk_ref, dv_ref, k_ref, *, group, head_dim):
+    q_ref = raw_ref
     blk = BLOCK
     n_tiles = WINDOW // blk + 1
     n_halo = WINDOW // blk
@@ -180,10 +197,11 @@
     dk_ref[...] = jnp.zeros(dk_ref.shape, jnp.float32)
     dv_ref[...] = jnp.zeros(dv_ref.shape, jnp.float32)
     gain = gain_ref[...]
+    k_ref[...] = normed_rows(kraw_ref[...].astype(jnp.float32), kgain_ref[...])
     gain_sum = jnp.zeros((1, head_dim), jnp.float32)
     for qb in range(n_q):
         q_first = qb * blk
-        q_g = stacked(q_ref, group, head_dim, q_first)
+        q_g = normed_stack(q_ref, gain, group, head_dim, q_first)
         do_g = stacked(do_ref, group, head_dim, q_first)
         log_sums = lse_ref[qb * gb:(qb + 1) * gb, :]
         delta = delta_ref[qb * gb:(qb + 1) * gb, :]
@@ -254,9 +272,9 @@
     )(dk_own, dv_own, back, key_raw, key_gain.reshape(1, head_dim))
 
 
-def attention_grads(query_norm, grad_rows, halo_pieces, key_norm, value_proj, own_doc, all_doc, key_heads,
+def attention_grads(grad_rows, halo_pieces, value_proj, own_doc, all_doc, key_heads,
                     head_dim, query_raw, query_gain, key_raw, key_gain):
-    tok_rows, q_cols = query_norm.shape
+    tok_rows, q_cols = query_raw.shape
     key_rows = WINDOW + tok_rows
     group = q_cols // (key_heads * head_dim)
     blk = BLOCK
@@ -284,7 +302,7 @@
         outs = pl.pallas_call(
             functools.partial(halo_kernel, group=group, head_dim=head_dim, n_alias=len(buffers)),
             grid=(n_piece,),
-            in_specs=doc_specs + [qcol, qcol, hcol, hcol, kcol, kcol, gain_spec]
+            in_specs=doc_specs + [qcol, qcol, hcol, hcol, kcol, kcol, gain_spec, gain_spec]
             + [pl.BlockSpec(memory_space=pl.ANY)] * len(buffers),
             out_specs=[
                 qcol,
@@ -304,8 +322,9 @@
                 pltpu.VMEM((WINDOW, head_dim), jnp.float32),
                 pltpu.VMEM((WINDOW, head_dim), jnp.float32),
                 pltpu.VMEM((WINDOW, head_dim), jnp.bfloat16),
+                pltpu.VMEM((tok_rows, head_dim), jnp.bfloat16),
             ],
-            input_output_aliases={9 + i: i for i in range(len(buffers))},
+            input_output_aliases={10 + i: i for i in range(len(buffers))},
             compiler_params=params,
             cost_estimate=pl.CostEstimate(
                 flops=n_piece * (2 * n_q * n_tiles + 5 * halo_tiles) * tile_flops,
@@ -313,7 +332,8 @@
                 bytes_accessed=n_piece * (2 * 2 * tok_rows * gw + 2 * 2 * key_rows * head_dim
                                           + 4 * tok_rows * gw + 2 * 2 * WINDOW * head_dim),
             ),
-        )(qdoc, kdoc, query_norm, grad_rows, hk, hv, key_norm, value_proj, key_gain.reshape(1, head_dim), *buffers)
+        )(qdoc, kdoc, query_raw, grad_rows, hk, hv, key_raw, value_proj, key_gain.reshape(1, head_dim),
+          query_gain.reshape(1, head_dim), *buffers)
         buffers = tuple(outs[:4])
         kparts.append(outs[4])
     dq_half, dkv_halo, log_sums, delta = buffers
@@ -325,8 +345,9 @@
     query_grad, qgain_parts, kown_parts, dk_own, dv_own = pl.pallas_call(
         functools.partial(own_kernel, group=group, head_dim=head_dim),
         grid=(key_heads,),
-        in_specs=doc_specs + [qcol, qcol, kcol, kcol, stat, stat, qcol, qcol, gain_spec, kcol],
+        in_specs=doc_specs + [qcol, kcol, stat, stat, qcol, qcol, gain_spec, kcol, gain_spec],
         out_specs=[qcol, part_spec, part_spec, kcol, kcol],
+        scratch_shapes=[pltpu.VMEM((tok_rows, head_dim), jnp.bfloat16)],
         out_shape=[
             jax.ShapeDtypeStruct((tok_rows, q_cols), jnp.bfloat16),
             part_shape,
@@ -341,8 +362,8 @@
             bytes_accessed=2 * 2 * tok_rows * q_cols + 2 * 2 * tok_rows * kv_cols + 2 * 4 * tok_rows * q_cols
             + 2 * 4 * tok_rows * kv_cols,
         ),
-    )(qdoc, kdoc, query_norm, grad_rows, key_norm, value_proj, log_sums, delta, dq_half, query_raw,
-      query_gain.reshape(1, head_dim), key_raw)
+    )(qdoc, kdoc, grad_rows, value_proj, log_sums, delta, dq_half, query_raw,
+      query_gain.reshape(1, head_dim), key_raw, key_gain.reshape(1, head_dim))
     key_part = jnp.sum(kown_parts, axis=(0, 1))
     for part in kparts:
         key_part = key_part + jnp.sum(part, axis=(0, 1))
@@ -360,10 +381,6 @@
     own_doc = doc_index(own_pos, doc_ends)
     halo_raw = first_pos - WINDOW + jnp.arange(WINDOW, dtype=jnp.int32)
     halo_doc = jnp.where(halo_raw >= 0, doc_index(halo_raw, doc_ends), -1)
-    query_hat, query_inv = norm_rows(query_raw, query_heads)
-    query_norm = (query_hat * query_gain).astype(jnp.bfloat16).reshape(tok_rows, query_heads * head_dim)
-    key_hat, key_inv = norm_rows(key_raw, key_heads)
-    key_norm = (key_hat * key_gain).astype(jnp.bfloat16).reshape(tok_rows, key_heads * head_dim)
     n_pieces = 2 if key_heads % 2 == 0 else 1
     width = key_heads * head_dim // n_pieces
     halo_pieces = []
@@ -375,7 +392,7 @@
         halo_pieces.append(shifted(send, "ctx", 1))
     all_doc = jnp.concatenate([halo_doc, own_doc])
     query_grad, query_part, key_part, dkv_halo, dk_own, dv_own = attention_grads(
-        query_norm, out_grad, halo_pieces, key_norm, value_proj, own_doc, all_doc, key_heads, head_dim,
+        out_grad, halo_pieces, value_proj, own_doc, all_doc, key_heads, head_dim,
         query_raw, query_gain, key_raw, key_gain,
     )
     gain_grads = butterfly_sum(jnp.stack([query_part, key_part]), ("head", "ctx"))

time: 154 us -> 146 us (0.948)
  other arithmetic: 17.1 us -> 2.33 us
  waiting for transfers between devices: 20.1 us -> 34.7 us
  local copies, waits for them, and re-layouts: 17.6 us -> 6.13 us
  starting transfers between devices: 24.3 us -> 27.8 us
    ppermute x5, waiting for transfers between devices: 0.01 us -> 16.1 us  [shifted(): lax.ppermute(value, axis, [(source, source + steps) for source in range(l...]
    reduce_sum x2 -> x0, other arithmetic: 7.88 us -> none  [norm_rows(): inverse = lax.rsqrt(jnp.mean(values * values, axis=-1, keepdims=True) + EPS)]
    mul x5 -> x0, local copies, waits for them, and re-layouts: 5.02 us -> none  [the longest x2 3.32 us: norm_rows(): return (values * inverse, inverse)]
    convert_element_type x2 -> x0, other arithmetic: 4.06 us -> none  [the longest x1 2.67 us: per_device(): (query_hat * query_gain).astype(jnp.bfloat16)]
    ppermute x5, starting transfers between devices: 16.8 us -> 19.3 us  [shifted(): lax.ppermute(value, axis, [(source, source + steps) for source in range(l...]
    unnamed x23 -> x16, local copies, waits for them, and re-layouts: 5.26 us -> 3.08 us
    rsqrt x2 -> x0, other arithmetic: 1.93 us -> none  [norm_rows(): inverse = lax.rsqrt(jnp.mean(values * values, axis=-1, keepdims=True) + EPS)]
  transfers between devices with their start and end apart: 10 -> 10, of which waited for: 5 -> 6; matrix products, arithmetic and copies ran while one was open for 20% -> 3% of each run, Pallas kernels for 31% -> 32%
where the time goes in v9:
time: 146 us
  Pallas kernels  74.2 us (51%)
  waiting for transfers between devices  34.7 us (24%)
  starting transfers between devices  27.8 us (19%)
  local copies, waits for them, and re-layouts  6.13 us (4%)
  other arithmetic  2.33 us (2%)
    pallas_call x2, Pallas kernels, attention_grads(): pl.pallas_call(functools.partial(halo_kernel, group=group, head_dim=head_...  42.4 us
    pallas_call x1, Pallas kernels, attention_grads(): pl.pallas_call(functools.partial(own_kernel, group=group, head_dim=head_d...  26.3 us
    ppermute x5, starting transfers between devices, shifted(): lax.ppermute(value, axis, [(source, source + steps) for source in range(l...  19.3 us
    ppermute x5, waiting for transfers between devices, butterfly_sum(): shifted_parts.append(lax.ppermute(value, axis, pairs))  18.6 us
    ppermute x5, waiting for transfers between devices, shifted(): lax.ppermute(value, axis, [(source, source + steps) for source in range(l...  16.1 us
    ppermute x5, starting transfers between devices, butterfly_sum(): shifted_parts.append(lax.ppermute(value, axis, pairs))  8.47 us
    pallas_call x1, Pallas kernels, kv_final(): pl.pallas_call(functools.partial(kv_final_kernel, head_dim=head_dim), gri...  5.53 us
    unnamed x16, local copies, waits for them, and re-layouts  3.08 us
  transfers between devices with their start and end apart: 10, of which 6 were waited for; matrix products, arithmetic and copies ran while one was open for 3% of the time, Pallas kernels for 32%

profile of v9, /device:TPU:0, one launch (start us, length us, event | category | flops | bytes accessed | tf_op | source)
XLA Modules:
  0.0 145.9 jit_solution(7695971409873057972)
XLA Ops:
  0.7 1.4 fusion.1
  2.0 4.9 %collective-permute-start.3 = (bf16[1024,256]{1,0:T(8,128)(2,1)S(1)}, bf16[1024,256]{1,0:T(8,128)(2,1)S(1)}, u32[]{:S(2)}, u32[]{:S(2)}) collective-permute-start(bf16[1024,256]{1,0:T(8,128)(2,1)S(1)} %get-tuple-element.45), channel_id=1, source_target_pairs={{0,4},{4,8},{8,12},{12,16},{16,20},{20,24},{24,28},{1,5},{5,9},{9,... | collective-permute-start | bytes 1572872 | tf_op jit(solution)/shard_map/ppermute | solution.py:22
  7.0 4.2 %collective-permute-start = (bf16[1024,256]{1,0:T(8,128)(2,1)S(1)}, bf16[1024,256]{1,0:T(8,128)(2,1)}, u32[]{:S(2)}, u32[]{:S(2)}) collective-permute-start(bf16[1024,256]{1,0:T(8,128)(2,1)S(1)} %get-tuple-element.47), channel_id=1, source_target_pairs={{0,4},{4,8},{8,12},{12,16},{16,20},{20,24},{24,28},{1,5},{5,9},{9,... | collective-permute-start | bytes 1572872 | tf_op jit(solution)/shard_map/ppermute | solution.py:22
  11.6 1.0 copy.24.qdoc_ref
  13.2 16.1 %collective-permute-done.hk_ref = bf16[1024,256]{1,0:T(8,128)(2,1)} collective-permute-done((bf16[1024,256]{1,0:T(8,128)(2,1)S(1)}, bf16[1024,256]{1,0:T(8,128)(2,1)}, u32[]{:S(2)}, u32[]{:S(2)}) %collective-permute-start) | collective-permute-done | bytes 524320 | tf_op jit(solution)/shard_map/ppermute | solution.py:22
  29.3 4.5 %collective-permute-start.1 = (bf16[1024,256]{1,0:T(8,128)(2,1)S(1)}, bf16[1024,256]{1,0:T(8,128)(2,1)S(1)}, u32[]{:S(2)}, u32[]{:S(2)}) collective-permute-start(bf16[1024,256]{1,0:T(8,128)(2,1)S(1)} %get-tuple-element.24), channel_id=1, source_target_pairs={{0,4},{4,8},{8,12},{12,16},{16,20},{20,24},{24,28},{1,5},{5,9},{9,... | collective-permute-start | bytes 1572872 | tf_op jit(solution)/shard_map/ppermute | solution.py:22
  33.8 4.4 %collective-permute-start.2 = (bf16[1024,256]{1,0:T(8,128)(2,1)S(1)}, bf16[1024,256]{1,0:T(8,128)(2,1)S(1)}, u32[]{:S(2)}, u32[]{:S(2)}) collective-permute-start(bf16[1024,256]{1,0:T(8,128)(2,1)S(1)} %get-tuple-element.25), channel_id=1, source_target_pairs={{0,4},{4,8},{8,12},{12,16},{16,20},{20,24},{24,28},{1,5},{5,9},{9,... | collective-permute-start | bytes 1572872 | tf_op jit(solution)/shard_map/ppermute | solution.py:22
  38.2 0.8 copy-done.7
  39.0 21.1 %shard_map.110 = (f32[1024,1024]{1,0:T(8,128)}, bf16[1024,1024]{1,0:T(8,128)(2,1)}, f32[8192,1]{1,0:T(8,128)}, f32[8192,1]{1,0:T(8,128)}, f32[2,1,128]{2,1,0:T(1,128)}) custom-call(s32[1024,1]{1,0:T(8,128)} %copy.24.qdoc_ref, s32[1,2048]{1,0:T(1,128)} %bitcast.13, bf16[1024,1024]{1,0:T(8,128)(2,1)} %raw_ref.2, bf16[1024,1024]{1,0:T(8,128)(2,1)} %do_ref.5, ...), custom_call_target="tpu_custom_call" | custom-call | flops 6039797760 | bytes 7340032 | tf_op jit(solution)/shard_map/pallas_call | solution.py:302
  60.1 0.8 copy-done.2
  61.0 21.3 %shard_map.111 = (f32[1024,1024]{1,0:T(8,128)}, bf16[1024,1024]{1,0:T(8,128)(2,1)}, f32[8192,1]{1,0:T(8,128)}, f32[8192,1]{1,0:T(8,128)}, f32[2,1,128]{2,1,0:T(1,128)}) custom-call(s32[1024,1]{1,0:T(8,128)} %copy.24.qdoc_ref, s32[1,2048]{1,0:T(1,128)} %bitcast.14, ...), custom_call_target="tpu_custom_call", output_to_operand_aliasing={{0}: (10, {}), {1}: (11, {}), {2}: (12, {}), {3}: (13, {})} | custom-call | flops 6039797760 | bytes 7340032 | tf_op jit(solution)/shard_map/pallas_call | solution.py:302
  82.3 1.3 collective-permute-start.4
  83.7 26.3 %shard_map.112 = (bf16[1024,1024]{1,0:T(8,128)(2,1)}, f32[4,1,128]{2,1,0:T(1,128)}, f32[4,1,128]{2,1,0:T(1,128)}, f32[1024,512]{1,0:T(8,128)}, f32[1024,512]{1,0:T(8,128)}) custom-call(s32[1024,1]{1,0:T(8,128)} %copy.24.qdoc_ref, s32[1,2048]{1,0:T(1,128)} %bitcast.15, bf16[1024,1024]{1,0:T(8,128)(2,1)} %do_ref.5, bf16[1024,512]{1,0:T(8,128)(2,1)} %v_ref.5, ...), custom_call_target="tpu_custom_call" | custom-call | flops 6710886400 | bytes 18874368 | tf_op jit(solution)/shard_map/pallas_call | solution.py:345
  111.5 1.1 collective-permute-done.5
  112.7 1.6 %collective-permute-start.6 = (f32[2,128]{1,0:T(2,128)S(1)}, f32[2,128]{1,0:T(2,128)S(1)}, u32[]{:S(2)}, u32[]{:S(2)}) collective-permute-start(f32[2,128]{1,0:T(2,128)S(1)} %fusion), channel_id=1, source_target_pairs={{0,2},{1,3},{2,0},{3,1},{4,6},{5,7},{6,4},{7,5},{8,10},{9,11},{10,... | collective-permute-start | bytes 3080 | tf_op jit(solution)/shard_map/ppermute | solution.py:44
  114.3 2.1 %collective-permute-done.6 = f32[2,128]{1,0:T(2,128)S(1)} collective-permute-done((f32[2,128]{1,0:T(2,128)S(1)}, f32[2,128]{1,0:T(2,128)S(1)}, u32[]{:S(2)}, u32[]{:S(2)}) %collective-permute-start.6) | collective-permute-done | bytes 1056 | tf_op jit(solution)/shard_map/ppermute | solution.py:44
  116.3 2.7 %collective-permute-start.7 = (f32[2,128]{1,0:T(2,128)S(1)}, f32[2,128]{1,0:T(2,128)S(1)}, u32[]{:S(2)}, u32[]{:S(2)}) collective-permute-start(f32[2,128]{1,0:T(2,128)S(1)} %fusion.3), channel_id=1, source_target_pairs={{0,4},{4,0},{8,12},{12,8},{16,20},{20,16},{24,28},{28,24},{1,5},{5... | collective-permute-start | bytes 3080 | tf_op jit(solution)/shard_map/ppermute | solution.py:44
  119.0 11.4 %collective-permute-done.7 = f32[2,128]{1,0:T(2,128)S(1)} collective-permute-done((f32[2,128]{1,0:T(2,128)S(1)}, f32[2,128]{1,0:T(2,128)S(1)}, u32[]{:S(2)}, u32[]{:S(2)}) %collective-permute-start.7) | collective-permute-done | bytes 1056 | tf_op jit(solution)/shard_map/ppermute | solution.py:44
  130.5 1.6 %collective-permute-start.8 = (f32[2,128]{1,0:T(2,128)S(1)}, f32[2,128]{1,0:T(2,128)S(1)}, u32[]{:S(2)}, u32[]{:S(2)}) collective-permute-start(f32[2,128]{1,0:T(2,128)S(1)} %add.69), channel_id=1, source_target_pairs={{0,8},{4,12},{8,0},{12,4},{16,24},{20,28},{24,16},{28,20},{1,9},{5... | collective-permute-start | bytes 3080 | tf_op jit(solution)/shard_map/ppermute | solution.py:44
  132.0 2.0 %collective-permute-done.8 = f32[2,128]{1,0:T(2,128)S(1)} collective-permute-done((f32[2,128]{1,0:T(2,128)S(1)}, f32[2,128]{1,0:T(2,128)S(1)}, u32[]{:S(2)}, u32[]{:S(2)}) %collective-permute-start.8) | collective-permute-done | bytes 1056 | tf_op jit(solution)/shard_map/ppermute | solution.py:44
  134.1 2.6 %collective-permute-start.9 = (f32[2,128]{1,0:T(2,128)S(1)}, f32[2,128]{1,0:T(2,128)S(1)}, u32[]{:S(2)}, u32[]{:S(2)}) collective-permute-start(f32[2,128]{1,0:T(2,128)S(1)} %add.70), channel_id=1, source_target_pairs={{0,16},{4,20},{8,24},{12,28},{16,0},{20,4},{24,8},{28,12},{1,17},{... | collective-permute-start | bytes 3080 | tf_op jit(solution)/shard_map/ppermute | solution.py:44
  136.6 1.9 %collective-permute-done.9 = f32[2,128]{1,0:T(2,128)S(1)} collective-permute-done((f32[2,128]{1,0:T(2,128)S(1)}, f32[2,128]{1,0:T(2,128)S(1)}, u32[]{:S(2)}, u32[]{:S(2)}) %collective-permute-start.9) | collective-permute-done | bytes 1056 | tf_op jit(solution)/shard_map/ppermute | solution.py:44
  139.1 1.3 copy-done.1
  140.4 5.5 %shard_map.113 = (bf16[1024,512]{1,0:T(8,128)(2,1)}, bf16[1024,512]{1,0:T(8,128)(2,1)}, f32[4,1,128]{2,1,0:T(1,128)}) custom-call(f32[1024,512]{1,0:T(8,128)} %get-tuple-element.34.dk_ref, f32[1024,512]{1,0:T(8,128)} %get-tuple-element.35.dv_ref, bf16[1024,1024]{1,0:T(8,128)(2,1)} %copy-done.1, bf16[1024,512]{1,0:T(8,128)(2,1)} %raw_ref.3, f32[1,128]{1,0:T(1,128)} %bitcast.22), custom_call_target="tpu_custom_call" | custom-call | tf_op jit(solution)/shard_map/pallas_call | solution.py:255
  (38 shorter events, 3.3 us)
Async XLA Ops:
  0.6 6.3 %copy-start = (bf16[1024,512]{1,0:T(8,128)(2,1)S(1)}, bf16[1024,512]{1,0:T(8,128)(2,1)}, u32[]{:S(2)}) copy-start(bf16[1024,512]{1,0:T(8,128)(2,1)} %raw_ref.3) | copy-start | bytes 3145732
  0.6 10.6 %copy-start.6 = (s32[16]{0:T(128)S(1)}, s32[16]{0:T(128)}, u32[]{:S(2)}) copy-start(s32[16]{0:T(128)} %param.13) | copy-start | bytes 196
  2.0 36.2 %collective-permute-start.3 = (bf16[1024,256]{1,0:T(8,128)(2,1)S(1)}, bf16[1024,256]{1,0:T(8,128)(2,1)S(1)}, u32[]{:S(2)}, u32[]{:S(2)}) collective-permute-start(bf16[1024,256]{1,0:T(8,128)(2,1)S(1)} %get-tuple-element.45), channel_id=1, source_target_pairs={{0,4},{4,8},{8,12},{12,16},{16,20},{20,24},{24,28},{1,5},{5,9},{9,... | collective-permute-start | bytes 1572872 | tf_op jit(solution)/shard_map/ppermute | solution.py:22
  7.0 22.3 %collective-permute-start = (bf16[1024,256]{1,0:T(8,128)(2,1)S(1)}, bf16[1024,256]{1,0:T(8,128)(2,1)}, u32[]{:S(2)}, u32[]{:S(2)}) collective-permute-start(bf16[1024,256]{1,0:T(8,128)(2,1)S(1)} %get-tuple-element.47), channel_id=1, source_target_pairs={{0,4},{4,8},{8,12},{12,16},{16,20},{20,24},{24,28},{1,5},{5,9},{9,... | collective-permute-start | bytes 1572872 | tf_op jit(solution)/shard_map/ppermute | solution.py:22
  29.3 30.8 %collective-permute-start.1 = (bf16[1024,256]{1,0:T(8,128)(2,1)S(1)}, bf16[1024,256]{1,0:T(8,128)(2,1)S(1)}, u32[]{:S(2)}, u32[]{:S(2)}) collective-permute-start(bf16[1024,256]{1,0:T(8,128)(2,1)S(1)} %get-tuple-element.24), channel_id=1, source_target_pairs={{0,4},{4,8},{8,12},{12,16},{16,20},{20,24},{24,28},{1,5},{5,9},{9,... | collective-permute-start | bytes 1572872 | tf_op jit(solution)/shard_map/ppermute | solution.py:22
  33.8 26.3 %collective-permute-start.2 = (bf16[1024,256]{1,0:T(8,128)(2,1)S(1)}, bf16[1024,256]{1,0:T(8,128)(2,1)S(1)}, u32[]{:S(2)}, u32[]{:S(2)}) collective-permute-start(bf16[1024,256]{1,0:T(8,128)(2,1)S(1)} %get-tuple-element.25), channel_id=1, source_target_pairs={{0,4},{4,8},{8,12},{12,16},{16,20},{20,24},{24,28},{1,5},{5,9},{9,... | collective-permute-start | bytes 1572872 | tf_op jit(solution)/shard_map/ppermute | solution.py:22
  38.2 0.8 copy-start.7
  60.1 0.8 copy-start.2
  60.1 0.9 copy-start.3
  61.0 22.6 %copy-start.5 = (f32[2,1,128]{2,1,0:T(1,128)S(1)}, f32[2,1,128]{2,1,0:T(1,128)}, u32[]{:S(2)}) copy-start(f32[2,1,128]{2,1,0:T(1,128)} %get-tuple-element.41) | copy-start | bytes 3076
  82.3 56.7 %collective-permute-start.4 = (bf16[1024,1024]{1,0:T(8,128)(2,1)}, bf16[1024,1024]{1,0:T(8,128)(2,1)S(1)}, u32[]{:S(2)}, u32[]{:S(2)}) collective-permute-start(bf16[1024,1024]{1,0:T(8,128)(2,1)} %get-tuple-element.36), channel_id=1, source_target_pairs={{4,0},{8,4},{12,8},{16,12},{20,16},{24,20},{28,24},{5,1},{9,5},{13... | collective-permute-start | bytes 6291464 | tf_op jit(solution)/shard_map/ppermute | solution.py:22
  83.7 27.7 %copy-start.4 = (f32[2,1,128]{2,1,0:T(1,128)S(1)}, f32[2,1,128]{2,1,0:T(1,128)}, u32[]{:S(2)}) copy-start(f32[2,1,128]{2,1,0:T(1,128)} %get-tuple-element.42) | copy-start | bytes 3076
  111.4 1.2 collective-permute-start.5
  112.7 3.6 %collective-permute-start.6 = (f32[2,128]{1,0:T(2,128)S(1)}, f32[2,128]{1,0:T(2,128)S(1)}, u32[]{:S(2)}, u32[]{:S(2)}) collective-permute-start(f32[2,128]{1,0:T(2,128)S(1)} %fusion), channel_id=1, source_target_pairs={{0,2},{1,3},{2,0},{3,1},{4,6},{5,7},{6,4},{7,5},{8,10},{9,11},{10,... | collective-permute-start | bytes 3080 | tf_op jit(solution)/shard_map/ppermute | solution.py:44
  116.3 14.1 %collective-permute-start.7 = (f32[2,128]{1,0:T(2,128)S(1)}, f32[2,128]{1,0:T(2,128)S(1)}, u32[]{:S(2)}, u32[]{:S(2)}) collective-permute-start(f32[2,128]{1,0:T(2,128)S(1)} %fusion.3), channel_id=1, source_target_pairs={{0,4},{4,0},{8,12},{12,8},{16,20},{20,16},{24,28},{28,24},{1,5},{5... | collective-permute-start | bytes 3080 | tf_op jit(solution)/shard_map/ppermute | solution.py:44
  130.5 3.6 %collective-permute-start.8 = (f32[2,128]{1,0:T(2,128)S(1)}, f32[2,128]{1,0:T(2,128)S(1)}, u32[]{:S(2)}, u32[]{:S(2)}) collective-permute-start(f32[2,128]{1,0:T(2,128)S(1)} %add.69), channel_id=1, source_target_pairs={{0,8},{4,12},{8,0},{12,4},{16,24},{20,28},{24,16},{28,20},{1,9},{5... | collective-permute-start | bytes 3080 | tf_op jit(solution)/shard_map/ppermute | solution.py:44
  134.1 4.5 %collective-permute-start.9 = (f32[2,128]{1,0:T(2,128)S(1)}, f32[2,128]{1,0:T(2,128)S(1)}, u32[]{:S(2)}, u32[]{:S(2)}) collective-permute-start(f32[2,128]{1,0:T(2,128)S(1)} %add.70), channel_id=1, source_target_pairs={{0,16},{4,20},{8,24},{12,28},{16,0},{20,4},{24,8},{28,12},{1,17},{... | collective-permute-start | bytes 3080 | tf_op jit(solution)/shard_map/ppermute | solution.py:44
  139.1 1.3 copy-start.1

commit v10 on v9

--- a/solution.py
+++ b/solution.py
@@ -293,16 +293,17 @@
     qdoc, kdoc = own_doc.reshape(tok_rows, 1), all_doc.reshape(1, key_rows)
     buffers = ()
     kparts = []
-    for piece, (hk, hv) in enumerate(halo_pieces):
+    for piece, halo in enumerate(halo_pieces):
         h0 = piece * n_piece
         qcol = pl.BlockSpec((tok_rows, gw), lambda h, h0=h0: (0, h + h0))
         kcol = pl.BlockSpec((tok_rows, head_dim), lambda h, h0=h0: (0, h + h0))
         hcol = pl.BlockSpec((WINDOW, head_dim), lambda h: (0, h))
+        vcol = pl.BlockSpec((WINDOW, head_dim), lambda h, n_piece=n_piece: (0, h + n_piece))
         stat = pl.BlockSpec((n_q * group * blk, 1), lambda h, h0=h0: (h + h0, 0))
         outs = pl.pallas_call(
             functools.partial(halo_kernel, group=group, head_dim=head_dim, n_alias=len(buffers)),
             grid=(n_piece,),
-            in_specs=doc_specs + [qcol, qcol, hcol, hcol, kcol, kcol, gain_spec, gain_spec]
+            in_specs=doc_specs + [qcol, qcol, hcol, vcol, kcol, kcol, gain_spec, gain_spec]
             + [pl.BlockSpec(memory_space=pl.ANY)] * len(buffers),
             out_specs=[
                 qcol,
@@ -332,7 +333,7 @@
                 bytes_accessed=n_piece * (2 * 2 * tok_rows * gw + 2 * 2 * key_rows * head_dim
                                           + 4 * tok_rows * gw + 2 * 2 * WINDOW * head_dim),
             ),
-        )(qdoc, kdoc, query_raw, grad_rows, hk, hv, key_raw, value_proj, key_gain.reshape(1, head_dim),
+        )(qdoc, kdoc, query_raw, grad_rows, halo, halo, key_raw, value_proj, key_gain.reshape(1, head_dim),
           query_gain.reshape(1, head_dim), *buffers)
         buffers = tuple(outs[:4])
         kparts.append(outs[4])
@@ -386,9 +387,9 @@
     halo_pieces = []
     for piece in range(n_pieces):
         cols = slice(piece * width, (piece + 1) * width)
-        send = (key_raw[tok_rows - WINDOW:, cols], value_proj[tok_rows - WINDOW:, cols])
+        send = jnp.concatenate([key_raw[tok_rows - WINDOW:, cols], value_proj[tok_rows - WINDOW:, cols]], axis=1)
         if halo_pieces:
-            send = lax.optimization_barrier((send, halo_pieces[-1][0]))[0]
+            send = lax.optimization_barrier((send, halo_pieces[-1]))[0]
         halo_pieces.append(shifted(send, "ctx", 1))
     all_doc = jnp.concatenate([halo_doc, own_doc])
     query_grad, query_part, key_part, dkv_halo, dk_own, dv_own = attention_grads(

time: 146 us -> 145 us (level)
  starting transfers between devices: 27.8 us -> 20.6 us
  waiting for transfers between devices: 34.7 us -> 40.3 us
    ppermute x5 -> x3, starting transfers between devices: 19.3 us -> 11.8 us  [shifted(): lax.ppermute(value, axis, [(source, source + steps) for source in range(l...]
    ppermute x5 -> x3, waiting for transfers between devices: 16.1 us -> 21.3 us  [shifted(): lax.ppermute(value, axis, [(source, source + steps) for source in range(l...]
    slice x1, local copies, waits for them, and re-layouts: 0.07 us -> 1.66 us  [per_device(): key_raw[tok_rows - WINDOW:, cols]]
    unnamed x16 -> x10, local copies, waits for them, and re-layouts: 3.08 us -> 2.33 us
  transfers between devices with their start and end apart: 10 -> 8, of which waited for: 6 -> 6; matrix products, arithmetic and copies ran while one was open for 3% -> 3% of each run, Pallas kernels for 32% -> 33%
where the time goes in v10:
time: 145 us; the launch traced here: 144 us
  Pallas kernels  74.4 us (51%)
  waiting for transfers between devices  40.3 us (28%)
  starting transfers between devices  20.6 us (14%)
  local copies, waits for them, and re-layouts  5.62 us (4%)
  other arithmetic  2.5 us (2%)
    pallas_call x2, Pallas kernels, attention_grads(): pl.pallas_call(functools.partial(halo_kernel, group=group, head_dim=head_...  42.6 us
    pallas_call x1, Pallas kernels, attention_grads(): pl.pallas_call(functools.partial(own_kernel, group=group, head_dim=head_d...  26.3 us
    ppermute x3, waiting for transfers between devices, shifted(): lax.ppermute(value, axis, [(source, source + steps) for source in range(l...  21.3 us
    ppermute x5, waiting for transfers between devices, butterfly_sum(): shifted_parts.append(lax.ppermute(value, axis, pairs))  19.1 us
    ppermute x3, starting transfers between devices, shifted(): lax.ppermute(value, axis, [(source, source + steps) for source in range(l...  11.8 us
    ppermute x5, starting transfers between devices, butterfly_sum(): shifted_parts.append(lax.ppermute(value, axis, pairs))  8.88 us
    pallas_call x1, Pallas kernels, kv_final(): pl.pallas_call(functools.partial(kv_final_kernel, head_dim=head_dim), gri...  5.53 us
  transfers between devices with their start and end apart: 8, of which 6 were waited for; matrix products, arithmetic and copies ran while one was open for 3% of the time, Pallas kernels for 33%

profile of v10, /device:TPU:0, one launch (start us, length us, event | category | flops | bytes accessed | tf_op | source)
XLA Modules:
  0.0 144.3 jit_solution(2536703398443529725)
XLA Ops:
  0.6 1.7 %fusion.1 = (bf16[1024,256]{1,0:T(8,128)(2,1)S(1)}, bf16[1024,256]{1,0:T(8,128)(2,1)S(1)}, bf16[1024,256]{1,0:T(8,128)(2,1)S(1)}, bf16[1024,256]{1,0:T(8,128)(2,1)S(1)}) fusion(bf16[1024,512]{1,0:T(8,128)(2,1)} %raw_ref.3, bf16[1024,512]{1,0:T(8,128)(2,1)} %v_ref.5), kind=kLoop, calls=%fused_computation.13 | loop fusion | bytes 4194304 | tf_op jit(solution)/shard_map/slice | solution.py:390
  2.4 5.9 %collective-permute-start = (bf16[1024,512]{1,0:T(8,128)(2,1)S(1)}, bf16[1024,512]{1,0:T(8,128)(2,1)}, u32[]{:S(2)}, u32[]{:S(2)}) collective-permute-start(bf16[1024,512]{1,0:T(8,128)(2,1)S(1)} %pad_maximum_fusion.1), channel_id=1, source_target_pairs={{0,4},{4,8},{8,12},{12,16},{16,20},{20,24},{24,28},{1,5},{5,9},{9,... | collective-permute-start | bytes 3145736 | tf_op jit(solution)/shard_map/ppermute | solution.py:22
  8.4 21.3 %collective-permute-done.hk_ref.hv_ref = bf16[1024,512]{1,0:T(8,128)(2,1)} collective-permute-done((bf16[1024,512]{1,0:T(8,128)(2,1)S(1)}, bf16[1024,512]{1,0:T(8,128)(2,1)}, u32[]{:S(2)}, u32[]{:S(2)}) %collective-permute-start) | collective-permute-done | bytes 1048608 | tf_op jit(solution)/shard_map/ppermute | solution.py:22
  29.7 4.5 %collective-permute-start.1 = (bf16[1024,512]{1,0:T(8,128)(2,1)S(1)}, bf16[1024,512]{1,0:T(8,128)(2,1)S(1)}, u32[]{:S(2)}, u32[]{:S(2)}) collective-permute-start(bf16[1024,512]{1,0:T(8,128)(2,1)S(1)} %pad_maximum_fusion), channel_id=1, source_target_pairs={{0,4},{4,8},{8,12},{12,16},{16,20},{20,24},{24,28},{1,5},{5,9},{9,... | collective-permute-start | bytes 3145736 | tf_op jit(solution)/shard_map/ppermute | solution.py:22
  34.6 1.0 copy.24.qdoc_ref
  35.6 0.6 pad_add_fusion
  36.2 21.1 %shard_map.110 = (f32[1024,1024]{1,0:T(8,128)}, bf16[1024,1024]{1,0:T(8,128)(2,1)}, f32[8192,1]{1,0:T(8,128)}, f32[8192,1]{1,0:T(8,128)}, f32[2,1,128]{2,1,0:T(1,128)}) custom-call(s32[1024,1]{1,0:T(8,128)} %copy.24.qdoc_ref, s32[1,2048]{1,0:T(1,128)} %bitcast.13, bf16[1024,1024]{1,0:T(8,128)(2,1)} %raw_ref.2, bf16[1024,1024]{1,0:T(8,128)(2,1)} %do_ref.5, ...), custom_call_target="tpu_custom_call" | custom-call | flops 6039797760 | bytes 7340032 | tf_op jit(solution)/shard_map/pallas_call | solution.py:303
  57.4 1.0 copy-done
  58.3 21.4 %shard_map.111 = (f32[1024,1024]{1,0:T(8,128)}, bf16[1024,1024]{1,0:T(8,128)(2,1)}, f32[8192,1]{1,0:T(8,128)}, f32[8192,1]{1,0:T(8,128)}, f32[2,1,128]{2,1,0:T(1,128)}) custom-call(s32[1024,1]{1,0:T(8,128)} %copy.24.qdoc_ref, s32[1,2048]{1,0:T(1,128)} %bitcast.14, ...), custom_call_target="tpu_custom_call", output_to_operand_aliasing={{0}: (10, {}), {1}: (11, {}), {2}: (12, {}), {3}: (13, {})} | custom-call | flops 6039797760 | bytes 7340032 | tf_op jit(solution)/shard_map/pallas_call | solution.py:303
  79.8 1.3 collective-permute-start.2
  81.1 26.3 %shard_map.112 = (bf16[1024,1024]{1,0:T(8,128)(2,1)}, f32[4,1,128]{2,1,0:T(1,128)}, f32[4,1,128]{2,1,0:T(1,128)}, f32[1024,512]{1,0:T(8,128)}, f32[1024,512]{1,0:T(8,128)}) custom-call(s32[1024,1]{1,0:T(8,128)} %copy.24.qdoc_ref, s32[1,2048]{1,0:T(1,128)} %bitcast.15, bf16[1024,1024]{1,0:T(8,128)(2,1)} %do_ref.5, bf16[1024,512]{1,0:T(8,128)(2,1)} %v_ref.5, ...), custom_call_target="tpu_custom_call" | custom-call | flops 6710886400 | bytes 18874368 | tf_op jit(solution)/shard_map/pallas_call | solution.py:346
  107.4 0.7 reduce_sum.56
  108.1 0.7 reduce_sum.57
  109.0 1.1 collective-permute-done.3
  110.1 1.6 %collective-permute-start.4 = (f32[2,128]{1,0:T(2,128)S(1)}, f32[2,128]{1,0:T(2,128)S(1)}, u32[]{:S(2)}, u32[]{:S(2)}) collective-permute-start(f32[2,128]{1,0:T(2,128)S(1)} %fusion), channel_id=1, source_target_pairs={{0,2},{1,3},{2,0},{3,1},{4,6},{5,7},{6,4},{7,5},{8,10},{9,11},{10,... | collective-permute-start | bytes 3080 | tf_op jit(solution)/shard_map/ppermute | solution.py:44
  111.7 2.1 %collective-permute-done.4 = f32[2,128]{1,0:T(2,128)S(1)} collective-permute-done((f32[2,128]{1,0:T(2,128)S(1)}, f32[2,128]{1,0:T(2,128)S(1)}, u32[]{:S(2)}, u32[]{:S(2)}) %collective-permute-start.4) | collective-permute-done | bytes 1056 | tf_op jit(solution)/shard_map/ppermute | solution.py:44
  113.8 3.1 %collective-permute-start.5 = (f32[2,128]{1,0:T(2,128)S(1)}, f32[2,128]{1,0:T(2,128)S(1)}, u32[]{:S(2)}, u32[]{:S(2)}) collective-permute-start(f32[2,128]{1,0:T(2,128)S(1)} %fusion.3), channel_id=1, source_target_pairs={{0,4},{4,0},{8,12},{12,8},{16,20},{20,16},{24,28},{28,24},{1,5},{5... | collective-permute-start | bytes 3080 | tf_op jit(solution)/shard_map/ppermute | solution.py:44
  116.8 12.0 %collective-permute-done.5 = f32[2,128]{1,0:T(2,128)S(1)} collective-permute-done((f32[2,128]{1,0:T(2,128)S(1)}, f32[2,128]{1,0:T(2,128)S(1)}, u32[]{:S(2)}, u32[]{:S(2)}) %collective-permute-start.5) | collective-permute-done | bytes 1056 | tf_op jit(solution)/shard_map/ppermute | solution.py:44
  128.8 1.6 %collective-permute-start.6 = (f32[2,128]{1,0:T(2,128)S(1)}, f32[2,128]{1,0:T(2,128)S(1)}, u32[]{:S(2)}, u32[]{:S(2)}) collective-permute-start(f32[2,128]{1,0:T(2,128)S(1)} %add.69), channel_id=1, source_target_pairs={{0,8},{4,12},{8,0},{12,4},{16,24},{20,28},{24,16},{28,20},{1,9},{5... | collective-permute-start | bytes 3080 | tf_op jit(solution)/shard_map/ppermute | solution.py:44
  130.4 2.0 %collective-permute-done.6 = f32[2,128]{1,0:T(2,128)S(1)} collective-permute-done((f32[2,128]{1,0:T(2,128)S(1)}, f32[2,128]{1,0:T(2,128)S(1)}, u32[]{:S(2)}, u32[]{:S(2)}) %collective-permute-start.6) | collective-permute-done | bytes 1056 | tf_op jit(solution)/shard_map/ppermute | solution.py:44
  132.4 2.6 %collective-permute-start.7 = (f32[2,128]{1,0:T(2,128)S(1)}, f32[2,128]{1,0:T(2,128)S(1)}, u32[]{:S(2)}, u32[]{:S(2)}) collective-permute-start(f32[2,128]{1,0:T(2,128)S(1)} %add.70), channel_id=1, source_target_pairs={{0,16},{4,20},{8,24},{12,28},{16,0},{20,4},{24,8},{28,12},{1,17},{... | collective-permute-start | bytes 3080 | tf_op jit(solution)/shard_map/ppermute | solution.py:44
  135.0 1.9 %collective-permute-done.7 = f32[2,128]{1,0:T(2,128)S(1)} collective-permute-done((f32[2,128]{1,0:T(2,128)S(1)}, f32[2,128]{1,0:T(2,128)S(1)}, u32[]{:S(2)}, u32[]{:S(2)}) %collective-permute-start.7) | collective-permute-done | bytes 1056 | tf_op jit(solution)/shard_map/ppermute | solution.py:44
  137.4 1.4 copy-done.1
  138.8 5.5 %shard_map.113 = (bf16[1024,512]{1,0:T(8,128)(2,1)}, bf16[1024,512]{1,0:T(8,128)(2,1)}, f32[4,1,128]{2,1,0:T(1,128)}) custom-call(f32[1024,512]{1,0:T(8,128)} %get-tuple-element.32.dk_ref, f32[1024,512]{1,0:T(8,128)} %get-tuple-element.33.dv_ref, bf16[1024,1024]{1,0:T(8,128)(2,1)} %copy-done.1, bf16[1024,512]{1,0:T(8,128)(2,1)} %raw_ref.3, f32[1,128]{1,0:T(1,128)} %bitcast.22), custom_call_target="tpu_custom_call" | custom-call | tf_op jit(solution)/shard_map/pallas_call | solution.py:255
  (29 shorter events, 1.2 us)
Async XLA Ops:
  2.3 31.9 %copy-start.4 = (s32[16]{0:T(128)S(1)}, s32[16]{0:T(128)}, u32[]{:S(2)}) copy-start(s32[16]{0:T(128)} %param.13) | copy-start | bytes 196
  2.4 27.3 %collective-permute-start = (bf16[1024,512]{1,0:T(8,128)(2,1)S(1)}, bf16[1024,512]{1,0:T(8,128)(2,1)}, u32[]{:S(2)}, u32[]{:S(2)}) collective-permute-start(bf16[1024,512]{1,0:T(8,128)(2,1)S(1)} %pad_maximum_fusion.1), channel_id=1, source_target_pairs={{0,4},{4,8},{8,12},{12,16},{16,20},{20,24},{24,28},{1,5},{5,9},{9,... | collective-permute-start | bytes 3145736 | tf_op jit(solution)/shard_map/ppermute | solution.py:22
  29.7 27.7 %collective-permute-start.1 = (bf16[1024,512]{1,0:T(8,128)(2,1)S(1)}, bf16[1024,512]{1,0:T(8,128)(2,1)S(1)}, u32[]{:S(2)}, u32[]{:S(2)}) collective-permute-start(bf16[1024,512]{1,0:T(8,128)(2,1)S(1)} %pad_maximum_fusion), channel_id=1, source_target_pairs={{0,4},{4,8},{8,12},{12,16},{16,20},{20,24},{24,28},{1,5},{5,9},{9,... | collective-permute-start | bytes 3145736 | tf_op jit(solution)/shard_map/ppermute | solution.py:22
  57.4 1.0 copy-start
  58.3 22.8 %copy-start.3 = (f32[2,1,128]{2,1,0:T(1,128)S(1)}, f32[2,1,128]{2,1,0:T(1,128)}, u32[]{:S(2)}) copy-start(f32[2,1,128]{2,1,0:T(1,128)} %get-tuple-element.39) | copy-start | bytes 3076
  79.8 57.6 %collective-permute-start.2 = (bf16[1024,1024]{1,0:T(8,128)(2,1)}, bf16[1024,1024]{1,0:T(8,128)(2,1)S(1)}, u32[]{:S(2)}, u32[]{:S(2)}) collective-permute-start(bf16[1024,1024]{1,0:T(8,128)(2,1)} %get-tuple-element.34), channel_id=1, source_target_pairs={{4,0},{8,4},{12,8},{16,12},{20,16},{24,20},{28,24},{5,1},{9,5},{13... | collective-permute-start | bytes 6291464 | tf_op jit(solution)/shard_map/ppermute | solution.py:22
  81.1 27.7 %copy-start.2 = (f32[2,1,128]{2,1,0:T(1,128)S(1)}, f32[2,1,128]{2,1,0:T(1,128)}, u32[]{:S(2)}) copy-start(f32[2,1,128]{2,1,0:T(1,128)} %get-tuple-element.40) | copy-start | bytes 3076
  108.9 1.2 collective-permute-start.3
  110.1 3.6 %collective-permute-start.4 = (f32[2,128]{1,0:T(2,128)S(1)}, f32[2,128]{1,0:T(2,128)S(1)}, u32[]{:S(2)}, u32[]{:S(2)}) collective-permute-start(f32[2,128]{1,0:T(2,128)S(1)} %fusion), channel_id=1, source_target_pairs={{0,2},{1,3},{2,0},{3,1},{4,6},{5,7},{6,4},{7,5},{8,10},{9,11},{10,... | collective-permute-start | bytes 3080 | tf_op jit(solution)/shard_map/ppermute | solution.py:44
  113.8 15.0 %collective-permute-start.5 = (f32[2,128]{1,0:T(2,128)S(1)}, f32[2,128]{1,0:T(2,128)S(1)}, u32[]{:S(2)}, u32[]{:S(2)}) collective-permute-start(f32[2,128]{1,0:T(2,128)S(1)} %fusion.3), channel_id=1, source_target_pairs={{0,4},{4,0},{8,12},{12,8},{16,20},{20,16},{24,28},{28,24},{1,5},{5... | collective-permute-start | bytes 3080 | tf_op jit(solution)/shard_map/ppermute | solution.py:44
  128.8 3.6 %collective-permute-start.6 = (f32[2,128]{1,0:T(2,128)S(1)}, f32[2,128]{1,0:T(2,128)S(1)}, u32[]{:S(2)}, u32[]{:S(2)}) collective-permute-start(f32[2,128]{1,0:T(2,128)S(1)} %add.69), channel_id=1, source_target_pairs={{0,8},{4,12},{8,0},{12,4},{16,24},{20,28},{24,16},{28,20},{1,9},{5... | collective-permute-start | bytes 3080 | tf_op jit(solution)/shard_map/ppermute | solution.py:44
  132.4 4.5 %collective-permute-start.7 = (f32[2,128]{1,0:T(2,128)S(1)}, f32[2,128]{1,0:T(2,128)S(1)}, u32[]{:S(2)}, u32[]{:S(2)}) collective-permute-start(f32[2,128]{1,0:T(2,128)S(1)} %add.70), channel_id=1, source_target_pairs={{0,16},{4,20},{8,24},{12,28},{16,0},{20,4},{24,8},{28,12},{1,17},{... | collective-permute-start | bytes 3080 | tf_op jit(solution)/shard_map/ppermute | solution.py:44
  137.4 1.4 copy-start.1

commit v11 on v10

--- a/solution.py
+++ b/solution.py
@@ -186,7 +186,8 @@
 
 
 def own_kernel(qdoc_ref, kdoc_ref, do_ref, v_ref, lse_ref, delta_ref, dq_in_ref, raw_ref, gain_ref,
-               kraw_ref, kgain_ref, qgrad_ref, qgain_ref, kpart_ref, dk_ref, dv_ref, k_ref, *, group, head_dim):
+               kraw_ref, kgain_ref, *refs, group, head_dim, n_alias):
+    qgrad_ref, qgain_ref, kpart_ref, dk_ref, dv_ref, k_ref = refs[n_alias:]
     q_ref = raw_ref
     blk = BLOCK
     n_tiles = WINDOW // blk + 1
@@ -292,32 +293,32 @@
     doc_specs = [pl.BlockSpec((tok_rows, 1), lambda h: (0, 0)), pl.BlockSpec((1, key_rows), lambda h: (0, 0))]
     qdoc, kdoc = own_doc.reshape(tok_rows, 1), all_doc.reshape(1, key_rows)
     buffers = ()
-    kparts = []
+    key_part = None
+    query_part = None
+    backs = []
     for piece, halo in enumerate(halo_pieces):
         h0 = piece * n_piece
+        if query_part is not None:
+            halo = lax.optimization_barrier((halo, query_part))[0]
         qcol = pl.BlockSpec((tok_rows, gw), lambda h, h0=h0: (0, h + h0))
         kcol = pl.BlockSpec((tok_rows, head_dim), lambda h, h0=h0: (0, h + h0))
         hcol = pl.BlockSpec((WINDOW, head_dim), lambda h: (0, h))
         vcol = pl.BlockSpec((WINDOW, head_dim), lambda h, n_piece=n_piece: (0, h + n_piece))
-        stat = pl.BlockSpec((n_q * group * blk, 1), lambda h, h0=h0: (h + h0, 0))
-        outs = pl.pallas_call(
-            functools.partial(halo_kernel, group=group, head_dim=head_dim, n_alias=len(buffers)),
+        local_q = pl.BlockSpec((tok_rows, gw), lambda h: (0, h))
+        stat = pl.BlockSpec((n_q * group * blk, 1), lambda h: (h, 0))
+        part_spec = pl.BlockSpec((1, 1, head_dim), lambda h: (h, 0, 0))
+        part_shape = jax.ShapeDtypeStruct((n_piece, 1, head_dim), jnp.float32)
+        dq_half, dkv_halo, log_sums, delta, khalo = pl.pallas_call(
+            functools.partial(halo_kernel, group=group, head_dim=head_dim, n_alias=0),
             grid=(n_piece,),
-            in_specs=doc_specs + [qcol, qcol, hcol, vcol, kcol, kcol, gain_spec, gain_spec]
-            + [pl.BlockSpec(memory_space=pl.ANY)] * len(buffers),
-            out_specs=[
-                qcol,
-                pl.BlockSpec((WINDOW, 2 * head_dim), lambda h, h0=h0: (0, h + h0)),
-                stat,
-                stat,
-                pl.BlockSpec((1, 1, head_dim), lambda h: (h, 0, 0)),
-            ],
+            in_specs=doc_specs + [qcol, qcol, hcol, vcol, kcol, kcol, gain_spec, gain_spec],
+            out_specs=[local_q, pl.BlockSpec((WINDOW, 2 * head_dim), lambda h: (0, h)), stat, stat, part_spec],
             out_shape=[
-                jax.ShapeDtypeStruct((tok_rows, q_cols), jnp.float32),
-                jax.ShapeDtypeStruct((WINDOW, 2 * kv_cols), jnp.bfloat16),
-                jax.ShapeDtypeStruct((stat_rows, 1), jnp.float32),
-                jax.ShapeDtypeStruct((stat_rows, 1), jnp.float32),
-                jax.ShapeDtypeStruct((n_piece, 1, head_dim), jnp.float32),
+                jax.ShapeDtypeStruct((tok_rows, gw * n_piece), jnp.float32),
+                jax.ShapeDtypeStruct((WINDOW, 2 * head_dim * n_piece), jnp.bfloat16),
+                jax.ShapeDtypeStruct((stat_rows * n_piece // key_heads, 1), jnp.float32),
+                jax.ShapeDtypeStruct((stat_rows * n_piece // key_heads, 1), jnp.float32),
+                part_shape,
             ],
             scratch_shapes=[
                 pltpu.VMEM((WINDOW, head_dim), jnp.float32),
@@ -325,7 +326,6 @@
                 pltpu.VMEM((WINDOW, head_dim), jnp.bfloat16),
                 pltpu.VMEM((tok_rows, head_dim), jnp.bfloat16),
             ],
-            input_output_aliases={10 + i: i for i in range(len(buffers))},
             compiler_params=params,
             cost_estimate=pl.CostEstimate(
                 flops=n_piece * (2 * n_q * n_tiles + 5 * halo_tiles) * tile_flops,
@@ -334,41 +334,40 @@
                                           + 4 * tok_rows * gw + 2 * 2 * WINDOW * head_dim),
             ),
         )(qdoc, kdoc, query_raw, grad_rows, halo, halo, key_raw, value_proj, key_gain.reshape(1, head_dim),
-          query_gain.reshape(1, head_dim), *buffers)
-        buffers = tuple(outs[:4])
-        kparts.append(outs[4])
-    dq_half, dkv_halo, log_sums, delta = buffers
-    qcol = pl.BlockSpec((tok_rows, gw), lambda h: (0, h))
-    kcol = pl.BlockSpec((tok_rows, head_dim), lambda h: (0, h))
-    stat = pl.BlockSpec((n_q * group * blk, 1), lambda h: (h, 0))
-    part_spec = pl.BlockSpec((1, 1, head_dim), lambda h: (h, 0, 0))
-    part_shape = jax.ShapeDtypeStruct((key_heads, 1, head_dim), jnp.float32)
-    query_grad, qgain_parts, kown_parts, dk_own, dv_own = pl.pallas_call(
-        functools.partial(own_kernel, group=group, head_dim=head_dim),
-        grid=(key_heads,),
-        in_specs=doc_specs + [qcol, kcol, stat, stat, qcol, qcol, gain_spec, kcol, gain_spec],
-        out_specs=[qcol, part_spec, part_spec, kcol, kcol],
-        scratch_shapes=[pltpu.VMEM((tok_rows, head_dim), jnp.bfloat16)],
-        out_shape=[
-            jax.ShapeDtypeStruct((tok_rows, q_cols), jnp.bfloat16),
-            part_shape,
-            part_shape,
-            jax.ShapeDtypeStruct((tok_rows, kv_cols), jnp.float32),
-            jax.ShapeDtypeStruct((tok_rows, kv_cols), jnp.float32),
-        ],
-        compiler_params=params,
-        cost_estimate=pl.CostEstimate(
-            flops=key_heads * own_tiles * 5 * tile_flops,
-            transcendentals=key_heads * own_tiles * group * blk * blk,
-            bytes_accessed=2 * 2 * tok_rows * q_cols + 2 * 2 * tok_rows * kv_cols + 2 * 4 * tok_rows * q_cols
-            + 2 * 4 * tok_rows * kv_cols,
-        ),
-    )(qdoc, kdoc, grad_rows, value_proj, log_sums, delta, dq_half, query_raw,
-      query_gain.reshape(1, head_dim), key_raw, key_gain.reshape(1, head_dim))
-    key_part = jnp.sum(kown_parts, axis=(0, 1))
-    for part in kparts:
-        key_part = key_part + jnp.sum(part, axis=(0, 1))
-    return query_grad, jnp.sum(qgain_parts, axis=(0, 1)), key_part, dkv_halo, dk_own, dv_own
+          query_gain.reshape(1, head_dim))
+        backs.append(shifted(dkv_halo, "ctx", -1))
+        outs = pl.pallas_call(
+            functools.partial(own_kernel, group=group, head_dim=head_dim, n_alias=len(buffers)),
+            grid=(n_piece,),
+            in_specs=doc_specs + [qcol, kcol, stat, stat, local_q, qcol, gain_spec, kcol, gain_spec]
+            + [pl.BlockSpec(memory_space=pl.ANY)] * len(buffers),
+            out_specs=[qcol, part_spec, part_spec, kcol, kcol],
+            out_shape=[
+                jax.ShapeDtypeStruct((tok_rows, q_cols), jnp.bfloat16),
+                part_shape,
+                part_shape,
+                jax.ShapeDtypeStruct((tok_rows, kv_cols), jnp.float32),
+                jax.ShapeDtypeStruct((tok_rows, kv_cols), jnp.float32),
+            ],
+            scratch_shapes=[pltpu.VMEM((tok_rows, head_dim), jnp.bfloat16)],
+            input_output_aliases=dict(zip(range(11, 11 + len(buffers)), (0, 3, 4))),
+            compiler_params=params,
+            cost_estimate=pl.CostEstimate(
+                flops=n_piece * own_tiles * 5 * tile_flops,
+                transcendentals=n_piece * own_tiles * group * blk * blk,
+                bytes_accessed=n_piece * (2 * 2 * tok_rows * gw + 2 * 2 * tok_rows * head_dim
+                                          + 2 * 4 * tok_rows * gw + 2 * 4 * tok_rows * head_dim),
+            ),
+        )(qdoc, kdoc, grad_rows, value_proj, log_sums, delta, dq_half, query_raw,
+          query_gain.reshape(1, head_dim), key_raw, key_gain.reshape(1, head_dim), *buffers)
+        query_grad, qparts, kparts, dk_own, dv_own = outs
+        buffers = (query_grad, dk_own, dv_own)
+        piece_q = jnp.sum(qparts, axis=(0, 1))
+        piece_k = jnp.sum(kparts, axis=(0, 1)) + jnp.sum(khalo, axis=(0, 1))
+        query_part = piece_q if query_part is None else query_part + piece_q
+        key_part = piece_k if key_part is None else key_part + piece_k
+    back = backs[0] if len(backs) == 1 else jnp.concatenate(backs, axis=1)
+    return query_grad, query_part, key_part, back, dk_own, dv_own
 
 
 def per_device(query_raw, key_raw, value_proj, query_gain, key_gain, out_grad, doc_lengths):
@@ -392,12 +391,11 @@
             send = lax.optimization_barrier((send, halo_pieces[-1]))[0]
         halo_pieces.append(shifted(send, "ctx", 1))
     all_doc = jnp.concatenate([halo_doc, own_doc])
-    query_grad, query_part, key_part, dkv_halo, dk_own, dv_own = attention_grads(
+    query_grad, query_part, key_part, back, dk_own, dv_own = attention_grads(
         out_grad, halo_pieces, value_proj, own_doc, all_doc, key_heads, head_dim,
         query_raw, query_gain, key_raw, key_gain,
     )
     gain_grads = butterfly_sum(jnp.stack([query_part, key_part]), ("head", "ctx"))
-    back = shifted(dkv_halo, "ctx", -1)
     key_grad, value_grad, _ = kv_final(dk_own, dv_own, back, key_raw, key_gain, key_heads, head_dim)
     return (query_grad, key_grad, value_grad, gain_grads[0], gain_grads[1])
 

time: 145 us -> 158 us (1.090)
  Pallas kernels: 74.4 us -> 79.1 us
  starting transfers between devices: 20.6 us -> 24.6 us
  other arithmetic: 2.5 us -> 6.09 us
  waiting for transfers between devices: 40.3 us -> 43.6 us
  local copies, waits for them, and re-layouts: 5.62 us -> 3.3 us
    pallas_call x1 -> x2, Pallas kernels: 26.3 us -> 30.9 us  [attention_grads(): pl.pallas_call(functools.partial(own_kernel, group=group, head_dim=head_d...]
    ppermute x5, waiting for transfers between devices: 19.1 us -> 22.7 us  [butterfly_sum(): shifted_parts.append(lax.ppermute(value, axis, pairs))]
    unnamed x10 -> x6, local copies, waits for them, and re-layouts: 2.33 us -> 0.01 us
    ppermute x3 -> x4, starting transfers between devices: 11.8 us -> 13.9 us  [shifted(): lax.ppermute(value, axis, [(source, source + steps) for source in range(l...]
    reduce_sum x4 -> x6, other arithmetic: 1.45 us -> 3.41 us  [the longest x4 2.03 us: attention_grads(): piece_k = jnp.sum(kparts, axis=(0, 1)) + jnp.sum(khalo, axis=(0, 1))]
    ppermute x5, starting transfers between devices: 8.88 us -> 10.7 us  [butterfly_sum(): shifted_parts.append(lax.ppermute(value, axis, pairs))]
    concatenate x0 -> x1, other arithmetic: none -> 1.62 us  [attention_grads(): back = backs[0] if len(backs) == 1 else jnp.concatenate(backs, axis=1)]
    ppermute x3 -> x4, waiting for transfers between devices: 21.3 us -> 21 us  [shifted(): lax.ppermute(value, axis, [(source, source + steps) for source in range(l...]
  transfers between devices with their start and end apart: 8 -> 9, of which waited for: 6 -> 6; matrix products, arithmetic and copies ran while one was open for 3% -> 4% of each run, Pallas kernels for 33% -> 47%
where the time goes in v11:
time: 158 us; the launch traced here: 157 us
  Pallas kernels  79.1 us (50%)
  waiting for transfers between devices  43.6 us (28%)
  starting transfers between devices  24.6 us (16%)
  other arithmetic  6.09 us (4%)
  local copies, waits for them, and re-layouts  3.3 us (2%)
    pallas_call x2, Pallas kernels, attention_grads(): pl.pallas_call(functools.partial(halo_kernel, group=group, head_dim=head_...  42.6 us
    pallas_call x2, Pallas kernels, attention_grads(): pl.pallas_call(functools.partial(own_kernel, group=group, head_dim=head_d...  30.9 us
    ppermute x5, waiting for transfers between devices, butterfly_sum(): shifted_parts.append(lax.ppermute(value, axis, pairs))  22.7 us
    ppermute x4, waiting for transfers between devices, shifted(): lax.ppermute(value, axis, [(source, source + steps) for source in range(l...  21 us
    ppermute x4, starting transfers between devices, shifted(): lax.ppermute(value, axis, [(source, source + steps) for source in range(l...  13.9 us
    ppermute x5, starting transfers between devices, butterfly_sum(): shifted_parts.append(lax.ppermute(value, axis, pairs))  10.7 us
    pallas_call x1, Pallas kernels, kv_final(): pl.pallas_call(functools.partial(kv_final_kernel, head_dim=head_dim), gri...  5.53 us
  transfers between devices with their start and end apart: 9, of which 6 were waited for; matrix products, arithmetic and copies ran while one was open for 4% of the time, Pallas kernels for 47%

profile of v11, /device:TPU:0, one launch (start us, length us, event | category | flops | bytes accessed | tf_op | source)
XLA Modules:
  0.0 157.4 jit_solution(17307807943872996129)
XLA Ops:
  0.6 1.7 %fusion.1 = (bf16[1024,256]{1,0:T(8,128)(2,1)S(1)}, bf16[1024,256]{1,0:T(8,128)(2,1)S(1)}, bf16[1024,256]{1,0:T(8,128)(2,1)S(1)}, bf16[1024,256]{1,0:T(8,128)(2,1)S(1)}) fusion(bf16[1024,512]{1,0:T(8,128)(2,1)} %raw_ref.5, bf16[1024,512]{1,0:T(8,128)(2,1)} %v_ref.7), kind=kLoop, calls=%fused_computation.15 | loop fusion | bytes 4194304 | tf_op jit(solution)/shard_map/slice | solution.py:389
  2.4 5.9 %collective-permute-start = (bf16[1024,512]{1,0:T(8,128)(2,1)S(1)}, bf16[1024,512]{1,0:T(8,128)(2,1)}, u32[]{:S(2)}, u32[]{:S(2)}) collective-permute-start(bf16[1024,512]{1,0:T(8,128)(2,1)S(1)} %pad_maximum_fusion.2), channel_id=1, source_target_pairs={{0,4},{4,8},{8,12},{12,16},{16,20},{20,24},{24,28},{1,5},{5,9},{9,... | collective-permute-start | bytes 3145736 | tf_op jit(solution)/shard_map/ppermute | solution.py:22
  8.7 21.0 %collective-permute-done.hk_ref.hv_ref = bf16[1024,512]{1,0:T(8,128)(2,1)} collective-permute-done((bf16[1024,512]{1,0:T(8,128)(2,1)S(1)}, bf16[1024,512]{1,0:T(8,128)(2,1)}, u32[]{:S(2)}, u32[]{:S(2)}) %collective-permute-start) | collective-permute-done | bytes 1048608 | tf_op jit(solution)/shard_map/ppermute | solution.py:22
  29.7 5.5 %collective-permute-start.1 = (bf16[1024,512]{1,0:T(8,128)(2,1)S(1)}, bf16[1024,512]{1,0:T(8,128)(2,1)}, u32[]{:S(2)}, u32[]{:S(2)}) collective-permute-start(bf16[1024,512]{1,0:T(8,128)(2,1)S(1)} %pad_maximum_fusion.1), channel_id=1, source_target_pairs={{0,4},{4,8},{8,12},{12,16},{16,20},{20,24},{24,28},{1,5},{5,9},{9,... | collective-permute-start | bytes 3145736 | tf_op jit(solution)/shard_map/ppermute | solution.py:22
  35.1 1.0 copy.25.qdoc_ref
  36.8 21.2 %shard_map.110 = (f32[1024,512]{1,0:T(8,128)}, bf16[1024,512]{1,0:T(8,128)(2,1)}, f32[4096,1]{1,0:T(8,128)}, f32[4096,1]{1,0:T(8,128)}, f32[2,1,128]{2,1,0:T(1,128)}) custom-call(s32[1024,1]{1,0:T(8,128)} %copy.25.qdoc_ref, s32[1,2048]{1,0:T(1,128)} %bitcast.13, bf16[1024,1024]{1,0:T(8,128)(2,1)} %raw_ref.4, bf16[1024,1024]{1,0:T(8,128)(2,1)} %do_ref.7, ...), custom_call_target="tpu_custom_call" | custom-call | flops 6039797760 | bytes 7340032 | tf_op jit(solution)/shard_map/pallas_call | solution.py:311
  57.9 0.7 reduce_sum.77
  58.6 15.4 %shard_map.111 = (bf16[1024,1024]{1,0:T(8,128)(2,1)}, f32[2,1,128]{2,1,0:T(1,128)}, f32[2,1,128]{2,1,0:T(1,128)}, f32[1024,512]{1,0:T(8,128)}, f32[1024,512]{1,0:T(8,128)}) custom-call(s32[1024,1]{1,0:T(8,128)} %copy.25.qdoc_ref, s32[1,2048]{1,0:T(1,128)} %bitcast.14, bf16[1024,1024]{1,0:T(8,128)(2,1)} %do_ref.7, bf16[1024,512]{1,0:T(8,128)(2,1)} %v_ref.7, ...), custom_call_target="tpu_custom_call" | custom-call | flops 3355443200 | bytes 9437184 | tf_op jit(solution)/shard_map/pallas_call | solution.py:339
  74.0 0.7 reduce_sum.74
  75.4 1.3 collective-permute-start.2
  76.7 21.4 %shard_map.112 = (f32[1024,512]{1,0:T(8,128)}, bf16[1024,512]{1,0:T(8,128)(2,1)}, f32[4096,1]{1,0:T(8,128)}, f32[4096,1]{1,0:T(8,128)}, f32[2,1,128]{2,1,0:T(1,128)}) custom-call(s32[1024,1]{1,0:T(8,128)} %copy.25.qdoc_ref, s32[1,2048]{1,0:T(1,128)} %bitcast.15, bf16[1024,1024]{1,0:T(8,128)(2,1)} %raw_ref.4, bf16[1024,1024]{1,0:T(8,128)(2,1)} %do_ref.7, ...), custom_call_target="tpu_custom_call" | custom-call | flops 6039797760 | bytes 7340032 | tf_op jit(solution)/shard_map/pallas_call | solution.py:311
  98.1 15.6 %shard_map.113 = (bf16[1024,1024]{1,0:T(8,128)(2,1)}, f32[2,1,128]{2,1,0:T(1,128)}, f32[2,1,128]{2,1,0:T(1,128)}, f32[1024,512]{1,0:T(8,128)}, f32[1024,512]{1,0:T(8,128)}) custom-call(s32[1024,1]{1,0:T(8,128)} %copy.25.qdoc_ref, s32[1,2048]{1,0:T(1,128)} %bitcast.16, ...), custom_call_target="tpu_custom_call", output_to_operand_aliasing={{0}: (11, {}), {3}: (12, {}), {4}: (13, {})} | custom-call | flops 3355443200 | bytes 9437184 | tf_op jit(solution)/shard_map/pallas_call | solution.py:339
  114.4 1.3 collective-permute-start.3
  116.4 1.1 collective-permute-done.4
  117.6 1.6 %collective-permute-start.5 = (f32[2,128]{1,0:T(2,128)S(1)}, f32[2,128]{1,0:T(2,128)S(1)}, u32[]{:S(2)}, u32[]{:S(2)}) collective-permute-start(f32[2,128]{1,0:T(2,128)S(1)} %fusion), channel_id=1, source_target_pairs={{0,2},{1,3},{2,0},{3,1},{4,6},{5,7},{6,4},{7,5},{8,10},{9,11},{10,... | collective-permute-start | bytes 3080 | tf_op jit(solution)/shard_map/ppermute | solution.py:44
  119.2 2.1 %collective-permute-done.5 = f32[2,128]{1,0:T(2,128)S(1)} collective-permute-done((f32[2,128]{1,0:T(2,128)S(1)}, f32[2,128]{1,0:T(2,128)S(1)}, u32[]{:S(2)}, u32[]{:S(2)}) %collective-permute-start.5) | collective-permute-done | bytes 1056 | tf_op jit(solution)/shard_map/ppermute | solution.py:44
  121.2 3.3 %collective-permute-start.6 = (f32[2,128]{1,0:T(2,128)S(1)}, f32[2,128]{1,0:T(2,128)S(1)}, u32[]{:S(2)}, u32[]{:S(2)}) collective-permute-start(f32[2,128]{1,0:T(2,128)S(1)} %fusion.3), channel_id=1, source_target_pairs={{0,4},{4,0},{8,12},{12,8},{16,20},{20,16},{24,28},{28,24},{1,5},{5... | collective-permute-start | bytes 3080 | tf_op jit(solution)/shard_map/ppermute | solution.py:44
  124.6 16.4 %collective-permute-done.6 = f32[2,128]{1,0:T(2,128)S(1)} collective-permute-done((f32[2,128]{1,0:T(2,128)S(1)}, f32[2,128]{1,0:T(2,128)S(1)}, u32[]{:S(2)}, u32[]{:S(2)}) %collective-permute-start.6) | collective-permute-done | bytes 1056 | tf_op jit(solution)/shard_map/ppermute | solution.py:44
  140.9 2.7 %collective-permute-start.7 = (f32[2,128]{1,0:T(2,128)S(1)}, f32[2,128]{1,0:T(2,128)S(1)}, u32[]{:S(2)}, u32[]{:S(2)}) collective-permute-start(f32[2,128]{1,0:T(2,128)S(1)} %add.96), channel_id=1, source_target_pairs={{0,8},{4,12},{8,0},{12,4},{16,24},{20,28},{24,16},{28,20},{1,9},{5... | collective-permute-start | bytes 3080 | tf_op jit(solution)/shard_map/ppermute | solution.py:44
  143.6 1.6 collective-permute-done.7
  145.2 3.0 %collective-permute-start.8 = (f32[2,128]{1,0:T(2,128)S(1)}, f32[2,128]{1,0:T(2,128)S(1)}, u32[]{:S(2)}, u32[]{:S(2)}) collective-permute-start(f32[2,128]{1,0:T(2,128)S(1)} %add.97), channel_id=1, source_target_pairs={{0,16},{4,20},{8,24},{12,28},{16,0},{20,4},{24,8},{28,12},{1,17},{... | collective-permute-start | bytes 3080 | tf_op jit(solution)/shard_map/ppermute | solution.py:44
  148.2 1.6 collective-permute-done.8
  150.3 1.6 %pad_maximum_fusion.back_ref = bf16[1024,1024]{1,0:T(8,128)(2,1)} fusion(bf16[1024,512]{1,0:T(8,128)(2,1)S(1)} %collective-permute-done.3, bf16[1024,512]{1,0:T(8,128)(2,1)S(1)} %collective-permute-done.2), kind=kLoop, calls=%fused_computation | loop fusion | flops 4194304 | bytes 4194304 | tf_op jit(solution)/shard_map/concatenate | solution.py:369
  151.9 5.5 %shard_map.114 = (bf16[1024,512]{1,0:T(8,128)(2,1)}, bf16[1024,512]{1,0:T(8,128)(2,1)}, f32[4,1,128]{2,1,0:T(1,128)}) custom-call(f32[1024,512]{1,0:T(8,128)} %get-tuple-element.42.dk_ref, f32[1024,512]{1,0:T(8,128)} %get-tuple-element.43.dv_ref, bf16[1024,1024]{1,0:T(8,128)(2,1)} %pad_maximum_fusion.back_ref, bf16[1024,512]{1,0:T(8,128)(2,1)} %raw_ref.5, ...), custom_call_target="tpu_custom_call" | custom-call | tf_op jit(solution)/shard_map/pallas_call | solution.py:256
  (32 shorter events, 3.8 us)
Async XLA Ops:
  2.3 6.0 %copy-start.1 = (s32[16]{0:T(128)S(1)}, s32[16]{0:T(128)}, u32[]{:S(2)}) copy-start(s32[16]{0:T(128)} %param.13) | copy-start | bytes 196
  2.4 27.3 %collective-permute-start = (bf16[1024,512]{1,0:T(8,128)(2,1)S(1)}, bf16[1024,512]{1,0:T(8,128)(2,1)}, u32[]{:S(2)}, u32[]{:S(2)}) collective-permute-start(bf16[1024,512]{1,0:T(8,128)(2,1)S(1)} %pad_maximum_fusion.2), channel_id=1, source_target_pairs={{0,4},{4,8},{8,12},{12,16},{16,20},{20,24},{24,28},{1,5},{5,9},{9,... | collective-permute-start | bytes 3145736 | tf_op jit(solution)/shard_map/ppermute | solution.py:22
  29.7 47.0 %collective-permute-start.1 = (bf16[1024,512]{1,0:T(8,128)(2,1)S(1)}, bf16[1024,512]{1,0:T(8,128)(2,1)}, u32[]{:S(2)}, u32[]{:S(2)}) collective-permute-start(bf16[1024,512]{1,0:T(8,128)(2,1)S(1)} %pad_maximum_fusion.1), channel_id=1, source_target_pairs={{0,4},{4,8},{8,12},{12,16},{16,20},{20,24},{24,28},{1,5},{5,9},{9,... | collective-permute-start | bytes 3145736 | tf_op jit(solution)/shard_map/ppermute | solution.py:22
  58.6 16.8 %copy-start.2 = (bf16[1024,512]{1,0:T(8,128)(2,1)S(1)}, bf16[1024,512]{1,0:T(8,128)(2,1)}, u32[]{:S(2)}) copy-start(bf16[1024,512]{1,0:T(8,128)(2,1)} %get-tuple-element.44) | copy-start | bytes 3145732
  75.4 74.9 %collective-permute-start.2 = (bf16[1024,512]{1,0:T(8,128)(2,1)S(1)}, bf16[1024,512]{1,0:T(8,128)(2,1)S(1)}, u32[]{:S(2)}, u32[]{:S(2)}) collective-permute-start(bf16[1024,512]{1,0:T(8,128)(2,1)S(1)} %copy-done.2), channel_id=1, source_target_pairs={{4,0},{8,4},{12,8},{16,12},{20,16},{24,20},{28,24},{5,1},{9,5},{13... | collective-permute-start | bytes 3145736 | tf_op jit(solution)/shard_map/ppermute | solution.py:22
  98.1 18.2 %copy-start = (f32[2,1,128]{2,1,0:T(1,128)S(1)}, f32[2,1,128]{2,1,0:T(1,128)}, u32[]{:S(2)}) copy-start(f32[2,1,128]{2,1,0:T(1,128)} %get-tuple-element.52) | copy-start | bytes 3076
  114.4 35.9 %collective-permute-start.3 = (bf16[1024,512]{1,0:T(8,128)(2,1)}, bf16[1024,512]{1,0:T(8,128)(2,1)S(1)}, u32[]{:S(2)}, u32[]{:S(2)}) collective-permute-start(bf16[1024,512]{1,0:T(8,128)(2,1)} %get-tuple-element.45), channel_id=1, source_target_pairs={{4,0},{8,4},{12,8},{16,12},{20,16},{24,20},{28,24},{5,1},{9,5},{13... | collective-permute-start | bytes 3145736 | tf_op jit(solution)/shard_map/ppermute | solution.py:22
  116.4 1.2 collective-permute-start.4
  117.6 3.6 %collective-permute-start.5 = (f32[2,128]{1,0:T(2,128)S(1)}, f32[2,128]{1,0:T(2,128)S(1)}, u32[]{:S(2)}, u32[]{:S(2)}) collective-permute-start(f32[2,128]{1,0:T(2,128)S(1)} %fusion), channel_id=1, source_target_pairs={{0,2},{1,3},{2,0},{3,1},{4,6},{5,7},{6,4},{7,5},{8,10},{9,11},{10,... | collective-permute-start | bytes 3080 | tf_op jit(solution)/shard_map/ppermute | solution.py:44
  121.2 19.7 %collective-permute-start.6 = (f32[2,128]{1,0:T(2,128)S(1)}, f32[2,128]{1,0:T(2,128)S(1)}, u32[]{:S(2)}, u32[]{:S(2)}) collective-permute-start(f32[2,128]{1,0:T(2,128)S(1)} %fusion.3), channel_id=1, source_target_pairs={{0,4},{4,0},{8,12},{12,8},{16,20},{20,16},{24,28},{28,24},{1,5},{5... | collective-permute-start | bytes 3080 | tf_op jit(solution)/shard_map/ppermute | solution.py:44
  140.9 4.2 %collective-permute-start.7 = (f32[2,128]{1,0:T(2,128)S(1)}, f32[2,128]{1,0:T(2,128)S(1)}, u32[]{:S(2)}, u32[]{:S(2)}) collective-permute-start(f32[2,128]{1,0:T(2,128)S(1)} %add.96), channel_id=1, source_target_pairs={{0,8},{4,12},{8,0},{12,4},{16,24},{20,28},{24,16},{28,20},{1,9},{5... | collective-permute-start | bytes 3080 | tf_op jit(solution)/shard_map/ppermute | solution.py:44
  145.2 4.6 %collective-permute-start.8 = (f32[2,128]{1,0:T(2,128)S(1)}, f32[2,128]{1,0:T(2,128)S(1)}, u32[]{:S(2)}, u32[]{:S(2)}) collective-permute-start(f32[2,128]{1,0:T(2,128)S(1)} %add.97), channel_id=1, source_target_pairs={{0,16},{4,20},{8,24},{12,28},{16,0},{20,4},{24,8},{28,12},{1,17},{... | collective-permute-start | bytes 3080 | tf_op jit(solution)/shard_map/ppermute | solution.py:44

commit v12 on v10

--- a/solution.py
+++ b/solution.py
@@ -115,8 +115,8 @@
     return dq_part, dk_part * scale, dv_part
 
 
-def halo_kernel(qdoc_ref, kdoc_ref, q_ref, do_ref, hk_ref, hv_ref, kraw_ref, v_ref, kgain_ref, qgain_ref, *refs,
-                group, head_dim, n_alias):
+def halo_kernel(qdoc_ref, kdoc_ref, q_ref, do_ref, hk_ref, hv_ref, kraw_ref, v_ref, kgain_ref, qgain_ref,
+                tot_ref, num_ref, *refs, group, head_dim, n_alias):
     dq_ref, dkv_ref, lse_ref, delta_ref, kpart_ref, dk_ref, dv_ref, kn_ref, k_ref = refs[n_alias:]
     blk = BLOCK
     n_tiles = WINDOW // blk + 1
@@ -142,10 +142,10 @@
         q_first = qb * blk
         q_g = normed_stack(q_ref, qgain, group, head_dim, q_first)
         do_g = stacked(do_ref, group, head_dim, q_first)
-        masks = [tile_mask(qdoc_ref, kdoc_ref, q_first, t, group)[0] for t in range(n_tiles)]
-        totals = jnp.zeros((gb, 1), jnp.float32)
-        numer = jnp.zeros((gb, head_dim), jnp.float32)
-        for t in range(n_tiles):
+        masks = [tile_mask(qdoc_ref, kdoc_ref, q_first, t, group)[0] for t in range(n_halo - qb)]
+        totals = tot_ref[qb * gb:(qb + 1) * gb, :]
+        numer = num_ref[qb * gb:(qb + 1) * gb, :]
+        for t in range(n_halo - qb):
             k_first = q_first + t * blk
             k_tile, v_tile = key_tile(k_first)
             scores = lax.dot_general(
@@ -174,6 +174,36 @@
     dkv_ref[:, head_dim:] = dv_ref[...].astype(jnp.bfloat16)
     halo_hat = halo_raw * halo_inv
     kpart_ref[...] = jnp.sum(dk_ref[...] * halo_hat, axis=0, keepdims=True).reshape(kpart_ref.shape)
+
+
+def stats_kernel(qdoc_ref, kdoc_ref, q_ref, kraw_ref, v_ref, kgain_ref, qgain_ref, tot_ref, num_ref, k_ref,
+                 *, group, head_dim):
+    blk = BLOCK
+    n_tiles = WINDOW // blk + 1
+    n_halo = WINDOW // blk
+    n_q = q_ref.shape[0] // blk
+    gb = group * blk
+    scale = QUERY_SCALAR ** (-0.5)
+    k_ref[...] = normed_rows(kraw_ref[...].astype(jnp.float32), kgain_ref[...])
+    qgain = qgain_ref[...]
+    for qb in range(n_q):
+        q_first = qb * blk
+        q_g = normed_stack(q_ref, qgain, group, head_dim, q_first)
+        totals = jnp.zeros((gb, 1), jnp.float32)
+        numer = jnp.zeros((gb, head_dim), jnp.float32)
+        for t in range(max(0, n_halo - qb), n_tiles):
+            live = tile_mask(qdoc_ref, kdoc_ref, q_first, t, group)[0]
+            own_first = q_first + t * blk - WINDOW
+            k_tile = k_ref[own_first:own_first + blk, :]
+            v_tile = v_ref[own_first:own_first + blk, :]
+            scores = lax.dot_general(
+                q_g, k_tile, (((1,), (1,)), ((), ())), preferred_element_type=jnp.float32
+            ) * scale
+            exp_s = jnp.where(live, jnp.exp(scores), 0.0)
+            totals = totals + jnp.sum(exp_s, axis=1, keepdims=True)
+            numer = numer + jnp.dot(exp_s.astype(jnp.bfloat16), v_tile, preferred_element_type=jnp.float32)
+        tot_ref[qb * gb:(qb + 1) * gb, :] = totals
+        num_ref[qb * gb:(qb + 1) * gb, :] = numer
 
 
 def norm_grad(raw, gain, upstream):
@@ -291,9 +321,34 @@
     gain_spec = pl.BlockSpec((1, head_dim), lambda h: (0, 0))
     doc_specs = [pl.BlockSpec((tok_rows, 1), lambda h: (0, 0)), pl.BlockSpec((1, key_rows), lambda h: (0, 0))]
     qdoc, kdoc = own_doc.reshape(tok_rows, 1), all_doc.reshape(1, key_rows)
+    qall = pl.BlockSpec((tok_rows, gw), lambda h: (0, h))
+    kall = pl.BlockSpec((tok_rows, head_dim), lambda h: (0, h))
+    totals, numer = pl.pallas_call(
+        functools.partial(stats_kernel, group=group, head_dim=head_dim),
+        grid=(key_heads,),
+        in_specs=doc_specs + [qall, kall, kall, gain_spec, gain_spec],
+        out_specs=[pl.BlockSpec((n_q * group * blk, 1), lambda h: (h, 0)),
+                   pl.BlockSpec((n_q * group * blk, head_dim), lambda h: (h, 0))],
+        out_shape=[jax.ShapeDtypeStruct((stat_rows, 1), jnp.float32),
+                   jax.ShapeDtypeStruct((stat_rows, head_dim), jnp.float32)],
+        scratch_shapes=[pltpu.VMEM((tok_rows, head_dim), jnp.bfloat16)],
+        compiler_params=params,
+        cost_estimate=pl.CostEstimate(
+            flops=key_heads * 2 * own_tiles * tile_flops,
+            transcendentals=key_heads * own_tiles * group * blk * blk,
+            bytes_accessed=2 * tok_rows * q_cols + 2 * 2 * tok_rows * kv_cols + 4 * stat_rows * (head_dim + 1),
+        ),
+    )(qdoc, kdoc, query_raw, key_raw, value_proj, key_gain.reshape(1, head_dim), query_gain.reshape(1, head_dim))
+    received = []
+    for send in halo_pieces:
+        if received:
+            send = lax.optimization_barrier((send, received[-1]))[0]
+            received.append(shifted(send, "ctx", 1))
+        else:
+            received.append(lax.optimization_barrier((shifted(send, "ctx", 1), totals, numer))[0])
     buffers = ()
     kparts = []
-    for piece, halo in enumerate(halo_pieces):
+    for piece, halo in enumerate(received):
         h0 = piece * n_piece
         qcol = pl.BlockSpec((tok_rows, gw), lambda h, h0=h0: (0, h + h0))
         kcol = pl.BlockSpec((tok_rows, head_dim), lambda h, h0=h0: (0, h + h0))
@@ -303,7 +358,9 @@
         outs = pl.pallas_call(
             functools.partial(halo_kernel, group=group, head_dim=head_dim, n_alias=len(buffers)),
             grid=(n_piece,),
-            in_specs=doc_specs + [qcol, qcol, hcol, vcol, kcol, kcol, gain_spec, gain_spec]
+            in_specs=doc_specs + [qcol, qcol, hcol, vcol, kcol, kcol, gain_spec, gain_spec,
+                                  pl.BlockSpec((n_q * group * blk, 1), lambda h, h0=h0: (h + h0, 0)),
+                                  pl.BlockSpec((n_q * group * blk, head_dim), lambda h, h0=h0: (h + h0, 0))]
             + [pl.BlockSpec(memory_space=pl.ANY)] * len(buffers),
             out_specs=[
                 qcol,
@@ -325,7 +382,7 @@
                 pltpu.VMEM((WINDOW, head_dim), jnp.bfloat16),
                 pltpu.VMEM((tok_rows, head_dim), jnp.bfloat16),
             ],
-            input_output_aliases={10 + i: i for i in range(len(buffers))},
+            input_output_aliases={12 + i: i for i in range(len(buffers))},
             compiler_params=params,
             cost_estimate=pl.CostEstimate(
                 flops=n_piece * (2 * n_q * n_tiles + 5 * halo_tiles) * tile_flops,
@@ -334,7 +391,7 @@
                                           + 4 * tok_rows * gw + 2 * 2 * WINDOW * head_dim),
             ),
         )(qdoc, kdoc, query_raw, grad_rows, halo, halo, key_raw, value_proj, key_gain.reshape(1, head_dim),
-          query_gain.reshape(1, head_dim), *buffers)
+          query_gain.reshape(1, head_dim), totals, numer, *buffers)
         buffers = tuple(outs[:4])
         kparts.append(outs[4])
     dq_half, dkv_halo, log_sums, delta = buffers
@@ -388,9 +445,7 @@
     for piece in range(n_pieces):
         cols = slice(piece * width, (piece + 1) * width)
         send = jnp.concatenate([key_raw[tok_rows - WINDOW:, cols], value_proj[tok_rows - WINDOW:, cols]], axis=1)
-        if halo_pieces:
-            send = lax.optimization_barrier((send, halo_pieces[-1]))[0]
-        halo_pieces.append(shifted(send, "ctx", 1))
+        halo_pieces.append(send)
     all_doc = jnp.concatenate([halo_doc, own_doc])
     query_grad, query_part, key_part, dkv_halo, dk_own, dv_own = attention_grads(
         out_grad, halo_pieces, value_proj, own_doc, all_doc, key_heads, head_dim,

time: 145 us -> 146 us (level)
  Pallas kernels: 74.4 us -> 88.9 us
  waiting for transfers between devices: 40.3 us -> 26.3 us
    ppermute x3, waiting for transfers between devices: 21.3 us -> 7.91 us  [shifted(): lax.ppermute(value, axis, [(source, source + steps) for source in range(l...]
    pallas_call x0 -> x1, Pallas kernels: none -> 11.4 us  [attention_grads(): pl.pallas_call(functools.partial(stats_kernel, group=group, head_dim=head...]
    pallas_call x2, Pallas kernels: 42.6 us -> 45.7 us  [attention_grads(): pl.pallas_call(functools.partial(halo_kernel, group=group, head_dim=head_...]
  transfers between devices with their start and end apart: 8 -> 8, of which waited for: 6 -> 6; matrix products, arithmetic and copies ran while one was open for 3% -> 3% of each run, Pallas kernels for 33% -> 42%
where the time goes in v12:
time: 146 us; the launch traced here: 145 us
  Pallas kernels  88.9 us (61%)
  waiting for transfers between devices  26.3 us (18%)
  starting transfers between devices  21.3 us (15%)
  local copies, waits for them, and re-layouts  5.6 us (4%)
  other arithmetic  2.48 us (2%)
    pallas_call x2, Pallas kernels, attention_grads(): pl.pallas_call(functools.partial(halo_kernel, group=group, head_dim=head_...  45.7 us
    pallas_call x1, Pallas kernels, attention_grads(): pl.pallas_call(functools.partial(own_kernel, group=group, head_dim=head_d...  26.3 us
    ppermute x5, waiting for transfers between devices, butterfly_sum(): shifted_parts.append(lax.ppermute(value, axis, pairs))  18.4 us
    ppermute x3, starting transfers between devices, shifted(): lax.ppermute(value, axis, [(source, source + steps) for source in range(l...  11.7 us
    pallas_call x1, Pallas kernels, attention_grads(): pl.pallas_call(functools.partial(stats_kernel, group=group, head_dim=head...  11.4 us
    ppermute x5, starting transfers between devices, butterfly_sum(): shifted_parts.append(lax.ppermute(value, axis, pairs))  9.54 us
    ppermute x3, waiting for transfers between devices, shifted(): lax.ppermute(value, axis, [(source, source + steps) for source in range(l...  7.91 us
    pallas_call x1, Pallas kernels, kv_final(): pl.pallas_call(functools.partial(kv_final_kernel, head_dim=head_dim), gri...  5.53 us
  transfers between devices with their start and end apart: 8, of which 6 were waited for; matrix products, arithmetic and copies ran while one was open for 3% of the time, Pallas kernels for 42%

profile of v12, /device:TPU:0, one launch (start us, length us, event | category | flops | bytes accessed | tf_op | source)
XLA Modules:
  0.0 145.4 jit_solution(5967426740293556096)
XLA Ops:
  0.6 1.7 %fusion.1 = (bf16[1024,256]{1,0:T(8,128)(2,1)S(1)}, bf16[1024,256]{1,0:T(8,128)(2,1)S(1)}, bf16[1024,256]{1,0:T(8,128)(2,1)S(1)}, bf16[1024,256]{1,0:T(8,128)(2,1)S(1)}) fusion(bf16[1024,512]{1,0:T(8,128)(2,1)} %raw_ref.3, bf16[1024,512]{1,0:T(8,128)(2,1)} %v_ref.7), kind=kLoop, calls=%fused_computation.13 | loop fusion | bytes 4194304 | tf_op jit(solution)/shard_map/slice | solution.py:447
  2.4 5.9 %collective-permute-start = (bf16[1024,512]{1,0:T(8,128)(2,1)S(1)}, bf16[1024,512]{1,0:T(8,128)(2,1)}, u32[]{:S(2)}, u32[]{:S(2)}) collective-permute-start(bf16[1024,512]{1,0:T(8,128)(2,1)S(1)} %pad_maximum_fusion.1), channel_id=1, source_target_pairs={{0,4},{4,8},{8,12},{12,16},{16,20},{20,24},{24,28},{1,5},{5,9},{9,... | collective-permute-start | bytes 3145736 | tf_op jit(solution)/shard_map/ppermute | solution.py:22
  8.6 1.0 copy.26.qdoc_ref
  10.3 11.4 %shard_map.110 = (f32[8192,1]{1,0:T(8,128)}, f32[8192,128]{1,0:T(8,128)}) custom-call(s32[1024,1]{1,0:T(8,128)} %copy.26.qdoc_ref, s32[1,2048]{1,0:T(1,128)} %bitcast.13, bf16[1024,1024]{1,0:T(8,128)(2,1)} %raw_ref.2, bf16[1024,512]{1,0:T(8,128)(2,1)} %raw_ref.3, bf16[1024,512]{1,0:T(8,128)(2,1)} %v_ref.7, f32[1,128]{1,0:T(1,128)} %bitcast.20, f32[1,128]{1,0:T(1,128)} %bitcast.26), custom_call_target="tpu_custom_call" | custom-call | flops 2684354560 | bytes 8421376 | tf_op jit(solution)/shard_map/pallas_call | solution.py:326
  21.8 7.9 %collective-permute-done.hk_ref.hv_ref = bf16[1024,512]{1,0:T(8,128)(2,1)} collective-permute-done((bf16[1024,512]{1,0:T(8,128)(2,1)S(1)}, bf16[1024,512]{1,0:T(8,128)(2,1)}, u32[]{:S(2)}, u32[]{:S(2)}) %collective-permute-start) | collective-permute-done | bytes 1048608 | tf_op jit(solution)/shard_map/ppermute | solution.py:22
  29.7 4.5 %collective-permute-start.1 = (bf16[1024,512]{1,0:T(8,128)(2,1)S(1)}, bf16[1024,512]{1,0:T(8,128)(2,1)S(1)}, u32[]{:S(2)}, u32[]{:S(2)}) collective-permute-start(bf16[1024,512]{1,0:T(8,128)(2,1)S(1)} %pad_maximum_fusion), channel_id=1, source_target_pairs={{0,4},{4,8},{8,12},{12,16},{16,20},{20,24},{24,28},{1,5},{5,9},{9,... | collective-permute-start | bytes 3145736 | tf_op jit(solution)/shard_map/ppermute | solution.py:22
  34.2 22.7 %shard_map.111 = (f32[1024,1024]{1,0:T(8,128)}, bf16[1024,1024]{1,0:T(8,128)(2,1)}, f32[8192,1]{1,0:T(8,128)}, f32[8192,1]{1,0:T(8,128)}, f32[2,1,128]{2,1,0:T(1,128)}) custom-call(s32[1024,1]{1,0:T(8,128)} %copy.26.qdoc_ref, s32[1,2048]{1,0:T(1,128)} %bitcast.14, bf16[1024,1024]{1,0:T(8,128)(2,1)} %raw_ref.2, bf16[1024,1024]{1,0:T(8,128)(2,1)} %do_ref.5, ...), custom_call_target="tpu_custom_call" | custom-call | flops 6039797760 | bytes 7340032 | tf_op jit(solution)/shard_map/pallas_call | solution.py:358
  56.9 1.0 copy-done
  57.9 23.0 %shard_map.112 = (f32[1024,1024]{1,0:T(8,128)}, bf16[1024,1024]{1,0:T(8,128)(2,1)}, f32[8192,1]{1,0:T(8,128)}, f32[8192,1]{1,0:T(8,128)}, f32[2,1,128]{2,1,0:T(1,128)}) custom-call(s32[1024,1]{1,0:T(8,128)} %copy.26.qdoc_ref, s32[1,2048]{1,0:T(1,128)} %bitcast.15, ...), custom_call_target="tpu_custom_call", output_to_operand_aliasing={{0}: (12, {}), {1}: (13, {}), {2}: (14, {}), {3}: (15, {})} | custom-call | flops 6039797760 | bytes 7340032 | tf_op jit(solution)/shard_map/pallas_call | solution.py:358
  80.9 1.3 collective-permute-start.2
  82.2 26.3 %shard_map.113 = (bf16[1024,1024]{1,0:T(8,128)(2,1)}, f32[4,1,128]{2,1,0:T(1,128)}, f32[4,1,128]{2,1,0:T(1,128)}, f32[1024,512]{1,0:T(8,128)}, f32[1024,512]{1,0:T(8,128)}) custom-call(s32[1024,1]{1,0:T(8,128)} %copy.26.qdoc_ref, s32[1,2048]{1,0:T(1,128)} %bitcast.16, bf16[1024,1024]{1,0:T(8,128)(2,1)} %do_ref.5, bf16[1024,512]{1,0:T(8,128)(2,1)} %v_ref.7, ...), custom_call_target="tpu_custom_call" | custom-call | flops 6710886400 | bytes 18874368 | tf_op jit(solution)/shard_map/pallas_call | solution.py:403
  108.5 0.7 reduce_sum.56
  109.2 0.7 reduce_sum.57
  110.0 1.1 collective-permute-done.3
  111.2 1.6 %collective-permute-start.4 = (f32[2,128]{1,0:T(2,128)S(1)}, f32[2,128]{1,0:T(2,128)S(1)}, u32[]{:S(2)}, u32[]{:S(2)}) collective-permute-start(f32[2,128]{1,0:T(2,128)S(1)} %fusion), channel_id=1, source_target_pairs={{0,2},{1,3},{2,0},{3,1},{4,6},{5,7},{6,4},{7,5},{8,10},{9,11},{10,... | collective-permute-start | bytes 3080 | tf_op jit(solution)/shard_map/ppermute | solution.py:44
  112.8 2.1 %collective-permute-done.4 = f32[2,128]{1,0:T(2,128)S(1)} collective-permute-done((f32[2,128]{1,0:T(2,128)S(1)}, f32[2,128]{1,0:T(2,128)S(1)}, u32[]{:S(2)}, u32[]{:S(2)}) %collective-permute-start.4) | collective-permute-done | bytes 1056 | tf_op jit(solution)/shard_map/ppermute | solution.py:44
  114.9 3.1 %collective-permute-start.5 = (f32[2,128]{1,0:T(2,128)S(1)}, f32[2,128]{1,0:T(2,128)S(1)}, u32[]{:S(2)}, u32[]{:S(2)}) collective-permute-start(f32[2,128]{1,0:T(2,128)S(1)} %fusion.3), channel_id=1, source_target_pairs={{0,4},{4,0},{8,12},{12,8},{16,20},{20,16},{24,28},{28,24},{1,5},{5... | collective-permute-start | bytes 3080 | tf_op jit(solution)/shard_map/ppermute | solution.py:44
  117.9 12.0 %collective-permute-done.5 = f32[2,128]{1,0:T(2,128)S(1)} collective-permute-done((f32[2,128]{1,0:T(2,128)S(1)}, f32[2,128]{1,0:T(2,128)S(1)}, u32[]{:S(2)}, u32[]{:S(2)}) %collective-permute-start.5) | collective-permute-done | bytes 1056 | tf_op jit(solution)/shard_map/ppermute | solution.py:44
  129.9 1.9 %collective-permute-start.6 = (f32[2,128]{1,0:T(2,128)S(1)}, f32[2,128]{1,0:T(2,128)S(1)}, u32[]{:S(2)}, u32[]{:S(2)}) collective-permute-start(f32[2,128]{1,0:T(2,128)S(1)} %add.69), channel_id=1, source_target_pairs={{0,8},{4,12},{8,0},{12,4},{16,24},{20,28},{24,16},{28,20},{1,9},{5... | collective-permute-start | bytes 3080 | tf_op jit(solution)/shard_map/ppermute | solution.py:44
  131.8 1.7 %collective-permute-done.6 = f32[2,128]{1,0:T(2,128)S(1)} collective-permute-done((f32[2,128]{1,0:T(2,128)S(1)}, f32[2,128]{1,0:T(2,128)S(1)}, u32[]{:S(2)}, u32[]{:S(2)}) %collective-permute-start.6) | collective-permute-done | bytes 1056 | tf_op jit(solution)/shard_map/ppermute | solution.py:44
  133.5 2.9 %collective-permute-start.7 = (f32[2,128]{1,0:T(2,128)S(1)}, f32[2,128]{1,0:T(2,128)S(1)}, u32[]{:S(2)}, u32[]{:S(2)}) collective-permute-start(f32[2,128]{1,0:T(2,128)S(1)} %add.70), channel_id=1, source_target_pairs={{0,16},{4,20},{8,24},{12,28},{16,0},{20,4},{24,8},{28,12},{1,17},{... | collective-permute-start | bytes 3080 | tf_op jit(solution)/shard_map/ppermute | solution.py:44
  136.4 1.6 %collective-permute-done.7 = f32[2,128]{1,0:T(2,128)S(1)} collective-permute-done((f32[2,128]{1,0:T(2,128)S(1)}, f32[2,128]{1,0:T(2,128)S(1)}, u32[]{:S(2)}, u32[]{:S(2)}) %collective-permute-start.7) | collective-permute-done | bytes 1056 | tf_op jit(solution)/shard_map/ppermute | solution.py:44
  138.5 1.3 copy-done.1
  139.9 5.5 %shard_map.114 = (bf16[1024,512]{1,0:T(8,128)(2,1)}, bf16[1024,512]{1,0:T(8,128)(2,1)}, f32[4,1,128]{2,1,0:T(1,128)}) custom-call(f32[1024,512]{1,0:T(8,128)} %get-tuple-element.38.dk_ref, f32[1024,512]{1,0:T(8,128)} %get-tuple-element.39.dv_ref, bf16[1024,1024]{1,0:T(8,128)(2,1)} %copy-done.1, bf16[1024,512]{1,0:T(8,128)(2,1)} %raw_ref.3, f32[1,128]{1,0:T(1,128)} %bitcast.24), custom_call_target="tpu_custom_call" | custom-call | tf_op jit(solution)/shard_map/pallas_call | solution.py:285
  (30 shorter events, 1.8 us)
Async XLA Ops:
  2.3 6.0 %copy-start.4 = (s32[16]{0:T(128)S(1)}, s32[16]{0:T(128)}, u32[]{:S(2)}) copy-start(s32[16]{0:T(128)} %param.13) | copy-start | bytes 196
  2.4 27.3 %collective-permute-start = (bf16[1024,512]{1,0:T(8,128)(2,1)S(1)}, bf16[1024,512]{1,0:T(8,128)(2,1)}, u32[]{:S(2)}, u32[]{:S(2)}) collective-permute-start(bf16[1024,512]{1,0:T(8,128)(2,1)S(1)} %pad_maximum_fusion.1), channel_id=1, source_target_pairs={{0,4},{4,8},{8,12},{12,16},{16,20},{20,24},{24,28},{1,5},{5,9},{9,... | collective-permute-start | bytes 3145736 | tf_op jit(solution)/shard_map/ppermute | solution.py:22
  29.7 27.3 %collective-permute-start.1 = (bf16[1024,512]{1,0:T(8,128)(2,1)S(1)}, bf16[1024,512]{1,0:T(8,128)(2,1)S(1)}, u32[]{:S(2)}, u32[]{:S(2)}) collective-permute-start(bf16[1024,512]{1,0:T(8,128)(2,1)S(1)} %pad_maximum_fusion), channel_id=1, source_target_pairs={{0,4},{4,8},{8,12},{12,16},{16,20},{20,24},{24,28},{1,5},{5,9},{9,... | collective-permute-start | bytes 3145736 | tf_op jit(solution)/shard_map/ppermute | solution.py:22
  56.9 1.0 copy-start
  57.9 24.3 %copy-start.3 = (f32[2,1,128]{2,1,0:T(1,128)S(1)}, f32[2,1,128]{2,1,0:T(1,128)}, u32[]{:S(2)}) copy-start(f32[2,1,128]{2,1,0:T(1,128)} %get-tuple-element.45) | copy-start | bytes 3076
  80.9 57.6 %collective-permute-start.2 = (bf16[1024,1024]{1,0:T(8,128)(2,1)}, bf16[1024,1024]{1,0:T(8,128)(2,1)S(1)}, u32[]{:S(2)}, u32[]{:S(2)}) collective-permute-start(bf16[1024,1024]{1,0:T(8,128)(2,1)} %get-tuple-element.40), channel_id=1, source_target_pairs={{4,0},{8,4},{12,8},{16,12},{20,16},{24,20},{28,24},{5,1},{9,5},{13... | collective-permute-start | bytes 6291464 | tf_op jit(solution)/shard_map/ppermute | solution.py:22
  82.2 27.7 %copy-start.2 = (f32[2,1,128]{2,1,0:T(1,128)S(1)}, f32[2,1,128]{2,1,0:T(1,128)}, u32[]{:S(2)}) copy-start(f32[2,1,128]{2,1,0:T(1,128)} %get-tuple-element.46) | copy-start | bytes 3076
  110.0 1.2 collective-permute-start.3
  111.2 3.6 %collective-permute-start.4 = (f32[2,128]{1,0:T(2,128)S(1)}, f32[2,128]{1,0:T(2,128)S(1)}, u32[]{:S(2)}, u32[]{:S(2)}) collective-permute-start(f32[2,128]{1,0:T(2,128)S(1)} %fusion), channel_id=1, source_target_pairs={{0,2},{1,3},{2,0},{3,1},{4,6},{5,7},{6,4},{7,5},{8,10},{9,11},{10,... | collective-permute-start | bytes 3080 | tf_op jit(solution)/shard_map/ppermute | solution.py:44
  114.9 15.1 %collective-permute-start.5 = (f32[2,128]{1,0:T(2,128)S(1)}, f32[2,128]{1,0:T(2,128)S(1)}, u32[]{:S(2)}, u32[]{:S(2)}) collective-permute-start(f32[2,128]{1,0:T(2,128)S(1)} %fusion.3), channel_id=1, source_target_pairs={{0,4},{4,0},{8,12},{12,8},{16,20},{20,16},{24,28},{28,24},{1,5},{5... | collective-permute-start | bytes 3080 | tf_op jit(solution)/shard_map/ppermute | solution.py:44
  129.9 3.6 %collective-permute-start.6 = (f32[2,128]{1,0:T(2,128)S(1)}, f32[2,128]{1,0:T(2,128)S(1)}, u32[]{:S(2)}, u32[]{:S(2)}) collective-permute-start(f32[2,128]{1,0:T(2,128)S(1)} %add.69), channel_id=1, source_target_pairs={{0,8},{4,12},{8,0},{12,4},{16,24},{20,28},{24,16},{28,20},{1,9},{5... | collective-permute-start | bytes 3080 | tf_op jit(solution)/shard_map/ppermute | solution.py:44
  133.5 4.5 %collective-permute-start.7 = (f32[2,128]{1,0:T(2,128)S(1)}, f32[2,128]{1,0:T(2,128)S(1)}, u32[]{:S(2)}, u32[]{:S(2)}) collective-permute-start(f32[2,128]{1,0:T(2,128)S(1)} %add.70), channel_id=1, source_target_pairs={{0,16},{4,20},{8,24},{12,28},{16,0},{20,4},{24,8},{28,12},{1,17},{... | collective-permute-start | bytes 3080 | tf_op jit(solution)/shard_map/ppermute | solution.py:44
  138.5 1.3 copy-start.1

commit v13 on v10

--- a/solution.py
+++ b/solution.py
@@ -230,9 +230,7 @@
     kpart_ref[...] = jnp.sum(dk_ref[...] * key_hat, axis=0, keepdims=True).reshape(kpart_ref.shape)
 
 
-def kv_final_kernel(dk_ref, dv_ref, back_ref, raw_ref, gain_ref, kgrad_ref, vgrad_ref, kgain_ref, *, head_dim):
-    tok_rows = dk_ref.shape[0]
-    lead = tok_rows - WINDOW
+def kv_final_kernel(dk_ref, dv_ref, back_ref, raw_ref, gain_ref, kgrad_ref, vgrad_ref, kgain_ref, *, head_dim, lead):
     back = back_ref[...].astype(jnp.float32)
     dk = dk_ref[...]
     dv = dv_ref[...]
@@ -251,24 +249,28 @@
 def kv_final(dk_own, dv_own, back, key_raw, key_gain, key_heads, head_dim):
     tok_rows = dk_own.shape[0]
     kv_cols = key_heads * head_dim
-    col_spec = pl.BlockSpec((tok_rows, head_dim), lambda h: (0, h))
+    splits = 2 if tok_rows == WINDOW and tok_rows % (2 * BLOCK) == 0 else 1
+    rows = tok_rows // splits
+    col_spec = pl.BlockSpec((rows, head_dim), lambda h, r: (r, h))
+    back_rows = WINDOW // splits
     return pl.pallas_call(
-        functools.partial(kv_final_kernel, head_dim=head_dim),
-        grid=(key_heads,),
+        functools.partial(kv_final_kernel, head_dim=head_dim, lead=tok_rows - WINDOW),
+        grid=(key_heads, splits),
         in_specs=[
             col_spec,
             col_spec,
-            pl.BlockSpec((WINDOW, 2 * head_dim), lambda h: (0, h)),
+            pl.BlockSpec((back_rows, 2 * head_dim), lambda h, r: (r, h)),
             col_spec,
-            pl.BlockSpec((1, head_dim), lambda h: (0, 0)),
+            pl.BlockSpec((1, head_dim), lambda h, r: (0, 0)),
         ],
-        out_specs=[col_spec, col_spec, pl.BlockSpec((1, 1, head_dim), lambda h: (h, 0, 0))],
+        out_specs=[col_spec, col_spec,
+                   pl.BlockSpec((1, 1, head_dim), lambda h, r, splits=splits: (h * splits + r, 0, 0))],
         out_shape=[
             jax.ShapeDtypeStruct((tok_rows, kv_cols), jnp.bfloat16),
             jax.ShapeDtypeStruct((tok_rows, kv_cols), jnp.bfloat16),
-            jax.ShapeDtypeStruct((key_heads, 1, head_dim), jnp.float32),
+            jax.ShapeDtypeStruct((key_heads * splits, 1, head_dim), jnp.float32),
         ],
-        compiler_params=pltpu.CompilerParams(dimension_semantics=("arbitrary",)),
+        compiler_params=pltpu.CompilerParams(dimension_semantics=("arbitrary", "arbitrary")),
     )(dk_own, dv_own, back, key_raw, key_gain.reshape(1, head_dim))
 
 

time: 145 us -> 146 us (level)
  Pallas kernels: 74.4 us -> 76.1 us
    pallas_call x1, Pallas kernels: 5.53 us -> 7.24 us  [kv_final(): pl.pallas_call(functools.partial(kv_final_kernel, head_dim=head_dim, lead...]
  transfers between devices with their start and end apart: 8 -> 8, of which waited for: 6 -> 6; matrix products, arithmetic and copies ran while one was open for 3% -> 3% of each run, Pallas kernels for 33% -> 32%
where the time goes in v13:
time: 146 us
  Pallas kernels  76.1 us (52%)
  waiting for transfers between devices  40.3 us (28%)
  starting transfers between devices  20.6 us (14%)
  local copies, waits for them, and re-layouts  5.62 us (4%)
  other arithmetic  2.5 us (2%)
    pallas_call x2, Pallas kernels, attention_grads(): pl.pallas_call(functools.partial(halo_kernel, group=group, head_dim=head_...  42.6 us
    pallas_call x1, Pallas kernels, attention_grads(): pl.pallas_call(functools.partial(own_kernel, group=group, head_dim=head_d...  26.3 us
    ppermute x3, waiting for transfers between devices, shifted(): lax.ppermute(value, axis, [(source, source + steps) for source in range(l...  21.3 us
    ppermute x5, waiting for transfers between devices, butterfly_sum(): shifted_parts.append(lax.ppermute(value, axis, pairs))  19.1 us
    ppermute x3, starting transfers between devices, shifted(): lax.ppermute(value, axis, [(source, source + steps) for source in range(l...  11.8 us
    ppermute x5, starting transfers between devices, butterfly_sum(): shifted_parts.append(lax.ppermute(value, axis, pairs))  8.88 us
    pallas_call x1, Pallas kernels, kv_final(): pl.pallas_call(functools.partial(kv_final_kernel, head_dim=head_dim, lead...  7.24 us
  transfers between devices with their start and end apart: 8, of which 6 were waited for; matrix products, arithmetic and copies ran while one was open for 3% of the time, Pallas kernels for 32%

profile of v13, /device:TPU:0, one launch (start us, length us, event | category | flops | bytes accessed | tf_op | source)
XLA Modules:
  0.0 146.0 jit_solution(14156224253137463071)
XLA Ops:
  0.6 1.7 %fusion.1 = (bf16[1024,256]{1,0:T(8,128)(2,1)S(1)}, bf16[1024,256]{1,0:T(8,128)(2,1)S(1)}, bf16[1024,256]{1,0:T(8,128)(2,1)S(1)}, bf16[1024,256]{1,0:T(8,128)(2,1)S(1)}) fusion(bf16[1024,512]{1,0:T(8,128)(2,1)} %raw_ref.3, bf16[1024,512]{1,0:T(8,128)(2,1)} %v_ref.5), kind=kLoop, calls=%fused_computation.13 | loop fusion | bytes 4194304 | tf_op jit(solution)/shard_map/slice | solution.py:392
  2.4 5.9 %collective-permute-start = (bf16[1024,512]{1,0:T(8,128)(2,1)S(1)}, bf16[1024,512]{1,0:T(8,128)(2,1)}, u32[]{:S(2)}, u32[]{:S(2)}) collective-permute-start(bf16[1024,512]{1,0:T(8,128)(2,1)S(1)} %pad_maximum_fusion.1), channel_id=1, source_target_pairs={{0,4},{4,8},{8,12},{12,16},{16,20},{20,24},{24,28},{1,5},{5,9},{9,... | collective-permute-start | bytes 3145736 | tf_op jit(solution)/shard_map/ppermute | solution.py:22
  8.4 21.3 %collective-permute-done.hk_ref.hv_ref = bf16[1024,512]{1,0:T(8,128)(2,1)} collective-permute-done((bf16[1024,512]{1,0:T(8,128)(2,1)S(1)}, bf16[1024,512]{1,0:T(8,128)(2,1)}, u32[]{:S(2)}, u32[]{:S(2)}) %collective-permute-start) | collective-permute-done | bytes 1048608 | tf_op jit(solution)/shard_map/ppermute | solution.py:22
  29.7 4.5 %collective-permute-start.1 = (bf16[1024,512]{1,0:T(8,128)(2,1)S(1)}, bf16[1024,512]{1,0:T(8,128)(2,1)S(1)}, u32[]{:S(2)}, u32[]{:S(2)}) collective-permute-start(bf16[1024,512]{1,0:T(8,128)(2,1)S(1)} %pad_maximum_fusion), channel_id=1, source_target_pairs={{0,4},{4,8},{8,12},{12,16},{16,20},{20,24},{24,28},{1,5},{5,9},{9,... | collective-permute-start | bytes 3145736 | tf_op jit(solution)/shard_map/ppermute | solution.py:22
  34.6 1.0 copy.24.qdoc_ref
  35.6 0.6 pad_add_fusion
  36.2 21.1 %shard_map.110 = (f32[1024,1024]{1,0:T(8,128)}, bf16[1024,1024]{1,0:T(8,128)(2,1)}, f32[8192,1]{1,0:T(8,128)}, f32[8192,1]{1,0:T(8,128)}, f32[2,1,128]{2,1,0:T(1,128)}) custom-call(s32[1024,1]{1,0:T(8,128)} %copy.24.qdoc_ref, s32[1,2048]{1,0:T(1,128)} %bitcast.13, bf16[1024,1024]{1,0:T(8,128)(2,1)} %raw_ref.2, bf16[1024,1024]{1,0:T(8,128)(2,1)} %do_ref.5, ...), custom_call_target="tpu_custom_call" | custom-call | flops 6039797760 | bytes 7340032 | tf_op jit(solution)/shard_map/pallas_call | solution.py:305
  57.4 1.0 copy-done
  58.3 21.4 %shard_map.111 = (f32[1024,1024]{1,0:T(8,128)}, bf16[1024,1024]{1,0:T(8,128)(2,1)}, f32[8192,1]{1,0:T(8,128)}, f32[8192,1]{1,0:T(8,128)}, f32[2,1,128]{2,1,0:T(1,128)}) custom-call(s32[1024,1]{1,0:T(8,128)} %copy.24.qdoc_ref, s32[1,2048]{1,0:T(1,128)} %bitcast.14, ...), custom_call_target="tpu_custom_call", output_to_operand_aliasing={{0}: (10, {}), {1}: (11, {}), {2}: (12, {}), {3}: (13, {})} | custom-call | flops 6039797760 | bytes 7340032 | tf_op jit(solution)/shard_map/pallas_call | solution.py:305
  79.8 1.3 collective-permute-start.2
  81.1 26.3 %shard_map.112 = (bf16[1024,1024]{1,0:T(8,128)(2,1)}, f32[4,1,128]{2,1,0:T(1,128)}, f32[4,1,128]{2,1,0:T(1,128)}, f32[1024,512]{1,0:T(8,128)}, f32[1024,512]{1,0:T(8,128)}) custom-call(s32[1024,1]{1,0:T(8,128)} %copy.24.qdoc_ref, s32[1,2048]{1,0:T(1,128)} %bitcast.15, bf16[1024,1024]{1,0:T(8,128)(2,1)} %do_ref.5, bf16[1024,512]{1,0:T(8,128)(2,1)} %v_ref.5, ...), custom_call_target="tpu_custom_call" | custom-call | flops 6710886400 | bytes 18874368 | tf_op jit(solution)/shard_map/pallas_call | solution.py:348
  107.4 0.7 reduce_sum.56
  108.1 0.7 reduce_sum.57
  109.0 1.1 collective-permute-done.3
  110.1 1.6 %collective-permute-start.4 = (f32[2,128]{1,0:T(2,128)S(1)}, f32[2,128]{1,0:T(2,128)S(1)}, u32[]{:S(2)}, u32[]{:S(2)}) collective-permute-start(f32[2,128]{1,0:T(2,128)S(1)} %fusion), channel_id=1, source_target_pairs={{0,2},{1,3},{2,0},{3,1},{4,6},{5,7},{6,4},{7,5},{8,10},{9,11},{10,... | collective-permute-start | bytes 3080 | tf_op jit(solution)/shard_map/ppermute | solution.py:44
  111.7 2.1 %collective-permute-done.4 = f32[2,128]{1,0:T(2,128)S(1)} collective-permute-done((f32[2,128]{1,0:T(2,128)S(1)}, f32[2,128]{1,0:T(2,128)S(1)}, u32[]{:S(2)}, u32[]{:S(2)}) %collective-permute-start.4) | collective-permute-done | bytes 1056 | tf_op jit(solution)/shard_map/ppermute | solution.py:44
  113.8 3.1 %collective-permute-start.5 = (f32[2,128]{1,0:T(2,128)S(1)}, f32[2,128]{1,0:T(2,128)S(1)}, u32[]{:S(2)}, u32[]{:S(2)}) collective-permute-start(f32[2,128]{1,0:T(2,128)S(1)} %fusion.3), channel_id=1, source_target_pairs={{0,4},{4,0},{8,12},{12,8},{16,20},{20,16},{24,28},{28,24},{1,5},{5... | collective-permute-start | bytes 3080 | tf_op jit(solution)/shard_map/ppermute | solution.py:44
  116.8 12.0 %collective-permute-done.5 = f32[2,128]{1,0:T(2,128)S(1)} collective-permute-done((f32[2,128]{1,0:T(2,128)S(1)}, f32[2,128]{1,0:T(2,128)S(1)}, u32[]{:S(2)}, u32[]{:S(2)}) %collective-permute-start.5) | collective-permute-done | bytes 1056 | tf_op jit(solution)/shard_map/ppermute | solution.py:44
  128.8 1.6 %collective-permute-start.6 = (f32[2,128]{1,0:T(2,128)S(1)}, f32[2,128]{1,0:T(2,128)S(1)}, u32[]{:S(2)}, u32[]{:S(2)}) collective-permute-start(f32[2,128]{1,0:T(2,128)S(1)} %add.69), channel_id=1, source_target_pairs={{0,8},{4,12},{8,0},{12,4},{16,24},{20,28},{24,16},{28,20},{1,9},{5... | collective-permute-start | bytes 3080 | tf_op jit(solution)/shard_map/ppermute | solution.py:44
  130.4 2.0 %collective-permute-done.6 = f32[2,128]{1,0:T(2,128)S(1)} collective-permute-done((f32[2,128]{1,0:T(2,128)S(1)}, f32[2,128]{1,0:T(2,128)S(1)}, u32[]{:S(2)}, u32[]{:S(2)}) %collective-permute-start.6) | collective-permute-done | bytes 1056 | tf_op jit(solution)/shard_map/ppermute | solution.py:44
  132.4 2.6 %collective-permute-start.7 = (f32[2,128]{1,0:T(2,128)S(1)}, f32[2,128]{1,0:T(2,128)S(1)}, u32[]{:S(2)}, u32[]{:S(2)}) collective-permute-start(f32[2,128]{1,0:T(2,128)S(1)} %add.70), channel_id=1, source_target_pairs={{0,16},{4,20},{8,24},{12,28},{16,0},{20,4},{24,8},{28,12},{1,17},{... | collective-permute-start | bytes 3080 | tf_op jit(solution)/shard_map/ppermute | solution.py:44
  135.0 1.9 %collective-permute-done.7 = f32[2,128]{1,0:T(2,128)S(1)} collective-permute-done((f32[2,128]{1,0:T(2,128)S(1)}, f32[2,128]{1,0:T(2,128)S(1)}, u32[]{:S(2)}, u32[]{:S(2)}) %collective-permute-start.7) | collective-permute-done | bytes 1056 | tf_op jit(solution)/shard_map/ppermute | solution.py:44
  137.4 1.4 copy-done.1
  138.8 7.2 %shard_map.113 = (bf16[1024,512]{1,0:T(8,128)(2,1)}, bf16[1024,512]{1,0:T(8,128)(2,1)}, f32[8,1,128]{2,1,0:T(1,128)}) custom-call(f32[1024,512]{1,0:T(8,128)} %get-tuple-element.32.dk_ref, f32[1024,512]{1,0:T(8,128)} %get-tuple-element.33.dv_ref, bf16[1024,1024]{1,0:T(8,128)(2,1)} %copy-done.1, bf16[1024,512]{1,0:T(8,128)(2,1)} %raw_ref.3, f32[1,128]{1,0:T(1,128)} %bitcast.22), custom_call_target="tpu_custom_call" | custom-call | tf_op jit(solution)/shard_map/pallas_call | solution.py:256
  (29 shorter events, 1.2 us)
Async XLA Ops:
  2.3 31.9 %copy-start.4 = (s32[16]{0:T(128)S(1)}, s32[16]{0:T(128)}, u32[]{:S(2)}) copy-start(s32[16]{0:T(128)} %param.13) | copy-start | bytes 196
  2.4 27.3 %collective-permute-start = (bf16[1024,512]{1,0:T(8,128)(2,1)S(1)}, bf16[1024,512]{1,0:T(8,128)(2,1)}, u32[]{:S(2)}, u32[]{:S(2)}) collective-permute-start(bf16[1024,512]{1,0:T(8,128)(2,1)S(1)} %pad_maximum_fusion.1), channel_id=1, source_target_pairs={{0,4},{4,8},{8,12},{12,16},{16,20},{20,24},{24,28},{1,5},{5,9},{9,... | collective-permute-start | bytes 3145736 | tf_op jit(solution)/shard_map/ppermute | solution.py:22
  29.7 27.7 %collective-permute-start.1 = (bf16[1024,512]{1,0:T(8,128)(2,1)S(1)}, bf16[1024,512]{1,0:T(8,128)(2,1)S(1)}, u32[]{:S(2)}, u32[]{:S(2)}) collective-permute-start(bf16[1024,512]{1,0:T(8,128)(2,1)S(1)} %pad_maximum_fusion), channel_id=1, source_target_pairs={{0,4},{4,8},{8,12},{12,16},{16,20},{20,24},{24,28},{1,5},{5,9},{9,... | collective-permute-start | bytes 3145736 | tf_op jit(solution)/shard_map/ppermute | solution.py:22
  57.4 1.0 copy-start
  58.3 22.8 %copy-start.3 = (f32[2,1,128]{2,1,0:T(1,128)S(1)}, f32[2,1,128]{2,1,0:T(1,128)}, u32[]{:S(2)}) copy-start(f32[2,1,128]{2,1,0:T(1,128)} %get-tuple-element.39) | copy-start | bytes 3076
  79.8 57.6 %collective-permute-start.2 = (bf16[1024,1024]{1,0:T(8,128)(2,1)}, bf16[1024,1024]{1,0:T(8,128)(2,1)S(1)}, u32[]{:S(2)}, u32[]{:S(2)}) collective-permute-start(bf16[1024,1024]{1,0:T(8,128)(2,1)} %get-tuple-element.34), channel_id=1, source_target_pairs={{4,0},{8,4},{12,8},{16,12},{20,16},{24,20},{28,24},{5,1},{9,5},{13... | collective-permute-start | bytes 6291464 | tf_op jit(solution)/shard_map/ppermute | solution.py:22
  81.1 27.7 %copy-start.2 = (f32[2,1,128]{2,1,0:T(1,128)S(1)}, f32[2,1,128]{2,1,0:T(1,128)}, u32[]{:S(2)}) copy-start(f32[2,1,128]{2,1,0:T(1,128)} %get-tuple-element.40) | copy-start | bytes 3076
  108.9 1.2 collective-permute-start.3
  110.1 3.6 %collective-permute-start.4 = (f32[2,128]{1,0:T(2,128)S(1)}, f32[2,128]{1,0:T(2,128)S(1)}, u32[]{:S(2)}, u32[]{:S(2)}) collective-permute-start(f32[2,128]{1,0:T(2,128)S(1)} %fusion), channel_id=1, source_target_pairs={{0,2},{1,3},{2,0},{3,1},{4,6},{5,7},{6,4},{7,5},{8,10},{9,11},{10,... | collective-permute-start | bytes 3080 | tf_op jit(solution)/shard_map/ppermute | solution.py:44
  113.8 15.0 %collective-permute-start.5 = (f32[2,128]{1,0:T(2,128)S(1)}, f32[2,128]{1,0:T(2,128)S(1)}, u32[]{:S(2)}, u32[]{:S(2)}) collective-permute-start(f32[2,128]{1,0:T(2,128)S(1)} %fusion.3), channel_id=1, source_target_pairs={{0,4},{4,0},{8,12},{12,8},{16,20},{20,16},{24,28},{28,24},{1,5},{5... | collective-permute-start | bytes 3080 | tf_op jit(solution)/shard_map/ppermute | solution.py:44
  128.8 3.6 %collective-permute-start.6 = (f32[2,128]{1,0:T(2,128)S(1)}, f32[2,128]{1,0:T(2,128)S(1)}, u32[]{:S(2)}, u32[]{:S(2)}) collective-permute-start(f32[2,128]{1,0:T(2,128)S(1)} %add.69), channel_id=1, source_target_pairs={{0,8},{4,12},{8,0},{12,4},{16,24},{20,28},{24,16},{28,20},{1,9},{5... | collective-permute-start | bytes 3080 | tf_op jit(solution)/shard_map/ppermute | solution.py:44
  132.4 4.5 %collective-permute-start.7 = (f32[2,128]{1,0:T(2,128)S(1)}, f32[2,128]{1,0:T(2,128)S(1)}, u32[]{:S(2)}, u32[]{:S(2)}) collective-permute-start(f32[2,128]{1,0:T(2,128)S(1)} %add.70), channel_id=1, source_target_pairs={{0,16},{4,20},{8,24},{12,28},{16,0},{20,4},{24,8},{28,12},{1,17},{... | collective-permute-start | bytes 3080 | tf_op jit(solution)/shard_map/ppermute | solution.py:44
  137.4 1.4 copy-start.1

commit v14 on v10

--- a/solution.py
+++ b/solution.py
@@ -142,7 +142,6 @@
         q_first = qb * blk
         q_g = normed_stack(q_ref, qgain, group, head_dim, q_first)
         do_g = stacked(do_ref, group, head_dim, q_first)
-        masks = [tile_mask(qdoc_ref, kdoc_ref, q_first, t, group)[0] for t in range(n_tiles)]
         totals = jnp.zeros((gb, 1), jnp.float32)
         numer = jnp.zeros((gb, head_dim), jnp.float32)
         for t in range(n_tiles):
@@ -151,7 +150,7 @@
             scores = lax.dot_general(
                 q_g, k_tile, (((1,), (1,)), ((), ())), preferred_element_type=jnp.float32
             ) * scale
-            exp_s = jnp.where(masks[t], jnp.exp(scores), 0.0)
+            exp_s = jnp.where(tile_mask(qdoc_ref, kdoc_ref, q_first, t, group)[0], jnp.exp(scores), 0.0)
             totals = totals + jnp.sum(exp_s, axis=1, keepdims=True)
             numer = numer + jnp.dot(exp_s.astype(jnp.bfloat16), v_tile, preferred_element_type=jnp.float32)
         log_sums = jnp.log(totals)
@@ -163,7 +162,8 @@
         for t in range(n_halo - qb):
             k_first = q_first + t * blk
             k_tile, v_tile = key_tile(k_first)
-            dq_part, dk_part, dv_part = grad_tile(q_g, do_g, k_tile, v_tile, masks[t], log_sums, delta)
+            live = tile_mask(qdoc_ref, kdoc_ref, q_first, t, group)[0]
+            dq_part, dk_part, dv_part = grad_tile(q_g, do_g, k_tile, v_tile, live, log_sums, delta)
             dq = dq + dq_part
             dk_ref[k_first:k_first + blk, :] += dk_part
             dv_ref[k_first:k_first + blk, :] += dv_part

time: 145 us -> 145 us (level)
  no operation moved by 1% of the time
where the time goes in v14:
time: 145 us
  Pallas kernels  74.7 us (52%)
  waiting for transfers between devices  40.3 us (28%)
  starting transfers between devices  20.7 us (14%)
  local copies, waits for them, and re-layouts  5.62 us (4%)
  other arithmetic  2.5 us (2%)
    pallas_call x2, Pallas kernels, attention_grads(): pl.pallas_call(functools.partial(halo_kernel, group=group, head_dim=head_...  42.9 us
    pallas_call x1, Pallas kernels, attention_grads(): pl.pallas_call(functools.partial(own_kernel, group=group, head_dim=head_d...  26.3 us
    ppermute x3, waiting for transfers between devices, shifted(): lax.ppermute(value, axis, [(source, source + steps) for source in range(l...  21.3 us
    ppermute x5, waiting for transfers between devices, butterfly_sum(): shifted_parts.append(lax.ppermute(value, axis, pairs))  19.1 us
    ppermute x3, starting transfers between devices, shifted(): lax.ppermute(value, axis, [(source, source + steps) for source in range(l...  11.8 us
    ppermute x5, starting transfers between devices, butterfly_sum(): shifted_parts.append(lax.ppermute(value, axis, pairs))  8.91 us
    pallas_call x1, Pallas kernels, kv_final(): pl.pallas_call(functools.partial(kv_final_kernel, head_dim=head_dim), gri...  5.53 us
  transfers between devices with their start and end apart: 8, of which 6 were waited for; matrix products, arithmetic and copies ran while one was open for 3% of the time, Pallas kernels for 33%

profile of v14, /device:TPU:0, one launch (start us, length us, event | category | flops | bytes accessed | tf_op | source)
XLA Modules:
  0.0 144.6 jit_solution(3725154435202929467)
XLA Ops:
  0.6 1.7 %fusion.1 = (bf16[1024,256]{1,0:T(8,128)(2,1)S(1)}, bf16[1024,256]{1,0:T(8,128)(2,1)S(1)}, bf16[1024,256]{1,0:T(8,128)(2,1)S(1)}, bf16[1024,256]{1,0:T(8,128)(2,1)S(1)}) fusion(bf16[1024,512]{1,0:T(8,128)(2,1)} %raw_ref.3, bf16[1024,512]{1,0:T(8,128)(2,1)} %v_ref.5), kind=kLoop, calls=%fused_computation.13 | loop fusion | bytes 4194304 | tf_op jit(solution)/shard_map/slice | solution.py:390
  2.4 5.9 %collective-permute-start = (bf16[1024,512]{1,0:T(8,128)(2,1)S(1)}, bf16[1024,512]{1,0:T(8,128)(2,1)}, u32[]{:S(2)}, u32[]{:S(2)}) collective-permute-start(bf16[1024,512]{1,0:T(8,128)(2,1)S(1)} %pad_maximum_fusion.1), channel_id=1, source_target_pairs={{0,4},{4,8},{8,12},{12,16},{16,20},{20,24},{24,28},{1,5},{5,9},{9,... | collective-permute-start | bytes 3145736 | tf_op jit(solution)/shard_map/ppermute | solution.py:22
  8.4 21.3 %collective-permute-done.hk_ref.hv_ref = bf16[1024,512]{1,0:T(8,128)(2,1)} collective-permute-done((bf16[1024,512]{1,0:T(8,128)(2,1)S(1)}, bf16[1024,512]{1,0:T(8,128)(2,1)}, u32[]{:S(2)}, u32[]{:S(2)}) %collective-permute-start) | collective-permute-done | bytes 1048608 | tf_op jit(solution)/shard_map/ppermute | solution.py:22
  29.7 4.5 %collective-permute-start.1 = (bf16[1024,512]{1,0:T(8,128)(2,1)S(1)}, bf16[1024,512]{1,0:T(8,128)(2,1)S(1)}, u32[]{:S(2)}, u32[]{:S(2)}) collective-permute-start(bf16[1024,512]{1,0:T(8,128)(2,1)S(1)} %pad_maximum_fusion), channel_id=1, source_target_pairs={{0,4},{4,8},{8,12},{12,16},{16,20},{20,24},{24,28},{1,5},{5,9},{9,... | collective-permute-start | bytes 3145736 | tf_op jit(solution)/shard_map/ppermute | solution.py:22
  34.6 1.0 copy.24.qdoc_ref
  35.6 0.6 pad_add_fusion
  36.2 21.3 %shard_map.110 = (f32[1024,1024]{1,0:T(8,128)}, bf16[1024,1024]{1,0:T(8,128)(2,1)}, f32[8192,1]{1,0:T(8,128)}, f32[8192,1]{1,0:T(8,128)}, f32[2,1,128]{2,1,0:T(1,128)}) custom-call(s32[1024,1]{1,0:T(8,128)} %copy.24.qdoc_ref, s32[1,2048]{1,0:T(1,128)} %bitcast.13, bf16[1024,1024]{1,0:T(8,128)(2,1)} %raw_ref.2, bf16[1024,1024]{1,0:T(8,128)(2,1)} %do_ref.5, ...), custom_call_target="tpu_custom_call" | custom-call | flops 6039797760 | bytes 7340032 | tf_op jit(solution)/shard_map/pallas_call | solution.py:303
  57.5 1.0 copy-done
  58.5 21.6 %shard_map.111 = (f32[1024,1024]{1,0:T(8,128)}, bf16[1024,1024]{1,0:T(8,128)(2,1)}, f32[8192,1]{1,0:T(8,128)}, f32[8192,1]{1,0:T(8,128)}, f32[2,1,128]{2,1,0:T(1,128)}) custom-call(s32[1024,1]{1,0:T(8,128)} %copy.24.qdoc_ref, s32[1,2048]{1,0:T(1,128)} %bitcast.14, ...), custom_call_target="tpu_custom_call", output_to_operand_aliasing={{0}: (10, {}), {1}: (11, {}), {2}: (12, {}), {3}: (13, {})} | custom-call | flops 6039797760 | bytes 7340032 | tf_op jit(solution)/shard_map/pallas_call | solution.py:303
  80.1 1.3 collective-permute-start.2
  81.5 26.3 %shard_map.112 = (bf16[1024,1024]{1,0:T(8,128)(2,1)}, f32[4,1,128]{2,1,0:T(1,128)}, f32[4,1,128]{2,1,0:T(1,128)}, f32[1024,512]{1,0:T(8,128)}, f32[1024,512]{1,0:T(8,128)}) custom-call(s32[1024,1]{1,0:T(8,128)} %copy.24.qdoc_ref, s32[1,2048]{1,0:T(1,128)} %bitcast.15, bf16[1024,1024]{1,0:T(8,128)(2,1)} %do_ref.5, bf16[1024,512]{1,0:T(8,128)(2,1)} %v_ref.5, ...), custom_call_target="tpu_custom_call" | custom-call | flops 6710886400 | bytes 18874368 | tf_op jit(solution)/shard_map/pallas_call | solution.py:346
  107.8 0.7 reduce_sum.56
  108.5 0.7 reduce_sum.57
  109.3 1.1 collective-permute-done.3
  110.5 1.6 %collective-permute-start.4 = (f32[2,128]{1,0:T(2,128)S(1)}, f32[2,128]{1,0:T(2,128)S(1)}, u32[]{:S(2)}, u32[]{:S(2)}) collective-permute-start(f32[2,128]{1,0:T(2,128)S(1)} %fusion), channel_id=1, source_target_pairs={{0,2},{1,3},{2,0},{3,1},{4,6},{5,7},{6,4},{7,5},{8,10},{9,11},{10,... | collective-permute-start | bytes 3080 | tf_op jit(solution)/shard_map/ppermute | solution.py:44
  112.0 2.1 %collective-permute-done.4 = f32[2,128]{1,0:T(2,128)S(1)} collective-permute-done((f32[2,128]{1,0:T(2,128)S(1)}, f32[2,128]{1,0:T(2,128)S(1)}, u32[]{:S(2)}, u32[]{:S(2)}) %collective-permute-start.4) | collective-permute-done | bytes 1056 | tf_op jit(solution)/shard_map/ppermute | solution.py:44
  114.1 3.1 %collective-permute-start.5 = (f32[2,128]{1,0:T(2,128)S(1)}, f32[2,128]{1,0:T(2,128)S(1)}, u32[]{:S(2)}, u32[]{:S(2)}) collective-permute-start(f32[2,128]{1,0:T(2,128)S(1)} %fusion.3), channel_id=1, source_target_pairs={{0,4},{4,0},{8,12},{12,8},{16,20},{20,16},{24,28},{28,24},{1,5},{5... | collective-permute-start | bytes 3080 | tf_op jit(solution)/shard_map/ppermute | solution.py:44
  117.2 12.0 %collective-permute-done.5 = f32[2,128]{1,0:T(2,128)S(1)} collective-permute-done((f32[2,128]{1,0:T(2,128)S(1)}, f32[2,128]{1,0:T(2,128)S(1)}, u32[]{:S(2)}, u32[]{:S(2)}) %collective-permute-start.5) | collective-permute-done | bytes 1056 | tf_op jit(solution)/shard_map/ppermute | solution.py:44
  129.2 1.6 %collective-permute-start.6 = (f32[2,128]{1,0:T(2,128)S(1)}, f32[2,128]{1,0:T(2,128)S(1)}, u32[]{:S(2)}, u32[]{:S(2)}) collective-permute-start(f32[2,128]{1,0:T(2,128)S(1)} %add.69), channel_id=1, source_target_pairs={{0,8},{4,12},{8,0},{12,4},{16,24},{20,28},{24,16},{28,20},{1,9},{5... | collective-permute-start | bytes 3080 | tf_op jit(solution)/shard_map/ppermute | solution.py:44
  130.8 2.0 %collective-permute-done.6 = f32[2,128]{1,0:T(2,128)S(1)} collective-permute-done((f32[2,128]{1,0:T(2,128)S(1)}, f32[2,128]{1,0:T(2,128)S(1)}, u32[]{:S(2)}, u32[]{:S(2)}) %collective-permute-start.6) | collective-permute-done | bytes 1056 | tf_op jit(solution)/shard_map/ppermute | solution.py:44
  132.7 2.6 %collective-permute-start.7 = (f32[2,128]{1,0:T(2,128)S(1)}, f32[2,128]{1,0:T(2,128)S(1)}, u32[]{:S(2)}, u32[]{:S(2)}) collective-permute-start(f32[2,128]{1,0:T(2,128)S(1)} %add.70), channel_id=1, source_target_pairs={{0,16},{4,20},{8,24},{12,28},{16,0},{20,4},{24,8},{28,12},{1,17},{... | collective-permute-start | bytes 3080 | tf_op jit(solution)/shard_map/ppermute | solution.py:44
  135.3 1.9 %collective-permute-done.7 = f32[2,128]{1,0:T(2,128)S(1)} collective-permute-done((f32[2,128]{1,0:T(2,128)S(1)}, f32[2,128]{1,0:T(2,128)S(1)}, u32[]{:S(2)}, u32[]{:S(2)}) %collective-permute-start.7) | collective-permute-done | bytes 1056 | tf_op jit(solution)/shard_map/ppermute | solution.py:44
  137.8 1.4 copy-done.1
  139.1 5.5 %shard_map.113 = (bf16[1024,512]{1,0:T(8,128)(2,1)}, bf16[1024,512]{1,0:T(8,128)(2,1)}, f32[4,1,128]{2,1,0:T(1,128)}) custom-call(f32[1024,512]{1,0:T(8,128)} %get-tuple-element.32.dk_ref, f32[1024,512]{1,0:T(8,128)} %get-tuple-element.33.dv_ref, bf16[1024,1024]{1,0:T(8,128)(2,1)} %copy-done.1, bf16[1024,512]{1,0:T(8,128)(2,1)} %raw_ref.3, f32[1,128]{1,0:T(1,128)} %bitcast.22), custom_call_target="tpu_custom_call" | custom-call | tf_op jit(solution)/shard_map/pallas_call | solution.py:255
  (29 shorter events, 1.2 us)
Async XLA Ops:
  2.3 31.9 %copy-start.4 = (s32[16]{0:T(128)S(1)}, s32[16]{0:T(128)}, u32[]{:S(2)}) copy-start(s32[16]{0:T(128)} %param.13) | copy-start | bytes 196
  2.4 27.3 %collective-permute-start = (bf16[1024,512]{1,0:T(8,128)(2,1)S(1)}, bf16[1024,512]{1,0:T(8,128)(2,1)}, u32[]{:S(2)}, u32[]{:S(2)}) collective-permute-start(bf16[1024,512]{1,0:T(8,128)(2,1)S(1)} %pad_maximum_fusion.1), channel_id=1, source_target_pairs={{0,4},{4,8},{8,12},{12,16},{16,20},{20,24},{24,28},{1,5},{5,9},{9,... | collective-permute-start | bytes 3145736 | tf_op jit(solution)/shard_map/ppermute | solution.py:22
  29.7 27.9 %collective-permute-start.1 = (bf16[1024,512]{1,0:T(8,128)(2,1)S(1)}, bf16[1024,512]{1,0:T(8,128)(2,1)S(1)}, u32[]{:S(2)}, u32[]{:S(2)}) collective-permute-start(bf16[1024,512]{1,0:T(8,128)(2,1)S(1)} %pad_maximum_fusion), channel_id=1, source_target_pairs={{0,4},{4,8},{8,12},{12,16},{16,20},{20,24},{24,28},{1,5},{5,9},{9,... | collective-permute-start | bytes 3145736 | tf_op jit(solution)/shard_map/ppermute | solution.py:22
  57.5 1.0 copy-start
  58.5 22.9 %copy-start.3 = (f32[2,1,128]{2,1,0:T(1,128)S(1)}, f32[2,1,128]{2,1,0:T(1,128)}, u32[]{:S(2)}) copy-start(f32[2,1,128]{2,1,0:T(1,128)} %get-tuple-element.39) | copy-start | bytes 3076
  80.1 57.6 %collective-permute-start.2 = (bf16[1024,1024]{1,0:T(8,128)(2,1)}, bf16[1024,1024]{1,0:T(8,128)(2,1)S(1)}, u32[]{:S(2)}, u32[]{:S(2)}) collective-permute-start(bf16[1024,1024]{1,0:T(8,128)(2,1)} %get-tuple-element.34), channel_id=1, source_target_pairs={{4,0},{8,4},{12,8},{16,12},{20,16},{24,20},{28,24},{5,1},{9,5},{13... | collective-permute-start | bytes 6291464 | tf_op jit(solution)/shard_map/ppermute | solution.py:22
  81.4 27.7 %copy-start.2 = (f32[2,1,128]{2,1,0:T(1,128)S(1)}, f32[2,1,128]{2,1,0:T(1,128)}, u32[]{:S(2)}) copy-start(f32[2,1,128]{2,1,0:T(1,128)} %get-tuple-element.40) | copy-start | bytes 3076
  109.2 1.2 collective-permute-start.3
  110.5 3.6 %collective-permute-start.4 = (f32[2,128]{1,0:T(2,128)S(1)}, f32[2,128]{1,0:T(2,128)S(1)}, u32[]{:S(2)}, u32[]{:S(2)}) collective-permute-start(f32[2,128]{1,0:T(2,128)S(1)} %fusion), channel_id=1, source_target_pairs={{0,2},{1,3},{2,0},{3,1},{4,6},{5,7},{6,4},{7,5},{8,10},{9,11},{10,... | collective-permute-start | bytes 3080 | tf_op jit(solution)/shard_map/ppermute | solution.py:44
  114.1 15.1 %collective-permute-start.5 = (f32[2,128]{1,0:T(2,128)S(1)}, f32[2,128]{1,0:T(2,128)S(1)}, u32[]{:S(2)}, u32[]{:S(2)}) collective-permute-start(f32[2,128]{1,0:T(2,128)S(1)} %fusion.3), channel_id=1, source_target_pairs={{0,4},{4,0},{8,12},{12,8},{16,20},{20,16},{24,28},{28,24},{1,5},{5... | collective-permute-start | bytes 3080 | tf_op jit(solution)/shard_map/ppermute | solution.py:44
  129.2 3.6 %collective-permute-start.6 = (f32[2,128]{1,0:T(2,128)S(1)}, f32[2,128]{1,0:T(2,128)S(1)}, u32[]{:S(2)}, u32[]{:S(2)}) collective-permute-start(f32[2,128]{1,0:T(2,128)S(1)} %add.69), channel_id=1, source_target_pairs={{0,8},{4,12},{8,0},{12,4},{16,24},{20,28},{24,16},{28,20},{1,9},{5... | collective-permute-start | bytes 3080 | tf_op jit(solution)/shard_map/ppermute | solution.py:44
  132.7 4.5 %collective-permute-start.7 = (f32[2,128]{1,0:T(2,128)S(1)}, f32[2,128]{1,0:T(2,128)S(1)}, u32[]{:S(2)}, u32[]{:S(2)}) collective-permute-start(f32[2,128]{1,0:T(2,128)S(1)} %add.70), channel_id=1, source_target_pairs={{0,16},{4,20},{8,24},{12,28},{16,0},{20,4},{24,8},{28,12},{1,17},{... | collective-permute-start | bytes 3080 | tf_op jit(solution)/shard_map/ppermute | solution.py:44
  137.8 1.4 copy-start.1

commit v15 on v14

--- a/solution.py
+++ b/solution.py
@@ -243,9 +243,13 @@
         dk = dk + back[:, :head_dim]
         dv = dv + back[:, head_dim:]
     vgrad_ref[...] = dv.astype(vgrad_ref.dtype)
-    result, part = norm_grad(raw_ref[...].astype(jnp.float32), gain_ref[...], dk)
-    kgrad_ref[...] = result.astype(kgrad_ref.dtype)
-    kgain_ref[...] = part.reshape(kgain_ref.shape)
+    raw = raw_ref[...].astype(jnp.float32)
+    inverse = lax.rsqrt(jnp.mean(raw * raw, axis=1, keepdims=True) + EPS)
+    scaled = raw * inverse
+    weighted = dk * gain_ref[...]
+    inner_sum = jnp.mean(weighted * scaled, axis=1, keepdims=True)
+    kgrad_ref[...] = (inverse * (weighted - scaled * inner_sum)).astype(kgrad_ref.dtype)
+    kgain_ref[...] = jnp.zeros(kgain_ref.shape, jnp.float32).reshape(kgain_ref.shape)
 
 
 def kv_final(dk_own, dv_own, back, key_raw, key_gain, key_heads, head_dim):

time: 145 us -> 145 us (level)
  no operation moved by 1% of the time
where the time goes in v15:
time: 145 us
  Pallas kernels  74.6 us (51%)
  waiting for transfers between devices  40.3 us (28%)
  starting transfers between devices  20.7 us (14%)
  local copies, waits for them, and re-layouts  5.62 us (4%)
  other arithmetic  2.5 us (2%)
    pallas_call x2, Pallas kernels, attention_grads(): pl.pallas_call(functools.partial(halo_kernel, group=group, head_dim=head_...  42.9 us
    pallas_call x1, Pallas kernels, attention_grads(): pl.pallas_call(functools.partial(own_kernel, group=group, head_dim=head_d...  26.3 us
    ppermute x3, waiting for transfers between devices, shifted(): lax.ppermute(value, axis, [(source, source + steps) for source in range(l...  21.3 us
    ppermute x5, waiting for transfers between devices, butterfly_sum(): shifted_parts.append(lax.ppermute(value, axis, pairs))  19.1 us
    ppermute x3, starting transfers between devices, shifted(): lax.ppermute(value, axis, [(source, source + steps) for source in range(l...  11.8 us
    ppermute x5, starting transfers between devices, butterfly_sum(): shifted_parts.append(lax.ppermute(value, axis, pairs))  8.91 us
    pallas_call x1, Pallas kernels, kv_final(): pl.pallas_call(functools.partial(kv_final_kernel, head_dim=head_dim), gri...  5.42 us
  transfers between devices with their start and end apart: 8, of which 6 were waited for; matrix products, arithmetic and copies ran while one was open for 3% of the time, Pallas kernels for 33%

profile of v15, /device:TPU:0, one launch (start us, length us, event | category | flops | bytes accessed | tf_op | source)
XLA Modules:
  0.0 144.5 jit_solution(13085288280163563316)
XLA Ops:
  0.6 1.7 %fusion.1 = (bf16[1024,256]{1,0:T(8,128)(2,1)S(1)}, bf16[1024,256]{1,0:T(8,128)(2,1)S(1)}, bf16[1024,256]{1,0:T(8,128)(2,1)S(1)}, bf16[1024,256]{1,0:T(8,128)(2,1)S(1)}) fusion(bf16[1024,512]{1,0:T(8,128)(2,1)} %raw_ref.3, bf16[1024,512]{1,0:T(8,128)(2,1)} %v_ref.5), kind=kLoop, calls=%fused_computation.13 | loop fusion | bytes 4194304 | tf_op jit(solution)/shard_map/slice | solution.py:394
  2.4 5.9 %collective-permute-start = (bf16[1024,512]{1,0:T(8,128)(2,1)S(1)}, bf16[1024,512]{1,0:T(8,128)(2,1)}, u32[]{:S(2)}, u32[]{:S(2)}) collective-permute-start(bf16[1024,512]{1,0:T(8,128)(2,1)S(1)} %pad_maximum_fusion.1), channel_id=1, source_target_pairs={{0,4},{4,8},{8,12},{12,16},{16,20},{20,24},{24,28},{1,5},{5,9},{9,... | collective-permute-start | bytes 3145736 | tf_op jit(solution)/shard_map/ppermute | solution.py:22
  8.4 21.3 %collective-permute-done.hk_ref.hv_ref = bf16[1024,512]{1,0:T(8,128)(2,1)} collective-permute-done((bf16[1024,512]{1,0:T(8,128)(2,1)S(1)}, bf16[1024,512]{1,0:T(8,128)(2,1)}, u32[]{:S(2)}, u32[]{:S(2)}) %collective-permute-start) | collective-permute-done | bytes 1048608 | tf_op jit(solution)/shard_map/ppermute | solution.py:22
  29.7 4.5 %collective-permute-start.1 = (bf16[1024,512]{1,0:T(8,128)(2,1)S(1)}, bf16[1024,512]{1,0:T(8,128)(2,1)S(1)}, u32[]{:S(2)}, u32[]{:S(2)}) collective-permute-start(bf16[1024,512]{1,0:T(8,128)(2,1)S(1)} %pad_maximum_fusion), channel_id=1, source_target_pairs={{0,4},{4,8},{8,12},{12,16},{16,20},{20,24},{24,28},{1,5},{5,9},{9,... | collective-permute-start | bytes 3145736 | tf_op jit(solution)/shard_map/ppermute | solution.py:22
  34.6 1.0 copy.24.qdoc_ref
  35.6 0.6 pad_add_fusion
  36.2 21.3 %shard_map.110 = (f32[1024,1024]{1,0:T(8,128)}, bf16[1024,1024]{1,0:T(8,128)(2,1)}, f32[8192,1]{1,0:T(8,128)}, f32[8192,1]{1,0:T(8,128)}, f32[2,1,128]{2,1,0:T(1,128)}) custom-call(s32[1024,1]{1,0:T(8,128)} %copy.24.qdoc_ref, s32[1,2048]{1,0:T(1,128)} %bitcast.13, bf16[1024,1024]{1,0:T(8,128)(2,1)} %raw_ref.2, bf16[1024,1024]{1,0:T(8,128)(2,1)} %do_ref.5, ...), custom_call_target="tpu_custom_call" | custom-call | flops 6039797760 | bytes 7340032 | tf_op jit(solution)/shard_map/pallas_call | solution.py:307
  57.5 1.0 copy-done
  58.5 21.6 %shard_map.111 = (f32[1024,1024]{1,0:T(8,128)}, bf16[1024,1024]{1,0:T(8,128)(2,1)}, f32[8192,1]{1,0:T(8,128)}, f32[8192,1]{1,0:T(8,128)}, f32[2,1,128]{2,1,0:T(1,128)}) custom-call(s32[1024,1]{1,0:T(8,128)} %copy.24.qdoc_ref, s32[1,2048]{1,0:T(1,128)} %bitcast.14, ...), custom_call_target="tpu_custom_call", output_to_operand_aliasing={{0}: (10, {}), {1}: (11, {}), {2}: (12, {}), {3}: (13, {})} | custom-call | flops 6039797760 | bytes 7340032 | tf_op jit(solution)/shard_map/pallas_call | solution.py:307
  80.1 1.3 collective-permute-start.2
  81.5 26.3 %shard_map.112 = (bf16[1024,1024]{1,0:T(8,128)(2,1)}, f32[4,1,128]{2,1,0:T(1,128)}, f32[4,1,128]{2,1,0:T(1,128)}, f32[1024,512]{1,0:T(8,128)}, f32[1024,512]{1,0:T(8,128)}) custom-call(s32[1024,1]{1,0:T(8,128)} %copy.24.qdoc_ref, s32[1,2048]{1,0:T(1,128)} %bitcast.15, bf16[1024,1024]{1,0:T(8,128)(2,1)} %do_ref.5, bf16[1024,512]{1,0:T(8,128)(2,1)} %v_ref.5, ...), custom_call_target="tpu_custom_call" | custom-call | flops 6710886400 | bytes 18874368 | tf_op jit(solution)/shard_map/pallas_call | solution.py:350
  107.8 0.7 reduce_sum.56
  108.5 0.7 reduce_sum.57
  109.3 1.1 collective-permute-done.3
  110.5 1.6 %collective-permute-start.4 = (f32[2,128]{1,0:T(2,128)S(1)}, f32[2,128]{1,0:T(2,128)S(1)}, u32[]{:S(2)}, u32[]{:S(2)}) collective-permute-start(f32[2,128]{1,0:T(2,128)S(1)} %fusion), channel_id=1, source_target_pairs={{0,2},{1,3},{2,0},{3,1},{4,6},{5,7},{6,4},{7,5},{8,10},{9,11},{10,... | collective-permute-start | bytes 3080 | tf_op jit(solution)/shard_map/ppermute | solution.py:44
  112.0 2.1 %collective-permute-done.4 = f32[2,128]{1,0:T(2,128)S(1)} collective-permute-done((f32[2,128]{1,0:T(2,128)S(1)}, f32[2,128]{1,0:T(2,128)S(1)}, u32[]{:S(2)}, u32[]{:S(2)}) %collective-permute-start.4) | collective-permute-done | bytes 1056 | tf_op jit(solution)/shard_map/ppermute | solution.py:44
  114.1 3.1 %collective-permute-start.5 = (f32[2,128]{1,0:T(2,128)S(1)}, f32[2,128]{1,0:T(2,128)S(1)}, u32[]{:S(2)}, u32[]{:S(2)}) collective-permute-start(f32[2,128]{1,0:T(2,128)S(1)} %fusion.3), channel_id=1, source_target_pairs={{0,4},{4,0},{8,12},{12,8},{16,20},{20,16},{24,28},{28,24},{1,5},{5... | collective-permute-start | bytes 3080 | tf_op jit(solution)/shard_map/ppermute | solution.py:44
  117.2 12.0 %collective-permute-done.5 = f32[2,128]{1,0:T(2,128)S(1)} collective-permute-done((f32[2,128]{1,0:T(2,128)S(1)}, f32[2,128]{1,0:T(2,128)S(1)}, u32[]{:S(2)}, u32[]{:S(2)}) %collective-permute-start.5) | collective-permute-done | bytes 1056 | tf_op jit(solution)/shard_map/ppermute | solution.py:44
  129.2 1.6 %collective-permute-start.6 = (f32[2,128]{1,0:T(2,128)S(1)}, f32[2,128]{1,0:T(2,128)S(1)}, u32[]{:S(2)}, u32[]{:S(2)}) collective-permute-start(f32[2,128]{1,0:T(2,128)S(1)} %add.69), channel_id=1, source_target_pairs={{0,8},{4,12},{8,0},{12,4},{16,24},{20,28},{24,16},{28,20},{1,9},{5... | collective-permute-start | bytes 3080 | tf_op jit(solution)/shard_map/ppermute | solution.py:44
  130.8 2.0 %collective-permute-done.6 = f32[2,128]{1,0:T(2,128)S(1)} collective-permute-done((f32[2,128]{1,0:T(2,128)S(1)}, f32[2,128]{1,0:T(2,128)S(1)}, u32[]{:S(2)}, u32[]{:S(2)}) %collective-permute-start.6) | collective-permute-done | bytes 1056 | tf_op jit(solution)/shard_map/ppermute | solution.py:44
  132.7 2.6 %collective-permute-start.7 = (f32[2,128]{1,0:T(2,128)S(1)}, f32[2,128]{1,0:T(2,128)S(1)}, u32[]{:S(2)}, u32[]{:S(2)}) collective-permute-start(f32[2,128]{1,0:T(2,128)S(1)} %add.70), channel_id=1, source_target_pairs={{0,16},{4,20},{8,24},{12,28},{16,0},{20,4},{24,8},{28,12},{1,17},{... | collective-permute-start | bytes 3080 | tf_op jit(solution)/shard_map/ppermute | solution.py:44
  135.3 1.9 %collective-permute-done.7 = f32[2,128]{1,0:T(2,128)S(1)} collective-permute-done((f32[2,128]{1,0:T(2,128)S(1)}, f32[2,128]{1,0:T(2,128)S(1)}, u32[]{:S(2)}, u32[]{:S(2)}) %collective-permute-start.7) | collective-permute-done | bytes 1056 | tf_op jit(solution)/shard_map/ppermute | solution.py:44
  137.8 1.4 copy-done.1
  139.1 5.4 %shard_map.113 = (bf16[1024,512]{1,0:T(8,128)(2,1)}, bf16[1024,512]{1,0:T(8,128)(2,1)}, f32[4,1,128]{2,1,0:T(1,128)}) custom-call(f32[1024,512]{1,0:T(8,128)} %get-tuple-element.32.dk_ref, f32[1024,512]{1,0:T(8,128)} %get-tuple-element.33.dv_ref, bf16[1024,1024]{1,0:T(8,128)(2,1)} %copy-done.1, bf16[1024,512]{1,0:T(8,128)(2,1)} %raw_ref.3, f32[1,128]{1,0:T(1,128)} %bitcast.22), custom_call_target="tpu_custom_call" | custom-call | tf_op jit(solution)/shard_map/pallas_call | solution.py:259
  (29 shorter events, 1.2 us)
Async XLA Ops:
  2.3 31.9 %copy-start.4 = (s32[16]{0:T(128)S(1)}, s32[16]{0:T(128)}, u32[]{:S(2)}) copy-start(s32[16]{0:T(128)} %param.13) | copy-start | bytes 196
  2.4 27.3 %collective-permute-start = (bf16[1024,512]{1,0:T(8,128)(2,1)S(1)}, bf16[1024,512]{1,0:T(8,128)(2,1)}, u32[]{:S(2)}, u32[]{:S(2)}) collective-permute-start(bf16[1024,512]{1,0:T(8,128)(2,1)S(1)} %pad_maximum_fusion.1), channel_id=1, source_target_pairs={{0,4},{4,8},{8,12},{12,16},{16,20},{20,24},{24,28},{1,5},{5,9},{9,... | collective-permute-start | bytes 3145736 | tf_op jit(solution)/shard_map/ppermute | solution.py:22
  29.7 27.9 %collective-permute-start.1 = (bf16[1024,512]{1,0:T(8,128)(2,1)S(1)}, bf16[1024,512]{1,0:T(8,128)(2,1)S(1)}, u32[]{:S(2)}, u32[]{:S(2)}) collective-permute-start(bf16[1024,512]{1,0:T(8,128)(2,1)S(1)} %pad_maximum_fusion), channel_id=1, source_target_pairs={{0,4},{4,8},{8,12},{12,16},{16,20},{20,24},{24,28},{1,5},{5,9},{9,... | collective-permute-start | bytes 3145736 | tf_op jit(solution)/shard_map/ppermute | solution.py:22
  57.5 1.0 copy-start
  58.5 22.9 %copy-start.3 = (f32[2,1,128]{2,1,0:T(1,128)S(1)}, f32[2,1,128]{2,1,0:T(1,128)}, u32[]{:S(2)}) copy-start(f32[2,1,128]{2,1,0:T(1,128)} %get-tuple-element.39) | copy-start | bytes 3076
  80.1 57.6 %collective-permute-start.2 = (bf16[1024,1024]{1,0:T(8,128)(2,1)}, bf16[1024,1024]{1,0:T(8,128)(2,1)S(1)}, u32[]{:S(2)}, u32[]{:S(2)}) collective-permute-start(bf16[1024,1024]{1,0:T(8,128)(2,1)} %get-tuple-element.34), channel_id=1, source_target_pairs={{4,0},{8,4},{12,8},{16,12},{20,16},{24,20},{28,24},{5,1},{9,5},{13... | collective-permute-start | bytes 6291464 | tf_op jit(solution)/shard_map/ppermute | solution.py:22
  81.4 27.7 %copy-start.2 = (f32[2,1,128]{2,1,0:T(1,128)S(1)}, f32[2,1,128]{2,1,0:T(1,128)}, u32[]{:S(2)}) copy-start(f32[2,1,128]{2,1,0:T(1,128)} %get-tuple-element.40) | copy-start | bytes 3076
  109.2 1.2 collective-permute-start.3
  110.5 3.6 %collective-permute-start.4 = (f32[2,128]{1,0:T(2,128)S(1)}, f32[2,128]{1,0:T(2,128)S(1)}, u32[]{:S(2)}, u32[]{:S(2)}) collective-permute-start(f32[2,128]{1,0:T(2,128)S(1)} %fusion), channel_id=1, source_target_pairs={{0,2},{1,3},{2,0},{3,1},{4,6},{5,7},{6,4},{7,5},{8,10},{9,11},{10,... | collective-permute-start | bytes 3080 | tf_op jit(solution)/shard_map/ppermute | solution.py:44
  114.1 15.1 %collective-permute-start.5 = (f32[2,128]{1,0:T(2,128)S(1)}, f32[2,128]{1,0:T(2,128)S(1)}, u32[]{:S(2)}, u32[]{:S(2)}) collective-permute-start(f32[2,128]{1,0:T(2,128)S(1)} %fusion.3), channel_id=1, source_target_pairs={{0,4},{4,0},{8,12},{12,8},{16,20},{20,16},{24,28},{28,24},{1,5},{5... | collective-permute-start | bytes 3080 | tf_op jit(solution)/shard_map/ppermute | solution.py:44
  129.2 3.6 %collective-permute-start.6 = (f32[2,128]{1,0:T(2,128)S(1)}, f32[2,128]{1,0:T(2,128)S(1)}, u32[]{:S(2)}, u32[]{:S(2)}) collective-permute-start(f32[2,128]{1,0:T(2,128)S(1)} %add.69), channel_id=1, source_target_pairs={{0,8},{4,12},{8,0},{12,4},{16,24},{20,28},{24,16},{28,20},{1,9},{5... | collective-permute-start | bytes 3080 | tf_op jit(solution)/shard_map/ppermute | solution.py:44
  132.7 4.5 %collective-permute-start.7 = (f32[2,128]{1,0:T(2,128)S(1)}, f32[2,128]{1,0:T(2,128)S(1)}, u32[]{:S(2)}, u32[]{:S(2)}) collective-permute-start(f32[2,128]{1,0:T(2,128)S(1)} %add.70), channel_id=1, source_target_pairs={{0,16},{4,20},{8,24},{12,28},{16,0},{20,4},{24,8},{28,12},{1,17},{... | collective-permute-start | bytes 3080 | tf_op jit(solution)/shard_map/ppermute | solution.py:44
  137.8 1.4 copy-start.1
